TPU v7x, 32 devices: a whole 2x2x4 slice. The times are simulated.
32 devices in a mesh: chk: 4 (over z), var: 8 (over y, x, core).
Axes of the slice: x: 2, y: 2, z: 4, core: 2. Of those that a mesh axis runs over, the one named last changes fastest.
Arguments:
- tile_bits: int32 [4, 8, 2, 4096], P('chk', 'var'), may hold values 0 or 1
- tile_pos: int32 [4, 8, 2, 2], P('chk', 'var'), may hold values from 0 to 3, as said below
- tile_count: int32 [4, 8], P('chk', 'var'), may hold values from 1 to 2, as said below
- edge_weight: float32 [4, 8, 2, 4096], P('chk', 'var'), may hold values from 0.1 to 1.9
- syndrome: int32 [1024, 128], P('chk'), may hold values 0 or 1
- channel_prior: float32 [2048], P('var'), may hold values from 1 to 6
- out_cot: float32 [2048, 128], P('var'), may hold values from -0.6 to 0.6
Outputs:
- marginals: float32 [2048, 128], P('var')
- weight_grad: float32 [4, 8, 2, 4096], P('chk', 'var')
- prior_grad: float32 [2048], P('var')
Inputs may be any that keep to these rules, and one draw needn't show every extreme that they name: `tile_pos`: in each grid cell the 2 slots name distinct tiles of its 4 x 4 block grid, check block first. `tile_count`: some grid cell uses all 2 slots.
All inputs are finite; a program needn't handle non-finite values. No bound on the sum of `tile_bits` or of `syndrome` on one device may be relied on, other than what follows from the above.
Results may differ from a plain program's by a relative error of at most 0.0003.
Values sent between devices are 32-bit elements; how exact they have to be, the bound alone decides.
No kernel may reach another device: no remote copies, remote signals or barrier semaphores. Data moves between devices by JAX's collectives and lax.ppermute only.
A program may use at most 256 MiB of HBM per device.

v0:
```python
import functools

import jax
import jax.numpy as jnp
from jax import lax
from jax.experimental import pallas as pl
from jax.sharding import PartitionSpec as P

TILE = 64
ITERS = 2


DAMP = 0.97
EXACT = lax.Precision.HIGHEST
F32 = jnp.float32
UNROLL = 4


def linear_both(values, axis):
    length = values.shape[axis]
    pieces = [lax.slice_in_dim(values, index, index + 1, axis=axis) for index in range(length)]
    ones = jnp.ones_like(pieces[0])
    prefix = [ones]
    for index in range(length - 1):
        prefix.append(prefix[-1] * pieces[index])
    suffix = [ones]
    for index in range(length - 1, 0, -1):
        suffix.append(suffix[-1] * pieces[index])
    suffix = suffix[::-1]
    whole = prefix[-1] * pieces[-1]
    return (jnp.concatenate(prefix, axis=axis), jnp.concatenate(suffix, axis=axis), whole)


def exclusive_both(values, axis):
    length = values.shape[axis]
    if length < 16 or length % 8 != 0:
        return linear_both(values, axis)
    shape = values.shape
    split = values.reshape(shape[:axis] + (length // 8, 8) + shape[axis + 1 :])
    inner_before, inner_after, group_whole = linear_both(split, axis + 1)
    outer_before, outer_after, whole = exclusive_both(group_whole, axis)
    before = (inner_before * outer_before).reshape(shape)
    after = (inner_after * outer_after).reshape(shape)
    whole = whole.reshape(shape[:axis] + (1,) + shape[axis + 1 :])
    return (before, after, whole)


def device_tables(bits, positions, count, check_blocks, column_blocks):
    slot_total = bits.shape[0]
    slots = jnp.arange(slot_total, dtype=jnp.int32)
    live = slots < count
    edge = jnp.where(live[:, None], bits, 0).astype(jnp.float32).reshape(slot_total, TILE, TILE)
    row_hot = (positions[:, 0:1] == jnp.arange(check_blocks, dtype=jnp.int32)[None, :]).astype(
        jnp.float32
    )
    col_hot = (positions[:, 1:2] == jnp.arange(column_blocks, dtype=jnp.int32)[None, :]).astype(
        jnp.float32
    )
    same_row = (positions[:, None, 0] == positions[None, :, 0]) & (slots[:, None] != slots[None, :])
    return (edge, row_hot, col_hot, same_row)


def _spread_row(ref, c, shape):
    return jnp.broadcast_to(ref[0, pl.ds(c, 1), :], shape)


def _fwd_products_kernel(has_u, *refs):
    if has_u:
        spread_ref, u_ref, em_ref, ba_ref, whole_ref, h_scr = refs
    else:
        spread_ref, em_ref, ba_ref, whole_ref, h_scr = refs
    n_c = em_ref.shape[1]
    shape = em_ref.shape[2:]

    def forward(c, carry):
        m = _spread_row(spread_ref, c, shape)
        if has_u:
            m = m - u_ref[0, c]
        h = jnp.where(em_ref[0, c] > 0, jnp.tanh(0.5 * m), 1.0)
        h_scr[c] = h
        ba_ref[0, c] = carry
        return carry * h

    whole = lax.fori_loop(0, n_c, forward, jnp.ones(shape, F32), unroll=UNROLL)
    whole_ref[0] = whole

    def backward(i, carry):
        c = n_c - 1 - i
        ba_ref[0, c] = ba_ref[0, c] * carry
        return carry * h_scr[c]

    lax.fori_loop(0, n_c, backward, jnp.ones(shape, F32), unroll=UNROLL)


def _fwd_messages_kernel(ba_ref, f_ref, ew_ref, u_ref, col_ref):
    n_c = ba_ref.shape[1]
    f = f_ref[0]

    def body(c, carry):
        x = ba_ref[0, c] * f
        u = ew_ref[0, c] * jnp.log((1.0 + DAMP * x) / (1.0 - DAMP * x))
        u_ref[0, c] = u
        col_ref[0, pl.ds(c, 1), :] = jnp.sum(u, axis=0, keepdims=True)
        return carry

    lax.fori_loop(0, n_c, body, 0, unroll=UNROLL)


def _bwd_messages_kernel(has_next, has_acc, *refs):
    refs = list(refs)
    gsp_ref = refs.pop(0)
    gm_ref = refs.pop(0) if has_next else None
    ba_ref, f_ref, ew_ref = refs[:3]
    refs = refs[3:]
    acc_ref = refs.pop(0) if has_acc else None
    gw_ref, gba_ref, d1_ref = refs
    n_c = ba_ref.shape[1]
    shape = ba_ref.shape[2:]
    f = f_ref[0]

    def body(c, total):
        gu = _spread_row(gsp_ref, c, shape)
        if has_next:
            gu = gu - gm_ref[0, c]
        ba = ba_ref[0, c]
        x = ba * f
        low = 1.0 - DAMP * x
        high = 1.0 + DAMP * x
        gw = gu * jnp.log(high / low)
        if has_acc:
            gw = gw + acc_ref[0, c]
        gw_ref[0, c] = gw
        gx = gu * ew_ref[0, c] * ((2.0 * DAMP) / (low * high))
        gba_ref[0, c] = gx * f
        return total + gx * ba

    d1_ref[0] = lax.fori_loop(0, n_c, body, jnp.zeros(shape, F32), unroll=UNROLL)


def _bwd_products_kernel(has_u, emit_gm, *refs):
    refs = list(refs)
    spread_ref = refs.pop(0)
    u_ref = refs.pop(0) if has_u else None
    em_ref, gba_ref, gwh_ref = refs[:3]
    refs = refs[3:]
    gm_ref = refs.pop(0) if emit_gm else None
    col_ref, h_scr, p_scr, q_scr = refs
    n_c = em_ref.shape[1]
    shape = em_ref.shape[2:]
    gwh = gwh_ref[0]

    def forward(c, carry):
        prod, grad = carry
        m = _spread_row(spread_ref, c, shape)
        if has_u:
            m = m - u_ref[0, c]
        h = jnp.where(em_ref[0, c] > 0, jnp.tanh(0.5 * m), 1.0)
        h_scr[c] = h
        p_scr[c] = prod
        q_scr[c] = grad
        return (prod * h, grad * h + gba_ref[0, c] * prod)

    ones = jnp.ones(shape, F32)
    zeros = jnp.zeros(shape, F32)
    lax.fori_loop(0, n_c, forward, (ones, zeros), unroll=UNROLL)

    def backward(i, carry):
        prod, grad = carry
        c = n_c - 1 - i
        h = h_scr[c]
        before = p_scr[c]
        gh = q_scr[c] * prod + before * (grad + gwh * prod)
        gm = jnp.where(em_ref[0, c] > 0, gh * (0.5 * (1.0 - h * h)), 0.0)
        if emit_gm:
            gm_ref[0, c] = gm
        col_ref[0, pl.ds(c, 1), :] = jnp.sum(gm, axis=0, keepdims=True)
        return (prod * h, grad * h + gba_ref[0, c] * prod)

    lax.fori_loop(0, n_c, backward, (ones, zeros), unroll=UNROLL)


def _big_spec(shape):
    return pl.BlockSpec((1,) + shape[1:], lambda k: (k, 0, 0, 0))


def _small_spec(shape):
    return pl.BlockSpec((1,) + shape[1:], lambda k: (k, 0, 0))


def _call(kernel, inputs, outputs, scratch=()):
    in_specs = [_big_spec(a.shape) if a.ndim == 4 else _small_spec(a.shape) for a in inputs]
    out_specs = [_big_spec(o.shape) if len(o.shape) == 4 else _small_spec(o.shape) for o in outputs]
    return pl.pallas_call(
        kernel,
        grid=(inputs[0].shape[0],),
        in_specs=in_specs,
        out_specs=out_specs,
        out_shape=list(outputs),
        scratch_shapes=list(scratch),
    )(*inputs)


def fwd_products(spread, u, em):
    k, c, r, s = em.shape
    has_u = u is not None
    inputs = [spread] + ([u] if has_u else []) + [em]
    outs = [jax.ShapeDtypeStruct(em.shape, F32), jax.ShapeDtypeStruct((k, r, s), F32)]
    from jax.experimental.pallas import tpu as pltpu

    return _call(
        functools.partial(_fwd_products_kernel, has_u),
        inputs,
        outs,
        [pltpu.VMEM((c, r, s), F32)],
    )


def fwd_messages(ba, f, ew):
    k, c, r, s = ba.shape
    outs = [jax.ShapeDtypeStruct(ba.shape, F32), jax.ShapeDtypeStruct((k, c, s), F32)]
    return _call(_fwd_messages_kernel, [ba, f, ew], outs)


def bwd_messages(gsp, gm, ba, f, ew, acc):
    k, c, r, s = ba.shape
    has_next = gm is not None
    has_acc = acc is not None
    inputs = [gsp] + ([gm] if has_next else []) + [ba, f, ew] + ([acc] if has_acc else [])
    outs = [
        jax.ShapeDtypeStruct(ba.shape, F32),
        jax.ShapeDtypeStruct(ba.shape, F32),
        jax.ShapeDtypeStruct((k, r, s), F32),
    ]
    return _call(functools.partial(_bwd_messages_kernel, has_next, has_acc), inputs, outs)


def bwd_products(spread, u, em, gba, gwh, emit_gm):
    from jax.experimental.pallas import tpu as pltpu

    k, c, r, s = em.shape
    has_u = u is not None
    inputs = [spread] + ([u] if has_u else []) + [em, gba, gwh]
    outs = ([jax.ShapeDtypeStruct(em.shape, F32)] if emit_gm else []) + [
        jax.ShapeDtypeStruct((k, c, s), F32)
    ]
    results = _call(
        functools.partial(_bwd_products_kernel, has_u, emit_gm),
        inputs,
        outs,
        [pltpu.VMEM((c, r, s), F32) for _ in range(3)],
    )
    if emit_gm:
        return results[0], results[1]
    return None, results[0]


def combine(whole, row_hot, same_row):
    slots = whole.shape[0]
    blocks = row_hot.shape[1]
    ones = jnp.ones_like(whole[0])
    rows = []
    for block in range(blocks):
        value = ones
        for k in range(slots):
            value = value * jnp.where(row_hot[k, block] > 0, whole[k], 1.0)
        rows.append(value)
    others_here = []
    for k in range(slots):
        value = ones
        for other in range(slots):
            if other != k:
                value = value * jnp.where(same_row[k, other], whole[other], 1.0)
        others_here.append(value)
    return jnp.stack(rows), jnp.stack(others_here)


def others_forward(rows, check_blocks):
    own = lax.axis_index("var")
    piece = lax.all_gather(rows, "var", axis=0, tiled=True)
    indices = jnp.arange(piece.shape[0], dtype=jnp.int32)
    keep = indices // check_blocks != own
    parts = []
    for block in range(check_blocks):
        pick = (keep & (indices % check_blocks == block))[:, None, None]
        parts.append(jnp.prod(jnp.where(pick, piece, 1.0), axis=0))
    return jnp.stack(parts), piece


def others_backward(row_piece, grads, check_blocks):
    own = lax.axis_index("var")
    grad_piece = lax.all_gather(grads, "var", axis=0, tiled=True)
    indices = jnp.arange(row_piece.shape[0], dtype=jnp.int32)
    keep = indices // check_blocks != own
    new_sums = []
    for block in range(check_blocks):
        pick = (keep & (indices % check_blocks == block))[:, None, None]
        factors = jnp.where(pick, row_piece, 1.0)
        weights = jnp.where(pick, grad_piece, 0.0)
        before, after, whole = exclusive_both(factors, 0)
        new_sums.append(jnp.sum(weights * before * after, axis=0))
    return jnp.stack(new_sums)


def body(tile_bits, tile_pos, tile_count, edge_weight, syndrome, channel_prior, out_cot):
    slot_total = tile_bits.shape[2]
    shots = syndrome.shape[1]
    check_blocks = syndrome.shape[0] // TILE
    column_blocks = channel_prior.shape[0] // TILE
    edge, row_hot, col_hot, same_row = device_tables(
        tile_bits[0, 0], tile_pos[0, 0], tile_count[0, 0], check_blocks, column_blocks
    )
    weight = edge_weight[0, 0].reshape(slot_total, TILE, TILE)
    edge_t = jnp.swapaxes(edge, 1, 2)
    dense = (slot_total, TILE, TILE, shots)
    em = jnp.broadcast_to(edge_t[..., None], dense)
    ew = jnp.broadcast_to((edge_t * jnp.swapaxes(weight, 1, 2))[..., None], dense)
    sign_dev = (1.0 - 2.0 * syndrome.astype(jnp.float32)).reshape(check_blocks, TILE, shots)
    sign_slot = jnp.einsum("kc,crs->krs", row_hot, sign_dev, precision=EXACT)
    prior_dev = channel_prior.reshape(column_blocks, TILE)
    prior_slot = jnp.einsum("kv,vc->kc", col_hot, prior_dev, precision=EXACT)
    spread = jnp.broadcast_to(prior_slot[:, :, None], (slot_total, TILE, shots))
    u = None
    saved = []
    total = None
    for step in range(ITERS):
        ba, whole = fwd_products(spread, u, em)
        rows, others_here = combine(whole, row_hot, same_row)
        others, piece = others_forward(rows, check_blocks)
        others_slot = jnp.einsum("kc,crs->krs", row_hot, others, precision=EXACT)
        factor = sign_slot * others_here * others_slot
        saved.append((spread, u, ba, whole, factor, others_here, others_slot, piece))
        u, colsum = fwd_messages(ba, factor, ew)
        column = jnp.einsum("kv,kcs->vcs", col_hot, colsum, precision=EXACT)
        total = prior_dev[:, :, None] + lax.psum(column, "chk")
        spread = jnp.einsum("kv,vcs->kcs", col_hot, total, precision=EXACT)
    marginals = total.reshape(column_blocks * TILE, shots)

    grad_total = out_cot.reshape(column_blocks, TILE, shots)
    prior_grad = jnp.zeros((column_blocks, TILE), jnp.float32)
    grad_m = None
    acc = None
    for step in reversed(range(ITERS)):
        spread_t, u_prev, ba, whole, factor, others_here, others_slot, piece = saved[step]
        prior_grad = prior_grad + jnp.sum(grad_total, axis=2)
        grad_spread = jnp.einsum("kv,vcs->kcs", col_hot, grad_total, precision=EXACT)
        acc, grad_ba, grad_factor = bwd_messages(grad_spread, grad_m, ba, factor, ew, acc)
        grad_here = grad_factor * sign_slot * others_slot
        grad_slot = grad_factor * sign_slot * others_here
        grad_others = jnp.einsum("kc,krs->crs", row_hot, grad_slot, precision=EXACT)
        grad_rows = others_backward(piece, grad_others, check_blocks)
        unused, pull = jax.vjp(lambda w: combine(w, row_hot, same_row), whole)
        grad_whole = pull((grad_rows, grad_here))[0]
        grad_m, colsum = bwd_products(spread_t, u_prev, em, grad_ba, grad_whole, step > 0)
        grad_total = lax.psum(
            jnp.einsum("kv,kcs->vcs", col_hot, colsum, precision=EXACT), "chk"
        )
    prior_grad = prior_grad + jnp.sum(grad_total, axis=2)
    weight_grad = edge * jnp.swapaxes(jnp.sum(acc, axis=3), 1, 2)
    return (
        marginals,
        weight_grad.reshape(1, 1, slot_total, TILE * TILE),
        prior_grad.reshape(column_blocks * TILE),
    )


def solution(mesh):
    placed = (
        P("chk", "var", None, None),
        P("chk", "var", None, None),
        P("chk", "var"),
        P("chk", "var", None, None),
        P("chk", None),
        P("var"),
        P("var", None),
    )
    return jax.shard_map(
        body,
        mesh=mesh,
        in_specs=placed,
        out_specs=(P("var", None), P("chk", "var", None, None), P("var")),
        check_vma=False,
    )
```

profile of v0, /device:TPU:0, one launch (start us, length us, event | category | flops | bytes accessed | tf_op | source)
XLA Modules:
  0.0 331.7 jit_solution(18247947640970426469)
XLA Ops:
  19.7 2.6 broadcast_in_dim.249.refs_1_.refs_2_
  22.3 4.5 %shard_map.94 = (f32[2,64,64,128]{3,2,1,0:T(8,128)}, f32[2,64,128]{2,1,0:T(8,128)}) custom-call(f32[2,64,128]{2,1,0:T(8,128)} %broadcast_in_dim.246.refs_0_, f32[2,64,64,128]{3,2,1,0:T(8,128)} %broadcast_in_dim.249.refs_1_.refs_2_), custom_call_target="tpu_custom_call" | custom-call | tf_op jit(solution)/shard_map/pallas_call | solution.py:193
  26.8 2.1 slice_select_fusion.7
  35.8 1.9 slice_select_fusion.6
  38.1 17.8 %all-gather.5.cloned.1.call-done = f32[32,64,128]{2,1,0:T(8,128)} async-done(((f32[4,64,128]{2,1,0:T(8,128)}), f32[32,64,128]{2,1,0:T(8,128)}) %all-gather.5.cloned.1.call-update) | async-done | bytes 1048592 | tf_op jit(solution)/shard_map/all_gather | solution.py:279
  55.9 1.7 fusion.128
  63.6 2.7 broadcast_in_dim.256.ew_ref.refs_3_.refs_4_
  66.3 5.9 %shard_map.95 = (f32[2,64,64,128]{3,2,1,0:T(8,128)}, f32[2,64,128]{2,1,0:T(8,128)}) custom-call(f32[2,64,64,128]{3,2,1,0:T(8,128)} %get-tuple-element.18.ba_ref.refs_2_, f32[2,64,128]{2,1,0:T(8,128)} %multiply_multiply_fusion.1.f_ref.refs_3_, f32[2,64,64,128]{3,2,1,0:T(8,128)} %broadcast_in_dim.256.ew_ref.refs_3_.refs_4_), custom_call_target="tpu_custom_call" | custom-call | tf_op jit(solution)/shard_map/pallas_call | solution.py:193
  72.2 1.9 fusion.72
  76.1 32.6 %all-reduce.25.cloned.1.call-done = f32[4,64,128]{2,0,1:T(4,128)} async-done(((f32[4,64,128]{2,0,1:T(4,128)}), f32[4,64,128]{2,0,1:T(4,128)}) %all-reduce.25.cloned.1.call-update) | async-done | bytes 131088 | tf_op jit(solution)/shard_map/psum | solution.py:334
  108.7 1.2 fusion.60
  110.6 5.8 %shard_map.96 = (f32[2,64,64,128]{3,2,1,0:T(8,128)}, f32[2,64,128]{2,1,0:T(8,128)}) custom-call(f32[2,64,128]{2,1,0:T(8,128)} %copy.94.refs_0_, f32[2,64,64,128]{3,2,1,0:T(8,128)} %get-tuple-element.21.refs_1_, f32[2,64,64,128]{3,2,1,0:T(8,128)} %broadcast_in_dim.249.refs_1_.refs_2_), custom_call_target="tpu_custom_call" | custom-call | tf_op jit(solution)/shard_map/pallas_call | solution.py:193
  116.3 2.0 slice_select_fusion.5
  122.0 1.3 broadcast_multiply_fusion.4
  123.3 2.4 broadcast_multiply_fusion.6
  125.7 1.2 slice_select_fusion.4
  126.8 15.5 %all-gather.7.cloned.1.call-done = f32[32,64,128]{2,1,0:T(8,128)} async-done(((f32[4,64,128]{2,1,0:T(8,128)}), f32[32,64,128]{2,1,0:T(8,128)}) %all-gather.7.cloned.1.call-update) | async-done | bytes 1048592 | tf_op jit(solution)/shard_map/all_gather | solution.py:279
  142.4 1.8 fusion.124
  151.6 7.0 %shard_map.98 = (f32[2,64,64,128]{3,2,1,0:T(8,128)}, f32[2,64,64,128]{3,2,1,0:T(8,128)}, f32[2,64,128]{2,1,0:T(8,128)}) custom-call(f32[2,64,128]{2,1,0:T(8,128)} %copy.100.refs_0_, f32[2,64,64,128]{3,2,1,0:T(8,128)} %get-tuple-element.22.ba_ref.refs_1_, f32[2,64,128]{2,1,0:T(8,128)} %multiply_multiply_fusion.f_ref.refs_2_, ...), custom_call_target="tpu_custom_call" | custom-call | tf_op jit(solution)/shard_map/pallas_call | solution.py:193
  159.5 1.8 slice_select_fusion.3
  162.7 1.8 fusion.39
  164.5 2.4 broadcast_multiply_fusion.15
  167.0 2.4 broadcast_multiply_fusion.14
  172.1 1.1 broadcast_multiply_fusion.11
  173.3 1.1 broadcast_multiply_fusion.13
  175.5 1.1 broadcast_multiply_fusion.12
  177.8 8.2 %all-gather.9.cloned.1.call-done = f32[32,64,128]{2,1,0:T(8,128)} async-done(((f32[4,64,128]{2,1,0:T(8,128)}), f32[32,64,128]{2,1,0:T(8,128)}) %all-gather.9.cloned.1.call-update) | async-done | bytes 1048592 | tf_op jit(solution)/shard_map/all_gather | solution.py:291
  186.0 4.4 %fusion.7 = (f32[64,128]{1,0:T(8,128)S(1)}, f32[64,128]{1,0:T(8,128)S(1)}, f32[64,128]{1,0:T(8,128)S(1)}, f32[64,128]{1,0:T(8,128)S(1)}) fusion(f32[4,8,64,128]{3,2,1,0:T(8,128)} %broadcast_multiply_fusion.14, f32[4,8,64,128]{3,2,1,0:T(8,128)} %broadcast_multiply_fusion.15, f32[32,64,128]{2,1,0:T(8,128)} %all-gather.9.cloned.1.call-done, ...), kind=kLoop, calls=%fused_computation.22 | loop fusion | flops 4161536 | bytes 9568384 | tf_op jit(solution)/shard_map/reduce_sum | solution.py:300
  191.1 8.2 %shard_map.99 = (f32[2,64,64,128]{3,2,1,0:T(8,128)}, f32[2,64,128]{2,1,0:T(8,128)}) custom-call(f32[2,64,128]{2,1,0:T(8,128)} %copy.94.refs_0_, f32[2,64,64,128]{3,2,1,0:T(8,128)} %get-tuple-element.21.refs_1_, f32[2,64,64,128]{3,2,1,0:T(8,128)} %broadcast_in_dim.249.refs_1_.refs_2_, f32[2,64,64,128]{3,2,1,0:T(8,128)} %get-tuple-element.25.refs_3_, ...), custom_call_target="tpu_custom_call" | custom-call | tf_op jit(solution)/shard_map/pallas_call | solution.py:193
  199.3 1.9 fusion.66
  202.8 33.0 %all-reduce.27.cloned.1.call-done = f32[4,64,128]{2,0,1:T(4,128)} async-done(((f32[4,64,128]{2,0,1:T(4,128)}), f32[4,64,128]{2,0,1:T(4,128)}) %all-reduce.27.cloned.1.call-update) | async-done | bytes 131088 | tf_op jit(solution)/shard_map/psum | solution.py:354
  235.8 1.2 fusion.99
  237.7 9.4 %shard_map.100 = (f32[2,64,64,128]{3,2,1,0:T(8,128)}, f32[2,64,64,128]{3,2,1,0:T(8,128)}, f32[2,64,128]{2,1,0:T(8,128)}) custom-call(f32[2,64,128]{2,1,0:T(8,128)} %copy.107.refs_0_, f32[2,64,64,128]{3,2,1,0:T(8,128)} %get-tuple-element.28.refs_1_, f32[2,64,64,128]{3,2,1,0:T(8,128)} %get-tuple-element.18.ba_ref.refs_2_, ...), custom_call_target="tpu_custom_call" | custom-call | tf_op jit(solution)/shard_map/pallas_call | solution.py:193
  247.1 1.5 copy_multiply_fusion.1
  249.7 2.0 broadcast_multiply_fusion
  251.7 5.9 %shard_map.97 = (f32[2,64,64,128]{3,2,1,0:T(8,128)}, f32[2,64,128]{2,1,0:T(8,128)}) custom-call(f32[2,64,64,128]{3,2,1,0:T(8,128)} %get-tuple-element.22.ba_ref.refs_1_, f32[2,64,128]{2,1,0:T(8,128)} %multiply_multiply_fusion.f_ref.refs_2_, f32[2,64,64,128]{3,2,1,0:T(8,128)} %broadcast_in_dim.256.ew_ref.refs_3_.refs_4_), custom_call_target="tpu_custom_call" | custom-call | tf_op jit(solution)/shard_map/pallas_call | solution.py:193
  257.7 2.0 fusion.70
  259.7 2.5 broadcast_multiply_fusion.1
  262.3 2.4 broadcast_multiply_fusion.7
  264.6 1.1 broadcast_multiply_fusion.3
  265.8 1.1 broadcast_multiply_fusion.5
  266.9 1.8 slice_select_fusion.1
  268.7 4.2 %all-gather.11.cloned.1.call-done = f32[32,64,128]{2,1,0:T(8,128)} async-done(((f32[4,64,128]{2,1,0:T(8,128)}), f32[32,64,128]{2,1,0:T(8,128)}) %all-gather.11.cloned.1.call-update) | async-done | bytes 1048592 | tf_op jit(solution)/shard_map/all_gather | solution.py:291
  273.0 3.5 %fusion.3 = (f32[64,128]{1,0:T(8,128)S(1)}, f32[64,128]{1,0:T(8,128)S(1)}, f32[64,128]{1,0:T(8,128)S(1)}, f32[64,128]{1,0:T(8,128)S(1)}) fusion(f32[4,8,64,128]{3,2,1,0:T(8,128)S(1)} %copy-done, f32[4,8,64,128]{3,2,1,0:T(8,128)} %broadcast_multiply_fusion.7, f32[32,64,128]{2,1,0:T(8,128)} %all-gather.11.cloned.1.call-done, ...), kind=kLoop, calls=%fused_computation.10 | loop fusion | flops 4161536 | bytes 9568384 | tf_op jit(solution)/shard_map/reduce_sum | solution.py:300
  277.2 6.5 %shard_map.101 = f32[2,64,128]{2,1,0:T(8,128)} custom-call(f32[2,64,128]{2,1,0:T(8,128)} %broadcast_in_dim.246.refs_0_, f32[2,64,64,128]{3,2,1,0:T(8,128)} %broadcast_in_dim.249.refs_1_.refs_2_, f32[2,64,64,128]{3,2,1,0:T(8,128)} %get-tuple-element.31.refs_2_, f32[2,64,128]{2,1,0:T(8,128)} %pad_add_fusion.refs_3_), custom_call_target="tpu_custom_call" | custom-call | tf_op jit(solution)/shard_map/pallas_call | solution.py:193
  283.8 1.9 fusion.62
  286.1 3.4 %reduce_sum.136 = f32[2,64,64]{2,1,0:T(8,128)S(1)} reduce(f32[2,64,64,128]{3,2,1,0:T(8,128)} %get-tuple-element.30, f32[]{:T(128)} %constant.135.clone.1), dimensions={3}, to_apply=%region_15.16 | reduce | flops 1040384 | bytes 4227076 | tf_op jit(solution)/shard_map/reduce_sum | solution.py:358
  290.3 31.0 %all-reduce.29.cloned.1.call-done = (f32[4,64,128]{2,0,1:T(4,128)}, f32[4,64,128]{2,0,1:T(4,128)}) async-done(((f32[4,64,128]{2,0,1:T(4,128)}, f32[4,64,128]{2,0,1:T(4,128)}), (f32[4,64,128]{2,0,1:T(4,128)}, f32[4,64,128]{2,0,1:T(4,128)})) %all-reduce.29.cloned.1.call-update) | async-done | bytes 262160 | tf_op jit(solution)/shard_map/psum | solution.py:334
  (379 shorter events, 49.1 us)
Async XLA Ops:
  7.2 48.7 %all-gather.5.cloned.1.call-start = ((), (), s32[]{:S(2)}) async-start(), calls=%async_computation | async-start | bytes 1179648 | tf_op jit(solution)/shard_map/all_gather | solution.py:279
  9.0 10.7 %copy-start.90 = (pred[2]{0:T(512)(128)(4,1)}, pred[2]{0:T(512)(128)(4,1)S(1)}, u32[]{:S(2)}) copy-start(pred[2]{0:T(512)(128)(4,1)S(1)} %iota_compare_fusion.15) | copy-start | bytes 10
  19.7 9.9 %copy-start.36 = (f32[256,128]{1,0:T(8,128)S(1)}, f32[256,128]{1,0:T(8,128)}, u32[]{:S(2)}) copy-start(f32[256,128]{1,0:T(8,128)} %param.13) | copy-start | bytes 393220
  22.3 15.5 %copy-start.54 = (s32[256,128]{1,0:T(8,128)S(1)}, s32[256,128]{1,0:T(8,128)}, u32[]{:S(2)}) copy-start(s32[256,128]{1,0:T(8,128)} %param.11) | copy-start | bytes 393220
  29.5 79.1 %all-reduce.25.cloned.1.call-start = ((), (), s32[]{:S(2)}) async-start(), calls=%async_computation.1 | async-start | bytes 262144 | tf_op jit(solution)/shard_map/psum | solution.py:334
  62.3 9.9 %copy-start.12 = (f32[4,8,64,128]{3,2,1,0:T(8,128)}, f32[4,8,64,128]{3,2,1,0:T(8,128)S(1)}, u32[]{:S(2)}) copy-start(f32[4,8,64,128]{3,2,1,0:T(8,128)S(1)} %get-tuple-element.155) | copy-start | bytes 3145732
  66.3 42.4 %copy-start.52 = (f32[4,64]{0,1:T(8,128)S(1)}, f32[4,64]{0,1:T(8,128)}, u32[]{:S(2)}) copy-start(f32[4,64]{0,1:T(8,128)} %copy.87) | copy-start | bytes 3076
  74.1 68.3 %all-gather.7.cloned.1.call-start = ((), (), s32[]{:S(2)}) async-start(), calls=%async_computation.2 | async-start | bytes 1179648 | tf_op jit(solution)/shard_map/all_gather | solution.py:279
  110.5 8.6 %copy-start.40 = (f32[4,1,64,128]{3,2,1,0:T(8,128)S(1)}, f32[4,1,64,128]{3,2,1,0:T(8,128)}, u32[]{:S(2)}) copy-start(f32[4,1,64,128]{3,2,1,0:T(8,128)} %get-tuple-element.158) | copy-start | bytes 393220
  110.5 9.3 %copy-start.41 = (f32[4,1,64,128]{3,2,1,0:T(8,128)S(1)}, f32[4,1,64,128]{3,2,1,0:T(8,128)}, u32[]{:S(2)}) copy-start(f32[4,1,64,128]{3,2,1,0:T(8,128)} %get-tuple-element.156) | copy-start | bytes 393220
  110.5 9.9 %copy-start.71 = (f32[1,1,64,128]{3,2,1,0:T(8,128)S(1)}, f32[1,1,64,128]{3,2,1,0:T(8,128)}, u32[]{:S(2)}) copy-start(f32[1,1,64,128]{3,2,1,0:T(8,128)} %get-tuple-element.220) | copy-start | bytes 98308
  110.5 9.9 %copy-start.72 = (f32[1,1,64,128]{3,2,1,0:T(8,128)S(1)}, f32[1,1,64,128]{3,2,1,0:T(8,128)}, u32[]{:S(2)}) copy-start(f32[1,1,64,128]{3,2,1,0:T(8,128)} %get-tuple-element.223) | copy-start | bytes 98308
  110.5 9.9 %copy-start.73 = (f32[1,1,64,128]{3,2,1,0:T(8,128)S(1)}, f32[1,1,64,128]{3,2,1,0:T(8,128)}, u32[]{:S(2)}) copy-start(f32[1,1,64,128]{3,2,1,0:T(8,128)} %get-tuple-element.224) | copy-start | bytes 98308
  110.5 9.9 %copy-start.80 = (f32[1,1,64,128]{3,2,1,0:T(8,128)S(1)}, f32[1,1,64,128]{3,2,1,0:T(8,128)}, u32[]{:S(2)}) copy-start(f32[1,1,64,128]{3,2,1,0:T(8,128)} %get-tuple-element.214) | copy-start | bytes 98308
  110.5 9.9 %copy-start.81 = (f32[1,1,64,128]{3,2,1,0:T(8,128)S(1)}, f32[1,1,64,128]{3,2,1,0:T(8,128)}, u32[]{:S(2)}) copy-start(f32[1,1,64,128]{3,2,1,0:T(8,128)} %get-tuple-element.217) | copy-start | bytes 98308
  110.6 9.9 %copy-start.82 = (f32[1,1,64,128]{3,2,1,0:T(8,128)S(1)}, f32[1,1,64,128]{3,2,1,0:T(8,128)}, u32[]{:S(2)}) copy-start(f32[1,1,64,128]{3,2,1,0:T(8,128)} %get-tuple-element.218) | copy-start | bytes 98308
  110.6 11.3 %copy-start.21 = (f32[4,8,64,128]{3,2,1,0:T(8,128)S(1)}, f32[4,8,64,128]{3,2,1,0:T(8,128)}, u32[]{:S(2)}) copy-start(f32[4,8,64,128]{3,2,1,0:T(8,128)} %copy-done.20) | copy-start | bytes 3145732
  119.1 66.9 %all-gather.9.cloned.1.call-start = ((), (), s32[]{:S(2)}) async-start(), calls=%async_computation.3 | async-start | bytes 1179648 | tf_op jit(solution)/shard_map/all_gather | solution.py:291
  159.5 9.9 %copy-start.59 = (f32[1,1,64,128]{3,2,1,0:T(8,128)S(1)}, f32[1,1,64,128]{3,2,1,0:T(8,128)}, u32[]{:S(2)}) copy-start(f32[1,1,64,128]{3,2,1,0:T(8,128)} %get-tuple-element.219) | copy-start | bytes 98308
  162.4 73.4 %all-reduce.27.cloned.1.call-start = ((), (), s32[]{:S(2)}) async-start(), calls=%async_computation.4 | async-start | bytes 262144 | tf_op jit(solution)/shard_map/psum | solution.py:354
  162.5 7.7 %copy-start.32 = (f32[4,8,64,128]{3,2,1,0:T(8,128)S(1)}, f32[4,8,64,128]{3,2,1,0:T(8,128)}, u32[]{:S(2)}) copy-start(f32[4,8,64,128]{3,2,1,0:T(8,128)} %copy-done.31) | copy-start | bytes 3145732
  162.5 7.7 %copy-start.62 = (f32[1,1,64,128]{3,2,1,0:T(8,128)S(1)}, f32[1,1,64,128]{3,2,1,0:T(8,128)}, u32[]{:S(2)}) copy-start(f32[1,1,64,128]{3,2,1,0:T(8,128)} %get-tuple-element.213) | copy-start | bytes 98308
  162.6 7.7 %copy-start.63 = (f32[1,1,64,128]{3,2,1,0:T(8,128)S(1)}, f32[1,1,64,128]{3,2,1,0:T(8,128)}, u32[]{:S(2)}) copy-start(f32[1,1,64,128]{3,2,1,0:T(8,128)} %get-tuple-element.215) | copy-start | bytes 98308
  162.6 7.7 %copy-start.64 = (f32[1,1,64,128]{3,2,1,0:T(8,128)S(1)}, f32[1,1,64,128]{3,2,1,0:T(8,128)}, u32[]{:S(2)}) copy-start(f32[1,1,64,128]{3,2,1,0:T(8,128)} %get-tuple-element.216) | copy-start | bytes 98308
  162.6 7.7 %copy-start.65 = (f32[1,1,64,128]{3,2,1,0:T(8,128)S(1)}, f32[1,1,64,128]{3,2,1,0:T(8,128)}, u32[]{:S(2)}) copy-start(f32[1,1,64,128]{3,2,1,0:T(8,128)} %get-tuple-element.246) | copy-start | bytes 98308
  162.6 7.7 %copy-start.66 = (f32[1,1,64,128]{3,2,1,0:T(8,128)S(1)}, f32[1,1,64,128]{3,2,1,0:T(8,128)}, u32[]{:S(2)}) copy-start(f32[1,1,64,128]{3,2,1,0:T(8,128)} %get-tuple-element.249) | copy-start | bytes 98308
  162.6 7.7 %copy-start.67 = (f32[1,1,64,128]{3,2,1,0:T(8,128)S(1)}, f32[1,1,64,128]{3,2,1,0:T(8,128)}, u32[]{:S(2)}) copy-start(f32[1,1,64,128]{3,2,1,0:T(8,128)} %get-tuple-element.250) | copy-start | bytes 98308
  162.6 7.7 %copy-start.74 = (f32[1,1,64,128]{3,2,1,0:T(8,128)S(1)}, f32[1,1,64,128]{3,2,1,0:T(8,128)}, u32[]{:S(2)}) copy-start(f32[1,1,64,128]{3,2,1,0:T(8,128)} %get-tuple-element.240) | copy-start | bytes 98308
  162.6 7.7 %copy-start.75 = (f32[1,1,64,128]{3,2,1,0:T(8,128)S(1)}, f32[1,1,64,128]{3,2,1,0:T(8,128)}, u32[]{:S(2)}) copy-start(f32[1,1,64,128]{3,2,1,0:T(8,128)} %get-tuple-element.243) | copy-start | bytes 98308
  162.6 7.7 %copy-start.76 = (f32[1,1,64,128]{3,2,1,0:T(8,128)S(1)}, f32[1,1,64,128]{3,2,1,0:T(8,128)}, u32[]{:S(2)}) copy-start(f32[1,1,64,128]{3,2,1,0:T(8,128)} %get-tuple-element.244) | copy-start | bytes 98308
  162.6 7.7 %copy-start.83 = (f32[1,1,64,128]{3,2,1,0:T(8,128)S(1)}, f32[1,1,64,128]{3,2,1,0:T(8,128)}, u32[]{:S(2)}) copy-start(f32[1,1,64,128]{3,2,1,0:T(8,128)} %get-tuple-element.252) | copy-start | bytes 98308
  162.6 7.7 %copy-start.84 = (f32[1,1,64,128]{3,2,1,0:T(8,128)S(1)}, f32[1,1,64,128]{3,2,1,0:T(8,128)}, u32[]{:S(2)}) copy-start(f32[1,1,64,128]{3,2,1,0:T(8,128)} %get-tuple-element.255) | copy-start | bytes 98308
  162.7 7.7 %copy-start.85 = (f32[1,1,64,128]{3,2,1,0:T(8,128)S(1)}, f32[1,1,64,128]{3,2,1,0:T(8,128)}, u32[]{:S(2)}) copy-start(f32[1,1,64,128]{3,2,1,0:T(8,128)} %get-tuple-element.256) | copy-start | bytes 98308
  162.7 8.4 %copy-start.3 = (f32[4,8,64,128]{3,2,1,0:T(8,128)S(1)}, f32[4,8,64,128]{3,2,1,0:T(8,128)}, u32[]{:S(2)}) copy-start(f32[4,8,64,128]{3,2,1,0:T(8,128)} %copy-done.2) | copy-start | bytes 3145732
  164.5 7.6 %copy-start.11 = (f32[4,8,64,128]{3,2,1,0:T(8,128)S(1)}, f32[4,8,64,128]{3,2,1,0:T(8,128)}, u32[]{:S(2)}) copy-start(f32[4,8,64,128]{3,2,1,0:T(8,128)} %copy-done.10) | copy-start | bytes 3145732
  201.2 71.7 %all-gather.11.cloned.1.call-start = ((), (), s32[]{:S(2)}) async-start(), calls=%async_computation.5 | async-start | bytes 1179648 | tf_op jit(solution)/shard_map/all_gather | solution.py:291
  237.7 9.4 %copy-start.43 = (f32[1,64,128]{2,1,0:T(8,128)S(1)}, f32[1,64,128]{2,1,0:T(8,128)}, u32[]{:S(2)}) copy-start(f32[1,64,128]{2,1,0:T(8,128)} %get-tuple-element.296) | copy-start | bytes 98308
  237.7 9.4 %copy-start.46 = (f32[1,64,128]{2,1,0:T(8,128)S(1)}, f32[1,64,128]{2,1,0:T(8,128)}, u32[]{:S(2)}) copy-start(f32[1,64,128]{2,1,0:T(8,128)} %slice_select_fusion.6) | copy-start | bytes 98308
  237.7 12.0 %copy-start.25 = (f32[4,8,64,128]{3,2,1,0:T(8,128)S(1)}, f32[4,8,64,128]{3,2,1,0:T(8,128)}, u32[]{:S(2)}) copy-start(f32[4,8,64,128]{3,2,1,0:T(8,128)} %constant_dynamic-update-slice_fusion.120) | copy-start | bytes 3145732
  249.7 71.7 %all-reduce.29.cloned.1.call-start = ((), (), s32[]{:S(2)}) async-start(), calls=%async_computation.6 | async-start | bytes 524288 | tf_op jit(solution)/shard_map/psum | solution.py:334
  251.7 10.5 %copy-start.37 = (f32[4,64,128]{2,1,0:T(8,128)S(1)}, f32[4,64,128]{2,1,0:T(8,128)}, u32[]{:S(2)}) copy-start(f32[4,64,128]{2,1,0:T(8,128)} %get-tuple-element.314) | copy-start | bytes 393220
  257.7 8.1 %copy-start.16 = (f32[4,8,64,128]{3,2,1,0:T(8,128)S(1)}, f32[4,8,64,128]{3,2,1,0:T(8,128)}, u32[]{:S(2)}) copy-start(f32[4,8,64,128]{3,2,1,0:T(8,128)} %copy-done.15) | copy-start | bytes 3145732
  257.7 8.1 %copy-start.39 = (f32[4,64,128]{2,1,0:T(8,128)S(1)}, f32[4,64,128]{2,1,0:T(8,128)}, u32[]{:S(2)}) copy-start(f32[4,64,128]{2,1,0:T(8,128)} %get-tuple-element.301) | copy-start | bytes 393220
  259.7 13.2 %copy-start = (f32[4,8,64,128]{3,2,1,0:T(8,128)S(1)}, f32[4,8,64,128]{3,2,1,0:T(8,128)}, u32[]{:S(2)}) copy-start(f32[4,8,64,128]{3,2,1,0:T(8,128)} %broadcast_multiply_fusion.6) | copy-start | bytes 3145732
  259.7 13.2 %copy-start.89 = (pred[32]{0:T(512)(128)(4,1)S(1)}, pred[32]{0:T(512)(128)(4,1)}, u32[]{:S(2)}) copy-start(pred[32]{0:T(512)(128)(4,1)} %get-tuple-element.329) | copy-start | bytes 100
  268.7 7.8 %copy-start.33 = (f32[2,64,128]{2,1,0:T(8,128)S(1)}, f32[2,64,128]{2,1,0:T(8,128)}, u32[]{:S(2)}) copy-start(f32[2,64,128]{2,1,0:T(8,128)} %get-tuple-element.19) | copy-start | bytes 196612
  277.2 8.6 %copy-start.35 = (f32[4,64,128]{2,0,1:T(4,128)S(1)}, f32[4,64,128]{2,0,1:T(4,128)}, u32[]{:S(2)}) copy-start(f32[4,64,128]{2,0,1:T(4,128)} %all-reduce.27.cloned.1.call-done) | copy-start | bytes 393220
  283.8 37.6 %copy-start.53 = (f32[4,64]{0,1:T(8,128)S(1)}, f32[4,64]{0,1:T(8,128)}, u32[]{:S(2)}) copy-start(f32[4,64]{0,1:T(8,128)} %copy.87) | copy-start | bytes 3076
  (51 other events, 200.0 us)
Sparse Core Ops, SparseCore 0:
  29.6 26.1 all-gather.4
  74.2 34.4 all-reduce.24
  119.2 23.1 all-gather.6
  162.5 23.4 all-gather.8
  201.4 34.4 all-reduce.26
  249.8 23.1 all-gather.10
  285.8 35.5 all-reduce.28
where the time goes:
time: 333 us; the launch traced here: 332 us
  waiting for transfers between devices  142 us (43%)
  other arithmetic  76 us (23%)
  Pallas kernels  53.2 us (16%)
  local copies, waits for them, and re-layouts  25.6 us (8%)
  between operations  21.7 us (7%)
  matrix products  12.4 us (4%)
    psum x2, waiting for transfers between devices, body(): total = prior_dev[:, :, None] + lax.psum(column, 'chk')  63.6 us
    pallas_call x8, Pallas kernels, _call(): pl.pallas_call(kernel, grid=(inputs[0].shape[0],), in_specs=in_specs, out...  53.2 us
    all_gather x2, waiting for transfers between devices, others_forward(): piece = lax.all_gather(rows, 'var', axis=0, tiled=True)  33.3 us
    psum x1, waiting for transfers between devices, body(): lax.psum(jnp.einsum('kv,kcs->vcs', col_hot, colsum, precision=EXACT), 'chk')  33 us
    mul x11, other arithmetic, exclusive_both(): before = (inner_before * outer_before).reshape(shape)  16.2 us
    all_gather x2, waiting for transfers between devices, others_backward(): grad_piece = lax.all_gather(grads, 'var', axis=0, tiled=True)  12.5 us
    mul x9, other arithmetic, exclusive_both(): after = (inner_after * outer_after).reshape(shape)  12.3 us
    select_n x6, other arithmetic, combine(): value = value * jnp.where(same_row[k, other], whole[other], 1.0)  10.9 us
  transfers between devices with their start and end apart: 7, of which 7 were waited for; matrix products, arithmetic and copies ran while one was open for 16% of the time, Pallas kernels for 2%

commit v1 on v0

--- a/solution.py
+++ b/solution.py
@@ -274,7 +274,54 @@
     return jnp.stack(rows), jnp.stack(others_here)
 
 
-def others_forward(rows, check_blocks):
+def _power_of_two(n):
+    return n > 1 and (n & (n - 1)) == 0
+
+
+def _swap(value, axis, n, step):
+    perm = [(j, j ^ (1 << step)) for j in range(n)]
+    return lax.ppermute(value, axis, perm)
+
+
+def checks_total(values, n):
+    if not _power_of_two(n):
+        return lax.psum(values, "chk")
+    step = 0
+    while (1 << step) < n:
+        values = values + _swap(values, "chk", n, step)
+        step += 1
+    return values
+
+
+def others_forward(rows, check_blocks, n):
+    if not _power_of_two(n):
+        return others_gather(rows, check_blocks)
+    full = rows
+    excl = jnp.ones_like(rows)
+    trail = []
+    step = 0
+    while (1 << step) < n:
+        other = _swap(full, "var", n, step)
+        trail.append((full, excl, other))
+        excl = excl * other
+        full = full * other
+        step += 1
+    return excl, trail
+
+
+def others_backward(trail, grads, check_blocks, n):
+    if not _power_of_two(n):
+        return others_scatter(trail, grads, check_blocks)
+    spread = grads
+    target = jnp.zeros_like(grads)
+    for step, (full, excl, other) in enumerate(trail):
+        other_spread = _swap(spread, "var", n, step)
+        target = target * other + excl * other_spread
+        spread = spread * other + other_spread * full
+    return target
+
+
+def others_gather(rows, check_blocks):
     own = lax.axis_index("var")
     piece = lax.all_gather(rows, "var", axis=0, tiled=True)
     indices = jnp.arange(piece.shape[0], dtype=jnp.int32)
@@ -286,7 +333,7 @@
     return jnp.stack(parts), piece
 
 
-def others_backward(row_piece, grads, check_blocks):
+def others_scatter(row_piece, grads, check_blocks):
     own = lax.axis_index("var")
     grad_piece = lax.all_gather(grads, "var", axis=0, tiled=True)
     indices = jnp.arange(row_piece.shape[0], dtype=jnp.int32)
@@ -301,7 +348,7 @@
     return jnp.stack(new_sums)
 
 
-def body(tile_bits, tile_pos, tile_count, edge_weight, syndrome, channel_prior, out_cot):
+def body(n_chk, n_var, tile_bits, tile_pos, tile_count, edge_weight, syndrome, channel_prior, out_cot):
     slot_total = tile_bits.shape[2]
     shots = syndrome.shape[1]
     check_blocks = syndrome.shape[0] // TILE
@@ -325,13 +372,13 @@
     for step in range(ITERS):
         ba, whole = fwd_products(spread, u, em)
         rows, others_here = combine(whole, row_hot, same_row)
-        others, piece = others_forward(rows, check_blocks)
+        others, piece = others_forward(rows, check_blocks, n_var)
         others_slot = jnp.einsum("kc,crs->krs", row_hot, others, precision=EXACT)
         factor = sign_slot * others_here * others_slot
         saved.append((spread, u, ba, whole, factor, others_here, others_slot, piece))
         u, colsum = fwd_messages(ba, factor, ew)
         column = jnp.einsum("kv,kcs->vcs", col_hot, colsum, precision=EXACT)
-        total = prior_dev[:, :, None] + lax.psum(column, "chk")
+        total = prior_dev[:, :, None] + checks_total(column, n_chk)
         spread = jnp.einsum("kv,vcs->kcs", col_hot, total, precision=EXACT)
     marginals = total.reshape(column_blocks * TILE, shots)
 
@@ -347,12 +394,12 @@
         grad_here = grad_factor * sign_slot * others_slot
         grad_slot = grad_factor * sign_slot * others_here
         grad_others = jnp.einsum("kc,krs->crs", row_hot, grad_slot, precision=EXACT)
-        grad_rows = others_backward(piece, grad_others, check_blocks)
+        grad_rows = others_backward(piece, grad_others, check_blocks, n_var)
         unused, pull = jax.vjp(lambda w: combine(w, row_hot, same_row), whole)
         grad_whole = pull((grad_rows, grad_here))[0]
         grad_m, colsum = bwd_products(spread_t, u_prev, em, grad_ba, grad_whole, step > 0)
-        grad_total = lax.psum(
-            jnp.einsum("kv,kcs->vcs", col_hot, colsum, precision=EXACT), "chk"
+        grad_total = checks_total(
+            jnp.einsum("kv,kcs->vcs", col_hot, colsum, precision=EXACT), n_chk
         )
     prior_grad = prior_grad + jnp.sum(grad_total, axis=2)
     weight_grad = edge * jnp.swapaxes(jnp.sum(acc, axis=3), 1, 2)
@@ -374,7 +421,7 @@
         P("var", None),
     )
     return jax.shard_map(
-        body,
+        functools.partial(body, mesh.shape["chk"], mesh.shape["var"]),
         mesh=mesh,
         in_specs=placed,
         out_specs=(P("var", None), P("chk", "var", None, None), P("var")),

time: 333 us -> 171 us (0.51)
  waiting for transfers between devices: 142 us -> 41.2 us
  other arithmetic: 76 us -> 18 us
  starting transfers between devices: 0.47 us -> 29.2 us
  between operations: 21.7 us -> 6.69 us
  local copies, waits for them, and re-layouts: 25.6 us -> 14.6 us
  matrix products: 12.4 us -> 6.85 us
    psum x3 -> x0, waiting for transfers between devices: 96.6 us -> none  [the longest x2 63.6 us: body(): total = prior_dev[:, :, None] + lax.psum(column, 'chk')]
    all_gather x4 -> x0, waiting for transfers between devices: 45.7 us -> none  [the longest x2 33.3 us: others_forward(): piece = lax.all_gather(rows, 'var', axis=0, tiled=True)]
    ppermute x0 -> x20, waiting for transfers between devices: none -> 41.2 us  [_swap(): return lax.ppermute(value, axis, perm)]
    ppermute x0 -> x20, starting transfers between devices: none -> 29.2 us  [_swap(): return lax.ppermute(value, axis, perm)]
    mul x20 -> x6, other arithmetic: 28.5 us -> 0.13 us  [the longest x4 0.08 us: others_forward(): full = full * other]
    reduce_sum x2 -> x0, other arithmetic: 7.89 us -> none  [others_backward(): new_sums.append(jnp.sum(weights * before * after, axis=0))]
    unnamed x224 -> x10, local copies, waits for them, and re-layouts: 7.65 us -> 0.02 us
    slice x8 -> x0, other arithmetic: 5.99 us -> none  [linear_both(): lax.slice_in_dim(values, index, index + 1, axis=axis)]
  transfers between devices with their start and end apart: 7 -> 20, of which waited for: 7 -> 16; matrix products, arithmetic and copies ran while one was open for 16% -> 9% of each run, Pallas kernels for 2% -> 7%
where the time goes in v1:
time: 171 us; the launch traced here: 170 us
  Pallas kernels  53.1 us (31%)
  waiting for transfers between devices  41.2 us (24%)
  starting transfers between devices  29.2 us (17%)
  other arithmetic  18 us (11%)
  local copies, waits for them, and re-layouts  14.6 us (9%)
  matrix products  6.85 us (4%)
  between operations  6.69 us (4%)
    pallas_call x8, Pallas kernels, _call(): pl.pallas_call(kernel, grid=(inputs[0].shape[0],), in_specs=in_specs, out...  53.1 us
    ppermute x20, waiting for transfers between devices, _swap(): return lax.ppermute(value, axis, perm)  41.2 us
    ppermute x20, starting transfers between devices, _swap(): return lax.ppermute(value, axis, perm)  29.2 us
    select_n x6, other arithmetic, combine(): value = value * jnp.where(same_row[k, other], whole[other], 1.0)  8.29 us
  transfers between devices with their start and end apart: 20, of which 16 were waited for; matrix products, arithmetic and copies ran while one was open for 9% of the time, Pallas kernels for 7%

profile of v1, /device:TPU:0, one launch (start us, length us, event | category | flops | bytes accessed | tf_op | source)
XLA Modules:
  0.0 169.6 jit_solution(15874389139905694873)
XLA Ops:
  12.3 2.6 %broadcast_in_dim.121.refs_1_.refs_2_ = f32[2,64,64,128]{3,2,1,0:T(8,128)} broadcast(f32[2,64,64]{2,1,0:T(8,128)S(1)} %get-tuple-element.38), dimensions={0,1,2} | broadcast | bytes 4227072 | tf_op jit(solution)/shard_map/broadcast_in_dim | solution.py:362
  14.9 4.4 %shard_map.94 = (f32[2,64,64,128]{3,2,1,0:T(8,128)}, f32[2,64,128]{2,1,0:T(8,128)}) custom-call(f32[2,64,128]{2,1,0:T(8,128)} %broadcast_in_dim.118.refs_0_, f32[2,64,64,128]{3,2,1,0:T(8,128)} %broadcast_in_dim.121.refs_1_.refs_2_), custom_call_target="tpu_custom_call" | custom-call | tf_op jit(solution)/shard_map/pallas_call | solution.py:193
  19.3 1.4 slice_select_fusion.7
  22.3 2.9 %collective-permute-start.1 = (f32[4,64,128]{2,1,0:T(8,128)S(1)}, f32[4,64,128]{2,1,0:T(8,128)S(1)}, u32[]{:S(2)}, u32[]{:S(2)}) collective-permute-start(f32[4,64,128]{2,1,0:T(8,128)S(1)} %fusion.56), channel_id=1, source_target_pairs={{0,2},{1,3},{2,0},{3,1},{4,6},{5,7},{6,4},{7,5},{8,10},{9,11},{10,... | collective-permute-start | bytes 393224 | tf_op jit(solution)/shard_map/ppermute | solution.py:283
  25.6 3.5 %collective-permute-done.1 = f32[4,64,128]{2,1,0:T(8,128)S(1)} collective-permute-done((f32[4,64,128]{2,1,0:T(8,128)S(1)}, f32[4,64,128]{2,1,0:T(8,128)S(1)}, u32[]{:S(2)}, u32[]{:S(2)}) %collective-permute-start.1) | collective-permute-done | bytes 131104 | tf_op jit(solution)/shard_map/ppermute | solution.py:283
  29.1 1.8 %collective-permute-start.2 = (f32[4,64,128]{2,1,0:T(8,128)S(1)}, f32[4,64,128]{2,1,0:T(8,128)S(1)}, u32[]{:S(2)}, u32[]{:S(2)}) collective-permute-start(f32[4,64,128]{2,1,0:T(8,128)S(1)} %fusion.63), channel_id=1, source_target_pairs={{0,4},{1,5},{2,6},{3,7},{4,0},{5,1},{6,2},{7,3},{8,12},{9,13},{10,... | collective-permute-start | bytes 393224 | tf_op jit(solution)/shard_map/ppermute | solution.py:283
  30.9 1.4 slice_select_fusion.6
  32.3 1.9 %collective-permute-done.2 = f32[4,64,128]{2,1,0:T(8,128)S(1)} collective-permute-done((f32[4,64,128]{2,1,0:T(8,128)S(1)}, f32[4,64,128]{2,1,0:T(8,128)S(1)}, u32[]{:S(2)}, u32[]{:S(2)}) %collective-permute-start.2) | collective-permute-done | bytes 131104 | tf_op jit(solution)/shard_map/ppermute | solution.py:283
  35.2 2.6 %broadcast_in_dim.123.ew_ref.refs_3_.refs_4_ = f32[2,64,64,128]{3,2,1,0:T(8,128)} broadcast(f32[2,64,64]{2,1,0:T(8,128)S(1)} %get-tuple-element.37), dimensions={0,1,2} | broadcast | bytes 4227072 | tf_op jit(solution)/shard_map/broadcast_in_dim | solution.py:363
  37.8 5.9 %shard_map.95 = (f32[2,64,64,128]{3,2,1,0:T(8,128)}, f32[2,64,128]{2,1,0:T(8,128)}) custom-call(f32[2,64,64,128]{3,2,1,0:T(8,128)} %get-tuple-element.18.ba_ref.refs_2_, f32[2,64,128]{2,1,0:T(8,128)} %multiply_multiply_fusion.1.f_ref.refs_3_, f32[2,64,64,128]{3,2,1,0:T(8,128)} %broadcast_in_dim.123.ew_ref.refs_3_.refs_4_), custom_call_target="tpu_custom_call" | custom-call | tf_op jit(solution)/shard_map/pallas_call | solution.py:193
  43.7 1.2 fusion.21
  44.9 1.8 %collective-permute-start.3 = (f32[4,64,128]{2,0,1:T(4,128)S(1)}, f32[4,64,128]{2,0,1:T(4,128)S(1)}, u32[]{:S(2)}, u32[]{:S(2)}) collective-permute-start(f32[4,64,128]{2,0,1:T(4,128)S(1)} %fusion.21), channel_id=1, source_target_pairs={{0,8},{8,0},{16,24},{24,16},{1,9},{9,1},{17,25},{25,17},{2,10},{10... | collective-permute-start | bytes 393224 | tf_op jit(solution)/shard_map/ppermute | solution.py:283
  46.7 3.2 %collective-permute-done.3 = f32[4,64,128]{2,0,1:T(4,128)S(1)} collective-permute-done((f32[4,64,128]{2,0,1:T(4,128)S(1)}, f32[4,64,128]{2,0,1:T(4,128)S(1)}, u32[]{:S(2)}, u32[]{:S(2)}) %collective-permute-start.3) | collective-permute-done | bytes 131104 | tf_op jit(solution)/shard_map/ppermute | solution.py:283
  50.0 3.2 %collective-permute-start.4 = (f32[4,64,128]{2,0,1:T(4,128)S(1)}, f32[4,64,128]{2,0,1:T(4,128)S(1)}, u32[]{:S(2)}, u32[]{:S(2)}) collective-permute-start(f32[4,64,128]{2,0,1:T(4,128)S(1)} %add.120), channel_id=1, source_target_pairs={{0,16},{8,24},{16,0},{24,8},{1,17},{9,25},{17,1},{25,9},{2,18},{10... | collective-permute-start | bytes 393224 | tf_op jit(solution)/shard_map/ppermute | solution.py:283
  53.3 4.3 %collective-permute-done.4 = f32[4,64,128]{2,0,1:T(4,128)S(1)} collective-permute-done((f32[4,64,128]{2,0,1:T(4,128)S(1)}, f32[4,64,128]{2,0,1:T(4,128)S(1)}, u32[]{:S(2)}, u32[]{:S(2)}) %collective-permute-start.4) | collective-permute-done | bytes 131104 | tf_op jit(solution)/shard_map/ppermute | solution.py:283
  58.5 5.7 %shard_map.96 = (f32[2,64,64,128]{3,2,1,0:T(8,128)}, f32[2,64,128]{2,1,0:T(8,128)}) custom-call(f32[2,64,128]{2,1,0:T(8,128)} %copy.109.refs_0_, f32[2,64,64,128]{3,2,1,0:T(8,128)} %get-tuple-element.21.refs_1_, f32[2,64,64,128]{3,2,1,0:T(8,128)} %broadcast_in_dim.121.refs_1_.refs_2_), custom_call_target="tpu_custom_call" | custom-call | tf_op jit(solution)/shard_map/pallas_call | solution.py:193
  64.2 1.4 slice_select_fusion.5
  65.7 1.3 collective-permute-done.5
  67.1 1.6 collective-permute-start.6
  69.6 3.1 %collective-permute-done.6 = f32[4,64,128]{2,1,0:T(8,128)S(1)} collective-permute-done((f32[4,64,128]{2,1,0:T(8,128)S(1)}, f32[4,64,128]{2,1,0:T(8,128)S(1)}, u32[]{:S(2)}, u32[]{:S(2)}) %collective-permute-start.6) | collective-permute-done | bytes 131104 | tf_op jit(solution)/shard_map/ppermute | solution.py:283
  72.7 1.6 collective-permute-start.7
  74.3 1.4 slice_select_fusion.4
  75.7 2.0 %collective-permute-done.7 = f32[4,64,128]{2,1,0:T(8,128)S(1)} collective-permute-done((f32[4,64,128]{2,1,0:T(8,128)S(1)}, f32[4,64,128]{2,1,0:T(8,128)S(1)}, u32[]{:S(2)}, u32[]{:S(2)}) %collective-permute-start.7) | collective-permute-done | bytes 131104 | tf_op jit(solution)/shard_map/ppermute | solution.py:283
  78.8 6.9 %shard_map.98 = (f32[2,64,64,128]{3,2,1,0:T(8,128)}, f32[2,64,64,128]{3,2,1,0:T(8,128)}, f32[2,64,128]{2,1,0:T(8,128)}) custom-call(f32[2,64,128]{2,1,0:T(8,128)} %copy.116.refs_0_, f32[2,64,64,128]{3,2,1,0:T(8,128)} %get-tuple-element.22.ba_ref.refs_1_, f32[2,64,128]{2,1,0:T(8,128)} %multiply_multiply_fusion.f_ref.refs_2_, ...), custom_call_target="tpu_custom_call" | custom-call | tf_op jit(solution)/shard_map/pallas_call | solution.py:193
  87.0 1.3 collective-permute-done.10
  88.4 1.6 collective-permute-start.11
  89.9 4.1 %collective-permute-done.11 = f32[4,64,128]{2,1,0:T(8,128)S(1)} collective-permute-done((f32[4,64,128]{2,1,0:T(8,128)S(1)}, f32[4,64,128]{2,1,0:T(8,128)S(1)}, u32[]{:S(2)}, u32[]{:S(2)}) %collective-permute-start.11) | collective-permute-done | bytes 131104 | tf_op jit(solution)/shard_map/ppermute | solution.py:283
  94.0 1.6 collective-permute-start.12
  95.6 1.3 slice_select_fusion.3
  96.9 2.1 %collective-permute-done.12 = f32[4,64,128]{2,1,0:T(8,128)S(1)} collective-permute-done((f32[4,64,128]{2,1,0:T(8,128)S(1)}, f32[4,64,128]{2,1,0:T(8,128)S(1)}, u32[]{:S(2)}, u32[]{:S(2)}) %collective-permute-start.12) | collective-permute-done | bytes 131104 | tf_op jit(solution)/shard_map/ppermute | solution.py:283
  99.9 8.3 %shard_map.99 = (f32[2,64,64,128]{3,2,1,0:T(8,128)}, f32[2,64,128]{2,1,0:T(8,128)}) custom-call(f32[2,64,128]{2,1,0:T(8,128)} %copy.109.refs_0_, f32[2,64,64,128]{3,2,1,0:T(8,128)} %get-tuple-element.21.refs_1_, f32[2,64,64,128]{3,2,1,0:T(8,128)} %broadcast_in_dim.121.refs_1_.refs_2_, f32[2,64,64,128]{3,2,1,0:T(8,128)} %get-tuple-element.25.refs_3_, ...), custom_call_target="tpu_custom_call" | custom-call | tf_op jit(solution)/shard_map/pallas_call | solution.py:193
  108.2 1.2 fusion.15
  110.2 4.2 %collective-permute-done.13 = f32[4,64,128]{2,0,1:T(4,128)S(1)} collective-permute-done((f32[4,64,128]{2,0,1:T(4,128)S(1)}, f32[4,64,128]{2,0,1:T(4,128)S(1)}, u32[]{:S(2)}, u32[]{:S(2)}) %collective-permute-start.13) | collective-permute-done | bytes 131104 | tf_op jit(solution)/shard_map/ppermute | solution.py:283
  114.4 2.2 %collective-permute-start.14 = (f32[4,64,128]{2,0,1:T(4,128)S(1)}, f32[4,64,128]{2,0,1:T(4,128)S(1)}, u32[]{:S(2)}, u32[]{:S(2)}) collective-permute-start(f32[4,64,128]{2,0,1:T(4,128)S(1)} %add.131), channel_id=1, source_target_pairs={{0,16},{8,24},{16,0},{24,8},{1,17},{9,25},{17,1},{25,9},{2,18},{10... | collective-permute-start | bytes 393224 | tf_op jit(solution)/shard_map/ppermute | solution.py:283
  116.6 5.9 %shard_map.97 = (f32[2,64,64,128]{3,2,1,0:T(8,128)}, f32[2,64,128]{2,1,0:T(8,128)}) custom-call(f32[2,64,64,128]{3,2,1,0:T(8,128)} %get-tuple-element.22.ba_ref.refs_1_, f32[2,64,128]{2,1,0:T(8,128)} %multiply_multiply_fusion.f_ref.refs_2_, f32[2,64,64,128]{3,2,1,0:T(8,128)} %broadcast_in_dim.123.ew_ref.refs_3_.refs_4_), custom_call_target="tpu_custom_call" | custom-call | tf_op jit(solution)/shard_map/pallas_call | solution.py:193
  123.5 9.4 %shard_map.100 = (f32[2,64,64,128]{3,2,1,0:T(8,128)}, f32[2,64,64,128]{3,2,1,0:T(8,128)}, f32[2,64,128]{2,1,0:T(8,128)}) custom-call(f32[2,64,128]{2,1,0:T(8,128)} %copy.124.refs_0_, f32[2,64,64,128]{3,2,1,0:T(8,128)} %get-tuple-element.28.refs_1_, f32[2,64,64,128]{3,2,1,0:T(8,128)} %get-tuple-element.18.ba_ref.refs_2_, ...), custom_call_target="tpu_custom_call" | custom-call | tf_op jit(solution)/shard_map/pallas_call | solution.py:193
  134.7 2.1 %collective-permute-start.8 = (f32[4,64,128]{2,0,1:T(4,128)S(1)}, f32[4,64,128]{2,0,1:T(4,128)S(1)}, u32[]{:S(2)}, u32[]{:S(2)}) collective-permute-start(f32[4,64,128]{2,0,1:T(4,128)S(1)} %fusion.19), channel_id=1, source_target_pairs={{0,8},{8,0},{16,24},{24,16},{1,9},{9,1},{17,25},{25,17},{2,10},{10... | collective-permute-start | bytes 393224 | tf_op jit(solution)/shard_map/ppermute | solution.py:283
  136.8 1.6 collective-permute-start.16
  138.5 2.4 %collective-permute-done.8 = f32[4,64,128]{2,0,1:T(4,128)S(1)} collective-permute-done((f32[4,64,128]{2,0,1:T(4,128)S(1)}, f32[4,64,128]{2,0,1:T(4,128)S(1)}, u32[]{:S(2)}, u32[]{:S(2)}) %collective-permute-start.8) | collective-permute-done | bytes 131104 | tf_op jit(solution)/shard_map/ppermute | solution.py:283
  142.5 1.6 collective-permute-start.17
  144.1 1.3 slice_select_fusion.1
  145.4 2.1 %collective-permute-done.17 = f32[4,64,128]{2,1,0:T(8,128)S(1)} collective-permute-done((f32[4,64,128]{2,1,0:T(8,128)S(1)}, f32[4,64,128]{2,1,0:T(8,128)S(1)}, u32[]{:S(2)}, u32[]{:S(2)}) %collective-permute-start.17) | collective-permute-done | bytes 131104 | tf_op jit(solution)/shard_map/ppermute | solution.py:283
  148.3 6.5 %shard_map.101 = f32[2,64,128]{2,1,0:T(8,128)} custom-call(f32[2,64,128]{2,1,0:T(8,128)} %broadcast_in_dim.118.refs_0_, f32[2,64,64,128]{3,2,1,0:T(8,128)} %broadcast_in_dim.121.refs_1_.refs_2_, f32[2,64,64,128]{3,2,1,0:T(8,128)} %get-tuple-element.31.refs_2_, f32[2,64,128]{2,1,0:T(8,128)} %pad_add_fusion.refs_3_), custom_call_target="tpu_custom_call" | custom-call | tf_op jit(solution)/shard_map/pallas_call | solution.py:193
  154.8 1.2 fusion.11
  156.0 1.1 collective-permute-start.18
  158.0 3.3 %reduce_sum.40 = f32[2,64,64]{2,1,0:T(8,128)S(1)} reduce(f32[2,64,64,128]{3,2,1,0:T(8,128)} %get-tuple-element.30, f32[]{:T(128)} %constant.39.clone.1), dimensions={3}, to_apply=%region_0.1 | reduce | flops 1040384 | bytes 4227076 | tf_op jit(solution)/shard_map/reduce_sum | solution.py:405
  161.4 2.2 %collective-permute-start.19 = (f32[4,64,128]{2,0,1:T(4,128)S(1)}, f32[4,64,128]{2,0,1:T(4,128)S(1)}, u32[]{:S(2)}, u32[]{:S(2)}) collective-permute-start(f32[4,64,128]{2,0,1:T(4,128)S(1)} %add.139), channel_id=1, source_target_pairs={{0,16},{8,24},{16,0},{24,8},{1,17},{9,25},{17,1},{25,9},{2,18},{10... | collective-permute-start | bytes 393224 | tf_op jit(solution)/shard_map/ppermute | solution.py:283
  164.7 4.0 %collective-permute-done.19 = f32[4,64,128]{2,0,1:T(4,128)S(1)} collective-permute-done((f32[4,64,128]{2,0,1:T(4,128)S(1)}, f32[4,64,128]{2,0,1:T(4,128)S(1)}, u32[]{:S(2)}, u32[]{:S(2)}) %collective-permute-start.19) | collective-permute-done | bytes 131104 | tf_op jit(solution)/shard_map/ppermute | solution.py:283
  (93 shorter events, 23.0 us)
Async XLA Ops:
  12.3 9.0 %copy-start.3 = (s32[256,128]{1,0:T(8,128)S(1)}, s32[256,128]{1,0:T(8,128)}, u32[]{:S(2)}) copy-start(s32[256,128]{1,0:T(8,128)} %param.11) | copy-start | bytes 393220
  20.8 1.5 collective-permute-start
  22.3 6.7 %collective-permute-start.1 = (f32[4,64,128]{2,1,0:T(8,128)S(1)}, f32[4,64,128]{2,1,0:T(8,128)S(1)}, u32[]{:S(2)}, u32[]{:S(2)}) collective-permute-start(f32[4,64,128]{2,1,0:T(8,128)S(1)} %fusion.56), channel_id=1, source_target_pairs={{0,2},{1,3},{2,0},{3,1},{4,6},{5,7},{6,4},{7,5},{8,10},{9,11},{10,... | collective-permute-start | bytes 393224 | tf_op jit(solution)/shard_map/ppermute | solution.py:283
  29.1 5.1 %collective-permute-start.2 = (f32[4,64,128]{2,1,0:T(8,128)S(1)}, f32[4,64,128]{2,1,0:T(8,128)S(1)}, u32[]{:S(2)}, u32[]{:S(2)}) collective-permute-start(f32[4,64,128]{2,1,0:T(8,128)S(1)} %fusion.63), channel_id=1, source_target_pairs={{0,4},{1,5},{2,6},{3,7},{4,0},{5,1},{6,2},{7,3},{8,12},{9,13},{10,... | collective-permute-start | bytes 393224 | tf_op jit(solution)/shard_map/ppermute | solution.py:283
  44.9 5.0 %collective-permute-start.3 = (f32[4,64,128]{2,0,1:T(4,128)S(1)}, f32[4,64,128]{2,0,1:T(4,128)S(1)}, u32[]{:S(2)}, u32[]{:S(2)}) collective-permute-start(f32[4,64,128]{2,0,1:T(4,128)S(1)} %fusion.21), channel_id=1, source_target_pairs={{0,8},{8,0},{16,24},{24,16},{1,9},{9,1},{17,25},{25,17},{2,10},{10... | collective-permute-start | bytes 393224 | tf_op jit(solution)/shard_map/ppermute | solution.py:283
  50.0 7.6 %collective-permute-start.4 = (f32[4,64,128]{2,0,1:T(4,128)S(1)}, f32[4,64,128]{2,0,1:T(4,128)S(1)}, u32[]{:S(2)}, u32[]{:S(2)}) collective-permute-start(f32[4,64,128]{2,0,1:T(4,128)S(1)} %add.120), channel_id=1, source_target_pairs={{0,16},{8,24},{16,0},{24,8},{1,17},{9,25},{17,1},{25,9},{2,18},{10... | collective-permute-start | bytes 393224 | tf_op jit(solution)/shard_map/ppermute | solution.py:283
  58.5 10.2 %copy-start.2 = (f32[256,128]{1,0:T(8,128)S(1)}, f32[256,128]{1,0:T(8,128)}, u32[]{:S(2)}) copy-start(f32[256,128]{1,0:T(8,128)} %param.13) | copy-start | bytes 393220
  65.7 1.4 collective-permute-start.5
  67.1 5.6 %collective-permute-start.6 = (f32[4,64,128]{2,1,0:T(8,128)S(1)}, f32[4,64,128]{2,1,0:T(8,128)S(1)}, u32[]{:S(2)}, u32[]{:S(2)}) collective-permute-start(f32[4,64,128]{2,1,0:T(8,128)S(1)} %fusion.55), channel_id=1, source_target_pairs={{0,2},{1,3},{2,0},{3,1},{4,6},{5,7},{6,4},{7,5},{8,10},{9,11},{10,... | collective-permute-start | bytes 393224 | tf_op jit(solution)/shard_map/ppermute | solution.py:283
  72.7 5.0 %collective-permute-start.7 = (f32[4,64,128]{2,1,0:T(8,128)S(1)}, f32[4,64,128]{2,1,0:T(8,128)S(1)}, u32[]{:S(2)}, u32[]{:S(2)}) collective-permute-start(f32[4,64,128]{2,1,0:T(8,128)S(1)} %fusion.62), channel_id=1, source_target_pairs={{0,4},{1,5},{2,6},{3,7},{4,0},{5,1},{6,2},{7,3},{8,12},{9,13},{10,... | collective-permute-start | bytes 393224 | tf_op jit(solution)/shard_map/ppermute | solution.py:283
  78.8 20.4 %copy-start.1 = (f32[2,64,128]{2,1,0:T(8,128)S(1)}, f32[2,64,128]{2,1,0:T(8,128)}, u32[]{:S(2)}) copy-start(f32[2,64,128]{2,1,0:T(8,128)} %get-tuple-element.23) | copy-start | bytes 196612
  86.9 1.4 collective-permute-start.10
  88.4 5.6 %collective-permute-start.11 = (f32[4,64,128]{2,1,0:T(8,128)S(1)}, f32[4,64,128]{2,1,0:T(8,128)S(1)}, u32[]{:S(2)}, u32[]{:S(2)}) collective-permute-start(f32[4,64,128]{2,1,0:T(8,128)S(1)} %multiply_add_fusion.5), channel_id=1, source_target_pairs={{0,2},{1,3},{2,0},{3,1},{4,6},{5,7},{6,4},{7,5},{8,10},{9,11},{10,... | collective-permute-start | bytes 393224 | tf_op jit(solution)/shard_map/ppermute | solution.py:283
  94.0 5.0 %collective-permute-start.12 = (f32[4,64,128]{2,1,0:T(8,128)S(1)}, f32[4,64,128]{2,1,0:T(8,128)S(1)}, u32[]{:S(2)}, u32[]{:S(2)}) collective-permute-start(f32[4,64,128]{2,1,0:T(8,128)S(1)} %multiply_add_fusion.4), channel_id=1, source_target_pairs={{0,4},{1,5},{2,6},{3,7},{4,0},{5,1},{6,2},{7,3},{8,12},{9,13},{10,... | collective-permute-start | bytes 393224 | tf_op jit(solution)/shard_map/ppermute | solution.py:283
  109.4 5.0 %collective-permute-start.13 = (f32[4,64,128]{2,0,1:T(4,128)S(1)}, f32[4,64,128]{2,0,1:T(4,128)S(1)}, u32[]{:S(2)}, u32[]{:S(2)}) collective-permute-start(f32[4,64,128]{2,0,1:T(4,128)S(1)} %fusion.15), channel_id=1, source_target_pairs={{0,8},{8,0},{16,24},{24,16},{1,9},{9,1},{17,25},{25,17},{2,10},{10... | collective-permute-start | bytes 393224 | tf_op jit(solution)/shard_map/ppermute | solution.py:283
  114.4 8.1 %collective-permute-start.14 = (f32[4,64,128]{2,0,1:T(4,128)S(1)}, f32[4,64,128]{2,0,1:T(4,128)S(1)}, u32[]{:S(2)}, u32[]{:S(2)}) collective-permute-start(f32[4,64,128]{2,0,1:T(4,128)S(1)} %add.131), channel_id=1, source_target_pairs={{0,16},{8,24},{16,0},{24,8},{1,17},{9,25},{17,1},{25,9},{2,18},{10... | collective-permute-start | bytes 393224 | tf_op jit(solution)/shard_map/ppermute | solution.py:283
  123.5 10.8 %copy-start.4 = (f32[2,64,128]{2,1,0:T(8,128)S(1)}, f32[2,64,128]{2,1,0:T(8,128)}, u32[]{:S(2)}) copy-start(f32[2,64,128]{2,1,0:T(8,128)} %get-tuple-element.24) | copy-start | bytes 196612
  132.9 14.7 %copy-start = (f32[2,64,128]{2,1,0:T(8,128)S(1)}, f32[2,64,128]{2,1,0:T(8,128)}, u32[]{:S(2)}) copy-start(f32[2,64,128]{2,1,0:T(8,128)} %get-tuple-element.19) | copy-start | bytes 196612
  134.2 2.5 %collective-permute-start.15 = (f32[4,64,128]{2,1,0:T(8,128)S(1)}, f32[4,64,128]{2,1,0:T(8,128)S(1)}, u32[]{:S(2)}, u32[]{:S(2)}) collective-permute-start(f32[4,64,128]{2,1,0:T(8,128)S(1)} %copy.130), channel_id=1, source_target_pairs={{0,1},{1,0},{2,3},{3,2},{4,5},{5,4},{6,7},{7,6},{8,9},{9,8},{10,11... | collective-permute-start | bytes 393224 | tf_op jit(solution)/shard_map/ppermute | solution.py:283
  134.7 6.2 %collective-permute-start.8 = (f32[4,64,128]{2,0,1:T(4,128)S(1)}, f32[4,64,128]{2,0,1:T(4,128)S(1)}, u32[]{:S(2)}, u32[]{:S(2)}) collective-permute-start(f32[4,64,128]{2,0,1:T(4,128)S(1)} %fusion.19), channel_id=1, source_target_pairs={{0,8},{8,0},{16,24},{24,16},{1,9},{9,1},{17,25},{25,17},{2,10},{10... | collective-permute-start | bytes 393224 | tf_op jit(solution)/shard_map/ppermute | solution.py:283
  136.8 5.7 %collective-permute-start.16 = (f32[4,64,128]{2,1,0:T(8,128)S(1)}, f32[4,64,128]{2,1,0:T(8,128)S(1)}, u32[]{:S(2)}, u32[]{:S(2)}) collective-permute-start(f32[4,64,128]{2,1,0:T(8,128)S(1)} %multiply_add_fusion.2), channel_id=1, source_target_pairs={{0,2},{1,3},{2,0},{3,1},{4,6},{5,7},{6,4},{7,5},{8,10},{9,11},{10,... | collective-permute-start | bytes 393224 | tf_op jit(solution)/shard_map/ppermute | solution.py:283
  140.9 16.2 %collective-permute-start.9 = (f32[4,64,128]{2,0,1:T(4,128)S(1)}, f32[4,64,128]{2,0,1:T(4,128)S(1)}, u32[]{:S(2)}, u32[]{:S(2)}) collective-permute-start(f32[4,64,128]{2,0,1:T(4,128)S(1)} %add.123), channel_id=1, source_target_pairs={{0,16},{8,24},{16,0},{24,8},{1,17},{9,25},{17,1},{25,9},{2,18},{10... | collective-permute-start | bytes 393224 | tf_op jit(solution)/shard_map/ppermute | solution.py:283
  142.5 5.0 %collective-permute-start.17 = (f32[4,64,128]{2,1,0:T(8,128)S(1)}, f32[4,64,128]{2,1,0:T(8,128)S(1)}, u32[]{:S(2)}, u32[]{:S(2)}) collective-permute-start(f32[4,64,128]{2,1,0:T(8,128)S(1)} %multiply_add_fusion.1), channel_id=1, source_target_pairs={{0,4},{1,5},{2,6},{3,7},{4,0},{5,1},{6,2},{7,3},{8,12},{9,13},{10,... | collective-permute-start | bytes 393224 | tf_op jit(solution)/shard_map/ppermute | solution.py:283
  156.0 5.3 %collective-permute-start.18 = (f32[4,64,128]{2,0,1:T(4,128)S(1)}, f32[4,64,128]{2,0,1:T(4,128)S(1)}, u32[]{:S(2)}, u32[]{:S(2)}) collective-permute-start(f32[4,64,128]{2,0,1:T(4,128)S(1)} %fusion.11), channel_id=1, source_target_pairs={{0,8},{8,0},{16,24},{24,16},{1,9},{9,1},{17,25},{25,17},{2,10},{10... | collective-permute-start | bytes 393224 | tf_op jit(solution)/shard_map/ppermute | solution.py:283
  161.4 7.3 %collective-permute-start.19 = (f32[4,64,128]{2,0,1:T(4,128)S(1)}, f32[4,64,128]{2,0,1:T(4,128)S(1)}, u32[]{:S(2)}, u32[]{:S(2)}) collective-permute-start(f32[4,64,128]{2,0,1:T(4,128)S(1)} %add.139), channel_id=1, source_target_pairs={{0,16},{8,24},{16,0},{24,8},{1,17},{9,25},{17,1},{25,9},{2,18},{10... | collective-permute-start | bytes 393224 | tf_op jit(solution)/shard_map/ppermute | solution.py:283

commit v2 on v1

--- a/solution.py
+++ b/solution.py
@@ -93,6 +93,7 @@
 
 
 def _fwd_messages_kernel(ba_ref, f_ref, ew_ref, u_ref, col_ref):
+    first = pl.program_id(1) == 0
     n_c = ba_ref.shape[1]
     f = f_ref[0]
 
@@ -100,7 +101,8 @@
         x = ba_ref[0, c] * f
         u = ew_ref[0, c] * jnp.log((1.0 + DAMP * x) / (1.0 - DAMP * x))
         u_ref[0, c] = u
-        col_ref[0, pl.ds(c, 1), :] = jnp.sum(u, axis=0, keepdims=True)
+        row = jnp.sum(u, axis=0, keepdims=True)
+        col_ref[0, pl.ds(c, 1), :] = jnp.where(first, row, col_ref[0, pl.ds(c, 1), :] + row)
         return carry
 
     lax.fori_loop(0, n_c, body, 0, unroll=UNROLL)
@@ -145,6 +147,7 @@
     refs = refs[3:]
     gm_ref = refs.pop(0) if emit_gm else None
     col_ref, h_scr, p_scr, q_scr = refs
+    first = pl.program_id(1) == 0
     n_c = em_ref.shape[1]
     shape = em_ref.shape[2:]
     gwh = gwh_ref[0]
@@ -173,63 +176,73 @@
         gm = jnp.where(em_ref[0, c] > 0, gh * (0.5 * (1.0 - h * h)), 0.0)
         if emit_gm:
             gm_ref[0, c] = gm
-        col_ref[0, pl.ds(c, 1), :] = jnp.sum(gm, axis=0, keepdims=True)
+        row = jnp.sum(gm, axis=0, keepdims=True)
+        col_ref[0, pl.ds(c, 1), :] = jnp.where(first, row, col_ref[0, pl.ds(c, 1), :] + row)
         return (prod * h, grad * h + gba_ref[0, c] * prod)
 
     lax.fori_loop(0, n_c, backward, (ones, zeros), unroll=UNROLL)
 
 
-def _big_spec(shape):
-    return pl.BlockSpec((1,) + shape[1:], lambda k: (k, 0, 0, 0))
-
-
-def _small_spec(shape):
-    return pl.BlockSpec((1,) + shape[1:], lambda k: (k, 0, 0))
+ROW_BLOCK = 32
+
+
+def _spec(kind, shape):
+    if kind == "dense":
+        return pl.BlockSpec((1, shape[1], ROW_BLOCK, shape[3]), lambda k, j: (k, 0, j, 0))
+    if kind == "rows":
+        return pl.BlockSpec((1, ROW_BLOCK, shape[2]), lambda k, j: (k, j, 0))
+    return pl.BlockSpec((1,) + tuple(shape[1:]), lambda k, j: (k, 0, 0))
 
 
 def _call(kernel, inputs, outputs, scratch=()):
-    in_specs = [_big_spec(a.shape) if a.ndim == 4 else _small_spec(a.shape) for a in inputs]
-    out_specs = [_big_spec(o.shape) if len(o.shape) == 4 else _small_spec(o.shape) for o in outputs]
+    in_specs = [_spec(kind, a.shape) for kind, a in inputs]
+    out_specs = [_spec(kind, o.shape) for kind, o in outputs]
+    dense = [a for kind, a in inputs if kind == "dense"][0]
     return pl.pallas_call(
         kernel,
-        grid=(inputs[0].shape[0],),
+        grid=(dense.shape[0], dense.shape[2] // ROW_BLOCK),
         in_specs=in_specs,
         out_specs=out_specs,
-        out_shape=list(outputs),
+        out_shape=[o for kind, o in outputs],
         scratch_shapes=list(scratch),
-    )(*inputs)
+    )(*[a for kind, a in inputs])
 
 
 def fwd_products(spread, u, em):
     k, c, r, s = em.shape
     has_u = u is not None
-    inputs = [spread] + ([u] if has_u else []) + [em]
-    outs = [jax.ShapeDtypeStruct(em.shape, F32), jax.ShapeDtypeStruct((k, r, s), F32)]
+    inputs = [("cols", spread)] + ([("dense", u)] if has_u else []) + [("dense", em)]
+    outs = [("dense", jax.ShapeDtypeStruct(em.shape, F32)), ("rows", jax.ShapeDtypeStruct((k, r, s), F32))]
     from jax.experimental.pallas import tpu as pltpu
 
     return _call(
         functools.partial(_fwd_products_kernel, has_u),
         inputs,
         outs,
-        [pltpu.VMEM((c, r, s), F32)],
+        [pltpu.VMEM((c, ROW_BLOCK, s), F32)],
     )
 
 
 def fwd_messages(ba, f, ew):
     k, c, r, s = ba.shape
-    outs = [jax.ShapeDtypeStruct(ba.shape, F32), jax.ShapeDtypeStruct((k, c, s), F32)]
-    return _call(_fwd_messages_kernel, [ba, f, ew], outs)
+    outs = [("dense", jax.ShapeDtypeStruct(ba.shape, F32)), ("cols", jax.ShapeDtypeStruct((k, c, s), F32))]
+    return _call(_fwd_messages_kernel, [("dense", ba), ("rows", f), ("dense", ew)], outs)
 
 
 def bwd_messages(gsp, gm, ba, f, ew, acc):
     k, c, r, s = ba.shape
     has_next = gm is not None
     has_acc = acc is not None
-    inputs = [gsp] + ([gm] if has_next else []) + [ba, f, ew] + ([acc] if has_acc else [])
+    inputs = (
+        [("cols", gsp)]
+        + ([("dense", gm)] if has_next else [])
+        + [("dense", ba), ("rows", f), ("dense", ew)]
+        + ([("dense", acc)] if has_acc else [])
+    )
     outs = [
-        jax.ShapeDtypeStruct(ba.shape, F32),
-        jax.ShapeDtypeStruct(ba.shape, F32),
-        jax.ShapeDtypeStruct((k, r, s), F32),
+        ("dense", jax.ShapeDtypeStruct(ba.shape, F32)),
+        ("dense", jax.ShapeDtypeStruct(ba.shape, F32)),
+        ("rows", jax.ShapeDtypeStruct((k, r, s), F32)),
     ]
     return _call(functools.partial(_bwd_messages_kernel, has_next, has_acc), inputs, outs)
 
@@ -239,15 +252,19 @@
 
     k, c, r, s = em.shape
     has_u = u is not None
-    inputs = [spread] + ([u] if has_u else []) + [em, gba, gwh]
-    outs = ([jax.ShapeDtypeStruct(em.shape, F32)] if emit_gm else []) + [
-        jax.ShapeDtypeStruct((k, c, s), F32)
+    inputs = [("cols", spread)] + ([("dense", u)] if has_u else []) + [
+        ("dense", em),
+        ("dense", gba),
+        ("rows", gwh),
+    ]
+    outs = ([("dense", jax.ShapeDtypeStruct(em.shape, F32))] if emit_gm else []) + [
+        ("cols", jax.ShapeDtypeStruct((k, c, s), F32))
     ]
     results = _call(
         functools.partial(_bwd_products_kernel, has_u, emit_gm),
         inputs,
         outs,
-        [pltpu.VMEM((c, r, s), F32) for _ in range(3)],
+        [pltpu.VMEM((c, ROW_BLOCK, s), F32) for _ in range(3)],
     )
     if emit_gm:
         return results[0], results[1]
@@ -359,8 +376,8 @@
     weight = edge_weight[0, 0].reshape(slot_total, TILE, TILE)
     edge_t = jnp.swapaxes(edge, 1, 2)
     dense = (slot_total, TILE, TILE, shots)
-    em = jnp.broadcast_to(edge_t[..., None], dense)
     ew = jnp.broadcast_to((edge_t * jnp.swapaxes(weight, 1, 2))[..., None], dense)
+    em = ew
     sign_dev = (1.0 - 2.0 * syndrome.astype(jnp.float32)).reshape(check_blocks, TILE, shots)
     sign_slot = jnp.einsum("kc,crs->krs", row_hot, sign_dev, precision=EXACT)
     prior_dev = channel_prior.reshape(column_blocks, TILE)

time: 171 us -> 177 us (1.035)
  Pallas kernels: 53.1 us -> 61.9 us
  local copies, waits for them, and re-layouts: 14.6 us -> 11.9 us
    pallas_call x8, Pallas kernels: 53.1 us -> 61.9 us  [_call(): pl.pallas_call(kernel, grid=(dense.shape[0], dense.shape[2] // ROW_BLOCK)...]
    broadcast_in_dim x1 -> x0, local copies, waits for them, and re-layouts: 2.56 us -> none  [body(): em = jnp.broadcast_to(edge_t[..., None], dense)]
  transfers between devices with their start and end apart: 20 -> 20, of which waited for: 16 -> 16; matrix products, arithmetic and copies ran while one was open for 9% -> 8% of each run, Pallas kernels for 7% -> 8%
where the time goes in v2:
time: 177 us; the launch traced here: 175 us
  Pallas kernels  61.9 us (35%)
  waiting for transfers between devices  41.2 us (23%)
  starting transfers between devices  29 us (16%)
  other arithmetic  18 us (10%)
  local copies, waits for them, and re-layouts  11.9 us (7%)
  matrix products  6.85 us (4%)
  between operations  6.64 us (4%)
    pallas_call x8, Pallas kernels, _call(): pl.pallas_call(kernel, grid=(dense.shape[0], dense.shape[2] // ROW_BLOCK)...  61.9 us
    ppermute x20, waiting for transfers between devices, _swap(): return lax.ppermute(value, axis, perm)  41.2 us
    ppermute x20, starting transfers between devices, _swap(): return lax.ppermute(value, axis, perm)  29 us
    select_n x6, other arithmetic, combine(): value = value * jnp.where(same_row[k, other], whole[other], 1.0)  8.29 us
  transfers between devices with their start and end apart: 20, of which 16 were waited for; matrix products, arithmetic and copies ran while one was open for 8% of the time, Pallas kernels for 8%

profile of v2, /device:TPU:0, one launch (start us, length us, event | category | flops | bytes accessed | tf_op | source)
XLA Modules:
  0.0 175.5 jit_solution(3513005652485233993)
XLA Ops:
  0.6 1.0 slice_reduce_fusion
  12.3 2.6 %broadcast_in_dim.115.refs_1_.ew_ref.refs_2_.refs_3_.refs_4_ = f32[2,64,64,128]{3,2,1,0:T(8,128)} broadcast(f32[2,64,64]{2,1,0:T(8,128)S(1)} %multiply_bitcast_fusion), dimensions={0,1,2} | broadcast | bytes 4227072 | tf_op jit(solution)/shard_map/broadcast_in_dim | solution.py:379
  14.9 5.9 %shard_map.94 = (f32[2,64,64,128]{3,2,1,0:T(8,128)}, f32[2,64,128]{2,1,0:T(8,128)}) custom-call(f32[2,64,128]{2,1,0:T(8,128)} %broadcast_in_dim.112.refs_0_, f32[2,64,64,128]{3,2,1,0:T(8,128)} %broadcast_in_dim.115.refs_1_.ew_ref.refs_2_.refs_3_.refs_4_), custom_call_target="tpu_custom_call" | custom-call | tf_op jit(solution)/shard_map/pallas_call | solution.py:201
  20.8 1.4 slice_select_fusion.7
  22.8 1.0 collective-permute-done
  23.8 2.9 %collective-permute-start.1 = (f32[4,64,128]{2,1,0:T(8,128)S(1)}, f32[4,64,128]{2,1,0:T(8,128)S(1)}, u32[]{:S(2)}, u32[]{:S(2)}) collective-permute-start(f32[4,64,128]{2,1,0:T(8,128)S(1)} %fusion.56), channel_id=1, source_target_pairs={{0,2},{1,3},{2,0},{3,1},{4,6},{5,7},{6,4},{7,5},{8,10},{9,11},{10,... | collective-permute-start | bytes 393224 | tf_op jit(solution)/shard_map/ppermute | solution.py:300
  27.0 3.5 %collective-permute-done.1 = f32[4,64,128]{2,1,0:T(8,128)S(1)} collective-permute-done((f32[4,64,128]{2,1,0:T(8,128)S(1)}, f32[4,64,128]{2,1,0:T(8,128)S(1)}, u32[]{:S(2)}, u32[]{:S(2)}) %collective-permute-start.1) | collective-permute-done | bytes 131104 | tf_op jit(solution)/shard_map/ppermute | solution.py:300
  30.5 1.8 %collective-permute-start.2 = (f32[4,64,128]{2,1,0:T(8,128)S(1)}, f32[4,64,128]{2,1,0:T(8,128)S(1)}, u32[]{:S(2)}, u32[]{:S(2)}) collective-permute-start(f32[4,64,128]{2,1,0:T(8,128)S(1)} %fusion.63), channel_id=1, source_target_pairs={{0,4},{1,5},{2,6},{3,7},{4,0},{5,1},{6,2},{7,3},{8,12},{9,13},{10,... | collective-permute-start | bytes 393224 | tf_op jit(solution)/shard_map/ppermute | solution.py:300
  32.4 1.4 slice_select_fusion.6
  33.8 1.9 %collective-permute-done.2 = f32[4,64,128]{2,1,0:T(8,128)S(1)} collective-permute-done((f32[4,64,128]{2,1,0:T(8,128)S(1)}, f32[4,64,128]{2,1,0:T(8,128)S(1)}, u32[]{:S(2)}, u32[]{:S(2)}) %collective-permute-start.2) | collective-permute-done | bytes 131104 | tf_op jit(solution)/shard_map/ppermute | solution.py:300
  36.6 7.1 %shard_map.95 = (f32[2,64,64,128]{3,2,1,0:T(8,128)}, f32[2,64,128]{2,1,0:T(8,128)}) custom-call(f32[2,64,64,128]{3,2,1,0:T(8,128)} %get-tuple-element.18.ba_ref.refs_2_, f32[2,64,128]{2,1,0:T(8,128)} %multiply_multiply_fusion.1.f_ref.refs_3_, f32[2,64,64,128]{3,2,1,0:T(8,128)} %broadcast_in_dim.115.refs_1_.ew_ref.refs_2_.refs_3_.refs_4_), custom_call_target="tpu_custom_call" | custom-call | tf_op jit(solution)/shard_map/pallas_call | solution.py:201
  43.7 1.2 fusion.21
  45.0 1.8 %collective-permute-start.3 = (f32[4,64,128]{2,0,1:T(4,128)S(1)}, f32[4,64,128]{2,0,1:T(4,128)S(1)}, u32[]{:S(2)}, u32[]{:S(2)}) collective-permute-start(f32[4,64,128]{2,0,1:T(4,128)S(1)} %fusion.21), channel_id=1, source_target_pairs={{0,8},{8,0},{16,24},{24,16},{1,9},{9,1},{17,25},{25,17},{2,10},{10... | collective-permute-start | bytes 393224 | tf_op jit(solution)/shard_map/ppermute | solution.py:300
  46.8 3.2 %collective-permute-done.3 = f32[4,64,128]{2,0,1:T(4,128)S(1)} collective-permute-done((f32[4,64,128]{2,0,1:T(4,128)S(1)}, f32[4,64,128]{2,0,1:T(4,128)S(1)}, u32[]{:S(2)}, u32[]{:S(2)}) %collective-permute-start.3) | collective-permute-done | bytes 131104 | tf_op jit(solution)/shard_map/ppermute | solution.py:300
  50.0 3.2 %collective-permute-start.4 = (f32[4,64,128]{2,0,1:T(4,128)S(1)}, f32[4,64,128]{2,0,1:T(4,128)S(1)}, u32[]{:S(2)}, u32[]{:S(2)}) collective-permute-start(f32[4,64,128]{2,0,1:T(4,128)S(1)} %add.120), channel_id=1, source_target_pairs={{0,16},{8,24},{16,0},{24,8},{1,17},{9,25},{17,1},{25,9},{2,18},{10... | collective-permute-start | bytes 393224 | tf_op jit(solution)/shard_map/ppermute | solution.py:300
  53.3 4.3 %collective-permute-done.4 = f32[4,64,128]{2,0,1:T(4,128)S(1)} collective-permute-done((f32[4,64,128]{2,0,1:T(4,128)S(1)}, f32[4,64,128]{2,0,1:T(4,128)S(1)}, u32[]{:S(2)}, u32[]{:S(2)}) %collective-permute-start.4) | collective-permute-done | bytes 131104 | tf_op jit(solution)/shard_map/ppermute | solution.py:300
  58.6 6.9 %shard_map.96 = (f32[2,64,64,128]{3,2,1,0:T(8,128)}, f32[2,64,128]{2,1,0:T(8,128)}) custom-call(f32[2,64,128]{2,1,0:T(8,128)} %copy.109.refs_0_, f32[2,64,64,128]{3,2,1,0:T(8,128)} %get-tuple-element.21.refs_1_, f32[2,64,64,128]{3,2,1,0:T(8,128)} %broadcast_in_dim.115.refs_1_.ew_ref.refs_2_.refs_3_.refs_4_), custom_call_target="tpu_custom_call" | custom-call | tf_op jit(solution)/shard_map/pallas_call | solution.py:201
  65.4 1.4 slice_select_fusion.5
  67.0 1.3 collective-permute-done.5
  68.3 1.6 collective-permute-start.6
  70.8 3.1 %collective-permute-done.6 = f32[4,64,128]{2,1,0:T(8,128)S(1)} collective-permute-done((f32[4,64,128]{2,1,0:T(8,128)S(1)}, f32[4,64,128]{2,1,0:T(8,128)S(1)}, u32[]{:S(2)}, u32[]{:S(2)}) %collective-permute-start.6) | collective-permute-done | bytes 131104 | tf_op jit(solution)/shard_map/ppermute | solution.py:300
  74.0 1.6 collective-permute-start.7
  75.6 1.4 slice_select_fusion.4
  77.0 2.0 %collective-permute-done.7 = f32[4,64,128]{2,1,0:T(8,128)S(1)} collective-permute-done((f32[4,64,128]{2,1,0:T(8,128)S(1)}, f32[4,64,128]{2,1,0:T(8,128)S(1)}, u32[]{:S(2)}, u32[]{:S(2)}) %collective-permute-start.7) | collective-permute-done | bytes 131104 | tf_op jit(solution)/shard_map/ppermute | solution.py:300
  80.0 8.4 %shard_map.98 = (f32[2,64,64,128]{3,2,1,0:T(8,128)}, f32[2,64,64,128]{3,2,1,0:T(8,128)}, f32[2,64,128]{2,1,0:T(8,128)}) custom-call(f32[2,64,128]{2,1,0:T(8,128)} %copy.116.refs_0_, f32[2,64,64,128]{3,2,1,0:T(8,128)} %get-tuple-element.22.ba_ref.refs_1_, f32[2,64,128]{2,1,0:T(8,128)} %multiply_multiply_fusion.f_ref.refs_2_, ...), custom_call_target="tpu_custom_call" | custom-call | tf_op jit(solution)/shard_map/pallas_call | solution.py:201
  89.7 1.3 collective-permute-done.10
  91.1 1.6 collective-permute-start.11
  92.6 4.1 %collective-permute-done.11 = f32[4,64,128]{2,1,0:T(8,128)S(1)} collective-permute-done((f32[4,64,128]{2,1,0:T(8,128)S(1)}, f32[4,64,128]{2,1,0:T(8,128)S(1)}, u32[]{:S(2)}, u32[]{:S(2)}) %collective-permute-start.11) | collective-permute-done | bytes 131104 | tf_op jit(solution)/shard_map/ppermute | solution.py:300
  96.7 1.6 collective-permute-start.12
  98.3 1.3 slice_select_fusion.3
  99.6 2.1 %collective-permute-done.12 = f32[4,64,128]{2,1,0:T(8,128)S(1)} collective-permute-done((f32[4,64,128]{2,1,0:T(8,128)S(1)}, f32[4,64,128]{2,1,0:T(8,128)S(1)}, u32[]{:S(2)}, u32[]{:S(2)}) %collective-permute-start.12) | collective-permute-done | bytes 131104 | tf_op jit(solution)/shard_map/ppermute | solution.py:300
  102.5 9.1 %shard_map.99 = (f32[2,64,64,128]{3,2,1,0:T(8,128)}, f32[2,64,128]{2,1,0:T(8,128)}) custom-call(f32[2,64,128]{2,1,0:T(8,128)} %copy.109.refs_0_, f32[2,64,64,128]{3,2,1,0:T(8,128)} %get-tuple-element.21.refs_1_, f32[2,64,64,128]{3,2,1,0:T(8,128)} %broadcast_in_dim.115.refs_1_.ew_ref.refs_2_.refs_3_.refs_4_, f32[2,64,64,128]{3,2,1,0:T(8,128)} %get-tuple-element.25.refs_3_, ...), custom_call_target="tpu_custom_call" | custom-call | tf_op jit(solution)/shard_map/pallas_call | solution.py:201
  111.6 1.2 fusion.15
  113.6 4.2 %collective-permute-done.13 = f32[4,64,128]{2,0,1:T(4,128)S(1)} collective-permute-done((f32[4,64,128]{2,0,1:T(4,128)S(1)}, f32[4,64,128]{2,0,1:T(4,128)S(1)}, u32[]{:S(2)}, u32[]{:S(2)}) %collective-permute-start.13) | collective-permute-done | bytes 131104 | tf_op jit(solution)/shard_map/ppermute | solution.py:300
  117.9 2.1 %collective-permute-start.14 = (f32[4,64,128]{2,0,1:T(4,128)S(1)}, f32[4,64,128]{2,0,1:T(4,128)S(1)}, u32[]{:S(2)}, u32[]{:S(2)}) collective-permute-start(f32[4,64,128]{2,0,1:T(4,128)S(1)} %add.131), channel_id=1, source_target_pairs={{0,16},{8,24},{16,0},{24,8},{1,17},{9,25},{17,1},{25,9},{2,18},{10... | collective-permute-start | bytes 393224 | tf_op jit(solution)/shard_map/ppermute | solution.py:300
  120.1 7.1 %shard_map.97 = (f32[2,64,64,128]{3,2,1,0:T(8,128)}, f32[2,64,128]{2,1,0:T(8,128)}) custom-call(f32[2,64,64,128]{3,2,1,0:T(8,128)} %get-tuple-element.22.ba_ref.refs_1_, f32[2,64,128]{2,1,0:T(8,128)} %multiply_multiply_fusion.f_ref.refs_2_, f32[2,64,64,128]{3,2,1,0:T(8,128)} %broadcast_in_dim.115.refs_1_.ew_ref.refs_2_.refs_3_.refs_4_), custom_call_target="tpu_custom_call" | custom-call | tf_op jit(solution)/shard_map/pallas_call | solution.py:201
  128.1 10.3 %shard_map.100 = (f32[2,64,64,128]{3,2,1,0:T(8,128)}, f32[2,64,64,128]{3,2,1,0:T(8,128)}, f32[2,64,128]{2,1,0:T(8,128)}) custom-call(f32[2,64,128]{2,1,0:T(8,128)} %copy.124.refs_0_, f32[2,64,64,128]{3,2,1,0:T(8,128)} %get-tuple-element.28.refs_1_, f32[2,64,64,128]{3,2,1,0:T(8,128)} %get-tuple-element.18.ba_ref.refs_2_, ...), custom_call_target="tpu_custom_call" | custom-call | tf_op jit(solution)/shard_map/pallas_call | solution.py:201
  140.2 2.1 %collective-permute-start.8 = (f32[4,64,128]{2,0,1:T(4,128)S(1)}, f32[4,64,128]{2,0,1:T(4,128)S(1)}, u32[]{:S(2)}, u32[]{:S(2)}) collective-permute-start(f32[4,64,128]{2,0,1:T(4,128)S(1)} %fusion.19), channel_id=1, source_target_pairs={{0,8},{8,0},{16,24},{24,16},{1,9},{9,1},{17,25},{25,17},{2,10},{10... | collective-permute-start | bytes 393224 | tf_op jit(solution)/shard_map/ppermute | solution.py:300
  142.3 1.6 collective-permute-start.16
  144.0 2.4 %collective-permute-done.8 = f32[4,64,128]{2,0,1:T(4,128)S(1)} collective-permute-done((f32[4,64,128]{2,0,1:T(4,128)S(1)}, f32[4,64,128]{2,0,1:T(4,128)S(1)}, u32[]{:S(2)}, u32[]{:S(2)}) %collective-permute-start.8) | collective-permute-done | bytes 131104 | tf_op jit(solution)/shard_map/ppermute | solution.py:300
  148.0 1.6 collective-permute-start.17
  149.6 1.3 slice_select_fusion.1
  150.9 2.1 %collective-permute-done.17 = f32[4,64,128]{2,1,0:T(8,128)S(1)} collective-permute-done((f32[4,64,128]{2,1,0:T(8,128)S(1)}, f32[4,64,128]{2,1,0:T(8,128)S(1)}, u32[]{:S(2)}, u32[]{:S(2)}) %collective-permute-start.17) | collective-permute-done | bytes 131104 | tf_op jit(solution)/shard_map/ppermute | solution.py:300
  153.8 7.2 %shard_map.101 = f32[2,64,128]{2,1,0:T(8,128)} custom-call(f32[2,64,128]{2,1,0:T(8,128)} %broadcast_in_dim.112.refs_0_, f32[2,64,64,128]{3,2,1,0:T(8,128)} %broadcast_in_dim.115.refs_1_.ew_ref.refs_2_.refs_3_.refs_4_, f32[2,64,64,128]{3,2,1,0:T(8,128)} %get-tuple-element.31.refs_2_, f32[2,64,128]{2,1,0:T(8,128)} %pad_add_fusion.refs_3_), custom_call_target="tpu_custom_call" | custom-call | tf_op jit(solution)/shard_map/pallas_call | solution.py:201
  161.0 1.2 fusion.11
  163.9 3.3 %reduce_sum.40 = f32[2,64,64]{2,1,0:T(8,128)S(1)} reduce(f32[2,64,64,128]{3,2,1,0:T(8,128)} %get-tuple-element.30, f32[]{:T(128)} %constant.39.clone.1), dimensions={3}, to_apply=%region_0.1 | reduce | flops 1040384 | bytes 4227076 | tf_op jit(solution)/shard_map/reduce_sum | solution.py:422
  167.3 2.5 %collective-permute-start.19 = (f32[4,64,128]{2,0,1:T(4,128)S(1)}, f32[4,64,128]{2,0,1:T(4,128)S(1)}, u32[]{:S(2)}, u32[]{:S(2)}) collective-permute-start(f32[4,64,128]{2,0,1:T(4,128)S(1)} %add.139), channel_id=1, source_target_pairs={{0,16},{8,24},{16,0},{24,8},{1,17},{9,25},{17,1},{25,9},{2,18},{10... | collective-permute-start | bytes 393224 | tf_op jit(solution)/shard_map/ppermute | solution.py:300
  170.9 3.7 %collective-permute-done.19 = f32[4,64,128]{2,0,1:T(4,128)S(1)} collective-permute-done((f32[4,64,128]{2,0,1:T(4,128)S(1)}, f32[4,64,128]{2,0,1:T(4,128)S(1)}, u32[]{:S(2)}, u32[]{:S(2)}) %collective-permute-start.19) | collective-permute-done | bytes 131104 | tf_op jit(solution)/shard_map/ppermute | solution.py:300
  (92 shorter events, 22.0 us)
Async XLA Ops:
  12.3 10.5 %copy-start.3 = (s32[256,128]{1,0:T(8,128)S(1)}, s32[256,128]{1,0:T(8,128)}, u32[]{:S(2)}) copy-start(s32[256,128]{1,0:T(8,128)} %param.11) | copy-start | bytes 393220
  22.2 1.5 collective-permute-start
  23.8 6.7 %collective-permute-start.1 = (f32[4,64,128]{2,1,0:T(8,128)S(1)}, f32[4,64,128]{2,1,0:T(8,128)S(1)}, u32[]{:S(2)}, u32[]{:S(2)}) collective-permute-start(f32[4,64,128]{2,1,0:T(8,128)S(1)} %fusion.56), channel_id=1, source_target_pairs={{0,2},{1,3},{2,0},{3,1},{4,6},{5,7},{6,4},{7,5},{8,10},{9,11},{10,... | collective-permute-start | bytes 393224 | tf_op jit(solution)/shard_map/ppermute | solution.py:300
  30.5 5.1 %collective-permute-start.2 = (f32[4,64,128]{2,1,0:T(8,128)S(1)}, f32[4,64,128]{2,1,0:T(8,128)S(1)}, u32[]{:S(2)}, u32[]{:S(2)}) collective-permute-start(f32[4,64,128]{2,1,0:T(8,128)S(1)} %fusion.63), channel_id=1, source_target_pairs={{0,4},{1,5},{2,6},{3,7},{4,0},{5,1},{6,2},{7,3},{8,12},{9,13},{10,... | collective-permute-start | bytes 393224 | tf_op jit(solution)/shard_map/ppermute | solution.py:300
  45.0 5.0 %collective-permute-start.3 = (f32[4,64,128]{2,0,1:T(4,128)S(1)}, f32[4,64,128]{2,0,1:T(4,128)S(1)}, u32[]{:S(2)}, u32[]{:S(2)}) collective-permute-start(f32[4,64,128]{2,0,1:T(4,128)S(1)} %fusion.21), channel_id=1, source_target_pairs={{0,8},{8,0},{16,24},{24,16},{1,9},{9,1},{17,25},{25,17},{2,10},{10... | collective-permute-start | bytes 393224 | tf_op jit(solution)/shard_map/ppermute | solution.py:300
  50.0 7.6 %collective-permute-start.4 = (f32[4,64,128]{2,0,1:T(4,128)S(1)}, f32[4,64,128]{2,0,1:T(4,128)S(1)}, u32[]{:S(2)}, u32[]{:S(2)}) collective-permute-start(f32[4,64,128]{2,0,1:T(4,128)S(1)} %add.120), channel_id=1, source_target_pairs={{0,16},{8,24},{16,0},{24,8},{1,17},{9,25},{17,1},{25,9},{2,18},{10... | collective-permute-start | bytes 393224 | tf_op jit(solution)/shard_map/ppermute | solution.py:300
  58.6 11.3 %copy-start.2 = (f32[256,128]{1,0:T(8,128)S(1)}, f32[256,128]{1,0:T(8,128)}, u32[]{:S(2)}) copy-start(f32[256,128]{1,0:T(8,128)} %param.13) | copy-start | bytes 393220
  66.9 1.4 collective-permute-start.5
  68.3 5.6 %collective-permute-start.6 = (f32[4,64,128]{2,1,0:T(8,128)S(1)}, f32[4,64,128]{2,1,0:T(8,128)S(1)}, u32[]{:S(2)}, u32[]{:S(2)}) collective-permute-start(f32[4,64,128]{2,1,0:T(8,128)S(1)} %fusion.55), channel_id=1, source_target_pairs={{0,2},{1,3},{2,0},{3,1},{4,6},{5,7},{6,4},{7,5},{8,10},{9,11},{10,... | collective-permute-start | bytes 393224 | tf_op jit(solution)/shard_map/ppermute | solution.py:300
  74.0 5.0 %collective-permute-start.7 = (f32[4,64,128]{2,1,0:T(8,128)S(1)}, f32[4,64,128]{2,1,0:T(8,128)S(1)}, u32[]{:S(2)}, u32[]{:S(2)}) collective-permute-start(f32[4,64,128]{2,1,0:T(8,128)S(1)} %fusion.62), channel_id=1, source_target_pairs={{0,4},{1,5},{2,6},{3,7},{4,0},{5,1},{6,2},{7,3},{8,12},{9,13},{10,... | collective-permute-start | bytes 393224 | tf_op jit(solution)/shard_map/ppermute | solution.py:300
  80.0 21.8 %copy-start.1 = (f32[2,64,128]{2,1,0:T(8,128)S(1)}, f32[2,64,128]{2,1,0:T(8,128)}, u32[]{:S(2)}) copy-start(f32[2,64,128]{2,1,0:T(8,128)} %get-tuple-element.23) | copy-start | bytes 196612
  89.6 1.4 collective-permute-start.10
  91.1 5.6 %collective-permute-start.11 = (f32[4,64,128]{2,1,0:T(8,128)S(1)}, f32[4,64,128]{2,1,0:T(8,128)S(1)}, u32[]{:S(2)}, u32[]{:S(2)}) collective-permute-start(f32[4,64,128]{2,1,0:T(8,128)S(1)} %multiply_add_fusion.5), channel_id=1, source_target_pairs={{0,2},{1,3},{2,0},{3,1},{4,6},{5,7},{6,4},{7,5},{8,10},{9,11},{10,... | collective-permute-start | bytes 393224 | tf_op jit(solution)/shard_map/ppermute | solution.py:300
  96.7 5.0 %collective-permute-start.12 = (f32[4,64,128]{2,1,0:T(8,128)S(1)}, f32[4,64,128]{2,1,0:T(8,128)S(1)}, u32[]{:S(2)}, u32[]{:S(2)}) collective-permute-start(f32[4,64,128]{2,1,0:T(8,128)S(1)} %multiply_add_fusion.4), channel_id=1, source_target_pairs={{0,4},{1,5},{2,6},{3,7},{4,0},{5,1},{6,2},{7,3},{8,12},{9,13},{10,... | collective-permute-start | bytes 393224 | tf_op jit(solution)/shard_map/ppermute | solution.py:300
  112.8 5.0 %collective-permute-start.13 = (f32[4,64,128]{2,0,1:T(4,128)S(1)}, f32[4,64,128]{2,0,1:T(4,128)S(1)}, u32[]{:S(2)}, u32[]{:S(2)}) collective-permute-start(f32[4,64,128]{2,0,1:T(4,128)S(1)} %fusion.15), channel_id=1, source_target_pairs={{0,8},{8,0},{16,24},{24,16},{1,9},{9,1},{17,25},{25,17},{2,10},{10... | collective-permute-start | bytes 393224 | tf_op jit(solution)/shard_map/ppermute | solution.py:300
  117.9 9.3 %collective-permute-start.14 = (f32[4,64,128]{2,0,1:T(4,128)S(1)}, f32[4,64,128]{2,0,1:T(4,128)S(1)}, u32[]{:S(2)}, u32[]{:S(2)}) collective-permute-start(f32[4,64,128]{2,0,1:T(4,128)S(1)} %add.131), channel_id=1, source_target_pairs={{0,16},{8,24},{16,0},{24,8},{1,17},{9,25},{17,1},{25,9},{2,18},{10... | collective-permute-start | bytes 393224 | tf_op jit(solution)/shard_map/ppermute | solution.py:300
  128.1 11.7 %copy-start.4 = (f32[2,64,128]{2,1,0:T(8,128)S(1)}, f32[2,64,128]{2,1,0:T(8,128)}, u32[]{:S(2)}) copy-start(f32[2,64,128]{2,1,0:T(8,128)} %get-tuple-element.24) | copy-start | bytes 196612
  138.4 14.7 %copy-start = (f32[2,64,128]{2,1,0:T(8,128)S(1)}, f32[2,64,128]{2,1,0:T(8,128)}, u32[]{:S(2)}) copy-start(f32[2,64,128]{2,1,0:T(8,128)} %get-tuple-element.19) | copy-start | bytes 196612
  139.7 2.5 %collective-permute-start.15 = (f32[4,64,128]{2,1,0:T(8,128)S(1)}, f32[4,64,128]{2,1,0:T(8,128)S(1)}, u32[]{:S(2)}, u32[]{:S(2)}) collective-permute-start(f32[4,64,128]{2,1,0:T(8,128)S(1)} %copy.130), channel_id=1, source_target_pairs={{0,1},{1,0},{2,3},{3,2},{4,5},{5,4},{6,7},{7,6},{8,9},{9,8},{10,11... | collective-permute-start | bytes 393224 | tf_op jit(solution)/shard_map/ppermute | solution.py:300
  140.2 6.2 %collective-permute-start.8 = (f32[4,64,128]{2,0,1:T(4,128)S(1)}, f32[4,64,128]{2,0,1:T(4,128)S(1)}, u32[]{:S(2)}, u32[]{:S(2)}) collective-permute-start(f32[4,64,128]{2,0,1:T(4,128)S(1)} %fusion.19), channel_id=1, source_target_pairs={{0,8},{8,0},{16,24},{24,16},{1,9},{9,1},{17,25},{25,17},{2,10},{10... | collective-permute-start | bytes 393224 | tf_op jit(solution)/shard_map/ppermute | solution.py:300
  142.3 5.7 %collective-permute-start.16 = (f32[4,64,128]{2,1,0:T(8,128)S(1)}, f32[4,64,128]{2,1,0:T(8,128)S(1)}, u32[]{:S(2)}, u32[]{:S(2)}) collective-permute-start(f32[4,64,128]{2,1,0:T(8,128)S(1)} %multiply_add_fusion.2), channel_id=1, source_target_pairs={{0,2},{1,3},{2,0},{3,1},{4,6},{5,7},{6,4},{7,5},{8,10},{9,11},{10,... | collective-permute-start | bytes 393224 | tf_op jit(solution)/shard_map/ppermute | solution.py:300
  146.4 16.6 %collective-permute-start.9 = (f32[4,64,128]{2,0,1:T(4,128)S(1)}, f32[4,64,128]{2,0,1:T(4,128)S(1)}, u32[]{:S(2)}, u32[]{:S(2)}) collective-permute-start(f32[4,64,128]{2,0,1:T(4,128)S(1)} %add.123), channel_id=1, source_target_pairs={{0,16},{8,24},{16,0},{24,8},{1,17},{9,25},{17,1},{25,9},{2,18},{10... | collective-permute-start | bytes 393224 | tf_op jit(solution)/shard_map/ppermute | solution.py:300
  148.0 5.0 %collective-permute-start.17 = (f32[4,64,128]{2,1,0:T(8,128)S(1)}, f32[4,64,128]{2,1,0:T(8,128)S(1)}, u32[]{:S(2)}, u32[]{:S(2)}) collective-permute-start(f32[4,64,128]{2,1,0:T(8,128)S(1)} %multiply_add_fusion.1), channel_id=1, source_target_pairs={{0,4},{1,5},{2,6},{3,7},{4,0},{5,1},{6,2},{7,3},{8,12},{9,13},{10,... | collective-permute-start | bytes 393224 | tf_op jit(solution)/shard_map/ppermute | solution.py:300
  162.2 5.0 %collective-permute-start.18 = (f32[4,64,128]{2,0,1:T(4,128)S(1)}, f32[4,64,128]{2,0,1:T(4,128)S(1)}, u32[]{:S(2)}, u32[]{:S(2)}) collective-permute-start(f32[4,64,128]{2,0,1:T(4,128)S(1)} %fusion.11), channel_id=1, source_target_pairs={{0,8},{8,0},{16,24},{24,16},{1,9},{9,1},{17,25},{25,17},{2,10},{10... | collective-permute-start | bytes 393224 | tf_op jit(solution)/shard_map/ppermute | solution.py:300
  167.3 7.3 %collective-permute-start.19 = (f32[4,64,128]{2,0,1:T(4,128)S(1)}, f32[4,64,128]{2,0,1:T(4,128)S(1)}, u32[]{:S(2)}, u32[]{:S(2)}) collective-permute-start(f32[4,64,128]{2,0,1:T(4,128)S(1)} %add.139), channel_id=1, source_target_pairs={{0,16},{8,24},{16,0},{24,8},{1,17},{9,25},{17,1},{25,9},{2,18},{10... | collective-permute-start | bytes 393224 | tf_op jit(solution)/shard_map/ppermute | solution.py:300

commit v3 on v2

--- a/solution.py
+++ b/solution.py
@@ -13,7 +13,7 @@
 DAMP = 0.97
 EXACT = lax.Precision.HIGHEST
 F32 = jnp.float32
-UNROLL = 4
+UNROLL = 8
 
 
 def linear_both(values, axis):
@@ -183,7 +183,7 @@
     lax.fori_loop(0, n_c, backward, (ones, zeros), unroll=UNROLL)
 
 
-ROW_BLOCK = 32
+ROW_BLOCK = 64
 
 
 def _spec(kind, shape):
@@ -269,6 +269,26 @@
     if emit_gm:
         return results[0], results[1]
     return None, results[0]
+
+
+def pick(hot, values):
+    parts = []
+    for k in range(hot.shape[0]):
+        value = jnp.zeros_like(values[0])
+        for j in range(hot.shape[1]):
+            value = value + jnp.where(hot[k, j] > 0, values[j], 0.0)
+        parts.append(value)
+    return jnp.stack(parts)
+
+
+def place(hot, values):
+    parts = []
+    for j in range(hot.shape[1]):
+        value = jnp.zeros_like(values[0])
+        for k in range(hot.shape[0]):
+            value = value + jnp.where(hot[k, j] > 0, values[k], 0.0)
+        parts.append(value)
+    return jnp.stack(parts)
 
 
 def combine(whole, row_hot, same_row):
@@ -390,13 +410,13 @@
         ba, whole = fwd_products(spread, u, em)
         rows, others_here = combine(whole, row_hot, same_row)
         others, piece = others_forward(rows, check_blocks, n_var)
-        others_slot = jnp.einsum("kc,crs->krs", row_hot, others, precision=EXACT)
+        others_slot = pick(row_hot, others)
         factor = sign_slot * others_here * others_slot
         saved.append((spread, u, ba, whole, factor, others_here, others_slot, piece))
         u, colsum = fwd_messages(ba, factor, ew)
-        column = jnp.einsum("kv,kcs->vcs", col_hot, colsum, precision=EXACT)
+        column = place(col_hot, colsum)
         total = prior_dev[:, :, None] + checks_total(column, n_chk)
-        spread = jnp.einsum("kv,vcs->kcs", col_hot, total, precision=EXACT)
+        spread = pick(col_hot, total)
     marginals = total.reshape(column_blocks * TILE, shots)
 
     grad_total = out_cot.reshape(column_blocks, TILE, shots)
@@ -406,17 +426,17 @@
     for step in reversed(range(ITERS)):
         spread_t, u_prev, ba, whole, factor, others_here, others_slot, piece = saved[step]
         prior_grad = prior_grad + jnp.sum(grad_total, axis=2)
-        grad_spread = jnp.einsum("kv,vcs->kcs", col_hot, grad_total, precision=EXACT)
+        grad_spread = pick(col_hot, grad_total)
         acc, grad_ba, grad_factor = bwd_messages(grad_spread, grad_m, ba, factor, ew, acc)
         grad_here = grad_factor * sign_slot * others_slot
         grad_slot = grad_factor * sign_slot * others_here
-        grad_others = jnp.einsum("kc,krs->crs", row_hot, grad_slot, precision=EXACT)
+        grad_others = place(row_hot, grad_slot)
         grad_rows = others_backward(piece, grad_others, check_blocks, n_var)
         unused, pull = jax.vjp(lambda w: combine(w, row_hot, same_row), whole)
         grad_whole = pull((grad_rows, grad_here))[0]
         grad_m, colsum = bwd_products(spread_t, u_prev, em, grad_ba, grad_whole, step > 0)
         grad_total = checks_total(
-            jnp.einsum("kv,kcs->vcs", col_hot, colsum, precision=EXACT), n_chk
+            place(col_hot, colsum), n_chk
         )
     prior_grad = prior_grad + jnp.sum(grad_total, axis=2)
     weight_grad = edge * jnp.swapaxes(jnp.sum(acc, axis=3), 1, 2)

time: 177 us -> 169 us (0.955)
  Pallas kernels: 61.9 us -> 52.3 us
  matrix products: 6.85 us -> 0.51 us
  other arithmetic: 18 us -> 23.1 us
  between operations: 6.64 us -> 11.6 us
  local copies, waits for them, and re-layouts: 11.9 us -> 9.81 us
    pallas_call x8, Pallas kernels: 61.9 us -> 52.3 us  [_call(): pl.pallas_call(kernel, grid=(dense.shape[0], dense.shape[2] // ROW_BLOCK)...]
    dot_general x11 -> x0, matrix products: 6.34 us -> none  [the longest x2 2.41 us: body(): jnp.einsum('kv,kcs->vcs', col_hot, colsum, precision=EXACT)]
    add x0 -> x10, other arithmetic: none -> 2.54 us  [the longest x6 2.44 us: place(): value = value + jnp.where(hot[k, j] > 0, values[k], 0.0)]
    another operation x0 -> x10, other arithmetic: none -> 1.97 us  [the longest x4 1.89 us: pick(): return jnp.stack(parts)]
    dot_general x5 -> x0, local copies, waits for them, and re-layouts: 1.9 us -> none  [the longest x2 1.24 us: body(): jnp.einsum('kv,vcs->kcs', col_hot, grad_total, precision=EXACT)]
  transfers between devices with their start and end apart: 20 -> 20, of which waited for: 16 -> 15; matrix products, arithmetic and copies ran while one was open for 8% -> 8% of each run, Pallas kernels for 8% -> 7%
where the time goes in v3:
time: 169 us; the launch traced here: 168 us
  Pallas kernels  52.3 us (31%)
  waiting for transfers between devices  41.9 us (25%)
  starting transfers between devices  28.4 us (17%)
  other arithmetic  23.1 us (14%)
  between operations  11.6 us (7%)
  local copies, waits for them, and re-layouts  9.81 us (6%)
    pallas_call x8, Pallas kernels, _call(): pl.pallas_call(kernel, grid=(dense.shape[0], dense.shape[2] // ROW_BLOCK)...  52.3 us
    ppermute x20, waiting for transfers between devices, _swap(): return lax.ppermute(value, axis, perm)  41.9 us
    ppermute x20, starting transfers between devices, _swap(): return lax.ppermute(value, axis, perm)  28.4 us
    select_n x6, other arithmetic, combine(): value = value * jnp.where(same_row[k, other], whole[other], 1.0)  8.29 us
  transfers between devices with their start and end apart: 20, of which 15 were waited for; matrix products, arithmetic and copies ran while one was open for 8% of the time, Pallas kernels for 7%

profile of v3, /device:TPU:0, one launch (start us, length us, event | category | flops | bytes accessed | tf_op | source)
XLA Modules:
  0.0 167.7 jit_solution(17188210703782711198)
XLA Ops:
  1.4 1.0 slice_reduce_fusion
  2.7 0.9 reshape_squeeze.3
  12.3 2.6 %broadcast_in_dim.205.refs_1_.ew_ref.refs_2_.refs_3_.refs_4_ = f32[2,64,64,128]{3,2,1,0:T(8,128)} broadcast(f32[2,64,64]{2,1,0:T(8,128)S(1)} %multiply_bitcast_fusion), dimensions={0,1,2} | broadcast | bytes 4227072 | tf_op jit(solution)/shard_map/broadcast_in_dim | solution.py:399
  14.8 4.3 %shard_map.94 = (f32[2,64,64,128]{3,2,1,0:T(8,128)}, f32[2,64,128]{2,1,0:T(8,128)}) custom-call(f32[2,64,128]{2,1,0:T(8,128)} %broadcast_in_dim.202.refs_0_, f32[2,64,64,128]{3,2,1,0:T(8,128)} %broadcast_in_dim.205.refs_1_.ew_ref.refs_2_.refs_3_.refs_4_), custom_call_target="tpu_custom_call" | custom-call | tf_op jit(solution)/shard_map/pallas_call | solution.py:201
  19.2 1.4 slice_select_fusion.7
  26.9 2.6 %collective-permute-start.1 = (f32[4,64,128]{2,1,0:T(8,128)S(1)}, f32[4,64,128]{2,1,0:T(8,128)S(1)}, u32[]{:S(2)}, u32[]{:S(2)}) collective-permute-start(f32[4,64,128]{2,1,0:T(8,128)S(1)} %fusion.17), channel_id=1, source_target_pairs={{0,2},{1,3},{2,0},{3,1},{4,6},{5,7},{6,4},{7,5},{8,10},{9,11},{10,... | collective-permute-start | bytes 393224 | tf_op jit(solution)/shard_map/ppermute | solution.py:320
  29.8 3.8 %collective-permute-done.1 = f32[4,64,128]{2,1,0:T(8,128)S(1)} collective-permute-done((f32[4,64,128]{2,1,0:T(8,128)S(1)}, f32[4,64,128]{2,1,0:T(8,128)S(1)}, u32[]{:S(2)}, u32[]{:S(2)}) %collective-permute-start.1) | collective-permute-done | bytes 131104 | tf_op jit(solution)/shard_map/ppermute | solution.py:320
  33.6 1.8 %collective-permute-start.2 = (f32[4,64,128]{2,1,0:T(8,128)S(1)}, f32[4,64,128]{2,1,0:T(8,128)S(1)}, u32[]{:S(2)}, u32[]{:S(2)}) collective-permute-start(f32[4,64,128]{2,1,0:T(8,128)S(1)} %fusion.26), channel_id=1, source_target_pairs={{0,4},{1,5},{2,6},{3,7},{4,0},{5,1},{6,2},{7,3},{8,12},{9,13},{10,... | collective-permute-start | bytes 393224 | tf_op jit(solution)/shard_map/ppermute | solution.py:320
  35.5 1.4 slice_select_fusion.6
  36.9 2.1 %collective-permute-done.2 = f32[4,64,128]{2,1,0:T(8,128)S(1)} collective-permute-done((f32[4,64,128]{2,1,0:T(8,128)S(1)}, f32[4,64,128]{2,1,0:T(8,128)S(1)}, u32[]{:S(2)}, u32[]{:S(2)}) %collective-permute-start.2) | collective-permute-done | bytes 131104 | tf_op jit(solution)/shard_map/ppermute | solution.py:320
  39.7 5.7 %shard_map.95 = (f32[2,64,64,128]{3,2,1,0:T(8,128)}, f32[2,64,128]{2,1,0:T(8,128)}) custom-call(f32[2,64,64,128]{3,2,1,0:T(8,128)} %get-tuple-element.18.ba_ref.refs_2_, f32[2,64,128]{2,1,0:T(8,128)} %multiply_multiply_fusion.1.f_ref.refs_3_, f32[2,64,64,128]{3,2,1,0:T(8,128)} %broadcast_in_dim.205.refs_1_.ew_ref.refs_2_.refs_3_.refs_4_), custom_call_target="tpu_custom_call" | custom-call | tf_op jit(solution)/shard_map/pallas_call | solution.py:201
  46.2 1.7 %collective-permute-start.3 = (f32[4,64,128]{2,1,0:T(8,128)S(1)}, f32[4,64,128]{2,1,0:T(8,128)S(1)}, u32[]{:S(2)}, u32[]{:S(2)}) collective-permute-start(f32[4,64,128]{2,1,0:T(8,128)S(1)} %pad_maximum_fusion.1), channel_id=1, source_target_pairs={{0,8},{8,0},{16,24},{24,16},{1,9},{9,1},{17,25},{25,17},{2,10},{10... | collective-permute-start | bytes 393224 | tf_op jit(solution)/shard_map/ppermute | solution.py:320
  47.9 3.3 %collective-permute-done.3 = f32[4,64,128]{2,1,0:T(8,128)S(1)} collective-permute-done((f32[4,64,128]{2,1,0:T(8,128)S(1)}, f32[4,64,128]{2,1,0:T(8,128)S(1)}, u32[]{:S(2)}, u32[]{:S(2)}) %collective-permute-start.3) | collective-permute-done | bytes 131104 | tf_op jit(solution)/shard_map/ppermute | solution.py:320
  51.3 2.7 %collective-permute-start.4 = (f32[4,64,128]{2,1,0:T(8,128)S(1)}, f32[4,64,128]{2,1,0:T(8,128)S(1)}, u32[]{:S(2)}, u32[]{:S(2)}) collective-permute-start(f32[4,64,128]{2,1,0:T(8,128)S(1)} %fusion.15), channel_id=1, source_target_pairs={{0,16},{8,24},{16,0},{24,8},{1,17},{9,25},{17,1},{25,9},{2,18},{10... | collective-permute-start | bytes 393224 | tf_op jit(solution)/shard_map/ppermute | solution.py:320
  54.0 4.6 %collective-permute-done.4 = f32[4,64,128]{2,1,0:T(8,128)S(1)} collective-permute-done((f32[4,64,128]{2,1,0:T(8,128)S(1)}, f32[4,64,128]{2,1,0:T(8,128)S(1)}, u32[]{:S(2)}, u32[]{:S(2)}) %collective-permute-start.4) | collective-permute-done | bytes 131104 | tf_op jit(solution)/shard_map/ppermute | solution.py:320
  59.4 5.7 %shard_map.96 = (f32[2,64,64,128]{3,2,1,0:T(8,128)}, f32[2,64,128]{2,1,0:T(8,128)}) custom-call(f32[2,64,128]{2,1,0:T(8,128)} %pad_maximum_fusion.10.refs_0_, f32[2,64,64,128]{3,2,1,0:T(8,128)} %get-tuple-element.21.refs_1_, f32[2,64,64,128]{3,2,1,0:T(8,128)} %broadcast_in_dim.205.refs_1_.ew_ref.refs_2_.refs_3_.refs_4_), custom_call_target="tpu_custom_call" | custom-call | tf_op jit(solution)/shard_map/pallas_call | solution.py:201
  65.1 1.4 slice_select_fusion.5
  66.6 1.3 collective-permute-done.5
  68.0 1.6 collective-permute-start.6
  70.2 3.4 %collective-permute-done.6 = f32[4,64,128]{2,1,0:T(8,128)S(1)} collective-permute-done((f32[4,64,128]{2,1,0:T(8,128)S(1)}, f32[4,64,128]{2,1,0:T(8,128)S(1)}, u32[]{:S(2)}, u32[]{:S(2)}) %collective-permute-start.6) | collective-permute-done | bytes 131104 | tf_op jit(solution)/shard_map/ppermute | solution.py:320
  73.6 1.6 collective-permute-start.7
  75.2 1.4 slice_select_fusion.4
  76.6 2.0 %collective-permute-done.7 = f32[4,64,128]{2,1,0:T(8,128)S(1)} collective-permute-done((f32[4,64,128]{2,1,0:T(8,128)S(1)}, f32[4,64,128]{2,1,0:T(8,128)S(1)}, u32[]{:S(2)}, u32[]{:S(2)}) %collective-permute-start.7) | collective-permute-done | bytes 131104 | tf_op jit(solution)/shard_map/ppermute | solution.py:320
  79.3 6.8 %shard_map.98 = (f32[2,64,64,128]{3,2,1,0:T(8,128)}, f32[2,64,64,128]{3,2,1,0:T(8,128)}, f32[2,64,128]{2,1,0:T(8,128)}) custom-call(f32[2,64,128]{2,1,0:T(8,128)} %pad_maximum_fusion.13.refs_0_, f32[2,64,64,128]{3,2,1,0:T(8,128)} %get-tuple-element.22.ba_ref.refs_1_, f32[2,64,128]{2,1,0:T(8,128)} %multiply_multiply_fusion.f_ref.refs_2_, ...), custom_call_target="tpu_custom_call" | custom-call | tf_op jit(solution)/shard_map/pallas_call | solution.py:201
  87.1 1.3 collective-permute-done.10
  88.5 1.6 collective-permute-start.11
  90.1 4.0 %collective-permute-done.11 = f32[4,64,128]{2,1,0:T(8,128)S(1)} collective-permute-done((f32[4,64,128]{2,1,0:T(8,128)S(1)}, f32[4,64,128]{2,1,0:T(8,128)S(1)}, u32[]{:S(2)}, u32[]{:S(2)}) %collective-permute-start.11) | collective-permute-done | bytes 131104 | tf_op jit(solution)/shard_map/ppermute | solution.py:320
  94.1 1.6 collective-permute-start.12
  95.8 1.3 slice_select_fusion.3
  97.1 2.1 %collective-permute-done.12 = f32[4,64,128]{2,1,0:T(8,128)S(1)} collective-permute-done((f32[4,64,128]{2,1,0:T(8,128)S(1)}, f32[4,64,128]{2,1,0:T(8,128)S(1)}, u32[]{:S(2)}, u32[]{:S(2)}) %collective-permute-start.12) | collective-permute-done | bytes 131104 | tf_op jit(solution)/shard_map/ppermute | solution.py:320
  100.0 8.4 %shard_map.99 = (f32[2,64,64,128]{3,2,1,0:T(8,128)}, f32[2,64,128]{2,1,0:T(8,128)}) custom-call(f32[2,64,128]{2,1,0:T(8,128)} %pad_maximum_fusion.10.refs_0_, f32[2,64,64,128]{3,2,1,0:T(8,128)} %get-tuple-element.21.refs_1_, f32[2,64,64,128]{3,2,1,0:T(8,128)} %broadcast_in_dim.205.refs_1_.ew_ref.refs_2_.refs_3_.refs_4_, ...), custom_call_target="tpu_custom_call" | custom-call | tf_op jit(solution)/shard_map/pallas_call | solution.py:201
  110.0 4.3 %collective-permute-done.13 = f32[4,64,128]{2,1,0:T(8,128)S(1)} collective-permute-done((f32[4,64,128]{2,1,0:T(8,128)S(1)}, f32[4,64,128]{2,1,0:T(8,128)S(1)}, u32[]{:S(2)}, u32[]{:S(2)}) %collective-permute-start.13) | collective-permute-done | bytes 131104 | tf_op jit(solution)/shard_map/ppermute | solution.py:320
  114.2 2.1 %collective-permute-start.14 = (f32[4,64,128]{2,1,0:T(8,128)S(1)}, f32[4,64,128]{2,1,0:T(8,128)S(1)}, u32[]{:S(2)}, u32[]{:S(2)}) collective-permute-start(f32[4,64,128]{2,1,0:T(8,128)S(1)} %fusion.13), channel_id=1, source_target_pairs={{0,16},{8,24},{16,0},{24,8},{1,17},{9,25},{17,1},{25,9},{2,18},{10... | collective-permute-start | bytes 393224 | tf_op jit(solution)/shard_map/ppermute | solution.py:320
  116.5 5.7 %shard_map.97 = (f32[2,64,64,128]{3,2,1,0:T(8,128)}, f32[2,64,128]{2,1,0:T(8,128)}) custom-call(f32[2,64,64,128]{3,2,1,0:T(8,128)} %get-tuple-element.22.ba_ref.refs_1_, f32[2,64,128]{2,1,0:T(8,128)} %multiply_multiply_fusion.f_ref.refs_2_, f32[2,64,64,128]{3,2,1,0:T(8,128)} %broadcast_in_dim.205.refs_1_.ew_ref.refs_2_.refs_3_.refs_4_), custom_call_target="tpu_custom_call" | custom-call | tf_op jit(solution)/shard_map/pallas_call | solution.py:201
  123.0 9.4 %shard_map.100 = (f32[2,64,64,128]{3,2,1,0:T(8,128)}, f32[2,64,64,128]{3,2,1,0:T(8,128)}, f32[2,64,128]{2,1,0:T(8,128)}) custom-call(f32[2,64,128]{2,1,0:T(8,128)} %pad_maximum_fusion.14.refs_0_, f32[2,64,64,128]{3,2,1,0:T(8,128)} %get-tuple-element.28.refs_1_, f32[2,64,64,128]{3,2,1,0:T(8,128)} %get-tuple-element.18.ba_ref.refs_2_, ...), custom_call_target="tpu_custom_call" | custom-call | tf_op jit(solution)/shard_map/pallas_call | solution.py:201
  132.4 0.9 fusion.4
  133.5 2.1 %collective-permute-start.8 = (f32[4,64,128]{2,1,0:T(8,128)S(1)}, f32[4,64,128]{2,1,0:T(8,128)S(1)}, u32[]{:S(2)}, u32[]{:S(2)}) collective-permute-start(f32[4,64,128]{2,1,0:T(8,128)S(1)} %pad_maximum_fusion.3), channel_id=1, source_target_pairs={{0,8},{8,0},{16,24},{24,16},{1,9},{9,1},{17,25},{25,17},{2,10},{10... | collective-permute-start | bytes 393224 | tf_op jit(solution)/shard_map/ppermute | solution.py:320
  135.6 1.6 collective-permute-start.16
  137.2 2.5 %collective-permute-done.8 = f32[4,64,128]{2,1,0:T(8,128)S(1)} collective-permute-done((f32[4,64,128]{2,1,0:T(8,128)S(1)}, f32[4,64,128]{2,1,0:T(8,128)S(1)}, u32[]{:S(2)}, u32[]{:S(2)}) %collective-permute-start.8) | collective-permute-done | bytes 131104 | tf_op jit(solution)/shard_map/ppermute | solution.py:320
  139.8 0.9 collective-permute-start.9
  141.3 1.6 collective-permute-start.17
  142.9 1.3 slice_select_fusion.1
  144.2 2.1 %collective-permute-done.17 = f32[4,64,128]{2,1,0:T(8,128)S(1)} collective-permute-done((f32[4,64,128]{2,1,0:T(8,128)S(1)}, f32[4,64,128]{2,1,0:T(8,128)S(1)}, u32[]{:S(2)}, u32[]{:S(2)}) %collective-permute-start.17) | collective-permute-done | bytes 131104 | tf_op jit(solution)/shard_map/ppermute | solution.py:320
  147.2 6.2 %shard_map.101 = f32[2,64,128]{2,1,0:T(8,128)} custom-call(f32[2,64,128]{2,1,0:T(8,128)} %broadcast_in_dim.202.refs_0_, f32[2,64,64,128]{3,2,1,0:T(8,128)} %broadcast_in_dim.205.refs_1_.ew_ref.refs_2_.refs_3_.refs_4_, f32[2,64,64,128]{3,2,1,0:T(8,128)} %get-tuple-element.31.refs_2_, f32[2,64,128]{2,1,0:T(8,128)} %pad_add_fusion.refs_3_), custom_call_target="tpu_custom_call" | custom-call | tf_op jit(solution)/shard_map/pallas_call | solution.py:201
  154.2 1.2 collective-permute-start.18
  156.2 3.3 %reduce_sum.40 = f32[2,64,64]{2,1,0:T(8,128)S(1)} reduce(f32[2,64,64,128]{3,2,1,0:T(8,128)} %get-tuple-element.30, f32[]{:T(128)} %constant.47.clone.1), dimensions={3}, to_apply=%region_0.1 | reduce | flops 1040384 | bytes 4227076 | tf_op jit(solution)/shard_map/reduce_sum | solution.py:442
  159.6 2.1 %collective-permute-start.19 = (f32[4,64,128]{2,1,0:T(8,128)S(1)}, f32[4,64,128]{2,1,0:T(8,128)S(1)}, u32[]{:S(2)}, u32[]{:S(2)}) collective-permute-start(f32[4,64,128]{2,1,0:T(8,128)S(1)} %fusion.12), channel_id=1, source_target_pairs={{0,16},{8,24},{16,0},{24,8},{1,17},{9,25},{17,1},{25,9},{2,18},{10... | collective-permute-start | bytes 393224 | tf_op jit(solution)/shard_map/ppermute | solution.py:320
  162.6 4.3 %collective-permute-done.19 = f32[4,64,128]{2,1,0:T(8,128)S(1)} collective-permute-done((f32[4,64,128]{2,1,0:T(8,128)S(1)}, f32[4,64,128]{2,1,0:T(8,128)S(1)}, u32[]{:S(2)}, u32[]{:S(2)}) %collective-permute-start.19) | collective-permute-done | bytes 131104 | tf_op jit(solution)/shard_map/ppermute | solution.py:320
  (94 shorter events, 18.6 us)
Async XLA Ops:
  12.3 14.5 %copy-start.3 = (s32[256,128]{1,0:T(8,128)S(1)}, s32[256,128]{1,0:T(8,128)}, u32[]{:S(2)}) copy-start(s32[256,128]{1,0:T(8,128)} %param.11) | copy-start | bytes 393220
  20.6 6.2 %collective-permute-start = (f32[4,64,128]{2,1,0:T(8,128)S(1)}, f32[4,64,128]{2,1,0:T(8,128)S(1)}, u32[]{:S(2)}, u32[]{:S(2)}) collective-permute-start(f32[4,64,128]{2,1,0:T(8,128)S(1)} %pad_maximum_fusion), channel_id=1, source_target_pairs={{0,1},{1,0},{2,3},{3,2},{4,5},{5,4},{6,7},{7,6},{8,9},{9,8},{10,11... | collective-permute-start | bytes 393224 | tf_op jit(solution)/shard_map/ppermute | solution.py:320
  26.9 6.7 %collective-permute-start.1 = (f32[4,64,128]{2,1,0:T(8,128)S(1)}, f32[4,64,128]{2,1,0:T(8,128)S(1)}, u32[]{:S(2)}, u32[]{:S(2)}) collective-permute-start(f32[4,64,128]{2,1,0:T(8,128)S(1)} %fusion.17), channel_id=1, source_target_pairs={{0,2},{1,3},{2,0},{3,1},{4,6},{5,7},{6,4},{7,5},{8,10},{9,11},{10,... | collective-permute-start | bytes 393224 | tf_op jit(solution)/shard_map/ppermute | solution.py:320
  33.6 5.4 %collective-permute-start.2 = (f32[4,64,128]{2,1,0:T(8,128)S(1)}, f32[4,64,128]{2,1,0:T(8,128)S(1)}, u32[]{:S(2)}, u32[]{:S(2)}) collective-permute-start(f32[4,64,128]{2,1,0:T(8,128)S(1)} %fusion.26), channel_id=1, source_target_pairs={{0,4},{1,5},{2,6},{3,7},{4,0},{5,1},{6,2},{7,3},{8,12},{9,13},{10,... | collective-permute-start | bytes 393224 | tf_op jit(solution)/shard_map/ppermute | solution.py:320
  46.2 5.0 %collective-permute-start.3 = (f32[4,64,128]{2,1,0:T(8,128)S(1)}, f32[4,64,128]{2,1,0:T(8,128)S(1)}, u32[]{:S(2)}, u32[]{:S(2)}) collective-permute-start(f32[4,64,128]{2,1,0:T(8,128)S(1)} %pad_maximum_fusion.1), channel_id=1, source_target_pairs={{0,8},{8,0},{16,24},{24,16},{1,9},{9,1},{17,25},{25,17},{2,10},{10... | collective-permute-start | bytes 393224 | tf_op jit(solution)/shard_map/ppermute | solution.py:320
  51.3 7.3 %collective-permute-start.4 = (f32[4,64,128]{2,1,0:T(8,128)S(1)}, f32[4,64,128]{2,1,0:T(8,128)S(1)}, u32[]{:S(2)}, u32[]{:S(2)}) collective-permute-start(f32[4,64,128]{2,1,0:T(8,128)S(1)} %fusion.15), channel_id=1, source_target_pairs={{0,16},{8,24},{16,0},{24,8},{1,17},{9,25},{17,1},{25,9},{2,18},{10... | collective-permute-start | bytes 393224 | tf_op jit(solution)/shard_map/ppermute | solution.py:320
  59.4 10.2 %copy-start.2 = (f32[256,128]{1,0:T(8,128)S(1)}, f32[256,128]{1,0:T(8,128)}, u32[]{:S(2)}) copy-start(f32[256,128]{1,0:T(8,128)} %param.13) | copy-start | bytes 393220
  66.5 1.4 collective-permute-start.5
  68.0 5.6 %collective-permute-start.6 = (f32[4,64,128]{2,1,0:T(8,128)S(1)}, f32[4,64,128]{2,1,0:T(8,128)S(1)}, u32[]{:S(2)}, u32[]{:S(2)}) collective-permute-start(f32[4,64,128]{2,1,0:T(8,128)S(1)} %fusion.16), channel_id=1, source_target_pairs={{0,2},{1,3},{2,0},{3,1},{4,6},{5,7},{6,4},{7,5},{8,10},{9,11},{10,... | collective-permute-start | bytes 393224 | tf_op jit(solution)/shard_map/ppermute | solution.py:320
  73.6 5.0 %collective-permute-start.7 = (f32[4,64,128]{2,1,0:T(8,128)S(1)}, f32[4,64,128]{2,1,0:T(8,128)S(1)}, u32[]{:S(2)}, u32[]{:S(2)}) collective-permute-start(f32[4,64,128]{2,1,0:T(8,128)S(1)} %fusion.25), channel_id=1, source_target_pairs={{0,4},{1,5},{2,6},{3,7},{4,0},{5,1},{6,2},{7,3},{8,12},{9,13},{10,... | collective-permute-start | bytes 393224 | tf_op jit(solution)/shard_map/ppermute | solution.py:320
  79.3 19.9 %copy-start.1 = (f32[2,64,128]{2,1,0:T(8,128)S(1)}, f32[2,64,128]{2,1,0:T(8,128)}, u32[]{:S(2)}) copy-start(f32[2,64,128]{2,1,0:T(8,128)} %get-tuple-element.23) | copy-start | bytes 196612
  87.0 1.4 collective-permute-start.10
  88.5 5.6 %collective-permute-start.11 = (f32[4,64,128]{2,1,0:T(8,128)S(1)}, f32[4,64,128]{2,1,0:T(8,128)S(1)}, u32[]{:S(2)}, u32[]{:S(2)}) collective-permute-start(f32[4,64,128]{2,1,0:T(8,128)S(1)} %multiply_add_fusion.5), channel_id=1, source_target_pairs={{0,2},{1,3},{2,0},{3,1},{4,6},{5,7},{6,4},{7,5},{8,10},{9,11},{10,... | collective-permute-start | bytes 393224 | tf_op jit(solution)/shard_map/ppermute | solution.py:320
  94.1 5.0 %collective-permute-start.12 = (f32[4,64,128]{2,1,0:T(8,128)S(1)}, f32[4,64,128]{2,1,0:T(8,128)S(1)}, u32[]{:S(2)}, u32[]{:S(2)}) collective-permute-start(f32[4,64,128]{2,1,0:T(8,128)S(1)} %multiply_add_fusion.4), channel_id=1, source_target_pairs={{0,4},{1,5},{2,6},{3,7},{4,0},{5,1},{6,2},{7,3},{8,12},{9,13},{10,... | collective-permute-start | bytes 393224 | tf_op jit(solution)/shard_map/ppermute | solution.py:320
  109.2 5.0 %collective-permute-start.13 = (f32[4,64,128]{2,1,0:T(8,128)S(1)}, f32[4,64,128]{2,1,0:T(8,128)S(1)}, u32[]{:S(2)}, u32[]{:S(2)}) collective-permute-start(f32[4,64,128]{2,1,0:T(8,128)S(1)} %pad_maximum_fusion.5), channel_id=1, source_target_pairs={{0,8},{8,0},{16,24},{24,16},{1,9},{9,1},{17,25},{25,17},{2,10},{10... | collective-permute-start | bytes 393224 | tf_op jit(solution)/shard_map/ppermute | solution.py:320
  114.2 8.0 %collective-permute-start.14 = (f32[4,64,128]{2,1,0:T(8,128)S(1)}, f32[4,64,128]{2,1,0:T(8,128)S(1)}, u32[]{:S(2)}, u32[]{:S(2)}) collective-permute-start(f32[4,64,128]{2,1,0:T(8,128)S(1)} %fusion.13), channel_id=1, source_target_pairs={{0,16},{8,24},{16,0},{24,8},{1,17},{9,25},{17,1},{25,9},{2,18},{10... | collective-permute-start | bytes 393224 | tf_op jit(solution)/shard_map/ppermute | solution.py:320
  123.0 10.4 %copy-start.4 = (f32[2,64,128]{2,1,0:T(8,128)S(1)}, f32[2,64,128]{2,1,0:T(8,128)}, u32[]{:S(2)}) copy-start(f32[2,64,128]{2,1,0:T(8,128)} %get-tuple-element.24) | copy-start | bytes 196612
  132.4 14.0 %copy-start = (f32[2,64,128]{2,1,0:T(8,128)S(1)}, f32[2,64,128]{2,1,0:T(8,128)}, u32[]{:S(2)}) copy-start(f32[2,64,128]{2,1,0:T(8,128)} %get-tuple-element.19) | copy-start | bytes 196612
  133.4 2.2 %collective-permute-start.15 = (f32[4,64,128]{2,1,0:T(8,128)S(1)}, f32[4,64,128]{2,1,0:T(8,128)S(1)}, u32[]{:S(2)}, u32[]{:S(2)}) collective-permute-start(f32[4,64,128]{2,1,0:T(8,128)S(1)} %pad_maximum_fusion.6), channel_id=1, source_target_pairs={{0,1},{1,0},{2,3},{3,2},{4,5},{5,4},{6,7},{7,6},{8,9},{9,8},{10,11... | collective-permute-start | bytes 393224 | tf_op jit(solution)/shard_map/ppermute | solution.py:320
  133.5 6.2 %collective-permute-start.8 = (f32[4,64,128]{2,1,0:T(8,128)S(1)}, f32[4,64,128]{2,1,0:T(8,128)S(1)}, u32[]{:S(2)}, u32[]{:S(2)}) collective-permute-start(f32[4,64,128]{2,1,0:T(8,128)S(1)} %pad_maximum_fusion.3), channel_id=1, source_target_pairs={{0,8},{8,0},{16,24},{24,16},{1,9},{9,1},{17,25},{25,17},{2,10},{10... | collective-permute-start | bytes 393224 | tf_op jit(solution)/shard_map/ppermute | solution.py:320
  135.6 5.7 %collective-permute-start.16 = (f32[4,64,128]{2,1,0:T(8,128)S(1)}, f32[4,64,128]{2,1,0:T(8,128)S(1)}, u32[]{:S(2)}, u32[]{:S(2)}) collective-permute-start(f32[4,64,128]{2,1,0:T(8,128)S(1)} %multiply_add_fusion.2), channel_id=1, source_target_pairs={{0,2},{1,3},{2,0},{3,1},{4,6},{5,7},{6,4},{7,5},{8,10},{9,11},{10,... | collective-permute-start | bytes 393224 | tf_op jit(solution)/shard_map/ppermute | solution.py:320
  139.8 15.7 %collective-permute-start.9 = (f32[4,64,128]{2,1,0:T(8,128)S(1)}, f32[4,64,128]{2,1,0:T(8,128)S(1)}, u32[]{:S(2)}, u32[]{:S(2)}) collective-permute-start(f32[4,64,128]{2,1,0:T(8,128)S(1)} %fusion.14), channel_id=1, source_target_pairs={{0,16},{8,24},{16,0},{24,8},{1,17},{9,25},{17,1},{25,9},{2,18},{10... | collective-permute-start | bytes 393224 | tf_op jit(solution)/shard_map/ppermute | solution.py:320
  141.3 5.0 %collective-permute-start.17 = (f32[4,64,128]{2,1,0:T(8,128)S(1)}, f32[4,64,128]{2,1,0:T(8,128)S(1)}, u32[]{:S(2)}, u32[]{:S(2)}) collective-permute-start(f32[4,64,128]{2,1,0:T(8,128)S(1)} %multiply_add_fusion.1), channel_id=1, source_target_pairs={{0,4},{1,5},{2,6},{3,7},{4,0},{5,1},{6,2},{7,3},{8,12},{9,13},{10,... | collective-permute-start | bytes 393224 | tf_op jit(solution)/shard_map/ppermute | solution.py:320
  154.2 5.3 %collective-permute-start.18 = (f32[4,64,128]{2,1,0:T(8,128)S(1)}, f32[4,64,128]{2,1,0:T(8,128)S(1)}, u32[]{:S(2)}, u32[]{:S(2)}) collective-permute-start(f32[4,64,128]{2,1,0:T(8,128)S(1)} %pad_maximum_fusion.7), channel_id=1, source_target_pairs={{0,8},{8,0},{16,24},{24,16},{1,9},{9,1},{17,25},{25,17},{2,10},{10... | collective-permute-start | bytes 393224 | tf_op jit(solution)/shard_map/ppermute | solution.py:320
  159.6 7.3 %collective-permute-start.19 = (f32[4,64,128]{2,1,0:T(8,128)S(1)}, f32[4,64,128]{2,1,0:T(8,128)S(1)}, u32[]{:S(2)}, u32[]{:S(2)}) collective-permute-start(f32[4,64,128]{2,1,0:T(8,128)S(1)} %fusion.12), channel_id=1, source_target_pairs={{0,16},{8,24},{16,0},{24,8},{1,17},{9,25},{17,1},{25,9},{2,18},{10... | collective-permute-start | bytes 393224 | tf_op jit(solution)/shard_map/ppermute | solution.py:320

commit v4 on v3

--- a/solution.py
+++ b/solution.py
@@ -64,25 +64,34 @@
     return jnp.broadcast_to(ref[0, pl.ds(c, 1), :], shape)
 
 
-def _fwd_products_kernel(has_u, *refs):
-    if has_u:
-        spread_ref, u_ref, em_ref, ba_ref, whole_ref, h_scr = refs
-    else:
-        spread_ref, em_ref, ba_ref, whole_ref, h_scr = refs
-    n_c = em_ref.shape[1]
-    shape = em_ref.shape[2:]
+def _row_block(pos_ref, k):
+    return pos_ref[2 * k]
+
+
+def _col_block(pos_ref, k):
+    return pos_ref[2 * k + 1]
+
+
+def _fwd_products_kernel(has_u, slots, blocks, pos_ref, *refs):
+    refs = list(refs)
+    spread_ref = refs.pop(0)
+    u_ref = refs.pop(0) if has_u else None
+    ew_ref, ba_ref, whole_ref, rows_ref, here_ref, h_scr = refs
+    k = pl.program_id(0)
+    n_c = ew_ref.shape[1]
+    shape = ew_ref.shape[2:]
 
     def forward(c, carry):
         m = _spread_row(spread_ref, c, shape)
         if has_u:
             m = m - u_ref[0, c]
-        h = jnp.where(em_ref[0, c] > 0, jnp.tanh(0.5 * m), 1.0)
+        h = jnp.where(ew_ref[0, c] > 0, jnp.tanh(0.5 * m), 1.0)
         h_scr[c] = h
         ba_ref[0, c] = carry
         return carry * h
 
     whole = lax.fori_loop(0, n_c, forward, jnp.ones(shape, F32), unroll=UNROLL)
-    whole_ref[0] = whole
+    whole_ref[k] = whole
 
     def backward(i, carry):
         c = n_c - 1 - i
@@ -91,34 +100,65 @@
 
     lax.fori_loop(0, n_c, backward, jnp.ones(shape, F32), unroll=UNROLL)
 
-
-def _fwd_messages_kernel(ba_ref, f_ref, ew_ref, u_ref, col_ref):
-    first = pl.program_id(1) == 0
+    @pl.when(k == slots - 1)
+    def _():
+        wholes = [whole_ref[j] for j in range(slots)]
+        rows_of = [_row_block(pos_ref, j) for j in range(slots)]
+        for block in range(blocks):
+            value = jnp.ones(shape, F32)
+            for j in range(slots):
+                value = value * jnp.where(rows_of[j] == block, wholes[j], 1.0)
+            rows_ref[block] = value
+        for j in range(slots):
+            value = jnp.ones(shape, F32)
+            for other in range(slots):
+                if other != j:
+                    value = value * jnp.where(rows_of[other] == rows_of[j], wholes[other], 1.0)
+            here_ref[j] = value
+
+
+def _fwd_messages_kernel(pos_ref, ba_ref, sign_ref, here_ref, others_ref, ew_ref, u_ref, col_ref):
+    k = pl.program_id(0)
     n_c = ba_ref.shape[1]
-    f = f_ref[0]
+
+    @pl.when(k == 0)
+    def _():
+        col_ref[...] = jnp.zeros(col_ref.shape, F32)
+
+    f = sign_ref[k] * here_ref[k] * others_ref[_row_block(pos_ref, k)]
+    q = _col_block(pos_ref, k)
 
     def body(c, carry):
         x = ba_ref[0, c] * f
         u = ew_ref[0, c] * jnp.log((1.0 + DAMP * x) / (1.0 - DAMP * x))
         u_ref[0, c] = u
-        row = jnp.sum(u, axis=0, keepdims=True)
-        col_ref[0, pl.ds(c, 1), :] = jnp.where(first, row, col_ref[0, pl.ds(c, 1), :] + row)
+        col_ref[q, pl.ds(c, 1), :] = col_ref[q, pl.ds(c, 1), :] + jnp.sum(u, axis=0, keepdims=True)
         return carry
 
     lax.fori_loop(0, n_c, body, 0, unroll=UNROLL)
 
 
-def _bwd_messages_kernel(has_next, has_acc, *refs):
+def _bwd_messages_kernel(has_next, has_acc, pos_ref, *refs):
     refs = list(refs)
     gsp_ref = refs.pop(0)
     gm_ref = refs.pop(0) if has_next else None
-    ba_ref, f_ref, ew_ref = refs[:3]
-    refs = refs[3:]
+    ba_ref, sign_ref, here_ref, others_ref, ew_ref = refs[:5]
+    refs = refs[5:]
     acc_ref = refs.pop(0) if has_acc else None
-    gw_ref, gba_ref, d1_ref = refs
+    gw_ref, gba_ref, ghere_ref, gothers_ref = refs
+    k = pl.program_id(0)
     n_c = ba_ref.shape[1]
     shape = ba_ref.shape[2:]
-    f = f_ref[0]
+
+    @pl.when(k == 0)
+    def _():
+        gothers_ref[...] = jnp.zeros(gothers_ref.shape, F32)
+
+    p = _row_block(pos_ref, k)
+    sign = sign_ref[k]
+    here = here_ref[k]
+    others = others_ref[p]
+    f = sign * here * others
 
     def body(c, total):
         gu = _spread_row(gsp_ref, c, shape)
@@ -136,28 +176,46 @@
         gba_ref[0, c] = gx * f
         return total + gx * ba
 
-    d1_ref[0] = lax.fori_loop(0, n_c, body, jnp.zeros(shape, F32), unroll=UNROLL)
-
-
-def _bwd_products_kernel(has_u, emit_gm, *refs):
+    grad_factor = lax.fori_loop(0, n_c, body, jnp.zeros(shape, F32), unroll=UNROLL)
+    ghere_ref[k] = grad_factor * sign * others
+    gothers_ref[p] = gothers_ref[p] + grad_factor * sign * here
+
+
+def _bwd_products_kernel(has_u, emit_gm, slots, pos_ref, *refs):
     refs = list(refs)
     spread_ref = refs.pop(0)
     u_ref = refs.pop(0) if has_u else None
-    em_ref, gba_ref, gwh_ref = refs[:3]
-    refs = refs[3:]
+    ew_ref, gba_ref, grows_ref, ghere_ref, whole_ref, here_ref = refs[:6]
+    refs = refs[6:]
     gm_ref = refs.pop(0) if emit_gm else None
     col_ref, h_scr, p_scr, q_scr = refs
-    first = pl.program_id(1) == 0
-    n_c = em_ref.shape[1]
-    shape = em_ref.shape[2:]
-    gwh = gwh_ref[0]
+    k = pl.program_id(0)
+    n_c = ew_ref.shape[1]
+    shape = ew_ref.shape[2:]
+
+    @pl.when(k == 0)
+    def _():
+        col_ref[...] = jnp.zeros(col_ref.shape, F32)
+
+    p = _row_block(pos_ref, k)
+    q = _col_block(pos_ref, k)
+    rows_of = [_row_block(pos_ref, j) for j in range(slots)]
+    gwh = grows_ref[p] * here_ref[k]
+    for other in range(slots):
+        term = jnp.where(rows_of[other] == p, ghere_ref[other], 0.0)
+        for third in range(slots):
+            if third != other:
+                term = term * jnp.where(
+                    (rows_of[third] == p) & (third != k), whole_ref[third], 1.0
+                )
+        gwh = gwh + jnp.where(other != k, term, 0.0)
 
     def forward(c, carry):
         prod, grad = carry
         m = _spread_row(spread_ref, c, shape)
         if has_u:
             m = m - u_ref[0, c]
-        h = jnp.where(em_ref[0, c] > 0, jnp.tanh(0.5 * m), 1.0)
+        h = jnp.where(ew_ref[0, c] > 0, jnp.tanh(0.5 * m), 1.0)
         h_scr[c] = h
         p_scr[c] = prod
         q_scr[c] = grad
@@ -173,98 +231,115 @@
         h = h_scr[c]
         before = p_scr[c]
         gh = q_scr[c] * prod + before * (grad + gwh * prod)
-        gm = jnp.where(em_ref[0, c] > 0, gh * (0.5 * (1.0 - h * h)), 0.0)
+        gm = jnp.where(ew_ref[0, c] > 0, gh * (0.5 * (1.0 - h * h)), 0.0)
         if emit_gm:
             gm_ref[0, c] = gm
-        row = jnp.sum(gm, axis=0, keepdims=True)
-        col_ref[0, pl.ds(c, 1), :] = jnp.where(first, row, col_ref[0, pl.ds(c, 1), :] + row)
+        col_ref[q, pl.ds(c, 1), :] = col_ref[q, pl.ds(c, 1), :] + jnp.sum(gm, axis=0, keepdims=True)
         return (prod * h, grad * h + gba_ref[0, c] * prod)
 
     lax.fori_loop(0, n_c, backward, (ones, zeros), unroll=UNROLL)
-
-
-ROW_BLOCK = 64
 
 
 def _spec(kind, shape):
     if kind == "dense":
-        return pl.BlockSpec((1, shape[1], ROW_BLOCK, shape[3]), lambda k, j: (k, 0, j, 0))
-    if kind == "rows":
-        return pl.BlockSpec((1, ROW_BLOCK, shape[2]), lambda k, j: (k, j, 0))
-    return pl.BlockSpec((1,) + tuple(shape[1:]), lambda k, j: (k, 0, 0))
-
-
-def _call(kernel, inputs, outputs, scratch=()):
-    in_specs = [_spec(kind, a.shape) for kind, a in inputs]
-    out_specs = [_spec(kind, o.shape) for kind, o in outputs]
+        return pl.BlockSpec((1,) + tuple(shape[1:]), lambda k, pos: (k, 0, 0, 0))
+    if kind == "column":
+        return pl.BlockSpec((1,) + tuple(shape[1:]), lambda k, pos: (pos[2 * k + 1], 0, 0))
+    return pl.BlockSpec(tuple(shape), lambda k, pos: (0,) * len(shape))
+
+
+def _call(kernel, pos, inputs, outputs, scratch=()):
+    from jax.experimental.pallas import tpu as pltpu
+
     dense = [a for kind, a in inputs if kind == "dense"][0]
+    grid_spec = pltpu.PrefetchScalarGridSpec(
+        num_scalar_prefetch=1,
+        grid=(dense.shape[0],),
+        in_specs=[_spec(kind, a.shape) for kind, a in inputs],
+        out_specs=[_spec(kind, o.shape) for kind, o in outputs],
+        scratch_shapes=list(scratch),
+    )
     return pl.pallas_call(
         kernel,
-        grid=(dense.shape[0], dense.shape[2] // ROW_BLOCK),
-        in_specs=in_specs,
-        out_specs=out_specs,
+        grid_spec=grid_spec,
         out_shape=[o for kind, o in outputs],
-        scratch_shapes=list(scratch),
-    )(*[a for kind, a in inputs])
-
-
-def fwd_products(spread, u, em):
-    k, c, r, s = em.shape
+    )(pos, *[a for kind, a in inputs])
+
+
+def _vmem(shape):
+    from jax.experimental.pallas import tpu as pltpu
+
+    return pltpu.VMEM(shape, F32)
+
+
+def fwd_products(pos, spread, u, ew, blocks):
+    k, c, r, s = ew.shape
     has_u = u is not None
-    inputs = [("cols", spread)] + ([("dense", u)] if has_u else []) + [("dense", em)]
-    outs = [("dense", jax.ShapeDtypeStruct(em.shape, F32)), ("rows", jax.ShapeDtypeStruct((k, r, s), F32))]
-    from jax.experimental.pallas import tpu as pltpu
-
+    inputs = [("column", spread)] + ([("dense", u)] if has_u else []) + [("dense", ew)]
+    outs = [
+        ("dense", jax.ShapeDtypeStruct(ew.shape, F32)),
+        ("full", jax.ShapeDtypeStruct((k, r, s), F32)),
+        ("full", jax.ShapeDtypeStruct((blocks, r, s), F32)),
+        ("full", jax.ShapeDtypeStruct((k, r, s), F32)),
+    ]
     return _call(
-        functools.partial(_fwd_products_kernel, has_u),
+        functools.partial(_fwd_products_kernel, has_u, k, blocks),
+        pos,
         inputs,
         outs,
-        [pltpu.VMEM((c, ROW_BLOCK, s), F32)],
-    )
-
-
-def fwd_messages(ba, f, ew):
+        [_vmem((c, r, s))],
+    )
+
+
+def fwd_messages(pos, ba, sign, here, others, ew, col_blocks):
     k, c, r, s = ba.shape
-    outs = [("dense", jax.ShapeDtypeStruct(ba.shape, F32)), ("cols", jax.ShapeDtypeStruct((k, c, s), F32))]
-    return _call(_fwd_messages_kernel, [("dense", ba), ("rows", f), ("dense", ew)], outs)
-
-
-def bwd_messages(gsp, gm, ba, f, ew, acc):
+    inputs = [("dense", ba), ("full", sign), ("full", here), ("full", others), ("dense", ew)]
+    outs = [
+        ("dense", jax.ShapeDtypeStruct(ba.shape, F32)),
+        ("full", jax.ShapeDtypeStruct((col_blocks, c, s), F32)),
+    ]
+    return _call(_fwd_messages_kernel, pos, inputs, outs)
+
+
+def bwd_messages(pos, gsp, gm, ba, sign, here, others, ew, acc):
     k, c, r, s = ba.shape
     has_next = gm is not None
     has_acc = acc is not None
     inputs = (
-        [("cols", gsp)]
+        [("column", gsp)]
         + ([("dense", gm)] if has_next else [])
-        + [("dense", ba), ("rows", f), ("dense", ew)]
+        + [("dense", ba), ("full", sign), ("full", here), ("full", others), ("dense", ew)]
         + ([("dense", acc)] if has_acc else [])
     )
     outs = [
         ("dense", jax.ShapeDtypeStruct(ba.shape, F32)),
         ("dense", jax.ShapeDtypeStruct(ba.shape, F32)),
-        ("rows", jax.ShapeDtypeStruct((k, r, s), F32)),
+        ("full", jax.ShapeDtypeStruct(here.shape, F32)),
+        ("full", jax.ShapeDtypeStruct(others.shape, F32)),
     ]
-    return _call(functools.partial(_bwd_messages_kernel, has_next, has_acc), inputs, outs)
-
-
-def bwd_products(spread, u, em, gba, gwh, emit_gm):
-    from jax.experimental.pallas import tpu as pltpu
-
-    k, c, r, s = em.shape
+    return _call(functools.partial(_bwd_messages_kernel, has_next, has_acc), pos, inputs, outs)
+
+
+def bwd_products(pos, spread, u, ew, gba, grows, ghere, whole, here, col_blocks, emit_gm):
+    k, c, r, s = ew.shape
     has_u = u is not None
-    inputs = [("cols", spread)] + ([("dense", u)] if has_u else []) + [
-        ("dense", em),
+    inputs = [("column", spread)] + ([("dense", u)] if has_u else []) + [
+        ("dense", ew),
         ("dense", gba),
-        ("rows", gwh),
+        ("full", grows),
+        ("full", ghere),
+        ("full", whole),
+        ("full", here),
     ]
-    outs = ([("dense", jax.ShapeDtypeStruct(em.shape, F32))] if emit_gm else []) + [
-        ("cols", jax.ShapeDtypeStruct((k, c, s), F32))
+    outs = ([("dense", jax.ShapeDtypeStruct(ew.shape, F32))] if emit_gm else []) + [
+        ("full", jax.ShapeDtypeStruct((col_blocks, c, s), F32))
     ]
     results = _call(
-        functools.partial(_bwd_products_kernel, has_u, emit_gm),
+        functools.partial(_bwd_products_kernel, has_u, emit_gm, k),
+        pos,
         inputs,
         outs,
-        [pltpu.VMEM((c, ROW_BLOCK, s), F32) for _ in range(3)],
+        [_vmem((c, r, s)) for _ in range(3)],
     )
     if emit_gm:
         return results[0], results[1]
@@ -393,30 +468,25 @@
     edge, row_hot, col_hot, same_row = device_tables(
         tile_bits[0, 0], tile_pos[0, 0], tile_count[0, 0], check_blocks, column_blocks
     )
+    pos = tile_pos[0, 0].reshape(slot_total * 2)
     weight = edge_weight[0, 0].reshape(slot_total, TILE, TILE)
     edge_t = jnp.swapaxes(edge, 1, 2)
     dense = (slot_total, TILE, TILE, shots)
     ew = jnp.broadcast_to((edge_t * jnp.swapaxes(weight, 1, 2))[..., None], dense)
-    em = ew
     sign_dev = (1.0 - 2.0 * syndrome.astype(jnp.float32)).reshape(check_blocks, TILE, shots)
     sign_slot = jnp.einsum("kc,crs->krs", row_hot, sign_dev, precision=EXACT)
     prior_dev = channel_prior.reshape(column_blocks, TILE)
-    prior_slot = jnp.einsum("kv,vc->kc", col_hot, prior_dev, precision=EXACT)
-    spread = jnp.broadcast_to(prior_slot[:, :, None], (slot_total, TILE, shots))
+    spread = jnp.broadcast_to(prior_dev[:, :, None], (column_blocks, TILE, shots))
     u = None
     saved = []
     total = None
     for step in range(ITERS):
-        ba, whole = fwd_products(spread, u, em)
-        rows, others_here = combine(whole, row_hot, same_row)
-        others, piece = others_forward(rows, check_blocks, n_var)
-        others_slot = pick(row_hot, others)
-        factor = sign_slot * others_here * others_slot
-        saved.append((spread, u, ba, whole, factor, others_here, others_slot, piece))
-        u, colsum = fwd_messages(ba, factor, ew)
-        column = place(col_hot, colsum)
+        ba, whole, rows, others_here = fwd_products(pos, spread, u, ew, check_blocks)
+        others, trail = others_forward(rows, check_blocks, n_var)
+        saved.append((spread, u, ba, whole, others_here, others, trail))
+        u, column = fwd_messages(pos, ba, sign_slot, others_here, others, ew, column_blocks)
         total = prior_dev[:, :, None] + checks_total(column, n_chk)
-        spread = pick(col_hot, total)
+        spread = total
     marginals = total.reshape(column_blocks * TILE, shots)
 
     grad_total = out_cot.reshape(column_blocks, TILE, shots)
@@ -424,20 +494,17 @@
     grad_m = None
     acc = None
     for step in reversed(range(ITERS)):
-        spread_t, u_prev, ba, whole, factor, others_here, others_slot, piece = saved[step]
+        spread_t, u_prev, ba, whole, others_here, others, trail = saved[step]
         prior_grad = prior_grad + jnp.sum(grad_total, axis=2)
-        grad_spread = pick(col_hot, grad_total)
-        acc, grad_ba, grad_factor = bwd_messages(grad_spread, grad_m, ba, factor, ew, acc)
-        grad_here = grad_factor * sign_slot * others_slot
-        grad_slot = grad_factor * sign_slot * others_here
-        grad_others = place(row_hot, grad_slot)
-        grad_rows = others_backward(piece, grad_others, check_blocks, n_var)
-        unused, pull = jax.vjp(lambda w: combine(w, row_hot, same_row), whole)
-        grad_whole = pull((grad_rows, grad_here))[0]
-        grad_m, colsum = bwd_products(spread_t, u_prev, em, grad_ba, grad_whole, step > 0)
-        grad_total = checks_total(
-            place(col_hot, colsum), n_chk
+        acc, grad_ba, grad_here, grad_others = bwd_messages(
+            pos, grad_total, grad_m, ba, sign_slot, others_here, others, ew, acc
         )
+        grad_rows = others_backward(trail, grad_others, check_blocks, n_var)
+        grad_m, column = bwd_products(
+            pos, spread_t, u_prev, ew, grad_ba, grad_rows, grad_here, whole, others_here,
+            column_blocks, step > 0,
+        )
+        grad_total = checks_total(column, n_chk)
     prior_grad = prior_grad + jnp.sum(grad_total, axis=2)
     weight_grad = edge * jnp.swapaxes(jnp.sum(acc, axis=3), 1, 2)
     return (

time: 169 us -> 168 us (level)
  waiting for transfers between devices: 41.9 us -> 53.2 us
  between operations: 11.6 us -> 1.46 us
  Pallas kernels: 52.3 us -> 60 us
  other arithmetic: 23.1 us -> 15.8 us
    ppermute x20, waiting for transfers between devices: 41.9 us -> 53.2 us  [_swap(): return lax.ppermute(value, axis, perm)]
    select_n x10 -> x0, other arithmetic: 8.38 us -> none  [the longest x6 8.29 us: combine(): value = value * jnp.where(same_row[k, other], whole[other], 1.0)]
    pallas_call x8, Pallas kernels: 52.3 us -> 60 us  [_call(): pl.pallas_call(kernel, grid_spec=grid_spec, out_shape=[o for kind, o in o...]
    mul x4 -> x0, other arithmetic: 3.01 us -> none  [the longest x2 1.75 us: body(): grad_here = grad_factor * sign_slot * others_slot]
    add x4, other arithmetic: 0.07 us -> 2.79 us  [checks_total(): values = values + _swap(values, 'chk', n, step)]
    add x10 -> x0, other arithmetic: 2.54 us -> none  [the longest x6 2.44 us: place(): value = value + jnp.where(hot[k, j] > 0, values[k], 0.0)]
    another operation x12 -> x0, other arithmetic: 1.99 us -> none  [the longest x4 1.89 us: pick(): return jnp.stack(parts)]
    slice x3 -> x0, local copies, waits for them, and re-layouts: 1.92 us -> none  [the longest x1 0.67 us: pick(): value = value + jnp.where(hot[k, j] > 0, values[j], 0.0)]
  transfers between devices with their start and end apart: 20 -> 20, of which waited for: 15 -> 16; matrix products, arithmetic and copies ran while one was open for 8% -> 5% of each run, Pallas kernels for 7% -> 8%
where the time goes in v4:
time: 168 us
  Pallas kernels  60 us (36%)
  waiting for transfers between devices  53.2 us (32%)
  starting transfers between devices  27.8 us (17%)
  other arithmetic  15.8 us (9%)
  local copies, waits for them, and re-layouts  8.94 us (5%)
    pallas_call x8, Pallas kernels, _call(): pl.pallas_call(kernel, grid_spec=grid_spec, out_shape=[o for kind, o in o...  60 us
    ppermute x20, waiting for transfers between devices, _swap(): return lax.ppermute(value, axis, perm)  53.2 us
    ppermute x20, starting transfers between devices, _swap(): return lax.ppermute(value, axis, perm)  27.8 us
  transfers between devices with their start and end apart: 20, of which 16 were waited for; matrix products, arithmetic and copies ran while one was open for 5% of the time, Pallas kernels for 8%

profile of v4, /device:TPU:0, one launch (start us, length us, event | category | flops | bytes accessed | tf_op | source)
XLA Modules:
  0.0 167.5 jit_solution(15159143409692150118)
XLA Ops:
  0.6 1.3 reshape_squeeze.6.pos_ref
  6.1 2.6 %broadcast_in_dim.16.refs_1_.ew_ref.refs_2_.refs_5_.refs_6_ = f32[2,64,64,128]{3,2,1,0:T(8,128)} broadcast(f32[2,64,64]{2,1,0:T(8,128)S(1)} %multiply_bitcast_fusion), dimensions={0,1,2} | broadcast | bytes 4227072 | tf_op jit(solution)/shard_map/broadcast_in_dim | solution.py:475
  8.6 5.1 %shard_map.94 = (f32[2,64,64,128]{3,2,1,0:T(8,128)}, f32[2,64,128]{2,1,0:T(8,128)}, f32[4,64,128]{2,1,0:T(8,128)}, f32[2,64,128]{2,1,0:T(8,128)}) custom-call(s32[4]{0:T(128)} %reshape_squeeze.6.pos_ref, f32[4,64,128]{2,1,0:T(8,128)} %add.79.refs_0_, f32[2,64,64,128]{3,2,1,0:T(8,128)} %broadcast_in_dim.16.refs_1_.ew_ref.refs_2_.refs_5_.refs_6_), custom_call_target="tpu_custom_call" | custom-call | tf_op jit(solution)/shard_map/pallas_call | solution.py:262
  14.2 1.2 collective-permute-done
  15.4 0.9 mul.91
  16.3 2.9 %collective-permute-start.1 = (f32[4,64,128]{2,1,0:T(8,128)S(1)}, f32[4,64,128]{2,1,0:T(8,128)S(1)}, u32[]{:S(2)}, u32[]{:S(2)}) collective-permute-start(f32[4,64,128]{2,1,0:T(8,128)S(1)} %mul.91), channel_id=1, source_target_pairs={{0,2},{1,3},{2,0},{3,1},{4,6},{5,7},{6,4},{7,5},{8,10},{9,11},{10,... | collective-permute-start | bytes 393224 | tf_op jit(solution)/shard_map/ppermute | solution.py:395
  19.4 3.7 %collective-permute-done.1 = f32[4,64,128]{2,1,0:T(8,128)S(1)} collective-permute-done((f32[4,64,128]{2,1,0:T(8,128)S(1)}, f32[4,64,128]{2,1,0:T(8,128)S(1)}, u32[]{:S(2)}, u32[]{:S(2)}) %collective-permute-start.1) | collective-permute-done | bytes 131104 | tf_op jit(solution)/shard_map/ppermute | solution.py:395
  23.1 1.8 %collective-permute-start.2 = (f32[4,64,128]{2,1,0:T(8,128)S(1)}, f32[4,64,128]{2,1,0:T(8,128)S(1)}, u32[]{:S(2)}, u32[]{:S(2)}) collective-permute-start(f32[4,64,128]{2,1,0:T(8,128)S(1)} %mul.93), channel_id=1, source_target_pairs={{0,4},{1,5},{2,6},{3,7},{4,0},{5,1},{6,2},{7,3},{8,12},{9,13},{10,... | collective-permute-start | bytes 393224 | tf_op jit(solution)/shard_map/ppermute | solution.py:395
  25.9 2.3 %collective-permute-done.2 = f32[4,64,128]{2,1,0:T(8,128)S(1)} collective-permute-done((f32[4,64,128]{2,1,0:T(8,128)S(1)}, f32[4,64,128]{2,1,0:T(8,128)S(1)}, u32[]{:S(2)}, u32[]{:S(2)}) %collective-permute-start.2) | collective-permute-done | bytes 131104 | tf_op jit(solution)/shard_map/ppermute | solution.py:395
  28.8 6.5 %shard_map.95 = (f32[2,64,64,128]{3,2,1,0:T(8,128)}, f32[4,64,128]{2,1,0:T(8,128)}) custom-call(s32[4]{0:T(128)} %reshape_squeeze.6.pos_ref, f32[2,64,64,128]{3,2,1,0:T(8,128)} %get-tuple-element.24.ba_ref.refs_2_, f32[2,64,128]{2,1,0:T(8,128)} %copy.21.sign_ref.refs_2_.refs_3_, f32[2,64,128]{2,1,0:T(8,128)} %get-tuple-element.25.here_ref.refs_4_.refs_6_, ...), custom_call_target="tpu_custom_call" | custom-call | tf_op jit(solution)/shard_map/pallas_call | solution.py:262
  35.3 1.8 %collective-permute-start.3 = (f32[4,64,128]{2,1,0:T(8,128)}, f32[4,64,128]{2,1,0:T(8,128)S(1)}, u32[]{:S(2)}, u32[]{:S(2)}) collective-permute-start(f32[4,64,128]{2,1,0:T(8,128)} %get-tuple-element.27), channel_id=1, source_target_pairs={{0,8},{8,0},{16,24},{24,16},{1,9},{9,1},{17,25},{25,17},{2,10},{10... | collective-permute-start | bytes 393224 | tf_op jit(solution)/shard_map/ppermute | solution.py:395
  37.1 3.4 %collective-permute-done.3 = f32[4,64,128]{2,1,0:T(8,128)S(1)} collective-permute-done((f32[4,64,128]{2,1,0:T(8,128)}, f32[4,64,128]{2,1,0:T(8,128)S(1)}, u32[]{:S(2)}, u32[]{:S(2)}) %collective-permute-start.3) | collective-permute-done | bytes 131104 | tf_op jit(solution)/shard_map/ppermute | solution.py:395
  40.5 0.9 add.80
  41.4 2.8 %collective-permute-start.4 = (f32[4,64,128]{2,1,0:T(8,128)S(1)}, f32[4,64,128]{2,1,0:T(8,128)S(1)}, u32[]{:S(2)}, u32[]{:S(2)}) collective-permute-start(f32[4,64,128]{2,1,0:T(8,128)S(1)} %add.80), channel_id=1, source_target_pairs={{0,16},{8,24},{16,0},{24,8},{1,17},{9,25},{17,1},{25,9},{2,18},{10... | collective-permute-start | bytes 393224 | tf_op jit(solution)/shard_map/ppermute | solution.py:395
  44.2 4.5 %collective-permute-done.4 = f32[4,64,128]{2,1,0:T(8,128)S(1)} collective-permute-done((f32[4,64,128]{2,1,0:T(8,128)S(1)}, f32[4,64,128]{2,1,0:T(8,128)S(1)}, u32[]{:S(2)}, u32[]{:S(2)}) %collective-permute-start.4) | collective-permute-done | bytes 131104 | tf_op jit(solution)/shard_map/ppermute | solution.py:395
  49.5 6.4 %shard_map.96 = (f32[2,64,64,128]{3,2,1,0:T(8,128)}, f32[2,64,128]{2,1,0:T(8,128)}, f32[4,64,128]{2,1,0:T(8,128)}, f32[2,64,128]{2,1,0:T(8,128)}) custom-call(s32[4]{0:T(128)} %reshape_squeeze.6.pos_ref, f32[4,64,128]{2,1,0:T(8,128)} %add_add_fusion.1.refs_0_, f32[2,64,64,128]{3,2,1,0:T(8,128)} %get-tuple-element.28.refs_1_, ...), custom_call_target="tpu_custom_call" | custom-call | tf_op jit(solution)/shard_map/pallas_call | solution.py:262
  55.9 1.5 collective-permute-done.5
  57.5 0.9 mul.95
  58.4 1.7 %collective-permute-start.6 = (f32[4,64,128]{2,1,0:T(8,128)S(1)}, f32[4,64,128]{2,1,0:T(8,128)S(1)}, u32[]{:S(2)}, u32[]{:S(2)}) collective-permute-start(f32[4,64,128]{2,1,0:T(8,128)S(1)} %mul.95), channel_id=1, source_target_pairs={{0,2},{1,3},{2,0},{3,1},{4,6},{5,7},{6,4},{7,5},{8,10},{9,11},{10,... | collective-permute-start | bytes 393224 | tf_op jit(solution)/shard_map/ppermute | solution.py:395
  60.1 3.9 %collective-permute-done.6 = f32[4,64,128]{2,1,0:T(8,128)S(1)} collective-permute-done((f32[4,64,128]{2,1,0:T(8,128)S(1)}, f32[4,64,128]{2,1,0:T(8,128)S(1)}, u32[]{:S(2)}, u32[]{:S(2)}) %collective-permute-start.6) | collective-permute-done | bytes 131104 | tf_op jit(solution)/shard_map/ppermute | solution.py:395
  64.1 1.8 %collective-permute-start.7 = (f32[4,64,128]{2,1,0:T(8,128)S(1)}, f32[4,64,128]{2,1,0:T(8,128)S(1)}, u32[]{:S(2)}, u32[]{:S(2)}) collective-permute-start(f32[4,64,128]{2,1,0:T(8,128)S(1)} %mul.97), channel_id=1, source_target_pairs={{0,4},{1,5},{2,6},{3,7},{4,0},{5,1},{6,2},{7,3},{8,12},{9,13},{10,... | collective-permute-start | bytes 393224 | tf_op jit(solution)/shard_map/ppermute | solution.py:395
  65.8 3.3 %collective-permute-done.7 = f32[4,64,128]{2,1,0:T(8,128)S(1)} collective-permute-done((f32[4,64,128]{2,1,0:T(8,128)S(1)}, f32[4,64,128]{2,1,0:T(8,128)S(1)}, u32[]{:S(2)}, u32[]{:S(2)}) %collective-permute-start.7) | collective-permute-done | bytes 131104 | tf_op jit(solution)/shard_map/ppermute | solution.py:395
  69.8 8.2 %shard_map.98 = (f32[2,64,64,128]{3,2,1,0:T(8,128)}, f32[2,64,64,128]{3,2,1,0:T(8,128)}, f32[2,64,128]{2,1,0:T(8,128)}, f32[4,64,128]{2,1,0:T(8,128)}) custom-call(s32[4]{0:T(128)} %reshape_squeeze.6.pos_ref, f32[4,64,128]{2,1,0:T(8,128)} %bitcast.13, f32[2,64,64,128]{3,2,1,0:T(8,128)} %get-tuple-element.29.ba_ref.refs_1_, ...), custom_call_target="tpu_custom_call" | custom-call | tf_op jit(solution)/shard_map/pallas_call | solution.py:262
  78.1 1.5 collective-permute-done.10
  79.6 0.9 multiply_add_fusion.5
  80.6 1.7 %collective-permute-start.11 = (f32[4,64,128]{2,1,0:T(8,128)S(1)}, f32[4,64,128]{2,1,0:T(8,128)S(1)}, u32[]{:S(2)}, u32[]{:S(2)}) collective-permute-start(f32[4,64,128]{2,1,0:T(8,128)S(1)} %multiply_add_fusion.5), channel_id=1, source_target_pairs={{0,2},{1,3},{2,0},{3,1},{4,6},{5,7},{6,4},{7,5},{8,10},{9,11},{10,... | collective-permute-start | bytes 393224 | tf_op jit(solution)/shard_map/ppermute | solution.py:395
  82.3 3.9 %collective-permute-done.11 = f32[4,64,128]{2,1,0:T(8,128)S(1)} collective-permute-done((f32[4,64,128]{2,1,0:T(8,128)S(1)}, f32[4,64,128]{2,1,0:T(8,128)S(1)}, u32[]{:S(2)}, u32[]{:S(2)}) %collective-permute-start.11) | collective-permute-done | bytes 131104 | tf_op jit(solution)/shard_map/ppermute | solution.py:395
  86.2 1.8 %collective-permute-start.12 = (f32[4,64,128]{2,1,0:T(8,128)S(1)}, f32[4,64,128]{2,1,0:T(8,128)S(1)}, u32[]{:S(2)}, u32[]{:S(2)}) collective-permute-start(f32[4,64,128]{2,1,0:T(8,128)S(1)} %multiply_add_fusion.4), channel_id=1, source_target_pairs={{0,4},{1,5},{2,6},{3,7},{4,0},{5,1},{6,2},{7,3},{8,12},{9,13},{10,... | collective-permute-start | bytes 393224 | tf_op jit(solution)/shard_map/ppermute | solution.py:395
  88.0 3.3 %collective-permute-done.12 = f32[4,64,128]{2,1,0:T(8,128)S(1)} collective-permute-done((f32[4,64,128]{2,1,0:T(8,128)S(1)}, f32[4,64,128]{2,1,0:T(8,128)S(1)}, u32[]{:S(2)}, u32[]{:S(2)}) %collective-permute-start.12) | collective-permute-done | bytes 131104 | tf_op jit(solution)/shard_map/ppermute | solution.py:395
  92.0 9.4 %shard_map.99 = (f32[2,64,64,128]{3,2,1,0:T(8,128)}, f32[4,64,128]{2,1,0:T(8,128)}) custom-call(s32[4]{0:T(128)} %reshape_squeeze.6.pos_ref, f32[4,64,128]{2,1,0:T(8,128)} %add_add_fusion.1.refs_0_, f32[2,64,64,128]{3,2,1,0:T(8,128)} %get-tuple-element.28.refs_1_, f32[2,64,64,128]{3,2,1,0:T(8,128)} %broadcast_in_dim.16.refs_1_.ew_ref.refs_2_.refs_5_.refs_6_, ...), custom_call_target="tpu_custom_call" | custom-call | tf_op jit(solution)/shard_map/pallas_call | solution.py:262
  101.4 0.9 collective-permute-start.13
  102.3 4.3 %collective-permute-done.13 = f32[4,64,128]{2,1,0:T(8,128)S(1)} collective-permute-done((f32[4,64,128]{2,1,0:T(8,128)}, f32[4,64,128]{2,1,0:T(8,128)S(1)}, u32[]{:S(2)}, u32[]{:S(2)}) %collective-permute-start.13) | collective-permute-done | bytes 131104 | tf_op jit(solution)/shard_map/ppermute | solution.py:395
  106.6 0.9 add.91
  107.5 2.3 %collective-permute-start.14 = (f32[4,64,128]{2,1,0:T(8,128)S(1)}, f32[4,64,128]{2,1,0:T(8,128)S(1)}, u32[]{:S(2)}, u32[]{:S(2)}) collective-permute-start(f32[4,64,128]{2,1,0:T(8,128)S(1)} %add.91), channel_id=1, source_target_pairs={{0,16},{8,24},{16,0},{24,8},{1,17},{9,25},{17,1},{25,9},{2,18},{10... | collective-permute-start | bytes 393224 | tf_op jit(solution)/shard_map/ppermute | solution.py:395
  109.8 5.1 %collective-permute-done.14 = f32[4,64,128]{2,1,0:T(8,128)S(1)} collective-permute-done((f32[4,64,128]{2,1,0:T(8,128)S(1)}, f32[4,64,128]{2,1,0:T(8,128)S(1)}, u32[]{:S(2)}, u32[]{:S(2)}) %collective-permute-start.14) | collective-permute-done | bytes 131104 | tf_op jit(solution)/shard_map/ppermute | solution.py:395
  115.5 10.3 %shard_map.100 = (f32[2,64,64,128]{3,2,1,0:T(8,128)}, f32[2,64,64,128]{3,2,1,0:T(8,128)}, f32[2,64,128]{2,1,0:T(8,128)}, f32[4,64,128]{2,1,0:T(8,128)}) custom-call(s32[4]{0:T(128)} %reshape_squeeze.6.pos_ref, f32[4,64,128]{2,1,0:T(8,128)} %get-tuple-element.46.refs_0_, f32[2,64,64,128]{3,2,1,0:T(8,128)} %get-tuple-element.38.refs_1_, ...), custom_call_target="tpu_custom_call" | custom-call | tf_op jit(solution)/shard_map/pallas_call | solution.py:262
  125.9 1.5 collective-permute-done.15
  127.5 0.9 multiply_add_fusion.2
  128.4 1.8 %collective-permute-start.16 = (f32[4,64,128]{2,1,0:T(8,128)S(1)}, f32[4,64,128]{2,1,0:T(8,128)S(1)}, u32[]{:S(2)}, u32[]{:S(2)}) collective-permute-start(f32[4,64,128]{2,1,0:T(8,128)S(1)} %multiply_add_fusion.2), channel_id=1, source_target_pairs={{0,2},{1,3},{2,0},{3,1},{4,6},{5,7},{6,4},{7,5},{8,10},{9,11},{10,... | collective-permute-start | bytes 393224 | tf_op jit(solution)/shard_map/ppermute | solution.py:395
  130.2 6.5 %shard_map.97 = (f32[2,64,64,128]{3,2,1,0:T(8,128)}, f32[4,64,128]{2,1,0:T(8,128)}) custom-call(s32[4]{0:T(128)} %reshape_squeeze.6.pos_ref, f32[2,64,64,128]{3,2,1,0:T(8,128)} %get-tuple-element.29.ba_ref.refs_1_, f32[2,64,128]{2,1,0:T(8,128)} %copy.21.sign_ref.refs_2_.refs_3_, f32[2,64,128]{2,1,0:T(8,128)} %get-tuple-element.30.here_ref.refs_3_.refs_7_, ...), custom_call_target="tpu_custom_call" | custom-call | tf_op jit(solution)/shard_map/pallas_call | solution.py:262
  136.8 1.6 collective-permute-start.17
  138.5 3.6 %collective-permute-done.8 = f32[4,64,128]{2,1,0:T(8,128)S(1)} collective-permute-done((f32[4,64,128]{2,1,0:T(8,128)}, f32[4,64,128]{2,1,0:T(8,128)S(1)}, u32[]{:S(2)}, u32[]{:S(2)}) %collective-permute-start.8) | collective-permute-done | bytes 131104 | tf_op jit(solution)/shard_map/ppermute | solution.py:395
  142.2 0.9 add.83
  143.1 1.8 %collective-permute-start.9 = (f32[4,64,128]{2,1,0:T(8,128)S(1)}, f32[4,64,128]{2,1,0:T(8,128)S(1)}, u32[]{:S(2)}, u32[]{:S(2)}) collective-permute-start(f32[4,64,128]{2,1,0:T(8,128)S(1)} %add.83), channel_id=1, source_target_pairs={{0,16},{8,24},{16,0},{24,8},{1,17},{9,25},{17,1},{25,9},{2,18},{10... | collective-permute-start | bytes 393224 | tf_op jit(solution)/shard_map/ppermute | solution.py:395
  145.6 7.6 %shard_map.101 = f32[4,64,128]{2,1,0:T(8,128)} custom-call(s32[4]{0:T(128)} %reshape_squeeze.6.pos_ref, f32[4,64,128]{2,1,0:T(8,128)} %add.79.refs_0_, f32[2,64,64,128]{3,2,1,0:T(8,128)} %broadcast_in_dim.16.refs_1_.ew_ref.refs_2_.refs_5_.refs_6_, f32[2,64,64,128]{3,2,1,0:T(8,128)} %get-tuple-element.41.refs_2_, f32[4,64,128]{2,1,0:T(8,128)} %multiply_add_fusion.refs_3_, ...), custom_call_target="tpu_custom_call" | custom-call | tf_op jit(solution)/shard_map/pallas_call | solution.py:262
  153.2 1.7 %collective-permute-start.18 = (f32[4,64,128]{2,1,0:T(8,128)}, f32[4,64,128]{2,1,0:T(8,128)S(1)}, u32[]{:S(2)}, u32[]{:S(2)}) collective-permute-start(f32[4,64,128]{2,1,0:T(8,128)} %shard_map.101), channel_id=1, source_target_pairs={{0,8},{8,0},{16,24},{24,16},{1,9},{9,1},{17,25},{25,17},{2,10},{10... | collective-permute-start | bytes 393224 | tf_op jit(solution)/shard_map/ppermute | solution.py:395
  155.8 3.3 %reduce_sum.40 = f32[2,64,64]{2,1,0:T(8,128)S(1)} reduce(f32[2,64,64,128]{3,2,1,0:T(8,128)} %get-tuple-element.40, f32[]{:T(128)} %constant.2.clone.1), dimensions={3}, to_apply=%region_0.1 | reduce | flops 1040384 | bytes 4227076 | tf_op jit(solution)/shard_map/reduce_sum | solution.py:509
  160.7 6.1 %collective-permute-done.19 = f32[4,64,128]{2,1,0:T(8,128)S(1)} collective-permute-done((f32[4,64,128]{2,1,0:T(8,128)S(1)}, f32[4,64,128]{2,1,0:T(8,128)S(1)}, u32[]{:S(2)}, u32[]{:S(2)}) %collective-permute-start.19) | collective-permute-done | bytes 131104 | tf_op jit(solution)/shard_map/ppermute | solution.py:395
  (54 shorter events, 12.9 us)
Async XLA Ops:
  6.1 13.2 %copy-start.4 = (s32[256,128]{1,0:T(8,128)S(1)}, s32[256,128]{1,0:T(8,128)}, u32[]{:S(2)}) copy-start(s32[256,128]{1,0:T(8,128)} %param.11) | copy-start | bytes 393220
  6.1 13.2 %copy-start.5 = (s32[1,1,2,2]{3,2,1,0:T(2,128)S(1)}, s32[1,1,2,2]{3,2,1,0:T(2,128)}, u32[]{:S(2)}) copy-start(s32[1,1,2,2]{3,2,1,0:T(2,128)} %param.8) | copy-start | bytes 52
  13.7 1.7 %collective-permute-start = (f32[4,64,128]{2,1,0:T(8,128)}, f32[4,64,128]{2,1,0:T(8,128)S(1)}, u32[]{:S(2)}, u32[]{:S(2)}) collective-permute-start(f32[4,64,128]{2,1,0:T(8,128)} %get-tuple-element.26), channel_id=1, source_target_pairs={{0,1},{1,0},{2,3},{3,2},{4,5},{5,4},{6,7},{7,6},{8,9},{9,8},{10,11... | collective-permute-start | bytes 393224 | tf_op jit(solution)/shard_map/ppermute | solution.py:395
  16.3 6.7 %collective-permute-start.1 = (f32[4,64,128]{2,1,0:T(8,128)S(1)}, f32[4,64,128]{2,1,0:T(8,128)S(1)}, u32[]{:S(2)}, u32[]{:S(2)}) collective-permute-start(f32[4,64,128]{2,1,0:T(8,128)S(1)} %mul.91), channel_id=1, source_target_pairs={{0,2},{1,3},{2,0},{3,1},{4,6},{5,7},{6,4},{7,5},{8,10},{9,11},{10,... | collective-permute-start | bytes 393224 | tf_op jit(solution)/shard_map/ppermute | solution.py:395
  23.1 5.1 %collective-permute-start.2 = (f32[4,64,128]{2,1,0:T(8,128)S(1)}, f32[4,64,128]{2,1,0:T(8,128)S(1)}, u32[]{:S(2)}, u32[]{:S(2)}) collective-permute-start(f32[4,64,128]{2,1,0:T(8,128)S(1)} %mul.93), channel_id=1, source_target_pairs={{0,4},{1,5},{2,6},{3,7},{4,0},{5,1},{6,2},{7,3},{8,12},{9,13},{10,... | collective-permute-start | bytes 393224 | tf_op jit(solution)/shard_map/ppermute | solution.py:395
  35.3 5.2 %collective-permute-start.3 = (f32[4,64,128]{2,1,0:T(8,128)}, f32[4,64,128]{2,1,0:T(8,128)S(1)}, u32[]{:S(2)}, u32[]{:S(2)}) collective-permute-start(f32[4,64,128]{2,1,0:T(8,128)} %get-tuple-element.27), channel_id=1, source_target_pairs={{0,8},{8,0},{16,24},{24,16},{1,9},{9,1},{17,25},{25,17},{2,10},{10... | collective-permute-start | bytes 393224 | tf_op jit(solution)/shard_map/ppermute | solution.py:395
  41.4 7.3 %collective-permute-start.4 = (f32[4,64,128]{2,1,0:T(8,128)S(1)}, f32[4,64,128]{2,1,0:T(8,128)S(1)}, u32[]{:S(2)}, u32[]{:S(2)}) collective-permute-start(f32[4,64,128]{2,1,0:T(8,128)S(1)} %add.80), channel_id=1, source_target_pairs={{0,16},{8,24},{16,0},{24,8},{1,17},{9,25},{17,1},{25,9},{2,18},{10... | collective-permute-start | bytes 393224 | tf_op jit(solution)/shard_map/ppermute | solution.py:395
  55.9 1.6 collective-permute-start.5
  58.4 5.6 %collective-permute-start.6 = (f32[4,64,128]{2,1,0:T(8,128)S(1)}, f32[4,64,128]{2,1,0:T(8,128)S(1)}, u32[]{:S(2)}, u32[]{:S(2)}) collective-permute-start(f32[4,64,128]{2,1,0:T(8,128)S(1)} %mul.95), channel_id=1, source_target_pairs={{0,2},{1,3},{2,0},{3,1},{4,6},{5,7},{6,4},{7,5},{8,10},{9,11},{10,... | collective-permute-start | bytes 393224 | tf_op jit(solution)/shard_map/ppermute | solution.py:395
  64.1 5.0 %collective-permute-start.7 = (f32[4,64,128]{2,1,0:T(8,128)S(1)}, f32[4,64,128]{2,1,0:T(8,128)S(1)}, u32[]{:S(2)}, u32[]{:S(2)}) collective-permute-start(f32[4,64,128]{2,1,0:T(8,128)S(1)} %mul.97), channel_id=1, source_target_pairs={{0,4},{1,5},{2,6},{3,7},{4,0},{5,1},{6,2},{7,3},{8,12},{9,13},{10,... | collective-permute-start | bytes 393224 | tf_op jit(solution)/shard_map/ppermute | solution.py:395
  69.8 9.9 %copy-start.3 = (f32[4,64,128]{2,1,0:T(8,128)S(1)}, f32[4,64,128]{2,1,0:T(8,128)}, u32[]{:S(2)}) copy-start(f32[4,64,128]{2,1,0:T(8,128)} %get-tuple-element.31) | copy-start | bytes 393220
  78.0 1.6 collective-permute-start.10
  80.6 5.6 %collective-permute-start.11 = (f32[4,64,128]{2,1,0:T(8,128)S(1)}, f32[4,64,128]{2,1,0:T(8,128)S(1)}, u32[]{:S(2)}, u32[]{:S(2)}) collective-permute-start(f32[4,64,128]{2,1,0:T(8,128)S(1)} %multiply_add_fusion.5), channel_id=1, source_target_pairs={{0,2},{1,3},{2,0},{3,1},{4,6},{5,7},{6,4},{7,5},{8,10},{9,11},{10,... | collective-permute-start | bytes 393224 | tf_op jit(solution)/shard_map/ppermute | solution.py:395
  86.2 5.0 %collective-permute-start.12 = (f32[4,64,128]{2,1,0:T(8,128)S(1)}, f32[4,64,128]{2,1,0:T(8,128)S(1)}, u32[]{:S(2)}, u32[]{:S(2)}) collective-permute-start(f32[4,64,128]{2,1,0:T(8,128)S(1)} %multiply_add_fusion.4), channel_id=1, source_target_pairs={{0,4},{1,5},{2,6},{3,7},{4,0},{5,1},{6,2},{7,3},{8,12},{9,13},{10,... | collective-permute-start | bytes 393224 | tf_op jit(solution)/shard_map/ppermute | solution.py:395
  101.4 5.2 %collective-permute-start.13 = (f32[4,64,128]{2,1,0:T(8,128)}, f32[4,64,128]{2,1,0:T(8,128)S(1)}, u32[]{:S(2)}, u32[]{:S(2)}) collective-permute-start(f32[4,64,128]{2,1,0:T(8,128)} %get-tuple-element.37), channel_id=1, source_target_pairs={{0,8},{8,0},{16,24},{24,16},{1,9},{9,1},{17,25},{25,17},{2,10},{10... | collective-permute-start | bytes 393224 | tf_op jit(solution)/shard_map/ppermute | solution.py:395
  107.5 7.3 %collective-permute-start.14 = (f32[4,64,128]{2,1,0:T(8,128)S(1)}, f32[4,64,128]{2,1,0:T(8,128)S(1)}, u32[]{:S(2)}, u32[]{:S(2)}) collective-permute-start(f32[4,64,128]{2,1,0:T(8,128)S(1)} %add.91), channel_id=1, source_target_pairs={{0,16},{8,24},{16,0},{24,8},{1,17},{9,25},{17,1},{25,9},{2,18},{10... | collective-permute-start | bytes 393224 | tf_op jit(solution)/shard_map/ppermute | solution.py:395
  115.5 12.0 %copy-start.2 = (f32[4,64,128]{2,1,0:T(8,128)S(1)}, f32[4,64,128]{2,1,0:T(8,128)}, u32[]{:S(2)}) copy-start(f32[4,64,128]{2,1,0:T(8,128)} %get-tuple-element.26) | copy-start | bytes 393220
  125.8 1.6 collective-permute-start.15
  128.4 10.0 %copy-start.1 = (f32[256,128]{1,0:T(8,128)S(1)}, f32[256,128]{1,0:T(8,128)}, u32[]{:S(2)}) copy-start(f32[256,128]{1,0:T(8,128)} %param.13) | copy-start | bytes 393220
  128.4 8.4 %collective-permute-start.16 = (f32[4,64,128]{2,1,0:T(8,128)S(1)}, f32[4,64,128]{2,1,0:T(8,128)S(1)}, u32[]{:S(2)}, u32[]{:S(2)}) collective-permute-start(f32[4,64,128]{2,1,0:T(8,128)S(1)} %multiply_add_fusion.2), channel_id=1, source_target_pairs={{0,2},{1,3},{2,0},{3,1},{4,6},{5,7},{6,4},{7,5},{8,10},{9,11},{10,... | collective-permute-start | bytes 393224 | tf_op jit(solution)/shard_map/ppermute | solution.py:395
  136.7 5.5 %collective-permute-start.8 = (f32[4,64,128]{2,1,0:T(8,128)}, f32[4,64,128]{2,1,0:T(8,128)S(1)}, u32[]{:S(2)}, u32[]{:S(2)}) collective-permute-start(f32[4,64,128]{2,1,0:T(8,128)} %get-tuple-element.32), channel_id=1, source_target_pairs={{0,8},{8,0},{16,24},{24,16},{1,9},{9,1},{17,25},{25,17},{2,10},{10... | collective-permute-start | bytes 393224 | tf_op jit(solution)/shard_map/ppermute | solution.py:395
  136.8 8.1 %collective-permute-start.17 = (f32[4,64,128]{2,1,0:T(8,128)S(1)}, f32[4,64,128]{2,1,0:T(8,128)S(1)}, u32[]{:S(2)}, u32[]{:S(2)}) collective-permute-start(f32[4,64,128]{2,1,0:T(8,128)S(1)} %multiply_add_fusion.1), channel_id=1, source_target_pairs={{0,4},{1,5},{2,6},{3,7},{4,0},{5,1},{6,2},{7,3},{8,12},{9,13},{10,... | collective-permute-start | bytes 393224 | tf_op jit(solution)/shard_map/ppermute | solution.py:395
  143.1 11.9 %collective-permute-start.9 = (f32[4,64,128]{2,1,0:T(8,128)S(1)}, f32[4,64,128]{2,1,0:T(8,128)S(1)}, u32[]{:S(2)}, u32[]{:S(2)}) collective-permute-start(f32[4,64,128]{2,1,0:T(8,128)S(1)} %add.83), channel_id=1, source_target_pairs={{0,16},{8,24},{16,0},{24,8},{1,17},{9,25},{17,1},{25,9},{2,18},{10... | collective-permute-start | bytes 393224 | tf_op jit(solution)/shard_map/ppermute | solution.py:395
  153.2 5.9 %copy-start = (f32[4,64,128]{2,1,0:T(8,128)S(1)}, f32[4,64,128]{2,1,0:T(8,128)}, u32[]{:S(2)}) copy-start(f32[4,64,128]{2,1,0:T(8,128)} %shard_map.101) | copy-start | bytes 393220
  153.2 5.8 %collective-permute-start.18 = (f32[4,64,128]{2,1,0:T(8,128)}, f32[4,64,128]{2,1,0:T(8,128)S(1)}, u32[]{:S(2)}, u32[]{:S(2)}) collective-permute-start(f32[4,64,128]{2,1,0:T(8,128)} %shard_map.101), channel_id=1, source_target_pairs={{0,8},{8,0},{16,24},{24,16},{1,9},{9,1},{17,25},{25,17},{2,10},{10... | collective-permute-start | bytes 393224 | tf_op jit(solution)/shard_map/ppermute | solution.py:395
  159.1 7.6 %collective-permute-start.19 = (f32[4,64,128]{2,1,0:T(8,128)S(1)}, f32[4,64,128]{2,1,0:T(8,128)S(1)}, u32[]{:S(2)}, u32[]{:S(2)}) collective-permute-start(f32[4,64,128]{2,1,0:T(8,128)S(1)} %add.99), channel_id=1, source_target_pairs={{0,16},{8,24},{16,0},{24,8},{1,17},{9,25},{17,1},{25,9},{2,18},{10... | collective-permute-start | bytes 393224 | tf_op jit(solution)/shard_map/ppermute | solution.py:395

commit v5 on v4

--- a/solution.py
+++ b/solution.py
@@ -405,9 +405,16 @@
     return values
 
 
-def others_forward(rows, check_blocks, n):
+def others_forward(rows, check_blocks, n, uniform=False):
     if not _power_of_two(n):
         return others_gather(rows, check_blocks)
+    if uniform:
+        shape = rows.shape
+        small = rows[:, :, 0].reshape(-1, shape[2])
+        others, trail = others_forward(small, check_blocks, n)
+        grow = lambda value: jnp.broadcast_to(value.reshape(shape[:2] + (1,)), shape)
+        trail = [tuple(grow(value) for value in entry) for entry in trail]
+        return grow(others), trail
     full = rows
     excl = jnp.ones_like(rows)
     trail = []
@@ -482,12 +489,13 @@
     total = None
     for step in range(ITERS):
         ba, whole, rows, others_here = fwd_products(pos, spread, u, ew, check_blocks)
-        others, trail = others_forward(rows, check_blocks, n_var)
+        others, trail = others_forward(rows, check_blocks, n_var, uniform=(step == 0 and (check_blocks * TILE) % shots == 0))
         saved.append((spread, u, ba, whole, others_here, others, trail))
         u, column = fwd_messages(pos, ba, sign_slot, others_here, others, ew, column_blocks)
-        total = prior_dev[:, :, None] + checks_total(column, n_chk)
-        spread = total
-    marginals = total.reshape(column_blocks * TILE, shots)
+        if step + 1 < ITERS:
+            total = prior_dev[:, :, None] + checks_total(column, n_chk)
+            spread = total
+    last_column = column
 
     grad_total = out_cot.reshape(column_blocks, TILE, shots)
     prior_grad = jnp.zeros((column_blocks, TILE), jnp.float32)
@@ -499,13 +507,23 @@
         acc, grad_ba, grad_here, grad_others = bwd_messages(
             pos, grad_total, grad_m, ba, sign_slot, others_here, others, ew, acc
         )
+        if step + 1 == ITERS:
+            last_column, grad_ba = lax.optimization_barrier((last_column, grad_ba))
+            total = prior_dev[:, :, None] + checks_total(last_column, n_chk)
+            marginals = total.reshape(column_blocks * TILE, shots)
         grad_rows = others_backward(trail, grad_others, check_blocks, n_var)
         grad_m, column = bwd_products(
             pos, spread_t, u_prev, ew, grad_ba, grad_rows, grad_here, whole, others_here,
             column_blocks, step > 0,
         )
-        grad_total = checks_total(column, n_chk)
-    prior_grad = prior_grad + jnp.sum(grad_total, axis=2)
+        if step > 0:
+            grad_total = checks_total(column, n_chk)
+    shot_sums = jnp.sum(column, axis=2)
+    if (column_blocks * TILE) % 128 == 0:
+        shot_sums = checks_total(shot_sums.reshape(-1, 128), n_chk).reshape(column_blocks, TILE)
+    else:
+        shot_sums = checks_total(shot_sums, n_chk)
+    prior_grad = prior_grad + shot_sums
     weight_grad = edge * jnp.swapaxes(jnp.sum(acc, axis=3), 1, 2)
     return (
         marginals,

time: 168 us -> 159 us (0.946)
  waiting for transfers between devices: 53.2 us -> 41.1 us
  local copies, waits for them, and re-layouts: 8.94 us -> 11.3 us
  starting transfers between devices: 27.8 us -> 29.5 us
    ppermute x20, waiting for transfers between devices: 53.2 us -> 41.1 us  [_swap(): return lax.ppermute(value, axis, perm)]
    ppermute x20, starting transfers between devices: 27.8 us -> 29.5 us  [_swap(): return lax.ppermute(value, axis, perm)]
  transfers between devices with their start and end apart: 20 -> 20, of which waited for: 16 -> 17; matrix products, arithmetic and copies ran while one was open for 5% -> 6% of each run, Pallas kernels for 8% -> 9%
where the time goes in v5:
time: 159 us; the launch traced here: 158 us
  Pallas kernels  60.1 us (38%)
  waiting for transfers between devices  41.1 us (26%)
  starting transfers between devices  29.5 us (19%)
  other arithmetic  14.6 us (9%)
  local copies, waits for them, and re-layouts  11.3 us (7%)
    pallas_call x8, Pallas kernels, _call(): pl.pallas_call(kernel, grid_spec=grid_spec, out_shape=[o for kind, o in o...  60.1 us
    ppermute x20, waiting for transfers between devices, _swap(): return lax.ppermute(value, axis, perm)  41.1 us
    ppermute x20, starting transfers between devices, _swap(): return lax.ppermute(value, axis, perm)  29.5 us
    reduce_sum x1, other arithmetic, body(): weight_grad = edge * jnp.swapaxes(jnp.sum(acc, axis=3), 1, 2)  3.34 us
  transfers between devices with their start and end apart: 20, of which 17 were waited for; matrix products, arithmetic and copies ran while one was open for 6% of the time, Pallas kernels for 9%

profile of v5, /device:TPU:0, one launch (start us, length us, event | category | flops | bytes accessed | tf_op | source)
XLA Modules:
  0.0 158.4 jit_solution(1999686955718849835)
XLA Ops:
  0.6 1.3 reshape_squeeze.9.pos_ref
  2.7 0.9 reshape_squeeze.10
  3.6 0.9 squeeze.10
  6.1 2.6 %broadcast_in_dim.79.refs_1_.ew_ref.refs_2_.refs_5_.refs_6_ = f32[2,64,64,128]{3,2,1,0:T(8,128)} broadcast(f32[2,64,64]{2,1,0:T(8,128)S(1)} %multiply_bitcast_fusion), dimensions={0,1,2} | broadcast | bytes 4227072 | tf_op jit(solution)/shard_map/broadcast_in_dim | solution.py:482
  8.6 5.1 %shard_map.94 = (f32[2,64,64,128]{3,2,1,0:T(8,128)}, f32[2,64,128]{2,1,0:T(8,128)}, f32[4,64,128]{2,1,0:T(8,128)}, f32[2,64,128]{2,1,0:T(8,128)}) custom-call(s32[4]{0:T(128)} %reshape_squeeze.9.pos_ref, f32[4,64,128]{2,1,0:T(8,128)} %add.79.refs_0_, f32[2,64,64,128]{3,2,1,0:T(8,128)} %broadcast_in_dim.79.refs_1_.ew_ref.refs_2_.refs_5_.refs_6_), custom_call_target="tpu_custom_call" | custom-call | tf_op jit(solution)/shard_map/pallas_call | solution.py:262
  13.7 1.0 slice_reduce_fusion
  15.3 0.8 collective-permute-done
  16.1 2.8 %collective-permute-start.1 = (f32[2,128]{1,0:T(2,128)S(1)}, f32[2,128]{1,0:T(2,128)S(1)}, u32[]{:S(2)}, u32[]{:S(2)}) collective-permute-start(f32[2,128]{1,0:T(2,128)S(1)} %mul.91), channel_id=1, source_target_pairs={{0,2},{1,3},{2,0},{3,1},{4,6},{5,7},{6,4},{7,5},{8,10},{9,11},{10,... | collective-permute-start | bytes 3080 | tf_op jit(solution)/shard_map/ppermute | solution.py:395
  19.0 1.4 collective-permute-done.1
  20.5 2.1 %collective-permute-start.2 = (f32[2,128]{1,0:T(2,128)S(1)}, f32[2,128]{1,0:T(2,128)S(1)}, u32[]{:S(2)}, u32[]{:S(2)}) collective-permute-start(f32[2,128]{1,0:T(2,128)S(1)} %mul.93), channel_id=1, source_target_pairs={{0,4},{1,5},{2,6},{3,7},{4,0},{5,1},{6,2},{7,3},{8,12},{9,13},{10,... | collective-permute-start | bytes 3080 | tf_op jit(solution)/shard_map/ppermute | solution.py:395
  24.9 6.5 %shard_map.95 = (f32[2,64,64,128]{3,2,1,0:T(8,128)}, f32[4,64,128]{2,1,0:T(8,128)}) custom-call(s32[4]{0:T(128)} %reshape_squeeze.9.pos_ref, f32[2,64,64,128]{3,2,1,0:T(8,128)} %get-tuple-element.26.ba_ref.refs_2_, f32[2,64,128]{2,1,0:T(8,128)} %copy.21.sign_ref.refs_2_.refs_3_, f32[2,64,128]{2,1,0:T(8,128)} %get-tuple-element.27.here_ref.refs_4_.refs_6_, ...), custom_call_target="tpu_custom_call" | custom-call | tf_op jit(solution)/shard_map/pallas_call | solution.py:262
  31.4 2.1 %collective-permute-start.3 = (f32[4,64,128]{2,1,0:T(8,128)}, f32[4,64,128]{2,1,0:T(8,128)S(1)}, u32[]{:S(2)}, u32[]{:S(2)}) collective-permute-start(f32[4,64,128]{2,1,0:T(8,128)} %get-tuple-element.29), channel_id=1, source_target_pairs={{0,8},{8,0},{16,24},{24,16},{1,9},{9,1},{17,25},{25,17},{2,10},{10... | collective-permute-start | bytes 393224 | tf_op jit(solution)/shard_map/ppermute | solution.py:395
  33.5 3.2 %collective-permute-done.3 = f32[4,64,128]{2,1,0:T(8,128)S(1)} collective-permute-done((f32[4,64,128]{2,1,0:T(8,128)}, f32[4,64,128]{2,1,0:T(8,128)S(1)}, u32[]{:S(2)}, u32[]{:S(2)}) %collective-permute-start.3) | collective-permute-done | bytes 131104 | tf_op jit(solution)/shard_map/ppermute | solution.py:395
  36.6 0.9 add.80
  37.5 3.1 %collective-permute-start.4 = (f32[4,64,128]{2,1,0:T(8,128)S(1)}, f32[4,64,128]{2,1,0:T(8,128)S(1)}, u32[]{:S(2)}, u32[]{:S(2)}) collective-permute-start(f32[4,64,128]{2,1,0:T(8,128)S(1)} %add.80), channel_id=1, source_target_pairs={{0,16},{8,24},{16,0},{24,8},{1,17},{9,25},{17,1},{25,9},{2,18},{10... | collective-permute-start | bytes 393224 | tf_op jit(solution)/shard_map/ppermute | solution.py:395
  40.6 3.0 %collective-permute-done.4 = f32[4,64,128]{2,1,0:T(8,128)S(1)} collective-permute-done((f32[4,64,128]{2,1,0:T(8,128)S(1)}, f32[4,64,128]{2,1,0:T(8,128)S(1)}, u32[]{:S(2)}, u32[]{:S(2)}) %collective-permute-start.4) | collective-permute-done | bytes 131104 | tf_op jit(solution)/shard_map/ppermute | solution.py:395
  44.4 6.4 %shard_map.96 = (f32[2,64,64,128]{3,2,1,0:T(8,128)}, f32[2,64,128]{2,1,0:T(8,128)}, f32[4,64,128]{2,1,0:T(8,128)}, f32[2,64,128]{2,1,0:T(8,128)}) custom-call(s32[4]{0:T(128)} %reshape_squeeze.9.pos_ref, f32[4,64,128]{2,1,0:T(8,128)} %add_add_fusion.1.refs_0_, f32[2,64,64,128]{3,2,1,0:T(8,128)} %get-tuple-element.30.refs_1_, ...), custom_call_target="tpu_custom_call" | custom-call | tf_op jit(solution)/shard_map/pallas_call | solution.py:262
  50.8 1.5 collective-permute-done.5
  52.3 0.9 mul.95
  53.3 3.3 %collective-permute-start.6 = (f32[4,64,128]{2,1,0:T(8,128)S(1)}, f32[4,64,128]{2,1,0:T(8,128)S(1)}, u32[]{:S(2)}, u32[]{:S(2)}) collective-permute-start(f32[4,64,128]{2,1,0:T(8,128)S(1)} %mul.95), channel_id=1, source_target_pairs={{0,2},{1,3},{2,0},{3,1},{4,6},{5,7},{6,4},{7,5},{8,10},{9,11},{10,... | collective-permute-start | bytes 393224 | tf_op jit(solution)/shard_map/ppermute | solution.py:395
  56.5 3.8 %collective-permute-done.6 = f32[4,64,128]{2,1,0:T(8,128)S(1)} collective-permute-done((f32[4,64,128]{2,1,0:T(8,128)S(1)}, f32[4,64,128]{2,1,0:T(8,128)S(1)}, u32[]{:S(2)}, u32[]{:S(2)}) %collective-permute-start.6) | collective-permute-done | bytes 131104 | tf_op jit(solution)/shard_map/ppermute | solution.py:395
  60.4 1.8 %collective-permute-start.7 = (f32[4,64,128]{2,1,0:T(8,128)S(1)}, f32[4,64,128]{2,1,0:T(8,128)S(1)}, u32[]{:S(2)}, u32[]{:S(2)}) collective-permute-start(f32[4,64,128]{2,1,0:T(8,128)S(1)} %mul.97), channel_id=1, source_target_pairs={{0,4},{1,5},{2,6},{3,7},{4,0},{5,1},{6,2},{7,3},{8,12},{9,13},{10,... | collective-permute-start | bytes 393224 | tf_op jit(solution)/shard_map/ppermute | solution.py:395
  62.2 3.3 %collective-permute-done.7 = f32[4,64,128]{2,1,0:T(8,128)S(1)} collective-permute-done((f32[4,64,128]{2,1,0:T(8,128)S(1)}, f32[4,64,128]{2,1,0:T(8,128)S(1)}, u32[]{:S(2)}, u32[]{:S(2)}) %collective-permute-start.7) | collective-permute-done | bytes 131104 | tf_op jit(solution)/shard_map/ppermute | solution.py:395
  66.2 8.2 %shard_map.98 = (f32[2,64,64,128]{3,2,1,0:T(8,128)}, f32[2,64,64,128]{3,2,1,0:T(8,128)}, f32[2,64,128]{2,1,0:T(8,128)}, f32[4,64,128]{2,1,0:T(8,128)}) custom-call(s32[4]{0:T(128)} %reshape_squeeze.9.pos_ref, f32[4,64,128]{2,1,0:T(8,128)} %bitcast.15, f32[2,64,64,128]{3,2,1,0:T(8,128)} %get-tuple-element.31.ba_ref.refs_1_, ...), custom_call_target="tpu_custom_call" | custom-call | tf_op jit(solution)/shard_map/pallas_call | solution.py:262
  74.5 1.5 collective-permute-done.10
  76.0 0.9 multiply_add_fusion.5
  77.0 1.7 %collective-permute-start.11 = (f32[4,64,128]{2,1,0:T(8,128)S(1)}, f32[4,64,128]{2,1,0:T(8,128)S(1)}, u32[]{:S(2)}, u32[]{:S(2)}) collective-permute-start(f32[4,64,128]{2,1,0:T(8,128)S(1)} %multiply_add_fusion.5), channel_id=1, source_target_pairs={{0,2},{1,3},{2,0},{3,1},{4,6},{5,7},{6,4},{7,5},{8,10},{9,11},{10,... | collective-permute-start | bytes 393224 | tf_op jit(solution)/shard_map/ppermute | solution.py:395
  78.7 3.9 %collective-permute-done.11 = f32[4,64,128]{2,1,0:T(8,128)S(1)} collective-permute-done((f32[4,64,128]{2,1,0:T(8,128)S(1)}, f32[4,64,128]{2,1,0:T(8,128)S(1)}, u32[]{:S(2)}, u32[]{:S(2)}) %collective-permute-start.11) | collective-permute-done | bytes 131104 | tf_op jit(solution)/shard_map/ppermute | solution.py:395
  82.6 1.8 %collective-permute-start.12 = (f32[4,64,128]{2,1,0:T(8,128)S(1)}, f32[4,64,128]{2,1,0:T(8,128)S(1)}, u32[]{:S(2)}, u32[]{:S(2)}) collective-permute-start(f32[4,64,128]{2,1,0:T(8,128)S(1)} %multiply_add_fusion.4), channel_id=1, source_target_pairs={{0,4},{1,5},{2,6},{3,7},{4,0},{5,1},{6,2},{7,3},{8,12},{9,13},{10,... | collective-permute-start | bytes 393224 | tf_op jit(solution)/shard_map/ppermute | solution.py:395
  84.4 6.5 %shard_map.97 = (f32[2,64,64,128]{3,2,1,0:T(8,128)}, f32[4,64,128]{2,1,0:T(8,128)}) custom-call(s32[4]{0:T(128)} %reshape_squeeze.9.pos_ref, f32[2,64,64,128]{3,2,1,0:T(8,128)} %get-tuple-element.31.ba_ref.refs_1_, f32[2,64,128]{2,1,0:T(8,128)} %copy.21.sign_ref.refs_2_.refs_3_, f32[2,64,128]{2,1,0:T(8,128)} %get-tuple-element.32.here_ref.refs_3_.refs_7_, ...), custom_call_target="tpu_custom_call" | custom-call | tf_op jit(solution)/shard_map/pallas_call | solution.py:262
  91.6 9.3 %shard_map.99 = (f32[2,64,64,128]{3,2,1,0:T(8,128)}, f32[4,64,128]{2,1,0:T(8,128)}) custom-call(s32[4]{0:T(128)} %reshape_squeeze.9.pos_ref, f32[4,64,128]{2,1,0:T(8,128)} %add_add_fusion.1.refs_0_, f32[2,64,64,128]{3,2,1,0:T(8,128)} %get-tuple-element.30.refs_1_, f32[2,64,64,128]{3,2,1,0:T(8,128)} %broadcast_in_dim.79.refs_1_.ew_ref.refs_2_.refs_5_.refs_6_, ...), custom_call_target="tpu_custom_call" | custom-call | tf_op jit(solution)/shard_map/pallas_call | solution.py:262
  101.6 4.5 %collective-permute-done.13 = f32[4,64,128]{2,1,0:T(8,128)S(1)} collective-permute-done((f32[4,64,128]{2,1,0:T(8,128)}, f32[4,64,128]{2,1,0:T(8,128)S(1)}, u32[]{:S(2)}, u32[]{:S(2)}) %collective-permute-start.13) | collective-permute-done | bytes 131104 | tf_op jit(solution)/shard_map/ppermute | solution.py:395
  106.1 0.9 add.91
  107.1 2.1 %collective-permute-start.14 = (f32[4,64,128]{2,1,0:T(8,128)S(1)}, f32[4,64,128]{2,1,0:T(8,128)S(1)}, u32[]{:S(2)}, u32[]{:S(2)}) collective-permute-start(f32[4,64,128]{2,1,0:T(8,128)S(1)} %add.91), channel_id=1, source_target_pairs={{0,16},{8,24},{16,0},{24,8},{1,17},{9,25},{17,1},{25,9},{2,18},{10... | collective-permute-start | bytes 393224 | tf_op jit(solution)/shard_map/ppermute | solution.py:395
  109.2 5.2 %collective-permute-done.14 = f32[4,64,128]{2,1,0:T(8,128)S(1)} collective-permute-done((f32[4,64,128]{2,1,0:T(8,128)S(1)}, f32[4,64,128]{2,1,0:T(8,128)S(1)}, u32[]{:S(2)}, u32[]{:S(2)}) %collective-permute-start.14) | collective-permute-done | bytes 131104 | tf_op jit(solution)/shard_map/ppermute | solution.py:395
  115.1 10.4 %shard_map.100 = (f32[2,64,64,128]{3,2,1,0:T(8,128)}, f32[2,64,64,128]{3,2,1,0:T(8,128)}, f32[2,64,128]{2,1,0:T(8,128)}, f32[4,64,128]{2,1,0:T(8,128)}) custom-call(s32[4]{0:T(128)} %reshape_squeeze.9.pos_ref, f32[4,64,128]{2,1,0:T(8,128)} %get-tuple-element.50.refs_0_, f32[2,64,64,128]{3,2,1,0:T(8,128)} %get-tuple-element.42.refs_1_, ...), custom_call_target="tpu_custom_call" | custom-call | tf_op jit(solution)/shard_map/pallas_call | solution.py:262
  125.7 1.5 collective-permute-done.15
  127.1 1.0 multiply_add_fusion.2
  128.2 1.6 collective-permute-start.16
  130.1 3.7 %collective-permute-done.16 = f32[4,64,128]{2,1,0:T(8,128)S(1)} collective-permute-done((f32[4,64,128]{2,1,0:T(8,128)S(1)}, f32[4,64,128]{2,1,0:T(8,128)S(1)}, u32[]{:S(2)}, u32[]{:S(2)}) %collective-permute-start.16) | collective-permute-done | bytes 131104 | tf_op jit(solution)/shard_map/ppermute | solution.py:395
  134.5 0.8 collective-permute-done.8
  135.3 1.8 %collective-permute-start.9 = (f32[4,64,128]{2,1,0:T(8,128)S(1)}, f32[4,64,128]{2,1,0:T(8,128)S(1)}, u32[]{:S(2)}, u32[]{:S(2)}) collective-permute-start(f32[4,64,128]{2,1,0:T(8,128)S(1)} %add.83), channel_id=1, source_target_pairs={{0,16},{8,24},{16,0},{24,8},{1,17},{9,25},{17,1},{25,9},{2,18},{10... | collective-permute-start | bytes 393224 | tf_op jit(solution)/shard_map/ppermute | solution.py:395
  137.1 1.8 %collective-permute-done.17 = f32[4,64,128]{2,1,0:T(8,128)S(1)} collective-permute-done((f32[4,64,128]{2,1,0:T(8,128)S(1)}, f32[4,64,128]{2,1,0:T(8,128)S(1)}, u32[]{:S(2)}, u32[]{:S(2)}) %collective-permute-start.17) | collective-permute-done | bytes 131104 | tf_op jit(solution)/shard_map/ppermute | solution.py:395
  139.0 0.9 multiply_add_fusion.refs_3_
  139.9 7.6 %shard_map.101 = f32[4,64,128]{2,1,0:T(8,128)} custom-call(s32[4]{0:T(128)} %reshape_squeeze.9.pos_ref, f32[4,64,128]{2,1,0:T(8,128)} %add.79.refs_0_, f32[2,64,64,128]{3,2,1,0:T(8,128)} %broadcast_in_dim.79.refs_1_.ew_ref.refs_2_.refs_5_.refs_6_, f32[2,64,64,128]{3,2,1,0:T(8,128)} %get-tuple-element.45.refs_2_, f32[4,64,128]{2,1,0:T(8,128)} %multiply_add_fusion.refs_3_, ...), custom_call_target="tpu_custom_call" | custom-call | tf_op jit(solution)/shard_map/pallas_call | solution.py:262
  147.5 1.0 reduce_sum.42
  149.5 3.3 %reduce_sum.38 = f32[2,64,64]{2,1,0:T(8,128)S(1)} reduce(f32[2,64,64,128]{3,2,1,0:T(8,128)} %get-tuple-element.44, f32[]{:T(128)} %constant.2.clone.1), dimensions={3}, to_apply=%region_0.1 | reduce | flops 1040384 | bytes 4227076 | tf_op jit(solution)/shard_map/reduce_sum | solution.py:527
  152.9 3.4 %collective-permute-start.19 = (f32[2,128]{1,0:T(2,128)S(1)}, f32[2,128]{1,0:T(2,128)S(1)}, u32[]{:S(2)}, u32[]{:S(2)}) collective-permute-start(f32[2,128]{1,0:T(2,128)S(1)} %add.99), channel_id=1, source_target_pairs={{0,16},{8,24},{16,0},{24,8},{1,17},{9,25},{17,1},{25,9},{2,18},{10... | collective-permute-start | bytes 3080 | tf_op jit(solution)/shard_map/ppermute | solution.py:395
  (62 shorter events, 12.8 us)
Async XLA Ops:
  6.1 9.2 %copy-start.3 = (s32[256,128]{1,0:T(8,128)S(1)}, s32[256,128]{1,0:T(8,128)}, u32[]{:S(2)}) copy-start(s32[256,128]{1,0:T(8,128)} %param.11) | copy-start | bytes 393220
  6.1 12.9 %copy-start.4 = (s32[1,1,2,2]{3,2,1,0:T(2,128)S(1)}, s32[1,1,2,2]{3,2,1,0:T(2,128)}, u32[]{:S(2)}) copy-start(s32[1,1,2,2]{3,2,1,0:T(2,128)} %param.8) | copy-start | bytes 52
  14.8 1.3 collective-permute-start
  16.1 4.4 %collective-permute-start.1 = (f32[2,128]{1,0:T(2,128)S(1)}, f32[2,128]{1,0:T(2,128)S(1)}, u32[]{:S(2)}, u32[]{:S(2)}) collective-permute-start(f32[2,128]{1,0:T(2,128)S(1)} %mul.91), channel_id=1, source_target_pairs={{0,2},{1,3},{2,0},{3,1},{4,6},{5,7},{6,4},{7,5},{8,10},{9,11},{10,... | collective-permute-start | bytes 3080 | tf_op jit(solution)/shard_map/ppermute | solution.py:395
  20.5 3.6 %collective-permute-start.2 = (f32[2,128]{1,0:T(2,128)S(1)}, f32[2,128]{1,0:T(2,128)S(1)}, u32[]{:S(2)}, u32[]{:S(2)}) collective-permute-start(f32[2,128]{1,0:T(2,128)S(1)} %mul.93), channel_id=1, source_target_pairs={{0,4},{1,5},{2,6},{3,7},{4,0},{5,1},{6,2},{7,3},{8,12},{9,13},{10,... | collective-permute-start | bytes 3080 | tf_op jit(solution)/shard_map/ppermute | solution.py:395
  31.4 5.2 %collective-permute-start.3 = (f32[4,64,128]{2,1,0:T(8,128)}, f32[4,64,128]{2,1,0:T(8,128)S(1)}, u32[]{:S(2)}, u32[]{:S(2)}) collective-permute-start(f32[4,64,128]{2,1,0:T(8,128)} %get-tuple-element.29), channel_id=1, source_target_pairs={{0,8},{8,0},{16,24},{24,16},{1,9},{9,1},{17,25},{25,17},{2,10},{10... | collective-permute-start | bytes 393224 | tf_op jit(solution)/shard_map/ppermute | solution.py:395
  37.5 6.1 %collective-permute-start.4 = (f32[4,64,128]{2,1,0:T(8,128)S(1)}, f32[4,64,128]{2,1,0:T(8,128)S(1)}, u32[]{:S(2)}, u32[]{:S(2)}) collective-permute-start(f32[4,64,128]{2,1,0:T(8,128)S(1)} %add.80), channel_id=1, source_target_pairs={{0,16},{8,24},{16,0},{24,8},{1,17},{9,25},{17,1},{25,9},{2,18},{10... | collective-permute-start | bytes 393224 | tf_op jit(solution)/shard_map/ppermute | solution.py:395
  50.8 1.6 %collective-permute-start.5 = (f32[4,64,128]{2,1,0:T(8,128)}, f32[4,64,128]{2,1,0:T(8,128)S(1)}, u32[]{:S(2)}, u32[]{:S(2)}) collective-permute-start(f32[4,64,128]{2,1,0:T(8,128)} %get-tuple-element.33), channel_id=1, source_target_pairs={{0,1},{1,0},{2,3},{3,2},{4,5},{5,4},{6,7},{7,6},{8,9},{9,8},{10,11... | collective-permute-start | bytes 393224 | tf_op jit(solution)/shard_map/ppermute | solution.py:395
  53.3 7.1 %collective-permute-start.6 = (f32[4,64,128]{2,1,0:T(8,128)S(1)}, f32[4,64,128]{2,1,0:T(8,128)S(1)}, u32[]{:S(2)}, u32[]{:S(2)}) collective-permute-start(f32[4,64,128]{2,1,0:T(8,128)S(1)} %mul.95), channel_id=1, source_target_pairs={{0,2},{1,3},{2,0},{3,1},{4,6},{5,7},{6,4},{7,5},{8,10},{9,11},{10,... | collective-permute-start | bytes 393224 | tf_op jit(solution)/shard_map/ppermute | solution.py:395
  60.4 5.1 %collective-permute-start.7 = (f32[4,64,128]{2,1,0:T(8,128)S(1)}, f32[4,64,128]{2,1,0:T(8,128)S(1)}, u32[]{:S(2)}, u32[]{:S(2)}) collective-permute-start(f32[4,64,128]{2,1,0:T(8,128)S(1)} %mul.97), channel_id=1, source_target_pairs={{0,4},{1,5},{2,6},{3,7},{4,0},{5,1},{6,2},{7,3},{8,12},{9,13},{10,... | collective-permute-start | bytes 393224 | tf_op jit(solution)/shard_map/ppermute | solution.py:395
  66.1 9.9 %copy-start.1 = (f32[4,64,128]{2,1,0:T(8,128)S(1)}, f32[4,64,128]{2,1,0:T(8,128)}, u32[]{:S(2)}) copy-start(f32[4,64,128]{2,1,0:T(8,128)} %get-tuple-element.33) | copy-start | bytes 393220
  74.4 1.6 %collective-permute-start.10 = (f32[4,64,128]{2,1,0:T(8,128)}, f32[4,64,128]{2,1,0:T(8,128)S(1)}, u32[]{:S(2)}, u32[]{:S(2)}) collective-permute-start(f32[4,64,128]{2,1,0:T(8,128)} %get-tuple-element.38), channel_id=1, source_target_pairs={{0,1},{1,0},{2,3},{3,2},{4,5},{5,4},{6,7},{7,6},{8,9},{9,8},{10,11... | collective-permute-start | bytes 393224 | tf_op jit(solution)/shard_map/ppermute | solution.py:395
  77.0 5.6 %collective-permute-start.11 = (f32[4,64,128]{2,1,0:T(8,128)S(1)}, f32[4,64,128]{2,1,0:T(8,128)S(1)}, u32[]{:S(2)}, u32[]{:S(2)}) collective-permute-start(f32[4,64,128]{2,1,0:T(8,128)S(1)} %multiply_add_fusion.5), channel_id=1, source_target_pairs={{0,2},{1,3},{2,0},{3,1},{4,6},{5,7},{6,4},{7,5},{8,10},{9,11},{10,... | collective-permute-start | bytes 393224 | tf_op jit(solution)/shard_map/ppermute | solution.py:395
  82.6 8.3 %collective-permute-start.12 = (f32[4,64,128]{2,1,0:T(8,128)S(1)}, f32[4,64,128]{2,1,0:T(8,128)S(1)}, u32[]{:S(2)}, u32[]{:S(2)}) collective-permute-start(f32[4,64,128]{2,1,0:T(8,128)S(1)} %multiply_add_fusion.4), channel_id=1, source_target_pairs={{0,4},{1,5},{2,6},{3,7},{4,0},{5,1},{6,2},{7,3},{8,12},{9,13},{10,... | collective-permute-start | bytes 393224 | tf_op jit(solution)/shard_map/ppermute | solution.py:395
  100.9 5.2 %collective-permute-start.13 = (f32[4,64,128]{2,1,0:T(8,128)}, f32[4,64,128]{2,1,0:T(8,128)S(1)}, u32[]{:S(2)}, u32[]{:S(2)}) collective-permute-start(f32[4,64,128]{2,1,0:T(8,128)} %get-tuple-element.41), channel_id=1, source_target_pairs={{0,8},{8,0},{16,24},{24,16},{1,9},{9,1},{17,25},{25,17},{2,10},{10... | collective-permute-start | bytes 393224 | tf_op jit(solution)/shard_map/ppermute | solution.py:395
  107.1 7.3 %collective-permute-start.14 = (f32[4,64,128]{2,1,0:T(8,128)S(1)}, f32[4,64,128]{2,1,0:T(8,128)S(1)}, u32[]{:S(2)}, u32[]{:S(2)}) collective-permute-start(f32[4,64,128]{2,1,0:T(8,128)S(1)} %add.91), channel_id=1, source_target_pairs={{0,16},{8,24},{16,0},{24,8},{1,17},{9,25},{17,1},{25,9},{2,18},{10... | collective-permute-start | bytes 393224 | tf_op jit(solution)/shard_map/ppermute | solution.py:395
  115.1 14.7 %copy-start = (f32[256,128]{1,0:T(8,128)S(1)}, f32[256,128]{1,0:T(8,128)}, u32[]{:S(2)}) copy-start(f32[256,128]{1,0:T(8,128)} %param.13) | copy-start | bytes 393220
  115.1 14.9 %copy-start.2 = (f32[4,64,128]{2,1,0:T(8,128)S(1)}, f32[4,64,128]{2,1,0:T(8,128)}, u32[]{:S(2)}) copy-start(f32[4,64,128]{2,1,0:T(8,128)} %get-tuple-element.36) | copy-start | bytes 393220
  125.5 1.6 %collective-permute-start.15 = (f32[4,64,128]{2,1,0:T(8,128)}, f32[4,64,128]{2,1,0:T(8,128)S(1)}, u32[]{:S(2)}, u32[]{:S(2)}) collective-permute-start(f32[4,64,128]{2,1,0:T(8,128)} %get-tuple-element.46), channel_id=1, source_target_pairs={{0,1},{1,0},{2,3},{3,2},{4,5},{5,4},{6,7},{7,6},{8,9},{9,8},{10,11... | collective-permute-start | bytes 393224 | tf_op jit(solution)/shard_map/ppermute | solution.py:395
  128.2 5.6 %collective-permute-start.16 = (f32[4,64,128]{2,1,0:T(8,128)S(1)}, f32[4,64,128]{2,1,0:T(8,128)S(1)}, u32[]{:S(2)}, u32[]{:S(2)}) collective-permute-start(f32[4,64,128]{2,1,0:T(8,128)S(1)} %multiply_add_fusion.2), channel_id=1, source_target_pairs={{0,2},{1,3},{2,0},{3,1},{4,6},{5,7},{6,4},{7,5},{8,10},{9,11},{10,... | collective-permute-start | bytes 393224 | tf_op jit(solution)/shard_map/ppermute | solution.py:395
  130.0 5.3 %collective-permute-start.8 = (f32[4,64,128]{2,1,0:T(8,128)S(1)}, f32[4,64,128]{2,1,0:T(8,128)S(1)}, u32[]{:S(2)}, u32[]{:S(2)}) collective-permute-start(f32[4,64,128]{2,1,0:T(8,128)S(1)} %copy-done.2), channel_id=1, source_target_pairs={{0,8},{8,0},{16,24},{24,16},{1,9},{9,1},{17,25},{25,17},{2,10},{10... | collective-permute-start | bytes 393224 | tf_op jit(solution)/shard_map/ppermute | solution.py:395
  133.9 5.0 %collective-permute-start.17 = (f32[4,64,128]{2,1,0:T(8,128)S(1)}, f32[4,64,128]{2,1,0:T(8,128)S(1)}, u32[]{:S(2)}, u32[]{:S(2)}) collective-permute-start(f32[4,64,128]{2,1,0:T(8,128)S(1)} %multiply_add_fusion.1), channel_id=1, source_target_pairs={{0,4},{1,5},{2,6},{3,7},{4,0},{5,1},{6,2},{7,3},{8,12},{9,13},{10,... | collective-permute-start | bytes 393224 | tf_op jit(solution)/shard_map/ppermute | solution.py:395
  135.3 13.4 %collective-permute-start.9 = (f32[4,64,128]{2,1,0:T(8,128)S(1)}, f32[4,64,128]{2,1,0:T(8,128)S(1)}, u32[]{:S(2)}, u32[]{:S(2)}) collective-permute-start(f32[4,64,128]{2,1,0:T(8,128)S(1)} %add.83), channel_id=1, source_target_pairs={{0,16},{8,24},{16,0},{24,8},{1,17},{9,25},{17,1},{25,9},{2,18},{10... | collective-permute-start | bytes 393224 | tf_op jit(solution)/shard_map/ppermute | solution.py:395
  148.6 4.2 %collective-permute-start.18 = (f32[2,128]{1,0:T(2,128)S(1)}, f32[2,128]{1,0:T(2,128)S(1)}, u32[]{:S(2)}, u32[]{:S(2)}) collective-permute-start(f32[2,128]{1,0:T(2,128)S(1)} %reshape.60), channel_id=1, source_target_pairs={{0,8},{8,0},{16,24},{24,16},{1,9},{9,1},{17,25},{25,17},{2,10},{10... | collective-permute-start | bytes 3080 | tf_op jit(solution)/shard_map/ppermute | solution.py:395
  152.9 5.0 %collective-permute-start.19 = (f32[2,128]{1,0:T(2,128)S(1)}, f32[2,128]{1,0:T(2,128)S(1)}, u32[]{:S(2)}, u32[]{:S(2)}) collective-permute-start(f32[2,128]{1,0:T(2,128)S(1)} %add.99), channel_id=1, source_target_pairs={{0,16},{8,24},{16,0},{24,8},{1,17},{9,25},{17,1},{25,9},{2,18},{10... | collective-permute-start | bytes 3080 | tf_op jit(solution)/shard_map/ppermute | solution.py:395

commit v6 on v5

--- a/solution.py
+++ b/solution.py
@@ -72,6 +72,14 @@
     return pos_ref[2 * k + 1]
 
 
+def _columns(pos_ref, k, slots, n_c):
+    return pos_ref[2 * slots + k], 3 * slots + k * n_c
+
+
+def _loop(count, body, init):
+    return lax.fori_loop(0, count, body, init)
+
+
 def _fwd_products_kernel(has_u, slots, blocks, pos_ref, *refs):
     refs = list(refs)
     spread_ref = refs.pop(0)
@@ -81,7 +89,10 @@
     n_c = ew_ref.shape[1]
     shape = ew_ref.shape[2:]
 
-    def forward(c, carry):
+    count, base = _columns(pos_ref, k, slots, n_c)
+
+    def forward(i, carry):
+        c = pos_ref[base + i]
         m = _spread_row(spread_ref, c, shape)
         if has_u:
             m = m - u_ref[0, c]
@@ -90,15 +101,15 @@
         ba_ref[0, c] = carry
         return carry * h
 
-    whole = lax.fori_loop(0, n_c, forward, jnp.ones(shape, F32), unroll=UNROLL)
+    whole = _loop(count, forward, jnp.ones(shape, F32))
     whole_ref[k] = whole
 
     def backward(i, carry):
-        c = n_c - 1 - i
+        c = pos_ref[base + count - 1 - i]
         ba_ref[0, c] = ba_ref[0, c] * carry
         return carry * h_scr[c]
 
-    lax.fori_loop(0, n_c, backward, jnp.ones(shape, F32), unroll=UNROLL)
+    _loop(count, backward, jnp.ones(shape, F32))
 
     @pl.when(k == slots - 1)
     def _():
@@ -117,9 +128,10 @@
             here_ref[j] = value
 
 
-def _fwd_messages_kernel(pos_ref, ba_ref, sign_ref, here_ref, others_ref, ew_ref, u_ref, col_ref):
+def _fwd_messages_kernel(slots, pos_ref, ba_ref, sign_ref, here_ref, others_ref, ew_ref, u_ref, col_ref):
     k = pl.program_id(0)
     n_c = ba_ref.shape[1]
+    count, base = _columns(pos_ref, k, slots, n_c)
 
     @pl.when(k == 0)
     def _():
@@ -128,17 +140,18 @@
     f = sign_ref[k] * here_ref[k] * others_ref[_row_block(pos_ref, k)]
     q = _col_block(pos_ref, k)
 
-    def body(c, carry):
+    def body(i, carry):
+        c = pos_ref[base + i]
         x = ba_ref[0, c] * f
         u = ew_ref[0, c] * jnp.log((1.0 + DAMP * x) / (1.0 - DAMP * x))
         u_ref[0, c] = u
         col_ref[q, pl.ds(c, 1), :] = col_ref[q, pl.ds(c, 1), :] + jnp.sum(u, axis=0, keepdims=True)
         return carry
 
-    lax.fori_loop(0, n_c, body, 0, unroll=UNROLL)
-
-
-def _bwd_messages_kernel(has_next, has_acc, pos_ref, *refs):
+    _loop(count, body, 0)
+
+
+def _bwd_messages_kernel(has_next, has_acc, slots, pos_ref, *refs):
     refs = list(refs)
     gsp_ref = refs.pop(0)
     gm_ref = refs.pop(0) if has_next else None
@@ -159,8 +172,10 @@
     here = here_ref[k]
     others = others_ref[p]
     f = sign * here * others
-
-    def body(c, total):
+    count, base = _columns(pos_ref, k, slots, n_c)
+
+    def body(i, total):
+        c = pos_ref[base + i]
         gu = _spread_row(gsp_ref, c, shape)
         if has_next:
             gu = gu - gm_ref[0, c]
@@ -176,7 +191,7 @@
         gba_ref[0, c] = gx * f
         return total + gx * ba
 
-    grad_factor = lax.fori_loop(0, n_c, body, jnp.zeros(shape, F32), unroll=UNROLL)
+    grad_factor = _loop(count, body, jnp.zeros(shape, F32))
     ghere_ref[k] = grad_factor * sign * others
     gothers_ref[p] = gothers_ref[p] + grad_factor * sign * here
 
@@ -210,8 +225,11 @@
                 )
         gwh = gwh + jnp.where(other != k, term, 0.0)
 
-    def forward(c, carry):
+    count, base = _columns(pos_ref, k, slots, n_c)
+
+    def forward(i, carry):
         prod, grad = carry
+        c = pos_ref[base + i]
         m = _spread_row(spread_ref, c, shape)
         if has_u:
             m = m - u_ref[0, c]
@@ -223,11 +241,11 @@
 
     ones = jnp.ones(shape, F32)
     zeros = jnp.zeros(shape, F32)
-    lax.fori_loop(0, n_c, forward, (ones, zeros), unroll=UNROLL)
+    _loop(count, forward, (ones, zeros))
 
     def backward(i, carry):
         prod, grad = carry
-        c = n_c - 1 - i
+        c = pos_ref[base + count - 1 - i]
         h = h_scr[c]
         before = p_scr[c]
         gh = q_scr[c] * prod + before * (grad + gwh * prod)
@@ -237,7 +255,7 @@
         col_ref[q, pl.ds(c, 1), :] = col_ref[q, pl.ds(c, 1), :] + jnp.sum(gm, axis=0, keepdims=True)
         return (prod * h, grad * h + gba_ref[0, c] * prod)
 
-    lax.fori_loop(0, n_c, backward, (ones, zeros), unroll=UNROLL)
+    _loop(count, backward, (ones, zeros))
 
 
 def _spec(kind, shape):
@@ -298,7 +316,7 @@
         ("dense", jax.ShapeDtypeStruct(ba.shape, F32)),
         ("full", jax.ShapeDtypeStruct((col_blocks, c, s), F32)),
     ]
-    return _call(_fwd_messages_kernel, pos, inputs, outs)
+    return _call(functools.partial(_fwd_messages_kernel, k), pos, inputs, outs)
 
 
 def bwd_messages(pos, gsp, gm, ba, sign, here, others, ew, acc):
@@ -317,7 +335,7 @@
         ("full", jax.ShapeDtypeStruct(here.shape, F32)),
         ("full", jax.ShapeDtypeStruct(others.shape, F32)),
     ]
-    return _call(functools.partial(_bwd_messages_kernel, has_next, has_acc), pos, inputs, outs)
+    return _call(functools.partial(_bwd_messages_kernel, has_next, has_acc, k), pos, inputs, outs)
 
 
 def bwd_products(pos, spread, u, ew, gba, grows, ghere, whole, here, col_blocks, emit_gm):
@@ -475,9 +493,17 @@
     edge, row_hot, col_hot, same_row = device_tables(
         tile_bits[0, 0], tile_pos[0, 0], tile_count[0, 0], check_blocks, column_blocks
     )
-    pos = tile_pos[0, 0].reshape(slot_total * 2)
     weight = edge_weight[0, 0].reshape(slot_total, TILE, TILE)
     edge_t = jnp.swapaxes(edge, 1, 2)
+    filled = jnp.any(edge_t > 0, axis=2)
+    order = jnp.argsort(jnp.where(filled, 0, 1).astype(jnp.int32), axis=1, stable=True)
+    pos = jnp.concatenate(
+        [
+            tile_pos[0, 0].reshape(slot_total * 2),
+            jnp.sum(filled.astype(jnp.int32), axis=1),
+            order.astype(jnp.int32).reshape(slot_total * TILE),
+        ]
+    )
     dense = (slot_total, TILE, TILE, shots)
     ew = jnp.broadcast_to((edge_t * jnp.swapaxes(weight, 1, 2))[..., None], dense)
     sign_dev = (1.0 - 2.0 * syndrome.astype(jnp.float32)).reshape(check_blocks, TILE, shots)
@@ -524,7 +550,7 @@
     else:
         shot_sums = checks_total(shot_sums, n_chk)
     prior_grad = prior_grad + shot_sums
-    weight_grad = edge * jnp.swapaxes(jnp.sum(acc, axis=3), 1, 2)
+    weight_grad = jnp.where(edge > 0, jnp.swapaxes(jnp.sum(acc, axis=3), 1, 2), 0.0)
     return (
         marginals,
         weight_grad.reshape(1, 1, slot_total, TILE * TILE),

time: 159 us -> 158 us (level)
  waiting for transfers between devices: 41.1 us -> 46.6 us
  Pallas kernels: 60.1 us -> 55.3 us
  starting transfers between devices: 29.5 us -> 25.6 us
  other arithmetic: 14.6 us -> 16.5 us
    ppermute x20, waiting for transfers between devices: 41.1 us -> 46.6 us  [_swap(): return lax.ppermute(value, axis, perm)]
    pallas_call x8, Pallas kernels: 60.1 us -> 55.3 us  [_call(): pl.pallas_call(kernel, grid_spec=grid_spec, out_shape=[o for kind, o in o...]
    ppermute x20, starting transfers between devices: 29.5 us -> 25.6 us  [_swap(): return lax.ppermute(value, axis, perm)]
    reduce_sum x1 -> x2, other arithmetic: 3.34 us -> 3.46 us  [the longest x1 3.34 us: body(): jnp.sum(acc, axis=3)]
  transfers between devices with their start and end apart: 20 -> 20, of which waited for: 17 -> 16; matrix products, arithmetic and copies ran while one was open for 6% -> 6% of each run, Pallas kernels for 9% -> 8%
where the time goes in v6:
time: 158 us; the launch traced here: 157 us
  Pallas kernels  55.3 us (35%)
  waiting for transfers between devices  46.6 us (29%)
  starting transfers between devices  25.6 us (16%)
  other arithmetic  16.5 us (10%)
  local copies, waits for them, and re-layouts  11 us (7%)
    pallas_call x8, Pallas kernels, _call(): pl.pallas_call(kernel, grid_spec=grid_spec, out_shape=[o for kind, o in o...  55.3 us
    ppermute x20, waiting for transfers between devices, _swap(): return lax.ppermute(value, axis, perm)  46.6 us
    ppermute x20, starting transfers between devices, _swap(): return lax.ppermute(value, axis, perm)  25.6 us
    reduce_sum x1, other arithmetic, body(): jnp.sum(acc, axis=3)  3.34 us
  transfers between devices with their start and end apart: 20, of which 16 were waited for; matrix products, arithmetic and copies ran while one was open for 6% of the time, Pallas kernels for 8%

profile of v6, /device:TPU:0, one launch (start us, length us, event | category | flops | bytes accessed | tf_op | source)
XLA Modules:
  0.0 156.8 jit_solution(16923308612927828099)
XLA Ops:
  0.6 0.9 squeeze.10
  2.7 1.0 sort.17
  5.4 0.9 reshape_squeeze.10
  7.8 2.5 %broadcast_in_dim.91.refs_1_.ew_ref.refs_2_.refs_5_.refs_6_ = f32[2,64,64,128]{3,2,1,0:T(8,128)} broadcast(f32[2,64,64]{2,1,0:T(8,128)S(1)} %multiply_bitcast_fusion), dimensions={0,1,2} | broadcast | bytes 4227072 | tf_op jit(solution)/shard_map/broadcast_in_dim | solution.py:508
  10.3 5.1 %shard_map.94 = (f32[2,64,64,128]{3,2,1,0:T(8,128)}, f32[2,64,128]{2,1,0:T(8,128)}, f32[4,64,128]{2,1,0:T(8,128)}, f32[2,64,128]{2,1,0:T(8,128)}) custom-call(s32[134]{0:T(256)} %pad_add_fusion.pos_ref, f32[4,64,128]{2,1,0:T(8,128)} %add.79.refs_0_, f32[2,64,64,128]{3,2,1,0:T(8,128)} %broadcast_in_dim.91.refs_1_.ew_ref.refs_2_.refs_5_.refs_6_), custom_call_target="tpu_custom_call" | custom-call | tf_op jit(solution)/shard_map/pallas_call | solution.py:280
  15.5 1.0 slice_reduce_fusion
  17.0 0.8 collective-permute-done
  17.8 2.7 %collective-permute-start.1 = (f32[2,128]{1,0:T(2,128)S(1)}, f32[2,128]{1,0:T(2,128)S(1)}, u32[]{:S(2)}, u32[]{:S(2)}) collective-permute-start(f32[2,128]{1,0:T(2,128)S(1)} %mul.88), channel_id=1, source_target_pairs={{0,2},{1,3},{2,0},{3,1},{4,6},{5,7},{6,4},{7,5},{8,10},{9,11},{10,... | collective-permute-start | bytes 3080 | tf_op jit(solution)/shard_map/ppermute | solution.py:413
  20.6 1.4 collective-permute-done.1
  22.1 2.1 %collective-permute-start.2 = (f32[2,128]{1,0:T(2,128)S(1)}, f32[2,128]{1,0:T(2,128)S(1)}, u32[]{:S(2)}, u32[]{:S(2)}) collective-permute-start(f32[2,128]{1,0:T(2,128)S(1)} %mul.90), channel_id=1, source_target_pairs={{0,4},{1,5},{2,6},{3,7},{4,0},{5,1},{6,2},{7,3},{8,12},{9,13},{10,... | collective-permute-start | bytes 3080 | tf_op jit(solution)/shard_map/ppermute | solution.py:413
  26.5 6.2 %shard_map.95 = (f32[2,64,64,128]{3,2,1,0:T(8,128)}, f32[4,64,128]{2,1,0:T(8,128)}) custom-call(s32[134]{0:T(256)} %pad_add_fusion.pos_ref, f32[2,64,64,128]{3,2,1,0:T(8,128)} %get-tuple-element.28.ba_ref.refs_2_, f32[2,64,128]{2,1,0:T(8,128)} %copy.32.sign_ref.refs_2_.refs_3_, f32[2,64,128]{2,1,0:T(8,128)} %get-tuple-element.29.here_ref.refs_4_.refs_6_, ...), custom_call_target="tpu_custom_call" | custom-call | tf_op jit(solution)/shard_map/pallas_call | solution.py:280
  32.7 1.8 %collective-permute-start.3 = (f32[4,64,128]{2,1,0:T(8,128)}, f32[4,64,128]{2,1,0:T(8,128)S(1)}, u32[]{:S(2)}, u32[]{:S(2)}) collective-permute-start(f32[4,64,128]{2,1,0:T(8,128)} %get-tuple-element.31), channel_id=1, source_target_pairs={{0,8},{8,0},{16,24},{24,16},{1,9},{9,1},{17,25},{25,17},{2,10},{10... | collective-permute-start | bytes 393224 | tf_op jit(solution)/shard_map/ppermute | solution.py:413
  34.5 3.4 %collective-permute-done.3 = f32[4,64,128]{2,1,0:T(8,128)S(1)} collective-permute-done((f32[4,64,128]{2,1,0:T(8,128)}, f32[4,64,128]{2,1,0:T(8,128)S(1)}, u32[]{:S(2)}, u32[]{:S(2)}) %collective-permute-start.3) | collective-permute-done | bytes 131104 | tf_op jit(solution)/shard_map/ppermute | solution.py:413
  37.9 0.9 add.80
  38.8 4.2 %collective-permute-start.4 = (f32[4,64,128]{2,1,0:T(8,128)S(1)}, f32[4,64,128]{2,1,0:T(8,128)S(1)}, u32[]{:S(2)}, u32[]{:S(2)}) collective-permute-start(f32[4,64,128]{2,1,0:T(8,128)S(1)} %add.80), channel_id=1, source_target_pairs={{0,16},{8,24},{16,0},{24,8},{1,17},{9,25},{17,1},{25,9},{2,18},{10... | collective-permute-start | bytes 393224 | tf_op jit(solution)/shard_map/ppermute | solution.py:413
  43.0 4.4 %collective-permute-done.4 = f32[4,64,128]{2,1,0:T(8,128)S(1)} collective-permute-done((f32[4,64,128]{2,1,0:T(8,128)S(1)}, f32[4,64,128]{2,1,0:T(8,128)S(1)}, u32[]{:S(2)}, u32[]{:S(2)}) %collective-permute-start.4) | collective-permute-done | bytes 131104 | tf_op jit(solution)/shard_map/ppermute | solution.py:413
  48.1 6.0 %shard_map.96 = (f32[2,64,64,128]{3,2,1,0:T(8,128)}, f32[2,64,128]{2,1,0:T(8,128)}, f32[4,64,128]{2,1,0:T(8,128)}, f32[2,64,128]{2,1,0:T(8,128)}) custom-call(s32[134]{0:T(256)} %pad_add_fusion.pos_ref, f32[4,64,128]{2,1,0:T(8,128)} %add_add_fusion.1.refs_0_, f32[2,64,64,128]{3,2,1,0:T(8,128)} %get-tuple-element.32.refs_1_, ...), custom_call_target="tpu_custom_call" | custom-call | tf_op jit(solution)/shard_map/pallas_call | solution.py:280
  54.1 1.5 collective-permute-done.5
  55.7 0.9 mul.92
  56.6 1.1 collective-permute-start.6
  57.7 4.5 %collective-permute-done.6 = f32[4,64,128]{2,1,0:T(8,128)S(1)} collective-permute-done((f32[4,64,128]{2,1,0:T(8,128)S(1)}, f32[4,64,128]{2,1,0:T(8,128)S(1)}, u32[]{:S(2)}, u32[]{:S(2)}) %collective-permute-start.6) | collective-permute-done | bytes 131104 | tf_op jit(solution)/shard_map/ppermute | solution.py:413
  62.3 1.6 %collective-permute-start.7 = (f32[4,64,128]{2,1,0:T(8,128)S(1)}, f32[4,64,128]{2,1,0:T(8,128)S(1)}, u32[]{:S(2)}, u32[]{:S(2)}) collective-permute-start(f32[4,64,128]{2,1,0:T(8,128)S(1)} %mul.94), channel_id=1, source_target_pairs={{0,4},{1,5},{2,6},{3,7},{4,0},{5,1},{6,2},{7,3},{8,12},{9,13},{10,... | collective-permute-start | bytes 393224 | tf_op jit(solution)/shard_map/ppermute | solution.py:413
  63.8 3.5 %collective-permute-done.7 = f32[4,64,128]{2,1,0:T(8,128)S(1)} collective-permute-done((f32[4,64,128]{2,1,0:T(8,128)S(1)}, f32[4,64,128]{2,1,0:T(8,128)S(1)}, u32[]{:S(2)}, u32[]{:S(2)}) %collective-permute-start.7) | collective-permute-done | bytes 131104 | tf_op jit(solution)/shard_map/ppermute | solution.py:413
  68.0 8.2 %shard_map.98 = (f32[2,64,64,128]{3,2,1,0:T(8,128)}, f32[2,64,64,128]{3,2,1,0:T(8,128)}, f32[2,64,128]{2,1,0:T(8,128)}, f32[4,64,128]{2,1,0:T(8,128)}) custom-call(s32[134]{0:T(256)} %pad_add_fusion.pos_ref, f32[4,64,128]{2,1,0:T(8,128)} %bitcast.15, f32[2,64,64,128]{3,2,1,0:T(8,128)} %get-tuple-element.33.ba_ref.refs_1_, ...), custom_call_target="tpu_custom_call" | custom-call | tf_op jit(solution)/shard_map/pallas_call | solution.py:280
  76.3 1.5 collective-permute-done.10
  77.8 0.9 multiply_add_fusion.5
  78.8 1.1 collective-permute-start.11
  79.9 4.5 %collective-permute-done.11 = f32[4,64,128]{2,1,0:T(8,128)S(1)} collective-permute-done((f32[4,64,128]{2,1,0:T(8,128)S(1)}, f32[4,64,128]{2,1,0:T(8,128)S(1)}, u32[]{:S(2)}, u32[]{:S(2)}) %collective-permute-start.11) | collective-permute-done | bytes 131104 | tf_op jit(solution)/shard_map/ppermute | solution.py:413
  84.4 1.4 collective-permute-start.12
  85.9 6.2 %shard_map.97 = (f32[2,64,64,128]{3,2,1,0:T(8,128)}, f32[4,64,128]{2,1,0:T(8,128)}) custom-call(s32[134]{0:T(256)} %pad_add_fusion.pos_ref, f32[2,64,64,128]{3,2,1,0:T(8,128)} %get-tuple-element.33.ba_ref.refs_1_, f32[2,64,128]{2,1,0:T(8,128)} %copy.32.sign_ref.refs_2_.refs_3_, f32[2,64,128]{2,1,0:T(8,128)} %get-tuple-element.34.here_ref.refs_3_.refs_7_, ...), custom_call_target="tpu_custom_call" | custom-call | tf_op jit(solution)/shard_map/pallas_call | solution.py:280
  92.7 7.8 %shard_map.99 = (f32[2,64,64,128]{3,2,1,0:T(8,128)}, f32[4,64,128]{2,1,0:T(8,128)}) custom-call(s32[134]{0:T(256)} %pad_add_fusion.pos_ref, f32[4,64,128]{2,1,0:T(8,128)} %add_add_fusion.1.refs_0_, f32[2,64,64,128]{3,2,1,0:T(8,128)} %get-tuple-element.32.refs_1_, f32[2,64,64,128]{3,2,1,0:T(8,128)} %broadcast_in_dim.91.refs_1_.ew_ref.refs_2_.refs_5_.refs_6_, ...), custom_call_target="tpu_custom_call" | custom-call | tf_op jit(solution)/shard_map/pallas_call | solution.py:280
  100.9 5.5 %collective-permute-done.13 = f32[4,64,128]{2,1,0:T(8,128)S(1)} collective-permute-done((f32[4,64,128]{2,1,0:T(8,128)}, f32[4,64,128]{2,1,0:T(8,128)S(1)}, u32[]{:S(2)}, u32[]{:S(2)}) %collective-permute-start.13) | collective-permute-done | bytes 131104 | tf_op jit(solution)/shard_map/ppermute | solution.py:413
  106.3 0.9 add.91
  107.3 2.3 %collective-permute-start.14 = (f32[4,64,128]{2,1,0:T(8,128)S(1)}, f32[4,64,128]{2,1,0:T(8,128)S(1)}, u32[]{:S(2)}, u32[]{:S(2)}) collective-permute-start(f32[4,64,128]{2,1,0:T(8,128)S(1)} %add.91), channel_id=1, source_target_pairs={{0,16},{8,24},{16,0},{24,8},{1,17},{9,25},{17,1},{25,9},{2,18},{10... | collective-permute-start | bytes 393224 | tf_op jit(solution)/shard_map/ppermute | solution.py:413
  109.6 5.9 %collective-permute-done.14 = f32[4,64,128]{2,1,0:T(8,128)S(1)} collective-permute-done((f32[4,64,128]{2,1,0:T(8,128)S(1)}, f32[4,64,128]{2,1,0:T(8,128)S(1)}, u32[]{:S(2)}, u32[]{:S(2)}) %collective-permute-start.14) | collective-permute-done | bytes 131104 | tf_op jit(solution)/shard_map/ppermute | solution.py:413
  116.1 9.9 %shard_map.100 = (f32[2,64,64,128]{3,2,1,0:T(8,128)}, f32[2,64,64,128]{3,2,1,0:T(8,128)}, f32[2,64,128]{2,1,0:T(8,128)}, f32[4,64,128]{2,1,0:T(8,128)}) custom-call(s32[134]{0:T(256)} %pad_add_fusion.pos_ref, f32[4,64,128]{2,1,0:T(8,128)} %get-tuple-element.52.refs_0_, f32[2,64,64,128]{3,2,1,0:T(8,128)} %get-tuple-element.44.refs_1_, ...), custom_call_target="tpu_custom_call" | custom-call | tf_op jit(solution)/shard_map/pallas_call | solution.py:280
  126.2 1.5 collective-permute-done.15
  127.7 1.0 multiply_add_fusion.2
  129.1 0.9 collective-permute-start.8
  130.0 4.4 %collective-permute-done.16 = f32[4,64,128]{2,1,0:T(8,128)S(1)} collective-permute-done((f32[4,64,128]{2,1,0:T(8,128)S(1)}, f32[4,64,128]{2,1,0:T(8,128)S(1)}, u32[]{:S(2)}, u32[]{:S(2)}) %collective-permute-start.16) | collective-permute-done | bytes 131104 | tf_op jit(solution)/shard_map/ppermute | solution.py:413
  134.5 1.2 collective-permute-start.17
  135.9 1.0 collective-permute-start.9
  136.8 2.7 %collective-permute-done.17 = f32[4,64,128]{2,1,0:T(8,128)S(1)} collective-permute-done((f32[4,64,128]{2,1,0:T(8,128)S(1)}, f32[4,64,128]{2,1,0:T(8,128)S(1)}, u32[]{:S(2)}, u32[]{:S(2)}) %collective-permute-start.17) | collective-permute-done | bytes 131104 | tf_op jit(solution)/shard_map/ppermute | solution.py:413
  139.5 0.9 multiply_add_fusion.refs_3_
  140.4 5.8 %shard_map.101 = f32[4,64,128]{2,1,0:T(8,128)} custom-call(s32[134]{0:T(256)} %pad_add_fusion.pos_ref, f32[4,64,128]{2,1,0:T(8,128)} %add.79.refs_0_, f32[2,64,64,128]{3,2,1,0:T(8,128)} %broadcast_in_dim.91.refs_1_.ew_ref.refs_2_.refs_5_.refs_6_, f32[2,64,64,128]{3,2,1,0:T(8,128)} %get-tuple-element.47.refs_2_, f32[4,64,128]{2,1,0:T(8,128)} %multiply_add_fusion.refs_3_, ...), custom_call_target="tpu_custom_call" | custom-call | tf_op jit(solution)/shard_map/pallas_call | solution.py:280
  146.2 1.0 reduce_sum.52
  148.1 3.3 %reduce_sum.48 = f32[2,64,64]{2,1,0:T(8,128)S(1)} reduce(f32[2,64,64,128]{3,2,1,0:T(8,128)} %get-tuple-element.46, f32[]{:T(128)} %constant.7.clone.1), dimensions={3}, to_apply=%region_3.4 | reduce | flops 1040384 | bytes 4227076 | tf_op jit(solution)/shard_map/reduce_sum | solution.py:553
  151.5 3.2 %collective-permute-start.19 = (f32[2,128]{1,0:T(2,128)S(1)}, f32[2,128]{1,0:T(2,128)S(1)}, u32[]{:S(2)}, u32[]{:S(2)}) collective-permute-start(f32[2,128]{1,0:T(2,128)S(1)} %add.99), channel_id=1, source_target_pairs={{0,16},{8,24},{16,0},{24,8},{1,17},{9,25},{17,1},{25,9},{2,18},{10... | collective-permute-start | bytes 3080 | tf_op jit(solution)/shard_map/ppermute | solution.py:413
  (70 shorter events, 13.8 us)
Async XLA Ops:
  7.8 9.2 %copy-start.3 = (s32[256,128]{1,0:T(8,128)S(1)}, s32[256,128]{1,0:T(8,128)}, u32[]{:S(2)}) copy-start(s32[256,128]{1,0:T(8,128)} %param.11) | copy-start | bytes 393220
  7.8 12.7 %copy-start.4 = (s32[1,1,2,2]{3,2,1,0:T(2,128)S(1)}, s32[1,1,2,2]{3,2,1,0:T(2,128)}, u32[]{:S(2)}) copy-start(s32[1,1,2,2]{3,2,1,0:T(2,128)} %param.8) | copy-start | bytes 52
  16.6 1.3 collective-permute-start
  17.8 4.2 %collective-permute-start.1 = (f32[2,128]{1,0:T(2,128)S(1)}, f32[2,128]{1,0:T(2,128)S(1)}, u32[]{:S(2)}, u32[]{:S(2)}) collective-permute-start(f32[2,128]{1,0:T(2,128)S(1)} %mul.88), channel_id=1, source_target_pairs={{0,2},{1,3},{2,0},{3,1},{4,6},{5,7},{6,4},{7,5},{8,10},{9,11},{10,... | collective-permute-start | bytes 3080 | tf_op jit(solution)/shard_map/ppermute | solution.py:413
  22.1 3.6 %collective-permute-start.2 = (f32[2,128]{1,0:T(2,128)S(1)}, f32[2,128]{1,0:T(2,128)S(1)}, u32[]{:S(2)}, u32[]{:S(2)}) collective-permute-start(f32[2,128]{1,0:T(2,128)S(1)} %mul.90), channel_id=1, source_target_pairs={{0,4},{1,5},{2,6},{3,7},{4,0},{5,1},{6,2},{7,3},{8,12},{9,13},{10,... | collective-permute-start | bytes 3080 | tf_op jit(solution)/shard_map/ppermute | solution.py:413
  32.7 5.2 %collective-permute-start.3 = (f32[4,64,128]{2,1,0:T(8,128)}, f32[4,64,128]{2,1,0:T(8,128)S(1)}, u32[]{:S(2)}, u32[]{:S(2)}) collective-permute-start(f32[4,64,128]{2,1,0:T(8,128)} %get-tuple-element.31), channel_id=1, source_target_pairs={{0,8},{8,0},{16,24},{24,16},{1,9},{9,1},{17,25},{25,17},{2,10},{10... | collective-permute-start | bytes 393224 | tf_op jit(solution)/shard_map/ppermute | solution.py:413
  38.8 8.6 %collective-permute-start.4 = (f32[4,64,128]{2,1,0:T(8,128)S(1)}, f32[4,64,128]{2,1,0:T(8,128)S(1)}, u32[]{:S(2)}, u32[]{:S(2)}) collective-permute-start(f32[4,64,128]{2,1,0:T(8,128)S(1)} %add.80), channel_id=1, source_target_pairs={{0,16},{8,24},{16,0},{24,8},{1,17},{9,25},{17,1},{25,9},{2,18},{10... | collective-permute-start | bytes 393224 | tf_op jit(solution)/shard_map/ppermute | solution.py:413
  54.1 1.6 %collective-permute-start.5 = (f32[4,64,128]{2,1,0:T(8,128)}, f32[4,64,128]{2,1,0:T(8,128)S(1)}, u32[]{:S(2)}, u32[]{:S(2)}) collective-permute-start(f32[4,64,128]{2,1,0:T(8,128)} %get-tuple-element.35), channel_id=1, source_target_pairs={{0,1},{1,0},{2,3},{3,2},{4,5},{5,4},{6,7},{7,6},{8,9},{9,8},{10,11... | collective-permute-start | bytes 393224 | tf_op jit(solution)/shard_map/ppermute | solution.py:413
  56.6 5.6 %collective-permute-start.6 = (f32[4,64,128]{2,1,0:T(8,128)S(1)}, f32[4,64,128]{2,1,0:T(8,128)S(1)}, u32[]{:S(2)}, u32[]{:S(2)}) collective-permute-start(f32[4,64,128]{2,1,0:T(8,128)S(1)} %mul.92), channel_id=1, source_target_pairs={{0,2},{1,3},{2,0},{3,1},{4,6},{5,7},{6,4},{7,5},{8,10},{9,11},{10,... | collective-permute-start | bytes 393224 | tf_op jit(solution)/shard_map/ppermute | solution.py:413
  62.3 5.0 %collective-permute-start.7 = (f32[4,64,128]{2,1,0:T(8,128)S(1)}, f32[4,64,128]{2,1,0:T(8,128)S(1)}, u32[]{:S(2)}, u32[]{:S(2)}) collective-permute-start(f32[4,64,128]{2,1,0:T(8,128)S(1)} %mul.94), channel_id=1, source_target_pairs={{0,4},{1,5},{2,6},{3,7},{4,0},{5,1},{6,2},{7,3},{8,12},{9,13},{10,... | collective-permute-start | bytes 393224 | tf_op jit(solution)/shard_map/ppermute | solution.py:413
  68.0 9.9 %copy-start.1 = (f32[4,64,128]{2,1,0:T(8,128)S(1)}, f32[4,64,128]{2,1,0:T(8,128)}, u32[]{:S(2)}) copy-start(f32[4,64,128]{2,1,0:T(8,128)} %get-tuple-element.35) | copy-start | bytes 393220
  76.2 1.6 %collective-permute-start.10 = (f32[4,64,128]{2,1,0:T(8,128)}, f32[4,64,128]{2,1,0:T(8,128)S(1)}, u32[]{:S(2)}, u32[]{:S(2)}) collective-permute-start(f32[4,64,128]{2,1,0:T(8,128)} %get-tuple-element.40), channel_id=1, source_target_pairs={{0,1},{1,0},{2,3},{3,2},{4,5},{5,4},{6,7},{7,6},{8,9},{9,8},{10,11... | collective-permute-start | bytes 393224 | tf_op jit(solution)/shard_map/ppermute | solution.py:413
  78.8 5.6 %collective-permute-start.11 = (f32[4,64,128]{2,1,0:T(8,128)S(1)}, f32[4,64,128]{2,1,0:T(8,128)S(1)}, u32[]{:S(2)}, u32[]{:S(2)}) collective-permute-start(f32[4,64,128]{2,1,0:T(8,128)S(1)} %multiply_add_fusion.5), channel_id=1, source_target_pairs={{0,2},{1,3},{2,0},{3,1},{4,6},{5,7},{6,4},{7,5},{8,10},{9,11},{10,... | collective-permute-start | bytes 393224 | tf_op jit(solution)/shard_map/ppermute | solution.py:413
  84.4 7.6 %collective-permute-start.12 = (f32[4,64,128]{2,1,0:T(8,128)S(1)}, f32[4,64,128]{2,1,0:T(8,128)S(1)}, u32[]{:S(2)}, u32[]{:S(2)}) collective-permute-start(f32[4,64,128]{2,1,0:T(8,128)S(1)} %multiply_add_fusion.4), channel_id=1, source_target_pairs={{0,4},{1,5},{2,6},{3,7},{4,0},{5,1},{6,2},{7,3},{8,12},{9,13},{10,... | collective-permute-start | bytes 393224 | tf_op jit(solution)/shard_map/ppermute | solution.py:413
  100.6 5.8 %collective-permute-start.13 = (f32[4,64,128]{2,1,0:T(8,128)}, f32[4,64,128]{2,1,0:T(8,128)S(1)}, u32[]{:S(2)}, u32[]{:S(2)}) collective-permute-start(f32[4,64,128]{2,1,0:T(8,128)} %get-tuple-element.43), channel_id=1, source_target_pairs={{0,8},{8,0},{16,24},{24,16},{1,9},{9,1},{17,25},{25,17},{2,10},{10... | collective-permute-start | bytes 393224 | tf_op jit(solution)/shard_map/ppermute | solution.py:413
  107.3 8.2 %collective-permute-start.14 = (f32[4,64,128]{2,1,0:T(8,128)S(1)}, f32[4,64,128]{2,1,0:T(8,128)S(1)}, u32[]{:S(2)}, u32[]{:S(2)}) collective-permute-start(f32[4,64,128]{2,1,0:T(8,128)S(1)} %add.91), channel_id=1, source_target_pairs={{0,16},{8,24},{16,0},{24,8},{1,17},{9,25},{17,1},{25,9},{2,18},{10... | collective-permute-start | bytes 393224 | tf_op jit(solution)/shard_map/ppermute | solution.py:413
  116.1 12.7 %copy-start = (f32[256,128]{1,0:T(8,128)S(1)}, f32[256,128]{1,0:T(8,128)}, u32[]{:S(2)}) copy-start(f32[256,128]{1,0:T(8,128)} %param.13) | copy-start | bytes 393220
  116.1 13.0 %copy-start.2 = (f32[4,64,128]{2,1,0:T(8,128)S(1)}, f32[4,64,128]{2,1,0:T(8,128)}, u32[]{:S(2)}) copy-start(f32[4,64,128]{2,1,0:T(8,128)} %get-tuple-element.38) | copy-start | bytes 393220
  126.1 1.6 %collective-permute-start.15 = (f32[4,64,128]{2,1,0:T(8,128)}, f32[4,64,128]{2,1,0:T(8,128)S(1)}, u32[]{:S(2)}, u32[]{:S(2)}) collective-permute-start(f32[4,64,128]{2,1,0:T(8,128)} %get-tuple-element.48), channel_id=1, source_target_pairs={{0,1},{1,0},{2,3},{3,2},{4,5},{5,4},{6,7},{7,6},{8,9},{9,8},{10,11... | collective-permute-start | bytes 393224 | tf_op jit(solution)/shard_map/ppermute | solution.py:413
  128.7 5.6 %collective-permute-start.16 = (f32[4,64,128]{2,1,0:T(8,128)S(1)}, f32[4,64,128]{2,1,0:T(8,128)S(1)}, u32[]{:S(2)}, u32[]{:S(2)}) collective-permute-start(f32[4,64,128]{2,1,0:T(8,128)S(1)} %multiply_add_fusion.2), channel_id=1, source_target_pairs={{0,2},{1,3},{2,0},{3,1},{4,6},{5,7},{6,4},{7,5},{8,10},{9,11},{10,... | collective-permute-start | bytes 393224 | tf_op jit(solution)/shard_map/ppermute | solution.py:413
  129.1 6.7 %collective-permute-start.8 = (f32[4,64,128]{2,1,0:T(8,128)S(1)}, f32[4,64,128]{2,1,0:T(8,128)S(1)}, u32[]{:S(2)}, u32[]{:S(2)}) collective-permute-start(f32[4,64,128]{2,1,0:T(8,128)S(1)} %copy-done.2), channel_id=1, source_target_pairs={{0,8},{8,0},{16,24},{24,16},{1,9},{9,1},{17,25},{25,17},{2,10},{10... | collective-permute-start | bytes 393224 | tf_op jit(solution)/shard_map/ppermute | solution.py:413
  134.5 5.0 %collective-permute-start.17 = (f32[4,64,128]{2,1,0:T(8,128)S(1)}, f32[4,64,128]{2,1,0:T(8,128)S(1)}, u32[]{:S(2)}, u32[]{:S(2)}) collective-permute-start(f32[4,64,128]{2,1,0:T(8,128)S(1)} %multiply_add_fusion.1), channel_id=1, source_target_pairs={{0,4},{1,5},{2,6},{3,7},{4,0},{5,1},{6,2},{7,3},{8,12},{9,13},{10,... | collective-permute-start | bytes 393224 | tf_op jit(solution)/shard_map/ppermute | solution.py:413
  135.9 11.5 %collective-permute-start.9 = (f32[4,64,128]{2,1,0:T(8,128)S(1)}, f32[4,64,128]{2,1,0:T(8,128)S(1)}, u32[]{:S(2)}, u32[]{:S(2)}) collective-permute-start(f32[4,64,128]{2,1,0:T(8,128)S(1)} %add.83), channel_id=1, source_target_pairs={{0,16},{8,24},{16,0},{24,8},{1,17},{9,25},{17,1},{25,9},{2,18},{10... | collective-permute-start | bytes 393224 | tf_op jit(solution)/shard_map/ppermute | solution.py:413
  147.3 4.1 %collective-permute-start.18 = (f32[2,128]{1,0:T(2,128)S(1)}, f32[2,128]{1,0:T(2,128)S(1)}, u32[]{:S(2)}, u32[]{:S(2)}) collective-permute-start(f32[2,128]{1,0:T(2,128)S(1)} %reshape.64), channel_id=1, source_target_pairs={{0,8},{8,0},{16,24},{24,16},{1,9},{9,1},{17,25},{25,17},{2,10},{10... | collective-permute-start | bytes 3080 | tf_op jit(solution)/shard_map/ppermute | solution.py:413
  151.5 4.7 %collective-permute-start.19 = (f32[2,128]{1,0:T(2,128)S(1)}, f32[2,128]{1,0:T(2,128)S(1)}, u32[]{:S(2)}, u32[]{:S(2)}) collective-permute-start(f32[2,128]{1,0:T(2,128)S(1)} %add.99), channel_id=1, source_target_pairs={{0,16},{8,24},{16,0},{24,8},{1,17},{9,25},{17,1},{25,9},{2,18},{10... | collective-permute-start | bytes 3080 | tf_op jit(solution)/shard_map/ppermute | solution.py:413

commit v7 on v6

--- a/solution.py
+++ b/solution.py
@@ -159,6 +159,7 @@
     refs = refs[5:]
     acc_ref = refs.pop(0) if has_acc else None
     gw_ref, gba_ref, ghere_ref, gothers_ref = refs
+    lanes = lax.broadcasted_iota(jnp.int32, (ba_ref.shape[2], gw_ref.shape[2]), 1)
     k = pl.program_id(0)
     n_c = ba_ref.shape[1]
     shape = ba_ref.shape[2:]
@@ -174,7 +175,8 @@
     f = sign * here * others
     count, base = _columns(pos_ref, k, slots, n_c)
 
-    def body(i, total):
+    def body(i, carry):
+        total, table = carry
         c = pos_ref[base + i]
         gu = _spread_row(gsp_ref, c, shape)
         if has_next:
@@ -183,15 +185,18 @@
         x = ba * f
         low = 1.0 - DAMP * x
         high = 1.0 + DAMP * x
-        gw = gu * jnp.log(high / low)
-        if has_acc:
-            gw = gw + acc_ref[0, c]
-        gw_ref[0, c] = gw
+        part = jnp.sum(gu * jnp.log(high / low), axis=1, keepdims=True)
+        table = jnp.where(lanes == c, part, table)
         gx = gu * ew_ref[0, c] * ((2.0 * DAMP) / (low * high))
         gba_ref[0, c] = gx * f
-        return total + gx * ba
-
-    grad_factor = _loop(count, body, jnp.zeros(shape, F32))
+        return (total + gx * ba, table)
+
+    grad_factor, table = _loop(
+        count, body, (jnp.zeros(shape, F32), jnp.zeros((shape[0], gw_ref.shape[2]), F32))
+    )
+    if has_acc:
+        table = table + acc_ref[k]
+    gw_ref[k] = table
     ghere_ref[k] = grad_factor * sign * others
     gothers_ref[p] = gothers_ref[p] + grad_factor * sign * here
 
@@ -327,10 +332,10 @@
         [("column", gsp)]
         + ([("dense", gm)] if has_next else [])
         + [("dense", ba), ("full", sign), ("full", here), ("full", others), ("dense", ew)]
-        + ([("dense", acc)] if has_acc else [])
+        + ([("full", acc)] if has_acc else [])
     )
     outs = [
-        ("dense", jax.ShapeDtypeStruct(ba.shape, F32)),
+        ("full", jax.ShapeDtypeStruct((k, r, 128), F32)),
         ("dense", jax.ShapeDtypeStruct(ba.shape, F32)),
         ("full", jax.ShapeDtypeStruct(here.shape, F32)),
         ("full", jax.ShapeDtypeStruct(others.shape, F32)),
@@ -550,7 +555,7 @@
     else:
         shot_sums = checks_total(shot_sums, n_chk)
     prior_grad = prior_grad + shot_sums
-    weight_grad = jnp.where(edge > 0, jnp.swapaxes(jnp.sum(acc, axis=3), 1, 2), 0.0)
+    weight_grad = jnp.where(edge > 0, acc[:, :, :TILE], 0.0)
     return (
         marginals,
         weight_grad.reshape(1, 1, slot_total, TILE * TILE),

time: 158 us -> 160 us (1.013)
  starting transfers between devices: 25.6 us -> 35.3 us
  waiting for transfers between devices: 46.6 us -> 41.8 us
  other arithmetic: 16.5 us -> 13 us
    ppermute x20, starting transfers between devices: 25.6 us -> 35.3 us  [_swap(): return lax.ppermute(value, axis, perm)]
    ppermute x20, waiting for transfers between devices: 46.6 us -> 41.8 us  [_swap(): return lax.ppermute(value, axis, perm)]
    reduce_sum x1 -> x0, other arithmetic: 3.34 us -> none  [body(): jnp.sum(acc, axis=3)]
  transfers between devices with their start and end apart: 20 -> 20, of which waited for: 16 -> 18; matrix products, arithmetic and copies ran while one was open for 6% -> 3% of each run, Pallas kernels for 8% -> 7%
where the time goes in v7:
time: 160 us; the launch traced here: 158 us
  Pallas kernels  55.3 us (35%)
  waiting for transfers between devices  41.8 us (26%)
  starting transfers between devices  35.3 us (22%)
  other arithmetic  13 us (8%)
  local copies, waits for them, and re-layouts  10.9 us (7%)
    pallas_call x8, Pallas kernels, _call(): pl.pallas_call(kernel, grid_spec=grid_spec, out_shape=[o for kind, o in o...  55.3 us
    ppermute x20, waiting for transfers between devices, _swap(): return lax.ppermute(value, axis, perm)  41.8 us
    ppermute x20, starting transfers between devices, _swap(): return lax.ppermute(value, axis, perm)  35.3 us
  transfers between devices with their start and end apart: 20, of which 18 were waited for; matrix products, arithmetic and copies ran while one was open for 3% of the time, Pallas kernels for 7%

profile of v7, /device:TPU:0, one launch (start us, length us, event | category | flops | bytes accessed | tf_op | source)
XLA Modules:
  0.0 158.1 jit_solution(17677749977927794765)
XLA Ops:
  0.6 0.9 squeeze.10
  2.5 1.0 sort.17
  5.2 0.9 reshape_squeeze.10
  7.6 2.6 %broadcast_in_dim.91.refs_1_.ew_ref.refs_2_.refs_5_.refs_6_ = f32[2,64,64,128]{3,2,1,0:T(8,128)} broadcast(f32[2,64,64]{2,1,0:T(8,128)S(1)} %copy.25), dimensions={0,1,2} | broadcast | bytes 4227072 | tf_op jit(solution)/shard_map/broadcast_in_dim | solution.py:513
  10.2 5.1 %shard_map.94 = (f32[2,64,64,128]{3,2,1,0:T(8,128)}, f32[2,64,128]{2,1,0:T(8,128)}, f32[4,64,128]{2,1,0:T(8,128)}, f32[2,64,128]{2,1,0:T(8,128)}) custom-call(s32[134]{0:T(256)} %pad_add_fusion.pos_ref, f32[4,64,128]{2,1,0:T(8,128)} %add.79.refs_0_, f32[2,64,64,128]{3,2,1,0:T(8,128)} %broadcast_in_dim.91.refs_1_.ew_ref.refs_2_.refs_5_.refs_6_), custom_call_target="tpu_custom_call" | custom-call | tf_op jit(solution)/shard_map/pallas_call | solution.py:285
  15.3 1.0 slice_reduce_fusion
  16.7 0.8 collective-permute-done
  17.5 2.8 %collective-permute-start.1 = (f32[2,128]{1,0:T(2,128)S(1)}, f32[2,128]{1,0:T(2,128)S(1)}, u32[]{:S(2)}, u32[]{:S(2)}) collective-permute-start(f32[2,128]{1,0:T(2,128)S(1)} %mul.88), channel_id=1, source_target_pairs={{0,2},{1,3},{2,0},{3,1},{4,6},{5,7},{6,4},{7,5},{8,10},{9,11},{10,... | collective-permute-start | bytes 3080 | tf_op jit(solution)/shard_map/ppermute | solution.py:418
  20.5 1.4 collective-permute-done.1
  21.9 2.1 %collective-permute-start.2 = (f32[2,128]{1,0:T(2,128)S(1)}, f32[2,128]{1,0:T(2,128)S(1)}, u32[]{:S(2)}, u32[]{:S(2)}) collective-permute-start(f32[2,128]{1,0:T(2,128)S(1)} %mul.90), channel_id=1, source_target_pairs={{0,4},{1,5},{2,6},{3,7},{4,0},{5,1},{6,2},{7,3},{8,12},{9,13},{10,... | collective-permute-start | bytes 3080 | tf_op jit(solution)/shard_map/ppermute | solution.py:418
  26.4 6.0 %shard_map.95 = (f32[2,64,64,128]{3,2,1,0:T(8,128)}, f32[4,64,128]{2,1,0:T(8,128)}) custom-call(s32[134]{0:T(256)} %pad_add_fusion.pos_ref, f32[2,64,64,128]{3,2,1,0:T(8,128)} %get-tuple-element.28.ba_ref.refs_2_, f32[2,64,128]{2,1,0:T(8,128)} %copy.27.sign_ref.refs_2_.refs_3_, f32[2,64,128]{2,1,0:T(8,128)} %get-tuple-element.29.here_ref.refs_4_.refs_6_, ...), custom_call_target="tpu_custom_call" | custom-call | tf_op jit(solution)/shard_map/pallas_call | solution.py:285
  32.4 2.0 %collective-permute-start.3 = (f32[4,64,128]{2,1,0:T(8,128)}, f32[4,64,128]{2,1,0:T(8,128)S(1)}, u32[]{:S(2)}, u32[]{:S(2)}) collective-permute-start(f32[4,64,128]{2,1,0:T(8,128)} %get-tuple-element.31), channel_id=1, source_target_pairs={{0,8},{8,0},{16,24},{24,16},{1,9},{9,1},{17,25},{25,17},{2,10},{10... | collective-permute-start | bytes 393224 | tf_op jit(solution)/shard_map/ppermute | solution.py:418
  34.4 3.2 %collective-permute-done.3 = f32[4,64,128]{2,1,0:T(8,128)S(1)} collective-permute-done((f32[4,64,128]{2,1,0:T(8,128)}, f32[4,64,128]{2,1,0:T(8,128)S(1)}, u32[]{:S(2)}, u32[]{:S(2)}) %collective-permute-start.3) | collective-permute-done | bytes 131104 | tf_op jit(solution)/shard_map/ppermute | solution.py:418
  37.6 0.9 add.80
  38.6 3.1 %collective-permute-start.4 = (f32[4,64,128]{2,1,0:T(8,128)S(1)}, f32[4,64,128]{2,1,0:T(8,128)S(1)}, u32[]{:S(2)}, u32[]{:S(2)}) collective-permute-start(f32[4,64,128]{2,1,0:T(8,128)S(1)} %add.80), channel_id=1, source_target_pairs={{0,16},{8,24},{16,0},{24,8},{1,17},{9,25},{17,1},{25,9},{2,18},{10... | collective-permute-start | bytes 393224 | tf_op jit(solution)/shard_map/ppermute | solution.py:418
  41.7 4.4 %collective-permute-done.4 = f32[4,64,128]{2,1,0:T(8,128)S(1)} collective-permute-done((f32[4,64,128]{2,1,0:T(8,128)S(1)}, f32[4,64,128]{2,1,0:T(8,128)S(1)}, u32[]{:S(2)}, u32[]{:S(2)}) %collective-permute-start.4) | collective-permute-done | bytes 131104 | tf_op jit(solution)/shard_map/ppermute | solution.py:418
  46.8 5.9 %shard_map.96 = (f32[2,64,64,128]{3,2,1,0:T(8,128)}, f32[2,64,128]{2,1,0:T(8,128)}, f32[4,64,128]{2,1,0:T(8,128)}, f32[2,64,128]{2,1,0:T(8,128)}) custom-call(s32[134]{0:T(256)} %pad_add_fusion.pos_ref, f32[4,64,128]{2,1,0:T(8,128)} %add_add_fusion.1.refs_0_, f32[2,64,64,128]{3,2,1,0:T(8,128)} %get-tuple-element.32.refs_1_, ...), custom_call_target="tpu_custom_call" | custom-call | tf_op jit(solution)/shard_map/pallas_call | solution.py:285
  52.7 1.5 collective-permute-done.5
  54.2 0.9 mul.92
  55.2 1.5 collective-permute-start.6
  56.7 4.1 %collective-permute-done.6 = f32[4,64,128]{2,1,0:T(8,128)S(1)} collective-permute-done((f32[4,64,128]{2,1,0:T(8,128)S(1)}, f32[4,64,128]{2,1,0:T(8,128)S(1)}, u32[]{:S(2)}, u32[]{:S(2)}) %collective-permute-start.6) | collective-permute-done | bytes 131104 | tf_op jit(solution)/shard_map/ppermute | solution.py:418
  60.8 2.1 %collective-permute-start.7 = (f32[4,64,128]{2,1,0:T(8,128)S(1)}, f32[4,64,128]{2,1,0:T(8,128)S(1)}, u32[]{:S(2)}, u32[]{:S(2)}) collective-permute-start(f32[4,64,128]{2,1,0:T(8,128)S(1)} %mul.94), channel_id=1, source_target_pairs={{0,4},{1,5},{2,6},{3,7},{4,0},{5,1},{6,2},{7,3},{8,12},{9,13},{10,... | collective-permute-start | bytes 393224 | tf_op jit(solution)/shard_map/ppermute | solution.py:418
  62.9 3.3 %collective-permute-done.7 = f32[4,64,128]{2,1,0:T(8,128)S(1)} collective-permute-done((f32[4,64,128]{2,1,0:T(8,128)S(1)}, f32[4,64,128]{2,1,0:T(8,128)S(1)}, u32[]{:S(2)}, u32[]{:S(2)}) %collective-permute-start.7) | collective-permute-done | bytes 131104 | tf_op jit(solution)/shard_map/ppermute | solution.py:418
  66.9 9.1 %shard_map.98 = (f32[2,64,128]{2,1,0:T(8,128)}, f32[2,64,64,128]{3,2,1,0:T(8,128)}, f32[2,64,128]{2,1,0:T(8,128)}, f32[4,64,128]{2,1,0:T(8,128)}) custom-call(s32[134]{0:T(256)} %pad_add_fusion.pos_ref, f32[4,64,128]{2,1,0:T(8,128)} %bitcast.13, f32[2,64,64,128]{3,2,1,0:T(8,128)} %get-tuple-element.33.ba_ref.refs_1_, ...), custom_call_target="tpu_custom_call" | custom-call | tf_op jit(solution)/shard_map/pallas_call | solution.py:285
  76.0 1.6 collective-permute-done.10
  77.5 0.9 multiply_add_fusion.5
  78.5 1.3 collective-permute-start.11
  79.7 4.3 %collective-permute-done.11 = f32[4,64,128]{2,1,0:T(8,128)S(1)} collective-permute-done((f32[4,64,128]{2,1,0:T(8,128)S(1)}, f32[4,64,128]{2,1,0:T(8,128)S(1)}, u32[]{:S(2)}, u32[]{:S(2)}) %collective-permute-start.11) | collective-permute-done | bytes 131104 | tf_op jit(solution)/shard_map/ppermute | solution.py:418
  84.1 2.3 %collective-permute-start.12 = (f32[4,64,128]{2,1,0:T(8,128)S(1)}, f32[4,64,128]{2,1,0:T(8,128)S(1)}, u32[]{:S(2)}, u32[]{:S(2)}) collective-permute-start(f32[4,64,128]{2,1,0:T(8,128)S(1)} %multiply_add_fusion.4), channel_id=1, source_target_pairs={{0,4},{1,5},{2,6},{3,7},{4,0},{5,1},{6,2},{7,3},{8,12},{9,13},{10,... | collective-permute-start | bytes 393224 | tf_op jit(solution)/shard_map/ppermute | solution.py:418
  86.4 6.1 %shard_map.97 = (f32[2,64,64,128]{3,2,1,0:T(8,128)}, f32[4,64,128]{2,1,0:T(8,128)}) custom-call(s32[134]{0:T(256)} %pad_add_fusion.pos_ref, f32[2,64,64,128]{3,2,1,0:T(8,128)} %get-tuple-element.33.ba_ref.refs_1_, f32[2,64,128]{2,1,0:T(8,128)} %copy.27.sign_ref.refs_2_.refs_3_, f32[2,64,128]{2,1,0:T(8,128)} %get-tuple-element.34.here_ref.refs_3_.refs_7_, ...), custom_call_target="tpu_custom_call" | custom-call | tf_op jit(solution)/shard_map/pallas_call | solution.py:285
  93.1 7.6 %shard_map.99 = (f32[2,64,64,128]{3,2,1,0:T(8,128)}, f32[4,64,128]{2,1,0:T(8,128)}) custom-call(s32[134]{0:T(256)} %pad_add_fusion.pos_ref, f32[4,64,128]{2,1,0:T(8,128)} %add_add_fusion.1.refs_0_, f32[2,64,64,128]{3,2,1,0:T(8,128)} %get-tuple-element.32.refs_1_, f32[2,64,64,128]{3,2,1,0:T(8,128)} %broadcast_in_dim.91.refs_1_.ew_ref.refs_2_.refs_5_.refs_6_, ...), custom_call_target="tpu_custom_call" | custom-call | tf_op jit(solution)/shard_map/pallas_call | solution.py:285
  100.8 2.6 %collective-permute-start.13 = (f32[4,64,128]{2,1,0:T(8,128)}, f32[4,64,128]{2,1,0:T(8,128)S(1)}, u32[]{:S(2)}, u32[]{:S(2)}) collective-permute-start(f32[4,64,128]{2,1,0:T(8,128)} %get-tuple-element.43), channel_id=1, source_target_pairs={{0,8},{8,0},{16,24},{24,16},{1,9},{9,1},{17,25},{25,17},{2,10},{10... | collective-permute-start | bytes 393224 | tf_op jit(solution)/shard_map/ppermute | solution.py:418
  103.3 3.6 %collective-permute-done.13 = f32[4,64,128]{2,1,0:T(8,128)S(1)} collective-permute-done((f32[4,64,128]{2,1,0:T(8,128)}, f32[4,64,128]{2,1,0:T(8,128)S(1)}, u32[]{:S(2)}, u32[]{:S(2)}) %collective-permute-start.13) | collective-permute-done | bytes 131104 | tf_op jit(solution)/shard_map/ppermute | solution.py:418
  107.0 0.9 add.91
  107.9 3.7 %collective-permute-start.14 = (f32[4,64,128]{2,1,0:T(8,128)S(1)}, f32[4,64,128]{2,1,0:T(8,128)S(1)}, u32[]{:S(2)}, u32[]{:S(2)}) collective-permute-start(f32[4,64,128]{2,1,0:T(8,128)S(1)} %add.91), channel_id=1, source_target_pairs={{0,16},{8,24},{16,0},{24,8},{1,17},{9,25},{17,1},{25,9},{2,18},{10... | collective-permute-start | bytes 393224 | tf_op jit(solution)/shard_map/ppermute | solution.py:418
  111.6 5.4 %collective-permute-done.14 = f32[4,64,128]{2,1,0:T(8,128)S(1)} collective-permute-done((f32[4,64,128]{2,1,0:T(8,128)S(1)}, f32[4,64,128]{2,1,0:T(8,128)S(1)}, u32[]{:S(2)}, u32[]{:S(2)}) %collective-permute-start.14) | collective-permute-done | bytes 131104 | tf_op jit(solution)/shard_map/ppermute | solution.py:418
  117.6 9.8 %shard_map.100 = (f32[2,64,128]{2,1,0:T(8,128)}, f32[2,64,64,128]{3,2,1,0:T(8,128)}, f32[2,64,128]{2,1,0:T(8,128)}, f32[4,64,128]{2,1,0:T(8,128)}) custom-call(s32[134]{0:T(256)} %pad_add_fusion.pos_ref, f32[4,64,128]{2,1,0:T(8,128)} %get-tuple-element.52.refs_0_, f32[2,64,64,128]{3,2,1,0:T(8,128)} %get-tuple-element.44.refs_1_, ...), custom_call_target="tpu_custom_call" | custom-call | tf_op jit(solution)/shard_map/pallas_call | solution.py:285
  127.6 1.5 collective-permute-done.15
  129.1 1.0 multiply_add_fusion.2
  130.9 0.9 collective-permute-start.8
  131.8 3.9 %collective-permute-done.16 = f32[4,64,128]{2,1,0:T(8,128)S(1)} collective-permute-done((f32[4,64,128]{2,1,0:T(8,128)S(1)}, f32[4,64,128]{2,1,0:T(8,128)S(1)}, u32[]{:S(2)}, u32[]{:S(2)}) %collective-permute-start.16) | collective-permute-done | bytes 131104 | tf_op jit(solution)/shard_map/ppermute | solution.py:418
  136.2 4.1 %collective-permute-start.9 = (f32[4,64,128]{2,1,0:T(8,128)S(1)}, f32[4,64,128]{2,1,0:T(8,128)S(1)}, u32[]{:S(2)}, u32[]{:S(2)}) collective-permute-start(f32[4,64,128]{2,1,0:T(8,128)S(1)} %add.83), channel_id=1, source_target_pairs={{0,16},{8,24},{16,0},{24,8},{1,17},{9,25},{17,1},{25,9},{2,18},{10... | collective-permute-start | bytes 393224 | tf_op jit(solution)/shard_map/ppermute | solution.py:418
  140.9 0.9 multiply_add_fusion.refs_3_
  141.8 5.8 %shard_map.101 = f32[4,64,128]{2,1,0:T(8,128)} custom-call(s32[134]{0:T(256)} %pad_add_fusion.pos_ref, f32[4,64,128]{2,1,0:T(8,128)} %add.79.refs_0_, f32[2,64,64,128]{3,2,1,0:T(8,128)} %broadcast_in_dim.91.refs_1_.ew_ref.refs_2_.refs_5_.refs_6_, f32[2,64,64,128]{3,2,1,0:T(8,128)} %get-tuple-element.47.refs_2_, f32[4,64,128]{2,1,0:T(8,128)} %multiply_add_fusion.refs_3_, ...), custom_call_target="tpu_custom_call" | custom-call | tf_op jit(solution)/shard_map/pallas_call | solution.py:285
  147.6 1.0 reduce_sum.42
  148.7 2.8 %collective-permute-start.18 = (f32[2,128]{1,0:T(2,128)S(1)}, f32[2,128]{1,0:T(2,128)S(1)}, u32[]{:S(2)}, u32[]{:S(2)}) collective-permute-start(f32[2,128]{1,0:T(2,128)S(1)} %reshape.64), channel_id=1, source_target_pairs={{0,8},{8,0},{16,24},{24,16},{1,9},{9,1},{17,25},{25,17},{2,10},{10... | collective-permute-start | bytes 3080 | tf_op jit(solution)/shard_map/ppermute | solution.py:418
  152.2 0.8 collective-permute-done.18
  153.0 3.0 %collective-permute-start.19 = (f32[2,128]{1,0:T(2,128)S(1)}, f32[2,128]{1,0:T(2,128)S(1)}, u32[]{:S(2)}, u32[]{:S(2)}) collective-permute-start(f32[2,128]{1,0:T(2,128)S(1)} %add.99), channel_id=1, source_target_pairs={{0,16},{8,24},{16,0},{24,8},{1,17},{9,25},{17,1},{25,9},{2,18},{10... | collective-permute-start | bytes 3080 | tf_op jit(solution)/shard_map/ppermute | solution.py:418
  (69 shorter events, 14.3 us)
Async XLA Ops:
  7.6 9.0 %copy-start.3 = (s32[256,128]{1,0:T(8,128)S(1)}, s32[256,128]{1,0:T(8,128)}, u32[]{:S(2)}) copy-start(s32[256,128]{1,0:T(8,128)} %param.11) | copy-start | bytes 393220
  7.6 12.7 %copy-start.5 = (s32[1,1,2,2]{3,2,1,0:T(2,128)S(1)}, s32[1,1,2,2]{3,2,1,0:T(2,128)}, u32[]{:S(2)}) copy-start(s32[1,1,2,2]{3,2,1,0:T(2,128)} %param.8) | copy-start | bytes 52
  16.4 1.1 collective-permute-start
  17.5 4.4 %collective-permute-start.1 = (f32[2,128]{1,0:T(2,128)S(1)}, f32[2,128]{1,0:T(2,128)S(1)}, u32[]{:S(2)}, u32[]{:S(2)}) collective-permute-start(f32[2,128]{1,0:T(2,128)S(1)} %mul.88), channel_id=1, source_target_pairs={{0,2},{1,3},{2,0},{3,1},{4,6},{5,7},{6,4},{7,5},{8,10},{9,11},{10,... | collective-permute-start | bytes 3080 | tf_op jit(solution)/shard_map/ppermute | solution.py:418
  21.9 3.7 %collective-permute-start.2 = (f32[2,128]{1,0:T(2,128)S(1)}, f32[2,128]{1,0:T(2,128)S(1)}, u32[]{:S(2)}, u32[]{:S(2)}) collective-permute-start(f32[2,128]{1,0:T(2,128)S(1)} %mul.90), channel_id=1, source_target_pairs={{0,4},{1,5},{2,6},{3,7},{4,0},{5,1},{6,2},{7,3},{8,12},{9,13},{10,... | collective-permute-start | bytes 3080 | tf_op jit(solution)/shard_map/ppermute | solution.py:418
  32.4 5.2 %collective-permute-start.3 = (f32[4,64,128]{2,1,0:T(8,128)}, f32[4,64,128]{2,1,0:T(8,128)S(1)}, u32[]{:S(2)}, u32[]{:S(2)}) collective-permute-start(f32[4,64,128]{2,1,0:T(8,128)} %get-tuple-element.31), channel_id=1, source_target_pairs={{0,8},{8,0},{16,24},{24,16},{1,9},{9,1},{17,25},{25,17},{2,10},{10... | collective-permute-start | bytes 393224 | tf_op jit(solution)/shard_map/ppermute | solution.py:418
  38.6 7.5 %collective-permute-start.4 = (f32[4,64,128]{2,1,0:T(8,128)S(1)}, f32[4,64,128]{2,1,0:T(8,128)S(1)}, u32[]{:S(2)}, u32[]{:S(2)}) collective-permute-start(f32[4,64,128]{2,1,0:T(8,128)S(1)} %add.80), channel_id=1, source_target_pairs={{0,16},{8,24},{16,0},{24,8},{1,17},{9,25},{17,1},{25,9},{2,18},{10... | collective-permute-start | bytes 393224 | tf_op jit(solution)/shard_map/ppermute | solution.py:418
  52.7 1.6 %collective-permute-start.5 = (f32[4,64,128]{2,1,0:T(8,128)}, f32[4,64,128]{2,1,0:T(8,128)S(1)}, u32[]{:S(2)}, u32[]{:S(2)}) collective-permute-start(f32[4,64,128]{2,1,0:T(8,128)} %get-tuple-element.35), channel_id=1, source_target_pairs={{0,1},{1,0},{2,3},{3,2},{4,5},{5,4},{6,7},{7,6},{8,9},{9,8},{10,11... | collective-permute-start | bytes 393224 | tf_op jit(solution)/shard_map/ppermute | solution.py:418
  55.2 5.6 %collective-permute-start.6 = (f32[4,64,128]{2,1,0:T(8,128)S(1)}, f32[4,64,128]{2,1,0:T(8,128)S(1)}, u32[]{:S(2)}, u32[]{:S(2)}) collective-permute-start(f32[4,64,128]{2,1,0:T(8,128)S(1)} %mul.92), channel_id=1, source_target_pairs={{0,2},{1,3},{2,0},{3,1},{4,6},{5,7},{6,4},{7,5},{8,10},{9,11},{10,... | collective-permute-start | bytes 393224 | tf_op jit(solution)/shard_map/ppermute | solution.py:418
  60.8 5.4 %collective-permute-start.7 = (f32[4,64,128]{2,1,0:T(8,128)S(1)}, f32[4,64,128]{2,1,0:T(8,128)S(1)}, u32[]{:S(2)}, u32[]{:S(2)}) collective-permute-start(f32[4,64,128]{2,1,0:T(8,128)S(1)} %mul.94), channel_id=1, source_target_pairs={{0,4},{1,5},{2,6},{3,7},{4,0},{5,1},{6,2},{7,3},{8,12},{9,13},{10,... | collective-permute-start | bytes 393224 | tf_op jit(solution)/shard_map/ppermute | solution.py:418
  66.9 10.6 %copy-start.1 = (f32[4,64,128]{2,1,0:T(8,128)S(1)}, f32[4,64,128]{2,1,0:T(8,128)}, u32[]{:S(2)}) copy-start(f32[4,64,128]{2,1,0:T(8,128)} %get-tuple-element.35) | copy-start | bytes 393220
  76.0 1.6 collective-permute-start.10
  78.5 5.6 %collective-permute-start.11 = (f32[4,64,128]{2,1,0:T(8,128)S(1)}, f32[4,64,128]{2,1,0:T(8,128)S(1)}, u32[]{:S(2)}, u32[]{:S(2)}) collective-permute-start(f32[4,64,128]{2,1,0:T(8,128)S(1)} %multiply_add_fusion.5), channel_id=1, source_target_pairs={{0,2},{1,3},{2,0},{3,1},{4,6},{5,7},{6,4},{7,5},{8,10},{9,11},{10,... | collective-permute-start | bytes 393224 | tf_op jit(solution)/shard_map/ppermute | solution.py:418
  84.1 8.3 %collective-permute-start.12 = (f32[4,64,128]{2,1,0:T(8,128)S(1)}, f32[4,64,128]{2,1,0:T(8,128)S(1)}, u32[]{:S(2)}, u32[]{:S(2)}) collective-permute-start(f32[4,64,128]{2,1,0:T(8,128)S(1)} %multiply_add_fusion.4), channel_id=1, source_target_pairs={{0,4},{1,5},{2,6},{3,7},{4,0},{5,1},{6,2},{7,3},{8,12},{9,13},{10,... | collective-permute-start | bytes 393224 | tf_op jit(solution)/shard_map/ppermute | solution.py:418
  100.8 6.2 %collective-permute-start.13 = (f32[4,64,128]{2,1,0:T(8,128)}, f32[4,64,128]{2,1,0:T(8,128)S(1)}, u32[]{:S(2)}, u32[]{:S(2)}) collective-permute-start(f32[4,64,128]{2,1,0:T(8,128)} %get-tuple-element.43), channel_id=1, source_target_pairs={{0,8},{8,0},{16,24},{24,16},{1,9},{9,1},{17,25},{25,17},{2,10},{10... | collective-permute-start | bytes 393224 | tf_op jit(solution)/shard_map/ppermute | solution.py:418
  107.9 9.1 %collective-permute-start.14 = (f32[4,64,128]{2,1,0:T(8,128)S(1)}, f32[4,64,128]{2,1,0:T(8,128)S(1)}, u32[]{:S(2)}, u32[]{:S(2)}) collective-permute-start(f32[4,64,128]{2,1,0:T(8,128)S(1)} %add.91), channel_id=1, source_target_pairs={{0,16},{8,24},{16,0},{24,8},{1,17},{9,25},{17,1},{25,9},{2,18},{10... | collective-permute-start | bytes 393224 | tf_op jit(solution)/shard_map/ppermute | solution.py:418
  117.6 13.0 %copy-start = (f32[256,128]{1,0:T(8,128)S(1)}, f32[256,128]{1,0:T(8,128)}, u32[]{:S(2)}) copy-start(f32[256,128]{1,0:T(8,128)} %param.13) | copy-start | bytes 393220
  117.6 13.3 %copy-start.2 = (f32[4,64,128]{2,1,0:T(8,128)S(1)}, f32[4,64,128]{2,1,0:T(8,128)}, u32[]{:S(2)}) copy-start(f32[4,64,128]{2,1,0:T(8,128)} %get-tuple-element.38) | copy-start | bytes 393220
  127.4 1.6 %collective-permute-start.15 = (f32[4,64,128]{2,1,0:T(8,128)}, f32[4,64,128]{2,1,0:T(8,128)S(1)}, u32[]{:S(2)}, u32[]{:S(2)}) collective-permute-start(f32[4,64,128]{2,1,0:T(8,128)} %get-tuple-element.48), channel_id=1, source_target_pairs={{0,1},{1,0},{2,3},{3,2},{4,5},{5,4},{6,7},{7,6},{8,9},{9,8},{10,11... | collective-permute-start | bytes 393224 | tf_op jit(solution)/shard_map/ppermute | solution.py:418
  130.1 5.6 %collective-permute-start.16 = (f32[4,64,128]{2,1,0:T(8,128)S(1)}, f32[4,64,128]{2,1,0:T(8,128)S(1)}, u32[]{:S(2)}, u32[]{:S(2)}) collective-permute-start(f32[4,64,128]{2,1,0:T(8,128)S(1)} %multiply_add_fusion.2), channel_id=1, source_target_pairs={{0,2},{1,3},{2,0},{3,1},{4,6},{5,7},{6,4},{7,5},{8,10},{9,11},{10,... | collective-permute-start | bytes 393224 | tf_op jit(solution)/shard_map/ppermute | solution.py:418
  130.9 5.3 %collective-permute-start.8 = (f32[4,64,128]{2,1,0:T(8,128)S(1)}, f32[4,64,128]{2,1,0:T(8,128)S(1)}, u32[]{:S(2)}, u32[]{:S(2)}) collective-permute-start(f32[4,64,128]{2,1,0:T(8,128)S(1)} %copy-done.2), channel_id=1, source_target_pairs={{0,8},{8,0},{16,24},{24,16},{1,9},{9,1},{17,25},{25,17},{2,10},{10... | collective-permute-start | bytes 393224 | tf_op jit(solution)/shard_map/ppermute | solution.py:418
  135.9 5.0 %collective-permute-start.17 = (f32[4,64,128]{2,1,0:T(8,128)S(1)}, f32[4,64,128]{2,1,0:T(8,128)S(1)}, u32[]{:S(2)}, u32[]{:S(2)}) collective-permute-start(f32[4,64,128]{2,1,0:T(8,128)S(1)} %multiply_add_fusion.1), channel_id=1, source_target_pairs={{0,4},{1,5},{2,6},{3,7},{4,0},{5,1},{6,2},{7,3},{8,12},{9,13},{10,... | collective-permute-start | bytes 393224 | tf_op jit(solution)/shard_map/ppermute | solution.py:418
  136.2 15.3 %collective-permute-start.9 = (f32[4,64,128]{2,1,0:T(8,128)S(1)}, f32[4,64,128]{2,1,0:T(8,128)S(1)}, u32[]{:S(2)}, u32[]{:S(2)}) collective-permute-start(f32[4,64,128]{2,1,0:T(8,128)S(1)} %add.83), channel_id=1, source_target_pairs={{0,16},{8,24},{16,0},{24,8},{1,17},{9,25},{17,1},{25,9},{2,18},{10... | collective-permute-start | bytes 393224 | tf_op jit(solution)/shard_map/ppermute | solution.py:418
  141.8 14.3 %copy-start.4 = (f32[2,64,128]{2,1,0:T(8,128)S(1)}, f32[2,64,128]{2,1,0:T(8,128)}, u32[]{:S(2)}) copy-start(f32[2,64,128]{2,1,0:T(8,128)} %get-tuple-element.46) | copy-start | bytes 196612
  148.7 4.3 %collective-permute-start.18 = (f32[2,128]{1,0:T(2,128)S(1)}, f32[2,128]{1,0:T(2,128)S(1)}, u32[]{:S(2)}, u32[]{:S(2)}) collective-permute-start(f32[2,128]{1,0:T(2,128)S(1)} %reshape.64), channel_id=1, source_target_pairs={{0,8},{8,0},{16,24},{24,16},{1,9},{9,1},{17,25},{25,17},{2,10},{10... | collective-permute-start | bytes 3080 | tf_op jit(solution)/shard_map/ppermute | solution.py:418
  153.0 4.6 %collective-permute-start.19 = (f32[2,128]{1,0:T(2,128)S(1)}, f32[2,128]{1,0:T(2,128)S(1)}, u32[]{:S(2)}, u32[]{:S(2)}) collective-permute-start(f32[2,128]{1,0:T(2,128)S(1)} %add.99), channel_id=1, source_target_pairs={{0,16},{8,24},{16,0},{24,8},{1,17},{9,25},{17,1},{25,9},{2,18},{10... | collective-permute-start | bytes 3080 | tf_op jit(solution)/shard_map/ppermute | solution.py:418

commit v8 on v6

--- a/solution.py
+++ b/solution.py
@@ -423,16 +423,16 @@
     return values
 
 
-def others_forward(rows, check_blocks, n, uniform=False):
+def others_uniform(rows, check_blocks, n, shape):
+    others, trail = others_forward(rows.reshape(-1, shape[2]), check_blocks, n)
+    grow = lambda value: jnp.broadcast_to(value.reshape(shape[:2] + (1,)), shape)
+    trail = [tuple(grow(value) for value in entry) for entry in trail]
+    return grow(others), trail
+
+
+def others_forward(rows, check_blocks, n):
     if not _power_of_two(n):
         return others_gather(rows, check_blocks)
-    if uniform:
-        shape = rows.shape
-        small = rows[:, :, 0].reshape(-1, shape[2])
-        others, trail = others_forward(small, check_blocks, n)
-        grow = lambda value: jnp.broadcast_to(value.reshape(shape[:2] + (1,)), shape)
-        trail = [tuple(grow(value) for value in entry) for entry in trail]
-        return grow(others), trail
     full = rows
     excl = jnp.ones_like(rows)
     trail = []
@@ -510,12 +510,23 @@
     sign_slot = jnp.einsum("kc,crs->krs", row_hot, sign_dev, precision=EXACT)
     prior_dev = channel_prior.reshape(column_blocks, TILE)
     spread = jnp.broadcast_to(prior_dev[:, :, None], (column_blocks, TILE, shots))
+    uniform = _power_of_two(n_var) and (check_blocks * TILE) % shots == 0
+    if uniform:
+        prior_slot = pick(col_hot, prior_dev)
+        first = jnp.where(edge_t > 0, jnp.tanh(0.5 * prior_slot[:, :, None]), 1.0)
+        first_rows = combine(jnp.prod(first, axis=1), row_hot, same_row)[0]
+        first_others = others_uniform(
+            first_rows, check_blocks, n_var, (check_blocks, TILE, shots)
+        )
     u = None
     saved = []
     total = None
     for step in range(ITERS):
         ba, whole, rows, others_here = fwd_products(pos, spread, u, ew, check_blocks)
-        others, trail = others_forward(rows, check_blocks, n_var, uniform=(step == 0 and (check_blocks * TILE) % shots == 0))
+        if step == 0 and uniform:
+            others, trail = first_others
+        else:
+            others, trail = others_forward(rows, check_blocks, n_var)
         saved.append((spread, u, ba, whole, others_here, others, trail))
         u, column = fwd_messages(pos, ba, sign_slot, others_here, others, ew, column_blocks)
         if step + 1 < ITERS:

time: 158 us -> 167 us (1.057)
  between operations: 1.5 us -> 11.6 us
  starting transfers between devices: 25.6 us -> 16.9 us
  waiting for transfers between devices: 46.6 us -> 50.3 us
  Pallas kernels: 55.3 us -> 57.4 us
  other arithmetic: 16.5 us -> 18.5 us
    ppermute x20, starting transfers between devices: 25.6 us -> 16.9 us  [_swap(): return lax.ppermute(value, axis, perm)]
    ppermute x20, waiting for transfers between devices: 46.6 us -> 50.3 us  [_swap(): return lax.ppermute(value, axis, perm)]
    pallas_call x8, Pallas kernels: 55.3 us -> 57.4 us  [_call(): pl.pallas_call(kernel, grid_spec=grid_spec, out_shape=[o for kind, o in o...]
  transfers between devices with their start and end apart: 20 -> 20, of which waited for: 16 -> 13; matrix products, arithmetic and copies ran while one was open for 6% -> 10% of each run, Pallas kernels for 8% -> 11%
where the time goes in v8:
time: 167 us
  Pallas kernels  57.4 us (34%)
  waiting for transfers between devices  50.3 us (30%)
  other arithmetic  18.5 us (11%)
  starting transfers between devices  16.9 us (10%)
  local copies, waits for them, and re-layouts  12.2 us (7%)
  between operations  11.6 us (7%)
    pallas_call x8, Pallas kernels, _call(): pl.pallas_call(kernel, grid_spec=grid_spec, out_shape=[o for kind, o in o...  57.4 us
    ppermute x20, waiting for transfers between devices, _swap(): return lax.ppermute(value, axis, perm)  50.3 us
    ppermute x20, starting transfers between devices, _swap(): return lax.ppermute(value, axis, perm)  16.9 us
    reduce_sum x1, other arithmetic, body(): jnp.sum(acc, axis=3)  3.34 us
  transfers between devices with their start and end apart: 20, of which 13 were waited for; matrix products, arithmetic and copies ran while one was open for 10% of the time, Pallas kernels for 11%

profile of v8, /device:TPU:0, one launch (start us, length us, event | category | flops | bytes accessed | tf_op | source)
XLA Modules:
  0.0 167.3 jit_solution(17052122007844198698)
XLA Ops:
  0.6 1.0 slice_reduce_fusion
  7.4 0.9 squeeze.7
  14.7 0.9 fusion.17
  16.3 0.9 reshape_squeeze.7
  17.4 0.9 multiply_subtract_fusion
  18.8 2.6 %collective-permute-start.1 = (f32[2,128]{1,0:T(2,128)S(1)}, f32[2,128]{1,0:T(2,128)S(1)}, u32[]{:S(2)}, u32[]{:S(2)}) collective-permute-start(f32[2,128]{1,0:T(2,128)S(1)} %mul.121), channel_id=1, source_target_pairs={{0,2},{1,3},{2,0},{3,1},{4,6},{5,7},{6,4},{7,5},{8,10},{9,11},{10,... | collective-permute-start | bytes 3080 | tf_op jit(solution)/shard_map/ppermute | solution.py:413
  21.4 0.8 reshape_squeeze.6
  22.3 1.0 sort.17
  23.5 1.6 collective-permute-start.2
  25.7 0.8 add.96
  27.1 0.8 add.97.refs_0_
  27.8 2.6 %broadcast_in_dim.124.refs_1_.ew_ref.refs_2_.refs_5_.refs_6_ = f32[2,64,64,128]{3,2,1,0:T(8,128)} broadcast(f32[2,64,64]{2,1,0:T(8,128)S(1)} %multiply_bitcast_fusion), dimensions={0,1,2} | broadcast | bytes 4227072 | tf_op jit(solution)/shard_map/broadcast_in_dim | solution.py:508
  30.4 5.0 %shard_map.94 = (f32[2,64,64,128]{3,2,1,0:T(8,128)}, f32[2,64,128]{2,1,0:T(8,128)}, f32[4,64,128]{2,1,0:T(8,128)}, f32[2,64,128]{2,1,0:T(8,128)}) custom-call(s32[134]{0:T(256)} %pad_add_fusion.pos_ref, f32[4,64,128]{2,1,0:T(8,128)} %add.97.refs_0_, f32[2,64,64,128]{3,2,1,0:T(8,128)} %broadcast_in_dim.124.refs_1_.ew_ref.refs_2_.refs_5_.refs_6_), custom_call_target="tpu_custom_call" | custom-call | tf_op jit(solution)/shard_map/pallas_call | solution.py:280
  36.3 6.6 %shard_map.95 = (f32[2,64,64,128]{3,2,1,0:T(8,128)}, f32[4,64,128]{2,1,0:T(8,128)}) custom-call(s32[134]{0:T(256)} %pad_add_fusion.pos_ref, f32[2,64,64,128]{3,2,1,0:T(8,128)} %get-tuple-element.27.ba_ref.refs_2_, f32[2,64,128]{2,1,0:T(8,128)} %copy.32.sign_ref.refs_2_.refs_3_, f32[2,64,128]{2,1,0:T(8,128)} %get-tuple-element.28.here_ref.refs_4_.refs_6_, ...), custom_call_target="tpu_custom_call" | custom-call | tf_op jit(solution)/shard_map/pallas_call | solution.py:280
  42.9 0.9 collective-permute-start.3
  43.8 4.8 %collective-permute-done.3 = f32[4,64,128]{2,1,0:T(8,128)S(1)} collective-permute-done((f32[4,64,128]{2,1,0:T(8,128)}, f32[4,64,128]{2,1,0:T(8,128)S(1)}, u32[]{:S(2)}, u32[]{:S(2)}) %collective-permute-start.3) | collective-permute-done | bytes 131104 | tf_op jit(solution)/shard_map/ppermute | solution.py:413
  48.6 0.9 add.104
  49.5 2.4 %collective-permute-start.4 = (f32[4,64,128]{2,1,0:T(8,128)S(1)}, f32[4,64,128]{2,1,0:T(8,128)S(1)}, u32[]{:S(2)}, u32[]{:S(2)}) collective-permute-start(f32[4,64,128]{2,1,0:T(8,128)S(1)} %add.104), channel_id=1, source_target_pairs={{0,16},{8,24},{16,0},{24,8},{1,17},{9,25},{17,1},{25,9},{2,18},{10... | collective-permute-start | bytes 393224 | tf_op jit(solution)/shard_map/ppermute | solution.py:413
  51.9 6.2 %collective-permute-done.4 = f32[4,64,128]{2,1,0:T(8,128)S(1)} collective-permute-done((f32[4,64,128]{2,1,0:T(8,128)S(1)}, f32[4,64,128]{2,1,0:T(8,128)S(1)}, u32[]{:S(2)}, u32[]{:S(2)}) %collective-permute-start.4) | collective-permute-done | bytes 131104 | tf_op jit(solution)/shard_map/ppermute | solution.py:413
  58.1 0.8 add_add_fusion.1.refs_0_
  58.9 6.4 %shard_map.96 = (f32[2,64,64,128]{3,2,1,0:T(8,128)}, f32[2,64,128]{2,1,0:T(8,128)}, f32[4,64,128]{2,1,0:T(8,128)}, f32[2,64,128]{2,1,0:T(8,128)}) custom-call(s32[134]{0:T(256)} %pad_add_fusion.pos_ref, f32[4,64,128]{2,1,0:T(8,128)} %add_add_fusion.1.refs_0_, f32[2,64,64,128]{3,2,1,0:T(8,128)} %get-tuple-element.30.refs_1_, ...), custom_call_target="tpu_custom_call" | custom-call | tf_op jit(solution)/shard_map/pallas_call | solution.py:280
  65.3 1.5 collective-permute-done.5
  66.9 0.9 mul.125
  67.9 5.5 %collective-permute-done.6 = f32[4,64,128]{2,1,0:T(8,128)S(1)} collective-permute-done((f32[4,64,128]{2,1,0:T(8,128)S(1)}, f32[4,64,128]{2,1,0:T(8,128)S(1)}, u32[]{:S(2)}, u32[]{:S(2)}) %collective-permute-start.6) | collective-permute-done | bytes 131104 | tf_op jit(solution)/shard_map/ppermute | solution.py:413
  73.7 4.8 %collective-permute-done.7 = f32[4,64,128]{2,1,0:T(8,128)S(1)} collective-permute-done((f32[4,64,128]{2,1,0:T(8,128)S(1)}, f32[4,64,128]{2,1,0:T(8,128)S(1)}, u32[]{:S(2)}, u32[]{:S(2)}) %collective-permute-start.7) | collective-permute-done | bytes 131104 | tf_op jit(solution)/shard_map/ppermute | solution.py:413
  79.2 8.0 %shard_map.98 = (f32[2,64,64,128]{3,2,1,0:T(8,128)}, f32[2,64,64,128]{3,2,1,0:T(8,128)}, f32[2,64,128]{2,1,0:T(8,128)}, f32[4,64,128]{2,1,0:T(8,128)}) custom-call(s32[134]{0:T(256)} %pad_add_fusion.pos_ref, f32[4,64,128]{2,1,0:T(8,128)} %bitcast.38, f32[2,64,64,128]{3,2,1,0:T(8,128)} %get-tuple-element.31.ba_ref.refs_1_, ...), custom_call_target="tpu_custom_call" | custom-call | tf_op jit(solution)/shard_map/pallas_call | solution.py:280
  87.2 1.5 collective-permute-done.10
  88.8 0.9 multiply_add_fusion.5
  90.2 5.1 %collective-permute-done.11 = f32[4,64,128]{2,1,0:T(8,128)S(1)} collective-permute-done((f32[4,64,128]{2,1,0:T(8,128)S(1)}, f32[4,64,128]{2,1,0:T(8,128)S(1)}, u32[]{:S(2)}, u32[]{:S(2)}) %collective-permute-start.11) | collective-permute-done | bytes 131104 | tf_op jit(solution)/shard_map/ppermute | solution.py:413
  95.6 6.6 %shard_map.97 = (f32[2,64,64,128]{3,2,1,0:T(8,128)}, f32[4,64,128]{2,1,0:T(8,128)}) custom-call(s32[134]{0:T(256)} %pad_add_fusion.pos_ref, f32[2,64,64,128]{3,2,1,0:T(8,128)} %get-tuple-element.31.ba_ref.refs_1_, f32[2,64,128]{2,1,0:T(8,128)} %copy.32.sign_ref.refs_2_.refs_3_, f32[2,64,128]{2,1,0:T(8,128)} %get-tuple-element.32.here_ref.refs_3_.refs_7_, ...), custom_call_target="tpu_custom_call" | custom-call | tf_op jit(solution)/shard_map/pallas_call | solution.py:280
  102.9 8.3 %shard_map.99 = (f32[2,64,64,128]{3,2,1,0:T(8,128)}, f32[4,64,128]{2,1,0:T(8,128)}) custom-call(s32[134]{0:T(256)} %pad_add_fusion.pos_ref, f32[4,64,128]{2,1,0:T(8,128)} %add_add_fusion.1.refs_0_, f32[2,64,64,128]{3,2,1,0:T(8,128)} %get-tuple-element.30.refs_1_, f32[2,64,64,128]{3,2,1,0:T(8,128)} %broadcast_in_dim.124.refs_1_.ew_ref.refs_2_.refs_5_.refs_6_, ...), custom_call_target="tpu_custom_call" | custom-call | tf_op jit(solution)/shard_map/pallas_call | solution.py:280
  111.2 5.2 %collective-permute-done.13 = f32[4,64,128]{2,1,0:T(8,128)S(1)} collective-permute-done((f32[4,64,128]{2,1,0:T(8,128)}, f32[4,64,128]{2,1,0:T(8,128)S(1)}, u32[]{:S(2)}, u32[]{:S(2)}) %collective-permute-start.13) | collective-permute-done | bytes 131104 | tf_op jit(solution)/shard_map/ppermute | solution.py:413
  116.4 0.9 add.115
  117.3 1.8 %collective-permute-start.14 = (f32[4,64,128]{2,1,0:T(8,128)S(1)}, f32[4,64,128]{2,1,0:T(8,128)S(1)}, u32[]{:S(2)}, u32[]{:S(2)}) collective-permute-start(f32[4,64,128]{2,1,0:T(8,128)S(1)} %add.115), channel_id=1, source_target_pairs={{0,16},{8,24},{16,0},{24,8},{1,17},{9,25},{17,1},{25,9},{2,18},{10... | collective-permute-start | bytes 393224 | tf_op jit(solution)/shard_map/ppermute | solution.py:413
  119.2 6.2 %collective-permute-done.14 = f32[4,64,128]{2,1,0:T(8,128)S(1)} collective-permute-done((f32[4,64,128]{2,1,0:T(8,128)S(1)}, f32[4,64,128]{2,1,0:T(8,128)S(1)}, u32[]{:S(2)}, u32[]{:S(2)}) %collective-permute-start.14) | collective-permute-done | bytes 131104 | tf_op jit(solution)/shard_map/ppermute | solution.py:413
  126.1 9.8 %shard_map.100 = (f32[2,64,64,128]{3,2,1,0:T(8,128)}, f32[2,64,64,128]{3,2,1,0:T(8,128)}, f32[2,64,128]{2,1,0:T(8,128)}, f32[4,64,128]{2,1,0:T(8,128)}) custom-call(s32[134]{0:T(256)} %pad_add_fusion.pos_ref, f32[4,64,128]{2,1,0:T(8,128)} %get-tuple-element.52.refs_0_, f32[2,64,64,128]{3,2,1,0:T(8,128)} %get-tuple-element.42.refs_1_, ...), custom_call_target="tpu_custom_call" | custom-call | tf_op jit(solution)/shard_map/pallas_call | solution.py:280
  136.1 1.5 collective-permute-done.15
  137.5 1.0 multiply_add_fusion.2
  139.6 4.5 %collective-permute-done.16 = f32[4,64,128]{2,1,0:T(8,128)S(1)} collective-permute-done((f32[4,64,128]{2,1,0:T(8,128)S(1)}, f32[4,64,128]{2,1,0:T(8,128)S(1)}, u32[]{:S(2)}, u32[]{:S(2)}) %collective-permute-start.16) | collective-permute-done | bytes 131104 | tf_op jit(solution)/shard_map/ppermute | solution.py:413
  144.3 2.0 %collective-permute-start.17 = (f32[4,64,128]{2,1,0:T(8,128)S(1)}, f32[4,64,128]{2,1,0:T(8,128)S(1)}, u32[]{:S(2)}, u32[]{:S(2)}) collective-permute-start(f32[4,64,128]{2,1,0:T(8,128)S(1)} %multiply_add_fusion.1), channel_id=1, source_target_pairs={{0,4},{1,5},{2,6},{3,7},{4,0},{5,1},{6,2},{7,3},{8,12},{9,13},{10,... | collective-permute-start | bytes 393224 | tf_op jit(solution)/shard_map/ppermute | solution.py:413
  146.9 2.4 %collective-permute-done.17 = f32[4,64,128]{2,1,0:T(8,128)S(1)} collective-permute-done((f32[4,64,128]{2,1,0:T(8,128)S(1)}, f32[4,64,128]{2,1,0:T(8,128)S(1)}, u32[]{:S(2)}, u32[]{:S(2)}) %collective-permute-start.17) | collective-permute-done | bytes 131104 | tf_op jit(solution)/shard_map/ppermute | solution.py:413
  149.3 0.9 multiply_add_fusion.refs_3_
  150.2 6.7 %shard_map.101 = f32[4,64,128]{2,1,0:T(8,128)} custom-call(s32[134]{0:T(256)} %pad_add_fusion.pos_ref, f32[4,64,128]{2,1,0:T(8,128)} %add.97.refs_0_, f32[2,64,64,128]{3,2,1,0:T(8,128)} %broadcast_in_dim.124.refs_1_.ew_ref.refs_2_.refs_5_.refs_6_, f32[2,64,64,128]{3,2,1,0:T(8,128)} %get-tuple-element.45.refs_2_, f32[4,64,128]{2,1,0:T(8,128)} %multiply_add_fusion.refs_3_, ...), custom_call_target="tpu_custom_call" | custom-call | tf_op jit(solution)/shard_map/pallas_call | solution.py:280
  157.0 1.0 reduce_sum.52
  158.1 0.8 add_add_fusion
  158.9 3.3 %reduce_sum.48 = f32[2,64,64]{2,1,0:T(8,128)S(1)} reduce(f32[2,64,64,128]{3,2,1,0:T(8,128)} %get-tuple-element.44, f32[]{:T(128)} %constant.27.clone.1), dimensions={3}, to_apply=%region_4.5 | reduce | flops 1040384 | bytes 4227076 | tf_op jit(solution)/shard_map/reduce_sum | solution.py:564
  162.2 2.7 %collective-permute-start.19 = (f32[2,128]{1,0:T(2,128)S(1)}, f32[2,128]{1,0:T(2,128)S(1)}, u32[]{:S(2)}, u32[]{:S(2)}) collective-permute-start(f32[2,128]{1,0:T(2,128)S(1)} %add.123), channel_id=1, source_target_pairs={{0,16},{8,24},{16,0},{24,8},{1,17},{9,25},{17,1},{25,9},{2,18},{10... | collective-permute-start | bytes 3080 | tf_op jit(solution)/shard_map/ppermute | solution.py:413
  165.8 1.0 collective-permute-done.19
  (73 shorter events, 12.1 us)
Async XLA Ops:
  15.9 2.9 %collective-permute-start = (f32[2,128]{1,0:T(2,128)S(1)}, f32[2,128]{1,0:T(2,128)S(1)}, u32[]{:S(2)}, u32[]{:S(2)}) collective-permute-start(f32[2,128]{1,0:T(2,128)S(1)} %reshape.126), channel_id=1, source_target_pairs={{0,1},{1,0},{2,3},{3,2},{4,5},{5,4},{6,7},{7,6},{8,9},{9,8},{10,11... | collective-permute-start | bytes 3080 | tf_op jit(solution)/shard_map/ppermute | solution.py:413
  18.8 4.7 %collective-permute-start.1 = (f32[2,128]{1,0:T(2,128)S(1)}, f32[2,128]{1,0:T(2,128)S(1)}, u32[]{:S(2)}, u32[]{:S(2)}) collective-permute-start(f32[2,128]{1,0:T(2,128)S(1)} %mul.121), channel_id=1, source_target_pairs={{0,2},{1,3},{2,0},{3,1},{4,6},{5,7},{6,4},{7,5},{8,10},{9,11},{10,... | collective-permute-start | bytes 3080 | tf_op jit(solution)/shard_map/ppermute | solution.py:413
  23.5 11.9 %collective-permute-start.2 = (f32[2,128]{1,0:T(2,128)S(1)}, f32[2,128]{1,0:T(2,128)S(1)}, u32[]{:S(2)}, u32[]{:S(2)}) collective-permute-start(f32[2,128]{1,0:T(2,128)S(1)} %mul.123), channel_id=1, source_target_pairs={{0,4},{1,5},{2,6},{3,7},{4,0},{5,1},{6,2},{7,3},{8,12},{9,13},{10,... | collective-permute-start | bytes 3080 | tf_op jit(solution)/shard_map/ppermute | solution.py:413
  42.9 5.7 %collective-permute-start.3 = (f32[4,64,128]{2,1,0:T(8,128)}, f32[4,64,128]{2,1,0:T(8,128)S(1)}, u32[]{:S(2)}, u32[]{:S(2)}) collective-permute-start(f32[4,64,128]{2,1,0:T(8,128)} %get-tuple-element.29), channel_id=1, source_target_pairs={{0,8},{8,0},{16,24},{24,16},{1,9},{9,1},{17,25},{25,17},{2,10},{10... | collective-permute-start | bytes 393224 | tf_op jit(solution)/shard_map/ppermute | solution.py:413
  49.5 8.6 %collective-permute-start.4 = (f32[4,64,128]{2,1,0:T(8,128)S(1)}, f32[4,64,128]{2,1,0:T(8,128)S(1)}, u32[]{:S(2)}, u32[]{:S(2)}) collective-permute-start(f32[4,64,128]{2,1,0:T(8,128)S(1)} %add.104), channel_id=1, source_target_pairs={{0,16},{8,24},{16,0},{24,8},{1,17},{9,25},{17,1},{25,9},{2,18},{10... | collective-permute-start | bytes 393224 | tf_op jit(solution)/shard_map/ppermute | solution.py:413
  65.3 1.6 collective-permute-start.5
  67.8 5.6 %collective-permute-start.6 = (f32[4,64,128]{2,1,0:T(8,128)S(1)}, f32[4,64,128]{2,1,0:T(8,128)S(1)}, u32[]{:S(2)}, u32[]{:S(2)}) collective-permute-start(f32[4,64,128]{2,1,0:T(8,128)S(1)} %mul.125), channel_id=1, source_target_pairs={{0,2},{1,3},{2,0},{3,1},{4,6},{5,7},{6,4},{7,5},{8,10},{9,11},{10,... | collective-permute-start | bytes 393224 | tf_op jit(solution)/shard_map/ppermute | solution.py:413
  73.4 5.0 %collective-permute-start.7 = (f32[4,64,128]{2,1,0:T(8,128)S(1)}, f32[4,64,128]{2,1,0:T(8,128)S(1)}, u32[]{:S(2)}, u32[]{:S(2)}) collective-permute-start(f32[4,64,128]{2,1,0:T(8,128)S(1)} %mul.127), channel_id=1, source_target_pairs={{0,4},{1,5},{2,6},{3,7},{4,0},{5,1},{6,2},{7,3},{8,12},{9,13},{10,... | collective-permute-start | bytes 393224 | tf_op jit(solution)/shard_map/ppermute | solution.py:413
  79.2 9.6 %copy-start.1 = (f32[4,64,128]{2,1,0:T(8,128)S(1)}, f32[4,64,128]{2,1,0:T(8,128)}, u32[]{:S(2)}) copy-start(f32[4,64,128]{2,1,0:T(8,128)} %get-tuple-element.33) | copy-start | bytes 393220
  87.2 1.6 collective-permute-start.10
  89.7 5.6 %collective-permute-start.11 = (f32[4,64,128]{2,1,0:T(8,128)S(1)}, f32[4,64,128]{2,1,0:T(8,128)S(1)}, u32[]{:S(2)}, u32[]{:S(2)}) collective-permute-start(f32[4,64,128]{2,1,0:T(8,128)S(1)} %multiply_add_fusion.5), channel_id=1, source_target_pairs={{0,2},{1,3},{2,0},{3,1},{4,6},{5,7},{6,4},{7,5},{8,10},{9,11},{10,... | collective-permute-start | bytes 393224 | tf_op jit(solution)/shard_map/ppermute | solution.py:413
  95.4 6.8 %collective-permute-start.12 = (f32[4,64,128]{2,1,0:T(8,128)S(1)}, f32[4,64,128]{2,1,0:T(8,128)S(1)}, u32[]{:S(2)}, u32[]{:S(2)}) collective-permute-start(f32[4,64,128]{2,1,0:T(8,128)S(1)} %multiply_add_fusion.4), channel_id=1, source_target_pairs={{0,4},{1,5},{2,6},{3,7},{4,0},{5,1},{6,2},{7,3},{8,12},{9,13},{10,... | collective-permute-start | bytes 393224 | tf_op jit(solution)/shard_map/ppermute | solution.py:413
  111.2 5.2 %collective-permute-start.13 = (f32[4,64,128]{2,1,0:T(8,128)}, f32[4,64,128]{2,1,0:T(8,128)S(1)}, u32[]{:S(2)}, u32[]{:S(2)}) collective-permute-start(f32[4,64,128]{2,1,0:T(8,128)} %get-tuple-element.41), channel_id=1, source_target_pairs={{0,8},{8,0},{16,24},{24,16},{1,9},{9,1},{17,25},{25,17},{2,10},{10... | collective-permute-start | bytes 393224 | tf_op jit(solution)/shard_map/ppermute | solution.py:413
  117.3 8.1 %collective-permute-start.14 = (f32[4,64,128]{2,1,0:T(8,128)S(1)}, f32[4,64,128]{2,1,0:T(8,128)S(1)}, u32[]{:S(2)}, u32[]{:S(2)}) collective-permute-start(f32[4,64,128]{2,1,0:T(8,128)S(1)} %add.115), channel_id=1, source_target_pairs={{0,16},{8,24},{16,0},{24,8},{1,17},{9,25},{17,1},{25,9},{2,18},{10... | collective-permute-start | bytes 393224 | tf_op jit(solution)/shard_map/ppermute | solution.py:413
  126.1 12.6 %copy-start = (f32[256,128]{1,0:T(8,128)S(1)}, f32[256,128]{1,0:T(8,128)}, u32[]{:S(2)}) copy-start(f32[256,128]{1,0:T(8,128)} %param.13) | copy-start | bytes 393220
  126.1 12.8 %copy-start.2 = (f32[4,64,128]{2,1,0:T(8,128)S(1)}, f32[4,64,128]{2,1,0:T(8,128)}, u32[]{:S(2)}) copy-start(f32[4,64,128]{2,1,0:T(8,128)} %get-tuple-element.36) | copy-start | bytes 393220
  135.9 1.6 collective-permute-start.15
  138.6 5.6 %collective-permute-start.16 = (f32[4,64,128]{2,1,0:T(8,128)S(1)}, f32[4,64,128]{2,1,0:T(8,128)S(1)}, u32[]{:S(2)}, u32[]{:S(2)}) collective-permute-start(f32[4,64,128]{2,1,0:T(8,128)S(1)} %multiply_add_fusion.2), channel_id=1, source_target_pairs={{0,2},{1,3},{2,0},{3,1},{4,6},{5,7},{6,4},{7,5},{8,10},{9,11},{10,... | collective-permute-start | bytes 393224 | tf_op jit(solution)/shard_map/ppermute | solution.py:413
  138.9 7.6 %collective-permute-start.8 = (f32[4,64,128]{2,1,0:T(8,128)S(1)}, f32[4,64,128]{2,1,0:T(8,128)S(1)}, u32[]{:S(2)}, u32[]{:S(2)}) collective-permute-start(f32[4,64,128]{2,1,0:T(8,128)S(1)} %copy-done.2), channel_id=1, source_target_pairs={{0,8},{8,0},{16,24},{24,16},{1,9},{9,1},{17,25},{25,17},{2,10},{10... | collective-permute-start | bytes 393224 | tf_op jit(solution)/shard_map/ppermute | solution.py:413
  144.3 5.0 %collective-permute-start.17 = (f32[4,64,128]{2,1,0:T(8,128)S(1)}, f32[4,64,128]{2,1,0:T(8,128)S(1)}, u32[]{:S(2)}, u32[]{:S(2)}) collective-permute-start(f32[4,64,128]{2,1,0:T(8,128)S(1)} %multiply_add_fusion.1), channel_id=1, source_target_pairs={{0,4},{1,5},{2,6},{3,7},{4,0},{5,1},{6,2},{7,3},{8,12},{9,13},{10,... | collective-permute-start | bytes 393224 | tf_op jit(solution)/shard_map/ppermute | solution.py:413
  146.5 11.6 %collective-permute-start.9 = (f32[4,64,128]{2,1,0:T(8,128)S(1)}, f32[4,64,128]{2,1,0:T(8,128)S(1)}, u32[]{:S(2)}, u32[]{:S(2)}) collective-permute-start(f32[4,64,128]{2,1,0:T(8,128)S(1)} %add.107), channel_id=1, source_target_pairs={{0,16},{8,24},{16,0},{24,8},{1,17},{9,25},{17,1},{25,9},{2,18},{10... | collective-permute-start | bytes 393224 | tf_op jit(solution)/shard_map/ppermute | solution.py:413
  158.1 4.1 %collective-permute-start.18 = (f32[2,128]{1,0:T(2,128)S(1)}, f32[2,128]{1,0:T(2,128)S(1)}, u32[]{:S(2)}, u32[]{:S(2)}) collective-permute-start(f32[2,128]{1,0:T(2,128)S(1)} %reshape.130), channel_id=1, source_target_pairs={{0,8},{8,0},{16,24},{24,16},{1,9},{9,1},{17,25},{25,17},{2,10},{10... | collective-permute-start | bytes 3080 | tf_op jit(solution)/shard_map/ppermute | solution.py:413
  162.2 4.5 %collective-permute-start.19 = (f32[2,128]{1,0:T(2,128)S(1)}, f32[2,128]{1,0:T(2,128)S(1)}, u32[]{:S(2)}, u32[]{:S(2)}) collective-permute-start(f32[2,128]{1,0:T(2,128)S(1)} %add.123), channel_id=1, source_target_pairs={{0,16},{8,24},{16,0},{24,8},{1,17},{9,25},{17,1},{25,9},{2,18},{10... | collective-permute-start | bytes 3080 | tf_op jit(solution)/shard_map/ppermute | solution.py:413

commit v9 on v6

--- a/solution.py
+++ b/solution.py
@@ -13,7 +13,7 @@
 DAMP = 0.97
 EXACT = lax.Precision.HIGHEST
 F32 = jnp.float32
-UNROLL = 8
+UNROLL = 4
 
 
 def linear_both(values, axis):
@@ -77,7 +77,13 @@
 
 
 def _loop(count, body, init):
-    return lax.fori_loop(0, count, body, init)
+    def group(j, carry):
+        for t in range(UNROLL):
+            carry = body(UNROLL * j + t, carry)
+        return carry
+
+    carry = lax.fori_loop(0, count // UNROLL, group, init)
+    return lax.fori_loop(UNROLL * (count // UNROLL), count, body, carry)
 
 
 def _fwd_products_kernel(has_u, slots, blocks, pos_ref, *refs):

time: 158 us -> 154 us (0.975)
  starting transfers between devices: 25.6 us -> 22.1 us
    ppermute x20, starting transfers between devices: 25.6 us -> 22.1 us  [_swap(): return lax.ppermute(value, axis, perm)]
where the time goes in v9:
time: 154 us; the launch traced here: 153 us
  Pallas kernels  54.9 us (36%)
  waiting for transfers between devices  46.6 us (30%)
  starting transfers between devices  22.1 us (14%)
  other arithmetic  16.5 us (11%)
  local copies, waits for them, and re-layouts  11 us (7%)
    pallas_call x8, Pallas kernels, _call(): pl.pallas_call(kernel, grid_spec=grid_spec, out_shape=[o for kind, o in o...  54.9 us
    ppermute x20, waiting for transfers between devices, _swap(): return lax.ppermute(value, axis, perm)  46.6 us
    ppermute x20, starting transfers between devices, _swap(): return lax.ppermute(value, axis, perm)  22.1 us
    reduce_sum x1, other arithmetic, body(): jnp.sum(acc, axis=3)  3.34 us
  transfers between devices with their start and end apart: 20, of which 16 were waited for; matrix products, arithmetic and copies ran while one was open for 6% of the time, Pallas kernels for 8%

profile of v9, /device:TPU:0, one launch (start us, length us, event | category | flops | bytes accessed | tf_op | source)
XLA Modules:
  0.0 152.9 jit_solution(10317075591448699083)
XLA Ops:
  0.6 0.9 squeeze.10
  2.7 1.0 sort.17
  5.4 0.9 reshape_squeeze.10
  7.8 2.5 %broadcast_in_dim.91.refs_1_.ew_ref.refs_2_.refs_5_.refs_6_ = f32[2,64,64,128]{3,2,1,0:T(8,128)} broadcast(f32[2,64,64]{2,1,0:T(8,128)S(1)} %multiply_bitcast_fusion), dimensions={0,1,2} | broadcast | bytes 4227072 | tf_op jit(solution)/shard_map/broadcast_in_dim | solution.py:514
  10.3 4.9 %shard_map.94 = (f32[2,64,64,128]{3,2,1,0:T(8,128)}, f32[2,64,128]{2,1,0:T(8,128)}, f32[4,64,128]{2,1,0:T(8,128)}, f32[2,64,128]{2,1,0:T(8,128)}) custom-call(s32[134]{0:T(256)} %pad_add_fusion.pos_ref, f32[4,64,128]{2,1,0:T(8,128)} %add.79.refs_0_, f32[2,64,64,128]{3,2,1,0:T(8,128)} %broadcast_in_dim.91.refs_1_.ew_ref.refs_2_.refs_5_.refs_6_), custom_call_target="tpu_custom_call" | custom-call | tf_op jit(solution)/shard_map/pallas_call | solution.py:286
  15.2 1.0 slice_reduce_fusion
  16.7 0.8 collective-permute-done
  17.5 2.8 %collective-permute-start.1 = (f32[2,128]{1,0:T(2,128)S(1)}, f32[2,128]{1,0:T(2,128)S(1)}, u32[]{:S(2)}, u32[]{:S(2)}) collective-permute-start(f32[2,128]{1,0:T(2,128)S(1)} %mul.88), channel_id=1, source_target_pairs={{0,2},{1,3},{2,0},{3,1},{4,6},{5,7},{6,4},{7,5},{8,10},{9,11},{10,... | collective-permute-start | bytes 3080 | tf_op jit(solution)/shard_map/ppermute | solution.py:419
  20.4 1.4 collective-permute-done.1
  21.9 1.9 %collective-permute-start.2 = (f32[2,128]{1,0:T(2,128)S(1)}, f32[2,128]{1,0:T(2,128)S(1)}, u32[]{:S(2)}, u32[]{:S(2)}) collective-permute-start(f32[2,128]{1,0:T(2,128)S(1)} %mul.90), channel_id=1, source_target_pairs={{0,4},{1,5},{2,6},{3,7},{4,0},{5,1},{6,2},{7,3},{8,12},{9,13},{10,... | collective-permute-start | bytes 3080 | tf_op jit(solution)/shard_map/ppermute | solution.py:419
  26.3 6.2 %shard_map.95 = (f32[2,64,64,128]{3,2,1,0:T(8,128)}, f32[4,64,128]{2,1,0:T(8,128)}) custom-call(s32[134]{0:T(256)} %pad_add_fusion.pos_ref, f32[2,64,64,128]{3,2,1,0:T(8,128)} %get-tuple-element.28.ba_ref.refs_2_, f32[2,64,128]{2,1,0:T(8,128)} %copy.32.sign_ref.refs_2_.refs_3_, f32[2,64,128]{2,1,0:T(8,128)} %get-tuple-element.29.here_ref.refs_4_.refs_6_, ...), custom_call_target="tpu_custom_call" | custom-call | tf_op jit(solution)/shard_map/pallas_call | solution.py:286
  32.5 2.3 %collective-permute-start.3 = (f32[4,64,128]{2,1,0:T(8,128)}, f32[4,64,128]{2,1,0:T(8,128)S(1)}, u32[]{:S(2)}, u32[]{:S(2)}) collective-permute-start(f32[4,64,128]{2,1,0:T(8,128)} %get-tuple-element.31), channel_id=1, source_target_pairs={{0,8},{8,0},{16,24},{24,16},{1,9},{9,1},{17,25},{25,17},{2,10},{10... | collective-permute-start | bytes 393224 | tf_op jit(solution)/shard_map/ppermute | solution.py:419
  34.7 3.2 %collective-permute-done.3 = f32[4,64,128]{2,1,0:T(8,128)S(1)} collective-permute-done((f32[4,64,128]{2,1,0:T(8,128)}, f32[4,64,128]{2,1,0:T(8,128)S(1)}, u32[]{:S(2)}, u32[]{:S(2)}) %collective-permute-start.3) | collective-permute-done | bytes 131104 | tf_op jit(solution)/shard_map/ppermute | solution.py:419
  37.9 0.9 add.80
  38.8 2.3 %collective-permute-start.4 = (f32[4,64,128]{2,1,0:T(8,128)S(1)}, f32[4,64,128]{2,1,0:T(8,128)S(1)}, u32[]{:S(2)}, u32[]{:S(2)}) collective-permute-start(f32[4,64,128]{2,1,0:T(8,128)S(1)} %add.80), channel_id=1, source_target_pairs={{0,16},{8,24},{16,0},{24,8},{1,17},{9,25},{17,1},{25,9},{2,18},{10... | collective-permute-start | bytes 393224 | tf_op jit(solution)/shard_map/ppermute | solution.py:419
  41.2 3.6 %collective-permute-done.4 = f32[4,64,128]{2,1,0:T(8,128)S(1)} collective-permute-done((f32[4,64,128]{2,1,0:T(8,128)S(1)}, f32[4,64,128]{2,1,0:T(8,128)S(1)}, u32[]{:S(2)}, u32[]{:S(2)}) %collective-permute-start.4) | collective-permute-done | bytes 131104 | tf_op jit(solution)/shard_map/ppermute | solution.py:419
  45.5 6.2 %shard_map.96 = (f32[2,64,64,128]{3,2,1,0:T(8,128)}, f32[2,64,128]{2,1,0:T(8,128)}, f32[4,64,128]{2,1,0:T(8,128)}, f32[2,64,128]{2,1,0:T(8,128)}) custom-call(s32[134]{0:T(256)} %pad_add_fusion.pos_ref, f32[4,64,128]{2,1,0:T(8,128)} %add_add_fusion.1.refs_0_, f32[2,64,64,128]{3,2,1,0:T(8,128)} %get-tuple-element.32.refs_1_, ...), custom_call_target="tpu_custom_call" | custom-call | tf_op jit(solution)/shard_map/pallas_call | solution.py:286
  51.7 1.5 %collective-permute-done.5 = f32[4,64,128]{2,1,0:T(8,128)S(1)} collective-permute-done((f32[4,64,128]{2,1,0:T(8,128)}, f32[4,64,128]{2,1,0:T(8,128)S(1)}, u32[]{:S(2)}, u32[]{:S(2)}) %collective-permute-start.5) | collective-permute-done | bytes 131104 | tf_op jit(solution)/shard_map/ppermute | solution.py:419
  53.3 0.9 mul.92
  54.2 2.1 %collective-permute-start.6 = (f32[4,64,128]{2,1,0:T(8,128)S(1)}, f32[4,64,128]{2,1,0:T(8,128)S(1)}, u32[]{:S(2)}, u32[]{:S(2)}) collective-permute-start(f32[4,64,128]{2,1,0:T(8,128)S(1)} %mul.92), channel_id=1, source_target_pairs={{0,2},{1,3},{2,0},{3,1},{4,6},{5,7},{6,4},{7,5},{8,10},{9,11},{10,... | collective-permute-start | bytes 393224 | tf_op jit(solution)/shard_map/ppermute | solution.py:419
  56.3 3.8 %collective-permute-done.6 = f32[4,64,128]{2,1,0:T(8,128)S(1)} collective-permute-done((f32[4,64,128]{2,1,0:T(8,128)S(1)}, f32[4,64,128]{2,1,0:T(8,128)S(1)}, u32[]{:S(2)}, u32[]{:S(2)}) %collective-permute-start.6) | collective-permute-done | bytes 131104 | tf_op jit(solution)/shard_map/ppermute | solution.py:419
  60.2 1.7 %collective-permute-start.7 = (f32[4,64,128]{2,1,0:T(8,128)S(1)}, f32[4,64,128]{2,1,0:T(8,128)S(1)}, u32[]{:S(2)}, u32[]{:S(2)}) collective-permute-start(f32[4,64,128]{2,1,0:T(8,128)S(1)} %mul.94), channel_id=1, source_target_pairs={{0,4},{1,5},{2,6},{3,7},{4,0},{5,1},{6,2},{7,3},{8,12},{9,13},{10,... | collective-permute-start | bytes 393224 | tf_op jit(solution)/shard_map/ppermute | solution.py:419
  61.8 3.4 %collective-permute-done.7 = f32[4,64,128]{2,1,0:T(8,128)S(1)} collective-permute-done((f32[4,64,128]{2,1,0:T(8,128)S(1)}, f32[4,64,128]{2,1,0:T(8,128)S(1)}, u32[]{:S(2)}, u32[]{:S(2)}) %collective-permute-start.7) | collective-permute-done | bytes 131104 | tf_op jit(solution)/shard_map/ppermute | solution.py:419
  66.0 7.7 %shard_map.98 = (f32[2,64,64,128]{3,2,1,0:T(8,128)}, f32[2,64,64,128]{3,2,1,0:T(8,128)}, f32[2,64,128]{2,1,0:T(8,128)}, f32[4,64,128]{2,1,0:T(8,128)}) custom-call(s32[134]{0:T(256)} %pad_add_fusion.pos_ref, f32[4,64,128]{2,1,0:T(8,128)} %bitcast.15, f32[2,64,64,128]{3,2,1,0:T(8,128)} %get-tuple-element.33.ba_ref.refs_1_, ...), custom_call_target="tpu_custom_call" | custom-call | tf_op jit(solution)/shard_map/pallas_call | solution.py:286
  73.7 1.5 %collective-permute-done.10 = f32[4,64,128]{2,1,0:T(8,128)S(1)} collective-permute-done((f32[4,64,128]{2,1,0:T(8,128)}, f32[4,64,128]{2,1,0:T(8,128)S(1)}, u32[]{:S(2)}, u32[]{:S(2)}) %collective-permute-start.10) | collective-permute-done | bytes 131104 | tf_op jit(solution)/shard_map/ppermute | solution.py:419
  75.3 0.9 multiply_add_fusion.5
  76.2 1.8 %collective-permute-start.11 = (f32[4,64,128]{2,1,0:T(8,128)S(1)}, f32[4,64,128]{2,1,0:T(8,128)S(1)}, u32[]{:S(2)}, u32[]{:S(2)}) collective-permute-start(f32[4,64,128]{2,1,0:T(8,128)S(1)} %multiply_add_fusion.5), channel_id=1, source_target_pairs={{0,2},{1,3},{2,0},{3,1},{4,6},{5,7},{6,4},{7,5},{8,10},{9,11},{10,... | collective-permute-start | bytes 393224 | tf_op jit(solution)/shard_map/ppermute | solution.py:419
  78.0 3.8 %collective-permute-done.11 = f32[4,64,128]{2,1,0:T(8,128)S(1)} collective-permute-done((f32[4,64,128]{2,1,0:T(8,128)S(1)}, f32[4,64,128]{2,1,0:T(8,128)S(1)}, u32[]{:S(2)}, u32[]{:S(2)}) %collective-permute-start.11) | collective-permute-done | bytes 131104 | tf_op jit(solution)/shard_map/ppermute | solution.py:419
  81.8 1.4 collective-permute-start.12
  83.3 6.2 %shard_map.97 = (f32[2,64,64,128]{3,2,1,0:T(8,128)}, f32[4,64,128]{2,1,0:T(8,128)}) custom-call(s32[134]{0:T(256)} %pad_add_fusion.pos_ref, f32[2,64,64,128]{3,2,1,0:T(8,128)} %get-tuple-element.33.ba_ref.refs_1_, f32[2,64,128]{2,1,0:T(8,128)} %copy.32.sign_ref.refs_2_.refs_3_, f32[2,64,128]{2,1,0:T(8,128)} %get-tuple-element.34.here_ref.refs_3_.refs_7_, ...), custom_call_target="tpu_custom_call" | custom-call | tf_op jit(solution)/shard_map/pallas_call | solution.py:286
  90.1 8.0 %shard_map.99 = (f32[2,64,64,128]{3,2,1,0:T(8,128)}, f32[4,64,128]{2,1,0:T(8,128)}) custom-call(s32[134]{0:T(256)} %pad_add_fusion.pos_ref, f32[4,64,128]{2,1,0:T(8,128)} %add_add_fusion.1.refs_0_, f32[2,64,64,128]{3,2,1,0:T(8,128)} %get-tuple-element.32.refs_1_, f32[2,64,64,128]{3,2,1,0:T(8,128)} %broadcast_in_dim.91.refs_1_.ew_ref.refs_2_.refs_5_.refs_6_, ...), custom_call_target="tpu_custom_call" | custom-call | tf_op jit(solution)/shard_map/pallas_call | solution.py:286
  98.1 1.3 collective-permute-start.13
  99.4 3.9 %collective-permute-done.13 = f32[4,64,128]{2,1,0:T(8,128)S(1)} collective-permute-done((f32[4,64,128]{2,1,0:T(8,128)}, f32[4,64,128]{2,1,0:T(8,128)S(1)}, u32[]{:S(2)}, u32[]{:S(2)}) %collective-permute-start.13) | collective-permute-done | bytes 131104 | tf_op jit(solution)/shard_map/ppermute | solution.py:419
  103.3 0.9 add.91
  104.3 1.0 collective-permute-start.14
  105.2 6.4 %collective-permute-done.14 = f32[4,64,128]{2,1,0:T(8,128)S(1)} collective-permute-done((f32[4,64,128]{2,1,0:T(8,128)S(1)}, f32[4,64,128]{2,1,0:T(8,128)S(1)}, u32[]{:S(2)}, u32[]{:S(2)}) %collective-permute-start.14) | collective-permute-done | bytes 131104 | tf_op jit(solution)/shard_map/ppermute | solution.py:419
  112.2 9.7 %shard_map.100 = (f32[2,64,64,128]{3,2,1,0:T(8,128)}, f32[2,64,64,128]{3,2,1,0:T(8,128)}, f32[2,64,128]{2,1,0:T(8,128)}, f32[4,64,128]{2,1,0:T(8,128)}) custom-call(s32[134]{0:T(256)} %pad_add_fusion.pos_ref, f32[4,64,128]{2,1,0:T(8,128)} %get-tuple-element.52.refs_0_, f32[2,64,64,128]{3,2,1,0:T(8,128)} %get-tuple-element.44.refs_1_, ...), custom_call_target="tpu_custom_call" | custom-call | tf_op jit(solution)/shard_map/pallas_call | solution.py:286
  122.1 1.5 collective-permute-done.15
  123.5 1.0 multiply_add_fusion.2
  125.2 5.0 %collective-permute-done.16 = f32[4,64,128]{2,1,0:T(8,128)S(1)} collective-permute-done((f32[4,64,128]{2,1,0:T(8,128)S(1)}, f32[4,64,128]{2,1,0:T(8,128)S(1)}, u32[]{:S(2)}, u32[]{:S(2)}) %collective-permute-start.16) | collective-permute-done | bytes 131104 | tf_op jit(solution)/shard_map/ppermute | solution.py:419
  130.3 1.4 collective-permute-start.17
  131.9 3.4 %collective-permute-done.17 = f32[4,64,128]{2,1,0:T(8,128)S(1)} collective-permute-done((f32[4,64,128]{2,1,0:T(8,128)S(1)}, f32[4,64,128]{2,1,0:T(8,128)S(1)}, u32[]{:S(2)}, u32[]{:S(2)}) %collective-permute-start.17) | collective-permute-done | bytes 131104 | tf_op jit(solution)/shard_map/ppermute | solution.py:419
  135.4 0.9 multiply_add_fusion.refs_3_
  136.2 6.3 %shard_map.101 = f32[4,64,128]{2,1,0:T(8,128)} custom-call(s32[134]{0:T(256)} %pad_add_fusion.pos_ref, f32[4,64,128]{2,1,0:T(8,128)} %add.79.refs_0_, f32[2,64,64,128]{3,2,1,0:T(8,128)} %broadcast_in_dim.91.refs_1_.ew_ref.refs_2_.refs_5_.refs_6_, f32[2,64,64,128]{3,2,1,0:T(8,128)} %get-tuple-element.47.refs_2_, f32[4,64,128]{2,1,0:T(8,128)} %multiply_add_fusion.refs_3_, ...), custom_call_target="tpu_custom_call" | custom-call | tf_op jit(solution)/shard_map/pallas_call | solution.py:286
  142.5 1.0 reduce_sum.52
  144.5 3.3 %reduce_sum.48 = f32[2,64,64]{2,1,0:T(8,128)S(1)} reduce(f32[2,64,64,128]{3,2,1,0:T(8,128)} %get-tuple-element.46, f32[]{:T(128)} %constant.7.clone.1), dimensions={3}, to_apply=%region_3.4 | reduce | flops 1040384 | bytes 4227076 | tf_op jit(solution)/shard_map/reduce_sum | solution.py:559
  147.8 1.1 collective-permute-start.19
  149.8 2.6 %collective-permute-done.19 = f32[2,128]{1,0:T(2,128)S(1)} collective-permute-done((f32[2,128]{1,0:T(2,128)S(1)}, f32[2,128]{1,0:T(2,128)S(1)}, u32[]{:S(2)}, u32[]{:S(2)}) %collective-permute-start.19) | collective-permute-done | bytes 1056 | tf_op jit(solution)/shard_map/ppermute | solution.py:419
  (70 shorter events, 13.3 us)
Async XLA Ops:
  7.8 8.9 %copy-start.3 = (s32[256,128]{1,0:T(8,128)S(1)}, s32[256,128]{1,0:T(8,128)}, u32[]{:S(2)}) copy-start(s32[256,128]{1,0:T(8,128)} %param.11) | copy-start | bytes 393220
  7.8 12.5 %copy-start.4 = (s32[1,1,2,2]{3,2,1,0:T(2,128)S(1)}, s32[1,1,2,2]{3,2,1,0:T(2,128)}, u32[]{:S(2)}) copy-start(s32[1,1,2,2]{3,2,1,0:T(2,128)} %param.8) | copy-start | bytes 52
  16.3 1.2 collective-permute-start
  17.5 4.4 %collective-permute-start.1 = (f32[2,128]{1,0:T(2,128)S(1)}, f32[2,128]{1,0:T(2,128)S(1)}, u32[]{:S(2)}, u32[]{:S(2)}) collective-permute-start(f32[2,128]{1,0:T(2,128)S(1)} %mul.88), channel_id=1, source_target_pairs={{0,2},{1,3},{2,0},{3,1},{4,6},{5,7},{6,4},{7,5},{8,10},{9,11},{10,... | collective-permute-start | bytes 3080 | tf_op jit(solution)/shard_map/ppermute | solution.py:419
  21.9 3.6 %collective-permute-start.2 = (f32[2,128]{1,0:T(2,128)S(1)}, f32[2,128]{1,0:T(2,128)S(1)}, u32[]{:S(2)}, u32[]{:S(2)}) collective-permute-start(f32[2,128]{1,0:T(2,128)S(1)} %mul.90), channel_id=1, source_target_pairs={{0,4},{1,5},{2,6},{3,7},{4,0},{5,1},{6,2},{7,3},{8,12},{9,13},{10,... | collective-permute-start | bytes 3080 | tf_op jit(solution)/shard_map/ppermute | solution.py:419
  32.5 5.4 %collective-permute-start.3 = (f32[4,64,128]{2,1,0:T(8,128)}, f32[4,64,128]{2,1,0:T(8,128)S(1)}, u32[]{:S(2)}, u32[]{:S(2)}) collective-permute-start(f32[4,64,128]{2,1,0:T(8,128)} %get-tuple-element.31), channel_id=1, source_target_pairs={{0,8},{8,0},{16,24},{24,16},{1,9},{9,1},{17,25},{25,17},{2,10},{10... | collective-permute-start | bytes 393224 | tf_op jit(solution)/shard_map/ppermute | solution.py:419
  38.8 5.9 %collective-permute-start.4 = (f32[4,64,128]{2,1,0:T(8,128)S(1)}, f32[4,64,128]{2,1,0:T(8,128)S(1)}, u32[]{:S(2)}, u32[]{:S(2)}) collective-permute-start(f32[4,64,128]{2,1,0:T(8,128)S(1)} %add.80), channel_id=1, source_target_pairs={{0,16},{8,24},{16,0},{24,8},{1,17},{9,25},{17,1},{25,9},{2,18},{10... | collective-permute-start | bytes 393224 | tf_op jit(solution)/shard_map/ppermute | solution.py:419
  51.7 1.6 %collective-permute-start.5 = (f32[4,64,128]{2,1,0:T(8,128)}, f32[4,64,128]{2,1,0:T(8,128)S(1)}, u32[]{:S(2)}, u32[]{:S(2)}) collective-permute-start(f32[4,64,128]{2,1,0:T(8,128)} %get-tuple-element.35), channel_id=1, source_target_pairs={{0,1},{1,0},{2,3},{3,2},{4,5},{5,4},{6,7},{7,6},{8,9},{9,8},{10,11... | collective-permute-start | bytes 393224 | tf_op jit(solution)/shard_map/ppermute | solution.py:419
  54.2 5.9 %collective-permute-start.6 = (f32[4,64,128]{2,1,0:T(8,128)S(1)}, f32[4,64,128]{2,1,0:T(8,128)S(1)}, u32[]{:S(2)}, u32[]{:S(2)}) collective-permute-start(f32[4,64,128]{2,1,0:T(8,128)S(1)} %mul.92), channel_id=1, source_target_pairs={{0,2},{1,3},{2,0},{3,1},{4,6},{5,7},{6,4},{7,5},{8,10},{9,11},{10,... | collective-permute-start | bytes 393224 | tf_op jit(solution)/shard_map/ppermute | solution.py:419
  60.2 5.1 %collective-permute-start.7 = (f32[4,64,128]{2,1,0:T(8,128)S(1)}, f32[4,64,128]{2,1,0:T(8,128)S(1)}, u32[]{:S(2)}, u32[]{:S(2)}) collective-permute-start(f32[4,64,128]{2,1,0:T(8,128)S(1)} %mul.94), channel_id=1, source_target_pairs={{0,4},{1,5},{2,6},{3,7},{4,0},{5,1},{6,2},{7,3},{8,12},{9,13},{10,... | collective-permute-start | bytes 393224 | tf_op jit(solution)/shard_map/ppermute | solution.py:419
  66.0 9.3 %copy-start.1 = (f32[4,64,128]{2,1,0:T(8,128)S(1)}, f32[4,64,128]{2,1,0:T(8,128)}, u32[]{:S(2)}) copy-start(f32[4,64,128]{2,1,0:T(8,128)} %get-tuple-element.35) | copy-start | bytes 393220
  73.6 1.6 %collective-permute-start.10 = (f32[4,64,128]{2,1,0:T(8,128)}, f32[4,64,128]{2,1,0:T(8,128)S(1)}, u32[]{:S(2)}, u32[]{:S(2)}) collective-permute-start(f32[4,64,128]{2,1,0:T(8,128)} %get-tuple-element.40), channel_id=1, source_target_pairs={{0,1},{1,0},{2,3},{3,2},{4,5},{5,4},{6,7},{7,6},{8,9},{9,8},{10,11... | collective-permute-start | bytes 393224 | tf_op jit(solution)/shard_map/ppermute | solution.py:419
  76.2 5.6 %collective-permute-start.11 = (f32[4,64,128]{2,1,0:T(8,128)S(1)}, f32[4,64,128]{2,1,0:T(8,128)S(1)}, u32[]{:S(2)}, u32[]{:S(2)}) collective-permute-start(f32[4,64,128]{2,1,0:T(8,128)S(1)} %multiply_add_fusion.5), channel_id=1, source_target_pairs={{0,2},{1,3},{2,0},{3,1},{4,6},{5,7},{6,4},{7,5},{8,10},{9,11},{10,... | collective-permute-start | bytes 393224 | tf_op jit(solution)/shard_map/ppermute | solution.py:419
  81.8 7.6 %collective-permute-start.12 = (f32[4,64,128]{2,1,0:T(8,128)S(1)}, f32[4,64,128]{2,1,0:T(8,128)S(1)}, u32[]{:S(2)}, u32[]{:S(2)}) collective-permute-start(f32[4,64,128]{2,1,0:T(8,128)S(1)} %multiply_add_fusion.4), channel_id=1, source_target_pairs={{0,4},{1,5},{2,6},{3,7},{4,0},{5,1},{6,2},{7,3},{8,12},{9,13},{10,... | collective-permute-start | bytes 393224 | tf_op jit(solution)/shard_map/ppermute | solution.py:419
  98.1 5.2 %collective-permute-start.13 = (f32[4,64,128]{2,1,0:T(8,128)}, f32[4,64,128]{2,1,0:T(8,128)S(1)}, u32[]{:S(2)}, u32[]{:S(2)}) collective-permute-start(f32[4,64,128]{2,1,0:T(8,128)} %get-tuple-element.43), channel_id=1, source_target_pairs={{0,8},{8,0},{16,24},{24,16},{1,9},{9,1},{17,25},{25,17},{2,10},{10... | collective-permute-start | bytes 393224 | tf_op jit(solution)/shard_map/ppermute | solution.py:419
  104.3 7.3 %collective-permute-start.14 = (f32[4,64,128]{2,1,0:T(8,128)S(1)}, f32[4,64,128]{2,1,0:T(8,128)S(1)}, u32[]{:S(2)}, u32[]{:S(2)}) collective-permute-start(f32[4,64,128]{2,1,0:T(8,128)S(1)} %add.91), channel_id=1, source_target_pairs={{0,16},{8,24},{16,0},{24,8},{1,17},{9,25},{17,1},{25,9},{2,18},{10... | collective-permute-start | bytes 393224 | tf_op jit(solution)/shard_map/ppermute | solution.py:419
  112.2 12.6 %copy-start = (f32[256,128]{1,0:T(8,128)S(1)}, f32[256,128]{1,0:T(8,128)}, u32[]{:S(2)}) copy-start(f32[256,128]{1,0:T(8,128)} %param.13) | copy-start | bytes 393220
  112.2 12.9 %copy-start.2 = (f32[4,64,128]{2,1,0:T(8,128)S(1)}, f32[4,64,128]{2,1,0:T(8,128)}, u32[]{:S(2)}) copy-start(f32[4,64,128]{2,1,0:T(8,128)} %get-tuple-element.38) | copy-start | bytes 393220
  121.9 1.6 %collective-permute-start.15 = (f32[4,64,128]{2,1,0:T(8,128)}, f32[4,64,128]{2,1,0:T(8,128)S(1)}, u32[]{:S(2)}, u32[]{:S(2)}) collective-permute-start(f32[4,64,128]{2,1,0:T(8,128)} %get-tuple-element.48), channel_id=1, source_target_pairs={{0,1},{1,0},{2,3},{3,2},{4,5},{5,4},{6,7},{7,6},{8,9},{9,8},{10,11... | collective-permute-start | bytes 393224 | tf_op jit(solution)/shard_map/ppermute | solution.py:419
  124.6 5.6 %collective-permute-start.16 = (f32[4,64,128]{2,1,0:T(8,128)S(1)}, f32[4,64,128]{2,1,0:T(8,128)S(1)}, u32[]{:S(2)}, u32[]{:S(2)}) collective-permute-start(f32[4,64,128]{2,1,0:T(8,128)S(1)} %multiply_add_fusion.2), channel_id=1, source_target_pairs={{0,2},{1,3},{2,0},{3,1},{4,6},{5,7},{6,4},{7,5},{8,10},{9,11},{10,... | collective-permute-start | bytes 393224 | tf_op jit(solution)/shard_map/ppermute | solution.py:419
  125.1 6.7 %collective-permute-start.8 = (f32[4,64,128]{2,1,0:T(8,128)S(1)}, f32[4,64,128]{2,1,0:T(8,128)S(1)}, u32[]{:S(2)}, u32[]{:S(2)}) collective-permute-start(f32[4,64,128]{2,1,0:T(8,128)S(1)} %copy-done.2), channel_id=1, source_target_pairs={{0,8},{8,0},{16,24},{24,16},{1,9},{9,1},{17,25},{25,17},{2,10},{10... | collective-permute-start | bytes 393224 | tf_op jit(solution)/shard_map/ppermute | solution.py:419
  130.3 5.0 %collective-permute-start.17 = (f32[4,64,128]{2,1,0:T(8,128)S(1)}, f32[4,64,128]{2,1,0:T(8,128)S(1)}, u32[]{:S(2)}, u32[]{:S(2)}) collective-permute-start(f32[4,64,128]{2,1,0:T(8,128)S(1)} %multiply_add_fusion.1), channel_id=1, source_target_pairs={{0,4},{1,5},{2,6},{3,7},{4,0},{5,1},{6,2},{7,3},{8,12},{9,13},{10,... | collective-permute-start | bytes 393224 | tf_op jit(solution)/shard_map/ppermute | solution.py:419
  131.9 11.9 %collective-permute-start.9 = (f32[4,64,128]{2,1,0:T(8,128)S(1)}, f32[4,64,128]{2,1,0:T(8,128)S(1)}, u32[]{:S(2)}, u32[]{:S(2)}) collective-permute-start(f32[4,64,128]{2,1,0:T(8,128)S(1)} %add.83), channel_id=1, source_target_pairs={{0,16},{8,24},{16,0},{24,8},{1,17},{9,25},{17,1},{25,9},{2,18},{10... | collective-permute-start | bytes 393224 | tf_op jit(solution)/shard_map/ppermute | solution.py:419
  143.6 4.2 %collective-permute-start.18 = (f32[2,128]{1,0:T(2,128)S(1)}, f32[2,128]{1,0:T(2,128)S(1)}, u32[]{:S(2)}, u32[]{:S(2)}) collective-permute-start(f32[2,128]{1,0:T(2,128)S(1)} %reshape.64), channel_id=1, source_target_pairs={{0,8},{8,0},{16,24},{24,16},{1,9},{9,1},{17,25},{25,17},{2,10},{10... | collective-permute-start | bytes 3080 | tf_op jit(solution)/shard_map/ppermute | solution.py:419
  147.8 4.5 %collective-permute-start.19 = (f32[2,128]{1,0:T(2,128)S(1)}, f32[2,128]{1,0:T(2,128)S(1)}, u32[]{:S(2)}, u32[]{:S(2)}) collective-permute-start(f32[2,128]{1,0:T(2,128)S(1)} %add.99), channel_id=1, source_target_pairs={{0,16},{8,24},{16,0},{24,8},{1,17},{9,25},{17,1},{25,9},{2,18},{10... | collective-permute-start | bytes 3080 | tf_op jit(solution)/shard_map/ppermute | solution.py:419

commit v10 on v9

--- a/solution.py
+++ b/solution.py
@@ -13,7 +13,7 @@
 DAMP = 0.97
 EXACT = lax.Precision.HIGHEST
 F32 = jnp.float32
-UNROLL = 4
+UNROLL = 8
 
 
 def linear_both(values, axis):

time: 154 us -> 155 us (level)
  starting transfers between devices: 22.1 us -> 31.5 us
  waiting for transfers between devices: 46.6 us -> 42.6 us
  Pallas kernels: 54.9 us -> 51.6 us
    ppermute x20, starting transfers between devices: 22.1 us -> 31.5 us  [_swap(): return lax.ppermute(value, axis, perm)]
    ppermute x20, waiting for transfers between devices: 46.6 us -> 42.6 us  [_swap(): return lax.ppermute(value, axis, perm)]
    pallas_call x8, Pallas kernels: 54.9 us -> 51.6 us  [_call(): pl.pallas_call(kernel, grid_spec=grid_spec, out_shape=[o for kind, o in o...]
  transfers between devices with their start and end apart: 20 -> 20, of which waited for: 16 -> 17; matrix products, arithmetic and copies ran while one was open for 6% -> 6% of each run, Pallas kernels for 8% -> 7%
where the time goes in v10:
time: 155 us
  Pallas kernels  51.6 us (33%)
  waiting for transfers between devices  42.6 us (27%)
  starting transfers between devices  31.5 us (20%)
  other arithmetic  16.5 us (11%)
  local copies, waits for them, and re-layouts  11 us (7%)
    pallas_call x8, Pallas kernels, _call(): pl.pallas_call(kernel, grid_spec=grid_spec, out_shape=[o for kind, o in o...  51.6 us
    ppermute x20, waiting for transfers between devices, _swap(): return lax.ppermute(value, axis, perm)  42.6 us
    ppermute x20, starting transfers between devices, _swap(): return lax.ppermute(value, axis, perm)  31.5 us
    reduce_sum x1, other arithmetic, body(): jnp.sum(acc, axis=3)  3.34 us
  transfers between devices with their start and end apart: 20, of which 17 were waited for; matrix products, arithmetic and copies ran while one was open for 6% of the time, Pallas kernels for 7%

profile of v10, /device:TPU:0, one launch (start us, length us, event | category | flops | bytes accessed | tf_op | source)
XLA Modules:
  0.0 155.0 jit_solution(8156683863635268002)
XLA Ops:
  0.6 0.9 squeeze.10
  2.7 1.0 sort.17
  5.4 0.9 reshape_squeeze.10
  7.8 2.5 %broadcast_in_dim.91.refs_1_.ew_ref.refs_2_.refs_5_.refs_6_ = f32[2,64,64,128]{3,2,1,0:T(8,128)} broadcast(f32[2,64,64]{2,1,0:T(8,128)S(1)} %multiply_bitcast_fusion), dimensions={0,1,2} | broadcast | bytes 4227072 | tf_op jit(solution)/shard_map/broadcast_in_dim | solution.py:514
  10.3 4.8 %shard_map.94 = (f32[2,64,64,128]{3,2,1,0:T(8,128)}, f32[2,64,128]{2,1,0:T(8,128)}, f32[4,64,128]{2,1,0:T(8,128)}, f32[2,64,128]{2,1,0:T(8,128)}) custom-call(s32[134]{0:T(256)} %pad_add_fusion.pos_ref, f32[4,64,128]{2,1,0:T(8,128)} %add.79.refs_0_, f32[2,64,64,128]{3,2,1,0:T(8,128)} %broadcast_in_dim.91.refs_1_.ew_ref.refs_2_.refs_5_.refs_6_), custom_call_target="tpu_custom_call" | custom-call | tf_op jit(solution)/shard_map/pallas_call | solution.py:286
  15.1 1.0 slice_reduce_fusion
  17.5 2.8 %collective-permute-start.1 = (f32[2,128]{1,0:T(2,128)S(1)}, f32[2,128]{1,0:T(2,128)S(1)}, u32[]{:S(2)}, u32[]{:S(2)}) collective-permute-start(f32[2,128]{1,0:T(2,128)S(1)} %mul.88), channel_id=1, source_target_pairs={{0,2},{1,3},{2,0},{3,1},{4,6},{5,7},{6,4},{7,5},{8,10},{9,11},{10,... | collective-permute-start | bytes 3080 | tf_op jit(solution)/shard_map/ppermute | solution.py:419
  20.4 1.4 collective-permute-done.1
  21.8 2.1 %collective-permute-start.2 = (f32[2,128]{1,0:T(2,128)S(1)}, f32[2,128]{1,0:T(2,128)S(1)}, u32[]{:S(2)}, u32[]{:S(2)}) collective-permute-start(f32[2,128]{1,0:T(2,128)S(1)} %mul.90), channel_id=1, source_target_pairs={{0,4},{1,5},{2,6},{3,7},{4,0},{5,1},{6,2},{7,3},{8,12},{9,13},{10,... | collective-permute-start | bytes 3080 | tf_op jit(solution)/shard_map/ppermute | solution.py:419
  26.3 5.6 %shard_map.95 = (f32[2,64,64,128]{3,2,1,0:T(8,128)}, f32[4,64,128]{2,1,0:T(8,128)}) custom-call(s32[134]{0:T(256)} %pad_add_fusion.pos_ref, f32[2,64,64,128]{3,2,1,0:T(8,128)} %get-tuple-element.28.ba_ref.refs_2_, f32[2,64,128]{2,1,0:T(8,128)} %copy.32.sign_ref.refs_2_.refs_3_, f32[2,64,128]{2,1,0:T(8,128)} %get-tuple-element.29.here_ref.refs_4_.refs_6_, ...), custom_call_target="tpu_custom_call" | custom-call | tf_op jit(solution)/shard_map/pallas_call | solution.py:286
  32.0 1.9 %collective-permute-start.3 = (f32[4,64,128]{2,1,0:T(8,128)}, f32[4,64,128]{2,1,0:T(8,128)S(1)}, u32[]{:S(2)}, u32[]{:S(2)}) collective-permute-start(f32[4,64,128]{2,1,0:T(8,128)} %get-tuple-element.31), channel_id=1, source_target_pairs={{0,8},{8,0},{16,24},{24,16},{1,9},{9,1},{17,25},{25,17},{2,10},{10... | collective-permute-start | bytes 393224 | tf_op jit(solution)/shard_map/ppermute | solution.py:419
  33.9 3.2 %collective-permute-done.3 = f32[4,64,128]{2,1,0:T(8,128)S(1)} collective-permute-done((f32[4,64,128]{2,1,0:T(8,128)}, f32[4,64,128]{2,1,0:T(8,128)S(1)}, u32[]{:S(2)}, u32[]{:S(2)}) %collective-permute-start.3) | collective-permute-done | bytes 131104 | tf_op jit(solution)/shard_map/ppermute | solution.py:419
  37.2 0.9 add.80
  38.1 3.1 %collective-permute-start.4 = (f32[4,64,128]{2,1,0:T(8,128)S(1)}, f32[4,64,128]{2,1,0:T(8,128)S(1)}, u32[]{:S(2)}, u32[]{:S(2)}) collective-permute-start(f32[4,64,128]{2,1,0:T(8,128)S(1)} %add.80), channel_id=1, source_target_pairs={{0,16},{8,24},{16,0},{24,8},{1,17},{9,25},{17,1},{25,9},{2,18},{10... | collective-permute-start | bytes 393224 | tf_op jit(solution)/shard_map/ppermute | solution.py:419
  41.2 4.4 %collective-permute-done.4 = f32[4,64,128]{2,1,0:T(8,128)S(1)} collective-permute-done((f32[4,64,128]{2,1,0:T(8,128)S(1)}, f32[4,64,128]{2,1,0:T(8,128)S(1)}, u32[]{:S(2)}, u32[]{:S(2)}) %collective-permute-start.4) | collective-permute-done | bytes 131104 | tf_op jit(solution)/shard_map/ppermute | solution.py:419
  46.3 5.6 %shard_map.96 = (f32[2,64,64,128]{3,2,1,0:T(8,128)}, f32[2,64,128]{2,1,0:T(8,128)}, f32[4,64,128]{2,1,0:T(8,128)}, f32[2,64,128]{2,1,0:T(8,128)}) custom-call(s32[134]{0:T(256)} %pad_add_fusion.pos_ref, f32[4,64,128]{2,1,0:T(8,128)} %add_add_fusion.1.refs_0_, f32[2,64,64,128]{3,2,1,0:T(8,128)} %get-tuple-element.32.refs_1_, ...), custom_call_target="tpu_custom_call" | custom-call | tf_op jit(solution)/shard_map/pallas_call | solution.py:286
  51.9 1.5 collective-permute-done.5
  53.5 0.9 mul.92
  54.4 2.0 %collective-permute-start.6 = (f32[4,64,128]{2,1,0:T(8,128)S(1)}, f32[4,64,128]{2,1,0:T(8,128)S(1)}, u32[]{:S(2)}, u32[]{:S(2)}) collective-permute-start(f32[4,64,128]{2,1,0:T(8,128)S(1)} %mul.92), channel_id=1, source_target_pairs={{0,2},{1,3},{2,0},{3,1},{4,6},{5,7},{6,4},{7,5},{8,10},{9,11},{10,... | collective-permute-start | bytes 393224 | tf_op jit(solution)/shard_map/ppermute | solution.py:419
  56.4 3.8 %collective-permute-done.6 = f32[4,64,128]{2,1,0:T(8,128)S(1)} collective-permute-done((f32[4,64,128]{2,1,0:T(8,128)S(1)}, f32[4,64,128]{2,1,0:T(8,128)S(1)}, u32[]{:S(2)}, u32[]{:S(2)}) %collective-permute-start.6) | collective-permute-done | bytes 131104 | tf_op jit(solution)/shard_map/ppermute | solution.py:419
  60.2 2.9 %collective-permute-start.7 = (f32[4,64,128]{2,1,0:T(8,128)S(1)}, f32[4,64,128]{2,1,0:T(8,128)S(1)}, u32[]{:S(2)}, u32[]{:S(2)}) collective-permute-start(f32[4,64,128]{2,1,0:T(8,128)S(1)} %mul.94), channel_id=1, source_target_pairs={{0,4},{1,5},{2,6},{3,7},{4,0},{5,1},{6,2},{7,3},{8,12},{9,13},{10,... | collective-permute-start | bytes 393224 | tf_op jit(solution)/shard_map/ppermute | solution.py:419
  63.1 3.0 %collective-permute-done.7 = f32[4,64,128]{2,1,0:T(8,128)S(1)} collective-permute-done((f32[4,64,128]{2,1,0:T(8,128)S(1)}, f32[4,64,128]{2,1,0:T(8,128)S(1)}, u32[]{:S(2)}, u32[]{:S(2)}) %collective-permute-start.7) | collective-permute-done | bytes 131104 | tf_op jit(solution)/shard_map/ppermute | solution.py:419
  66.7 7.8 %shard_map.98 = (f32[2,64,64,128]{3,2,1,0:T(8,128)}, f32[2,64,64,128]{3,2,1,0:T(8,128)}, f32[2,64,128]{2,1,0:T(8,128)}, f32[4,64,128]{2,1,0:T(8,128)}) custom-call(s32[134]{0:T(256)} %pad_add_fusion.pos_ref, f32[4,64,128]{2,1,0:T(8,128)} %bitcast.15, f32[2,64,64,128]{3,2,1,0:T(8,128)} %get-tuple-element.33.ba_ref.refs_1_, ...), custom_call_target="tpu_custom_call" | custom-call | tf_op jit(solution)/shard_map/pallas_call | solution.py:286
  74.6 1.5 collective-permute-done.10
  76.1 0.9 multiply_add_fusion.5
  77.1 1.0 collective-permute-start.11
  78.0 4.7 %collective-permute-done.11 = f32[4,64,128]{2,1,0:T(8,128)S(1)} collective-permute-done((f32[4,64,128]{2,1,0:T(8,128)S(1)}, f32[4,64,128]{2,1,0:T(8,128)S(1)}, u32[]{:S(2)}, u32[]{:S(2)}) %collective-permute-start.11) | collective-permute-done | bytes 131104 | tf_op jit(solution)/shard_map/ppermute | solution.py:419
  82.7 2.0 %collective-permute-start.12 = (f32[4,64,128]{2,1,0:T(8,128)S(1)}, f32[4,64,128]{2,1,0:T(8,128)S(1)}, u32[]{:S(2)}, u32[]{:S(2)}) collective-permute-start(f32[4,64,128]{2,1,0:T(8,128)S(1)} %multiply_add_fusion.4), channel_id=1, source_target_pairs={{0,4},{1,5},{2,6},{3,7},{4,0},{5,1},{6,2},{7,3},{8,12},{9,13},{10,... | collective-permute-start | bytes 393224 | tf_op jit(solution)/shard_map/ppermute | solution.py:419
  84.7 5.6 %shard_map.97 = (f32[2,64,64,128]{3,2,1,0:T(8,128)}, f32[4,64,128]{2,1,0:T(8,128)}) custom-call(s32[134]{0:T(256)} %pad_add_fusion.pos_ref, f32[2,64,64,128]{3,2,1,0:T(8,128)} %get-tuple-element.33.ba_ref.refs_1_, f32[2,64,128]{2,1,0:T(8,128)} %copy.32.sign_ref.refs_2_.refs_3_, f32[2,64,128]{2,1,0:T(8,128)} %get-tuple-element.34.here_ref.refs_3_.refs_7_, ...), custom_call_target="tpu_custom_call" | custom-call | tf_op jit(solution)/shard_map/pallas_call | solution.py:286
  91.0 7.3 %shard_map.99 = (f32[2,64,64,128]{3,2,1,0:T(8,128)}, f32[4,64,128]{2,1,0:T(8,128)}) custom-call(s32[134]{0:T(256)} %pad_add_fusion.pos_ref, f32[4,64,128]{2,1,0:T(8,128)} %add_add_fusion.1.refs_0_, f32[2,64,64,128]{3,2,1,0:T(8,128)} %get-tuple-element.32.refs_1_, f32[2,64,64,128]{3,2,1,0:T(8,128)} %broadcast_in_dim.91.refs_1_.ew_ref.refs_2_.refs_5_.refs_6_, ...), custom_call_target="tpu_custom_call" | custom-call | tf_op jit(solution)/shard_map/pallas_call | solution.py:286
  98.3 5.2 %collective-permute-done.13 = f32[4,64,128]{2,1,0:T(8,128)S(1)} collective-permute-done((f32[4,64,128]{2,1,0:T(8,128)}, f32[4,64,128]{2,1,0:T(8,128)S(1)}, u32[]{:S(2)}, u32[]{:S(2)}) %collective-permute-start.13) | collective-permute-done | bytes 131104 | tf_op jit(solution)/shard_map/ppermute | solution.py:419
  103.5 0.9 add.91
  104.4 2.1 %collective-permute-start.14 = (f32[4,64,128]{2,1,0:T(8,128)S(1)}, f32[4,64,128]{2,1,0:T(8,128)S(1)}, u32[]{:S(2)}, u32[]{:S(2)}) collective-permute-start(f32[4,64,128]{2,1,0:T(8,128)S(1)} %add.91), channel_id=1, source_target_pairs={{0,16},{8,24},{16,0},{24,8},{1,17},{9,25},{17,1},{25,9},{2,18},{10... | collective-permute-start | bytes 393224 | tf_op jit(solution)/shard_map/ppermute | solution.py:419
  106.5 5.3 %collective-permute-done.14 = f32[4,64,128]{2,1,0:T(8,128)S(1)} collective-permute-done((f32[4,64,128]{2,1,0:T(8,128)S(1)}, f32[4,64,128]{2,1,0:T(8,128)S(1)}, u32[]{:S(2)}, u32[]{:S(2)}) %collective-permute-start.14) | collective-permute-done | bytes 131104 | tf_op jit(solution)/shard_map/ppermute | solution.py:419
  112.4 9.6 %shard_map.100 = (f32[2,64,64,128]{3,2,1,0:T(8,128)}, f32[2,64,64,128]{3,2,1,0:T(8,128)}, f32[2,64,128]{2,1,0:T(8,128)}, f32[4,64,128]{2,1,0:T(8,128)}) custom-call(s32[134]{0:T(256)} %pad_add_fusion.pos_ref, f32[4,64,128]{2,1,0:T(8,128)} %get-tuple-element.52.refs_0_, f32[2,64,64,128]{3,2,1,0:T(8,128)} %get-tuple-element.44.refs_1_, ...), custom_call_target="tpu_custom_call" | custom-call | tf_op jit(solution)/shard_map/pallas_call | solution.py:286
  122.2 1.5 collective-permute-done.15
  123.7 1.0 multiply_add_fusion.2
  124.7 3.2 %collective-permute-start.16 = (f32[4,64,128]{2,1,0:T(8,128)S(1)}, f32[4,64,128]{2,1,0:T(8,128)S(1)}, u32[]{:S(2)}, u32[]{:S(2)}) collective-permute-start(f32[4,64,128]{2,1,0:T(8,128)S(1)} %multiply_add_fusion.2), channel_id=1, source_target_pairs={{0,2},{1,3},{2,0},{3,1},{4,6},{5,7},{6,4},{7,5},{8,10},{9,11},{10,... | collective-permute-start | bytes 393224 | tf_op jit(solution)/shard_map/ppermute | solution.py:419
  128.2 0.8 collective-permute-start.8
  129.0 2.7 %collective-permute-done.16 = f32[4,64,128]{2,1,0:T(8,128)S(1)} collective-permute-done((f32[4,64,128]{2,1,0:T(8,128)S(1)}, f32[4,64,128]{2,1,0:T(8,128)S(1)}, u32[]{:S(2)}, u32[]{:S(2)}) %collective-permute-start.16) | collective-permute-done | bytes 131104 | tf_op jit(solution)/shard_map/ppermute | solution.py:419
  132.1 1.4 collective-permute-done.8
  133.5 2.5 %collective-permute-start.9 = (f32[4,64,128]{2,1,0:T(8,128)S(1)}, f32[4,64,128]{2,1,0:T(8,128)S(1)}, u32[]{:S(2)}, u32[]{:S(2)}) collective-permute-start(f32[4,64,128]{2,1,0:T(8,128)S(1)} %add.83), channel_id=1, source_target_pairs={{0,16},{8,24},{16,0},{24,8},{1,17},{9,25},{17,1},{25,9},{2,18},{10... | collective-permute-start | bytes 393224 | tf_op jit(solution)/shard_map/ppermute | solution.py:419
  136.0 1.0 collective-permute-done.17
  136.9 0.9 multiply_add_fusion.refs_3_
  137.8 5.3 %shard_map.101 = f32[4,64,128]{2,1,0:T(8,128)} custom-call(s32[134]{0:T(256)} %pad_add_fusion.pos_ref, f32[4,64,128]{2,1,0:T(8,128)} %add.79.refs_0_, f32[2,64,64,128]{3,2,1,0:T(8,128)} %broadcast_in_dim.91.refs_1_.ew_ref.refs_2_.refs_5_.refs_6_, f32[2,64,64,128]{3,2,1,0:T(8,128)} %get-tuple-element.47.refs_2_, f32[4,64,128]{2,1,0:T(8,128)} %multiply_add_fusion.refs_3_, ...), custom_call_target="tpu_custom_call" | custom-call | tf_op jit(solution)/shard_map/pallas_call | solution.py:286
  143.2 1.0 reduce_sum.52
  145.6 3.3 %reduce_sum.48 = f32[2,64,64]{2,1,0:T(8,128)S(1)} reduce(f32[2,64,64,128]{3,2,1,0:T(8,128)} %get-tuple-element.46, f32[]{:T(128)} %constant.7.clone.1), dimensions={3}, to_apply=%region_3.4 | reduce | flops 1040384 | bytes 4227076 | tf_op jit(solution)/shard_map/reduce_sum | solution.py:559
  148.9 4.0 %collective-permute-start.19 = (f32[2,128]{1,0:T(2,128)S(1)}, f32[2,128]{1,0:T(2,128)S(1)}, u32[]{:S(2)}, u32[]{:S(2)}) collective-permute-start(f32[2,128]{1,0:T(2,128)S(1)} %add.99), channel_id=1, source_target_pairs={{0,16},{8,24},{16,0},{24,8},{1,17},{9,25},{17,1},{25,9},{2,18},{10... | collective-permute-start | bytes 3080 | tf_op jit(solution)/shard_map/ppermute | solution.py:419
  (70 shorter events, 14.9 us)
Async XLA Ops:
  7.8 8.9 %copy-start.3 = (s32[256,128]{1,0:T(8,128)S(1)}, s32[256,128]{1,0:T(8,128)}, u32[]{:S(2)}) copy-start(s32[256,128]{1,0:T(8,128)} %param.11) | copy-start | bytes 393220
  7.8 12.5 %copy-start.4 = (s32[1,1,2,2]{3,2,1,0:T(2,128)S(1)}, s32[1,1,2,2]{3,2,1,0:T(2,128)}, u32[]{:S(2)}) copy-start(s32[1,1,2,2]{3,2,1,0:T(2,128)} %param.8) | copy-start | bytes 52
  16.2 1.3 collective-permute-start
  17.5 4.4 %collective-permute-start.1 = (f32[2,128]{1,0:T(2,128)S(1)}, f32[2,128]{1,0:T(2,128)S(1)}, u32[]{:S(2)}, u32[]{:S(2)}) collective-permute-start(f32[2,128]{1,0:T(2,128)S(1)} %mul.88), channel_id=1, source_target_pairs={{0,2},{1,3},{2,0},{3,1},{4,6},{5,7},{6,4},{7,5},{8,10},{9,11},{10,... | collective-permute-start | bytes 3080 | tf_op jit(solution)/shard_map/ppermute | solution.py:419
  21.8 3.7 %collective-permute-start.2 = (f32[2,128]{1,0:T(2,128)S(1)}, f32[2,128]{1,0:T(2,128)S(1)}, u32[]{:S(2)}, u32[]{:S(2)}) collective-permute-start(f32[2,128]{1,0:T(2,128)S(1)} %mul.90), channel_id=1, source_target_pairs={{0,4},{1,5},{2,6},{3,7},{4,0},{5,1},{6,2},{7,3},{8,12},{9,13},{10,... | collective-permute-start | bytes 3080 | tf_op jit(solution)/shard_map/ppermute | solution.py:419
  32.0 5.2 %collective-permute-start.3 = (f32[4,64,128]{2,1,0:T(8,128)}, f32[4,64,128]{2,1,0:T(8,128)S(1)}, u32[]{:S(2)}, u32[]{:S(2)}) collective-permute-start(f32[4,64,128]{2,1,0:T(8,128)} %get-tuple-element.31), channel_id=1, source_target_pairs={{0,8},{8,0},{16,24},{24,16},{1,9},{9,1},{17,25},{25,17},{2,10},{10... | collective-permute-start | bytes 393224 | tf_op jit(solution)/shard_map/ppermute | solution.py:419
  38.1 7.4 %collective-permute-start.4 = (f32[4,64,128]{2,1,0:T(8,128)S(1)}, f32[4,64,128]{2,1,0:T(8,128)S(1)}, u32[]{:S(2)}, u32[]{:S(2)}) collective-permute-start(f32[4,64,128]{2,1,0:T(8,128)S(1)} %add.80), channel_id=1, source_target_pairs={{0,16},{8,24},{16,0},{24,8},{1,17},{9,25},{17,1},{25,9},{2,18},{10... | collective-permute-start | bytes 393224 | tf_op jit(solution)/shard_map/ppermute | solution.py:419
  51.9 1.6 %collective-permute-start.5 = (f32[4,64,128]{2,1,0:T(8,128)}, f32[4,64,128]{2,1,0:T(8,128)S(1)}, u32[]{:S(2)}, u32[]{:S(2)}) collective-permute-start(f32[4,64,128]{2,1,0:T(8,128)} %get-tuple-element.35), channel_id=1, source_target_pairs={{0,1},{1,0},{2,3},{3,2},{4,5},{5,4},{6,7},{7,6},{8,9},{9,8},{10,11... | collective-permute-start | bytes 393224 | tf_op jit(solution)/shard_map/ppermute | solution.py:419
  54.4 5.8 %collective-permute-start.6 = (f32[4,64,128]{2,1,0:T(8,128)S(1)}, f32[4,64,128]{2,1,0:T(8,128)S(1)}, u32[]{:S(2)}, u32[]{:S(2)}) collective-permute-start(f32[4,64,128]{2,1,0:T(8,128)S(1)} %mul.92), channel_id=1, source_target_pairs={{0,2},{1,3},{2,0},{3,1},{4,6},{5,7},{6,4},{7,5},{8,10},{9,11},{10,... | collective-permute-start | bytes 393224 | tf_op jit(solution)/shard_map/ppermute | solution.py:419
  60.2 5.9 %collective-permute-start.7 = (f32[4,64,128]{2,1,0:T(8,128)S(1)}, f32[4,64,128]{2,1,0:T(8,128)S(1)}, u32[]{:S(2)}, u32[]{:S(2)}) collective-permute-start(f32[4,64,128]{2,1,0:T(8,128)S(1)} %mul.94), channel_id=1, source_target_pairs={{0,4},{1,5},{2,6},{3,7},{4,0},{5,1},{6,2},{7,3},{8,12},{9,13},{10,... | collective-permute-start | bytes 393224 | tf_op jit(solution)/shard_map/ppermute | solution.py:419
  66.7 9.4 %copy-start.1 = (f32[4,64,128]{2,1,0:T(8,128)S(1)}, f32[4,64,128]{2,1,0:T(8,128)}, u32[]{:S(2)}) copy-start(f32[4,64,128]{2,1,0:T(8,128)} %get-tuple-element.35) | copy-start | bytes 393220
  74.5 1.6 %collective-permute-start.10 = (f32[4,64,128]{2,1,0:T(8,128)}, f32[4,64,128]{2,1,0:T(8,128)S(1)}, u32[]{:S(2)}, u32[]{:S(2)}) collective-permute-start(f32[4,64,128]{2,1,0:T(8,128)} %get-tuple-element.40), channel_id=1, source_target_pairs={{0,1},{1,0},{2,3},{3,2},{4,5},{5,4},{6,7},{7,6},{8,9},{9,8},{10,11... | collective-permute-start | bytes 393224 | tf_op jit(solution)/shard_map/ppermute | solution.py:419
  77.1 5.6 %collective-permute-start.11 = (f32[4,64,128]{2,1,0:T(8,128)S(1)}, f32[4,64,128]{2,1,0:T(8,128)S(1)}, u32[]{:S(2)}, u32[]{:S(2)}) collective-permute-start(f32[4,64,128]{2,1,0:T(8,128)S(1)} %multiply_add_fusion.5), channel_id=1, source_target_pairs={{0,2},{1,3},{2,0},{3,1},{4,6},{5,7},{6,4},{7,5},{8,10},{9,11},{10,... | collective-permute-start | bytes 393224 | tf_op jit(solution)/shard_map/ppermute | solution.py:419
  82.7 7.6 %collective-permute-start.12 = (f32[4,64,128]{2,1,0:T(8,128)S(1)}, f32[4,64,128]{2,1,0:T(8,128)S(1)}, u32[]{:S(2)}, u32[]{:S(2)}) collective-permute-start(f32[4,64,128]{2,1,0:T(8,128)S(1)} %multiply_add_fusion.4), channel_id=1, source_target_pairs={{0,4},{1,5},{2,6},{3,7},{4,0},{5,1},{6,2},{7,3},{8,12},{9,13},{10,... | collective-permute-start | bytes 393224 | tf_op jit(solution)/shard_map/ppermute | solution.py:419
  98.3 5.2 %collective-permute-start.13 = (f32[4,64,128]{2,1,0:T(8,128)}, f32[4,64,128]{2,1,0:T(8,128)S(1)}, u32[]{:S(2)}, u32[]{:S(2)}) collective-permute-start(f32[4,64,128]{2,1,0:T(8,128)} %get-tuple-element.43), channel_id=1, source_target_pairs={{0,8},{8,0},{16,24},{24,16},{1,9},{9,1},{17,25},{25,17},{2,10},{10... | collective-permute-start | bytes 393224 | tf_op jit(solution)/shard_map/ppermute | solution.py:419
  104.4 7.3 %collective-permute-start.14 = (f32[4,64,128]{2,1,0:T(8,128)S(1)}, f32[4,64,128]{2,1,0:T(8,128)S(1)}, u32[]{:S(2)}, u32[]{:S(2)}) collective-permute-start(f32[4,64,128]{2,1,0:T(8,128)S(1)} %add.91), channel_id=1, source_target_pairs={{0,16},{8,24},{16,0},{24,8},{1,17},{9,25},{17,1},{25,9},{2,18},{10... | collective-permute-start | bytes 393224 | tf_op jit(solution)/shard_map/ppermute | solution.py:419
  112.4 15.5 %copy-start = (f32[256,128]{1,0:T(8,128)S(1)}, f32[256,128]{1,0:T(8,128)}, u32[]{:S(2)}) copy-start(f32[256,128]{1,0:T(8,128)} %param.13) | copy-start | bytes 393220
  112.4 15.7 %copy-start.2 = (f32[4,64,128]{2,1,0:T(8,128)S(1)}, f32[4,64,128]{2,1,0:T(8,128)}, u32[]{:S(2)}) copy-start(f32[4,64,128]{2,1,0:T(8,128)} %get-tuple-element.38) | copy-start | bytes 393220
  122.1 1.6 %collective-permute-start.15 = (f32[4,64,128]{2,1,0:T(8,128)}, f32[4,64,128]{2,1,0:T(8,128)S(1)}, u32[]{:S(2)}, u32[]{:S(2)}) collective-permute-start(f32[4,64,128]{2,1,0:T(8,128)} %get-tuple-element.48), channel_id=1, source_target_pairs={{0,1},{1,0},{2,3},{3,2},{4,5},{5,4},{6,7},{7,6},{8,9},{9,8},{10,11... | collective-permute-start | bytes 393224 | tf_op jit(solution)/shard_map/ppermute | solution.py:419
  124.7 7.0 %collective-permute-start.16 = (f32[4,64,128]{2,1,0:T(8,128)S(1)}, f32[4,64,128]{2,1,0:T(8,128)S(1)}, u32[]{:S(2)}, u32[]{:S(2)}) collective-permute-start(f32[4,64,128]{2,1,0:T(8,128)S(1)} %multiply_add_fusion.2), channel_id=1, source_target_pairs={{0,2},{1,3},{2,0},{3,1},{4,6},{5,7},{6,4},{7,5},{8,10},{9,11},{10,... | collective-permute-start | bytes 393224 | tf_op jit(solution)/shard_map/ppermute | solution.py:419
  128.2 5.3 %collective-permute-start.8 = (f32[4,64,128]{2,1,0:T(8,128)S(1)}, f32[4,64,128]{2,1,0:T(8,128)S(1)}, u32[]{:S(2)}, u32[]{:S(2)}) collective-permute-start(f32[4,64,128]{2,1,0:T(8,128)S(1)} %copy-done.2), channel_id=1, source_target_pairs={{0,8},{8,0},{16,24},{24,16},{1,9},{9,1},{17,25},{25,17},{2,10},{10... | collective-permute-start | bytes 393224 | tf_op jit(solution)/shard_map/ppermute | solution.py:419
  131.8 5.1 %collective-permute-start.17 = (f32[4,64,128]{2,1,0:T(8,128)S(1)}, f32[4,64,128]{2,1,0:T(8,128)S(1)}, u32[]{:S(2)}, u32[]{:S(2)}) collective-permute-start(f32[4,64,128]{2,1,0:T(8,128)S(1)} %multiply_add_fusion.1), channel_id=1, source_target_pairs={{0,4},{1,5},{2,6},{3,7},{4,0},{5,1},{6,2},{7,3},{8,12},{9,13},{10,... | collective-permute-start | bytes 393224 | tf_op jit(solution)/shard_map/ppermute | solution.py:419
  133.5 11.4 %collective-permute-start.9 = (f32[4,64,128]{2,1,0:T(8,128)S(1)}, f32[4,64,128]{2,1,0:T(8,128)S(1)}, u32[]{:S(2)}, u32[]{:S(2)}) collective-permute-start(f32[4,64,128]{2,1,0:T(8,128)S(1)} %add.83), channel_id=1, source_target_pairs={{0,16},{8,24},{16,0},{24,8},{1,17},{9,25},{17,1},{25,9},{2,18},{10... | collective-permute-start | bytes 393224 | tf_op jit(solution)/shard_map/ppermute | solution.py:419
  144.3 4.7 %collective-permute-start.18 = (f32[2,128]{1,0:T(2,128)S(1)}, f32[2,128]{1,0:T(2,128)S(1)}, u32[]{:S(2)}, u32[]{:S(2)}) collective-permute-start(f32[2,128]{1,0:T(2,128)S(1)} %reshape.64), channel_id=1, source_target_pairs={{0,8},{8,0},{16,24},{24,16},{1,9},{9,1},{17,25},{25,17},{2,10},{10... | collective-permute-start | bytes 3080 | tf_op jit(solution)/shard_map/ppermute | solution.py:419
  148.9 5.5 %collective-permute-start.19 = (f32[2,128]{1,0:T(2,128)S(1)}, f32[2,128]{1,0:T(2,128)S(1)}, u32[]{:S(2)}, u32[]{:S(2)}) collective-permute-start(f32[2,128]{1,0:T(2,128)S(1)} %add.99), channel_id=1, source_target_pairs={{0,16},{8,24},{16,0},{24,8},{1,17},{9,25},{17,1},{25,9},{2,18},{10... | collective-permute-start | bytes 3080 | tf_op jit(solution)/shard_map/ppermute | solution.py:419

commit v11 on v9

--- a/solution.py
+++ b/solution.py
@@ -157,21 +157,25 @@
     _loop(count, body, 0)
 
 
-def _bwd_messages_kernel(has_next, has_acc, slots, pos_ref, *refs):
+def _bwd_messages_kernel(has_next, has_acc, emit_column, slots, pos_ref, *refs):
     refs = list(refs)
     gsp_ref = refs.pop(0)
     gm_ref = refs.pop(0) if has_next else None
     ba_ref, sign_ref, here_ref, others_ref, ew_ref = refs[:5]
     refs = refs[5:]
     acc_ref = refs.pop(0) if has_acc else None
-    gw_ref, gba_ref, ghere_ref, gothers_ref = refs
+    gw_ref, gba_ref, ghere_ref, gothers_ref = refs[:4]
+    col_ref = refs[4] if emit_column else None
     k = pl.program_id(0)
     n_c = ba_ref.shape[1]
     shape = ba_ref.shape[2:]
+    q = _col_block(pos_ref, k)
 
     @pl.when(k == 0)
     def _():
         gothers_ref[...] = jnp.zeros(gothers_ref.shape, F32)
+        if emit_column:
+            col_ref[...] = jnp.zeros(col_ref.shape, F32)
 
     p = _row_block(pos_ref, k)
     sign = sign_ref[k]
@@ -189,7 +193,11 @@
         x = ba * f
         low = 1.0 - DAMP * x
         high = 1.0 + DAMP * x
-        gw = gu * jnp.log(high / low)
+        ratio = jnp.log(high / low)
+        if emit_column:
+            u = ew_ref[0, c] * ratio
+            col_ref[q, pl.ds(c, 1), :] = col_ref[q, pl.ds(c, 1), :] + jnp.sum(u, axis=0, keepdims=True)
+        gw = gu * ratio
         if has_acc:
             gw = gw + acc_ref[0, c]
         gw_ref[0, c] = gw
@@ -325,7 +333,7 @@
     return _call(functools.partial(_fwd_messages_kernel, k), pos, inputs, outs)
 
 
-def bwd_messages(pos, gsp, gm, ba, sign, here, others, ew, acc):
+def bwd_messages(pos, gsp, gm, ba, sign, here, others, ew, acc, col_blocks=0):
     k, c, r, s = ba.shape
     has_next = gm is not None
     has_acc = acc is not None
@@ -341,7 +349,11 @@
         ("full", jax.ShapeDtypeStruct(here.shape, F32)),
         ("full", jax.ShapeDtypeStruct(others.shape, F32)),
     ]
-    return _call(functools.partial(_bwd_messages_kernel, has_next, has_acc, k), pos, inputs, outs)
+    if col_blocks:
+        outs.append(("full", jax.ShapeDtypeStruct((col_blocks, c, s), F32)))
+    return _call(
+        functools.partial(_bwd_messages_kernel, has_next, has_acc, col_blocks > 0, k), pos, inputs, outs
+    )
 
 
 def bwd_products(pos, spread, u, ew, gba, grows, ghere, whole, here, col_blocks, emit_gm):
@@ -523,11 +535,10 @@
         ba, whole, rows, others_here = fwd_products(pos, spread, u, ew, check_blocks)
         others, trail = others_forward(rows, check_blocks, n_var, uniform=(step == 0 and (check_blocks * TILE) % shots == 0))
         saved.append((spread, u, ba, whole, others_here, others, trail))
-        u, column = fwd_messages(pos, ba, sign_slot, others_here, others, ew, column_blocks)
         if step + 1 < ITERS:
+            u, column = fwd_messages(pos, ba, sign_slot, others_here, others, ew, column_blocks)
             total = prior_dev[:, :, None] + checks_total(column, n_chk)
             spread = total
-    last_column = column
 
     grad_total = out_cot.reshape(column_blocks, TILE, shots)
     prior_grad = jnp.zeros((column_blocks, TILE), jnp.float32)
@@ -536,13 +547,16 @@
     for step in reversed(range(ITERS)):
         spread_t, u_prev, ba, whole, others_here, others, trail = saved[step]
         prior_grad = prior_grad + jnp.sum(grad_total, axis=2)
-        acc, grad_ba, grad_here, grad_others = bwd_messages(
-            pos, grad_total, grad_m, ba, sign_slot, others_here, others, ew, acc
-        )
         if step + 1 == ITERS:
-            last_column, grad_ba = lax.optimization_barrier((last_column, grad_ba))
+            acc, grad_ba, grad_here, grad_others, last_column = bwd_messages(
+                pos, grad_total, grad_m, ba, sign_slot, others_here, others, ew, acc, column_blocks
+            )
             total = prior_dev[:, :, None] + checks_total(last_column, n_chk)
             marginals = total.reshape(column_blocks * TILE, shots)
+        else:
+            acc, grad_ba, grad_here, grad_others = bwd_messages(
+                pos, grad_total, grad_m, ba, sign_slot, others_here, others, ew, acc
+            )
         grad_rows = others_backward(trail, grad_others, check_blocks, n_var)
         grad_m, column = bwd_products(
             pos, spread_t, u_prev, ew, grad_ba, grad_rows, grad_here, whole, others_here,

time: 154 us -> 152 us (0.987)
  Pallas kernels: 54.9 us -> 46.2 us
  starting transfers between devices: 22.1 us -> 27 us
  waiting for transfers between devices: 46.6 us -> 48.5 us
    pallas_call x8 -> x7, Pallas kernels: 54.9 us -> 46.2 us  [_call(): pl.pallas_call(kernel, grid_spec=grid_spec, out_shape=[o for kind, o in o...]
    ppermute x20, starting transfers between devices: 22.1 us -> 27 us  [_swap(): return lax.ppermute(value, axis, perm)]
    ppermute x20, waiting for transfers between devices: 46.6 us -> 48.5 us  [_swap(): return lax.ppermute(value, axis, perm)]
  transfers between devices with their start and end apart: 20 -> 20, of which waited for: 16 -> 18; matrix products, arithmetic and copies ran while one was open for 6% -> 6% of each run, Pallas kernels for 8% -> 4%
where the time goes in v11:
time: 152 us; the launch traced here: 151 us
  waiting for transfers between devices  48.5 us (32%)
  Pallas kernels  46.2 us (30%)
  starting transfers between devices  27 us (18%)
  other arithmetic  16.5 us (11%)
  local copies, waits for them, and re-layouts  11 us (7%)
    ppermute x20, waiting for transfers between devices, _swap(): return lax.ppermute(value, axis, perm)  48.5 us
    pallas_call x7, Pallas kernels, _call(): pl.pallas_call(kernel, grid_spec=grid_spec, out_shape=[o for kind, o in o...  46.2 us
    ppermute x20, starting transfers between devices, _swap(): return lax.ppermute(value, axis, perm)  27 us
    reduce_sum x1, other arithmetic, body(): jnp.sum(acc, axis=3)  3.34 us
  transfers between devices with their start and end apart: 20, of which 18 were waited for; matrix products, arithmetic and copies ran while one was open for 6% of the time, Pallas kernels for 4%

profile of v11, /device:TPU:0, one launch (start us, length us, event | category | flops | bytes accessed | tf_op | source)
XLA Modules:
  0.0 151.1 jit_solution(951575507442228829)
XLA Ops:
  0.6 0.9 squeeze.10
  2.7 1.0 sort.17
  4.6 0.9 reshape_squeeze.10
  7.0 2.5 %broadcast_in_dim.91.refs_1_.ew_ref.refs_2_.refs_5_.refs_6_ = f32[2,64,64,128]{3,2,1,0:T(8,128)} broadcast(f32[2,64,64]{2,1,0:T(8,128)S(1)} %multiply_bitcast_fusion), dimensions={0,1,2} | broadcast | bytes 4227072 | tf_op jit(solution)/shard_map/broadcast_in_dim | solution.py:526
  10.3 4.8 %shard_map.94 = (f32[2,64,64,128]{3,2,1,0:T(8,128)}, f32[2,64,128]{2,1,0:T(8,128)}, f32[4,64,128]{2,1,0:T(8,128)}, f32[2,64,128]{2,1,0:T(8,128)}) custom-call(s32[134]{0:T(256)} %pad_add_fusion.pos_ref, f32[4,64,128]{2,1,0:T(8,128)} %add.79.refs_0_, f32[2,64,64,128]{3,2,1,0:T(8,128)} %broadcast_in_dim.91.refs_1_.ew_ref.refs_2_.refs_5_.refs_6_), custom_call_target="tpu_custom_call" | custom-call | tf_op jit(solution)/shard_map/pallas_call | solution.py:294
  15.1 1.0 slice_reduce_fusion
  17.6 2.8 %collective-permute-start.1 = (f32[2,128]{1,0:T(2,128)S(1)}, f32[2,128]{1,0:T(2,128)S(1)}, u32[]{:S(2)}, u32[]{:S(2)}) collective-permute-start(f32[2,128]{1,0:T(2,128)S(1)} %mul.88), channel_id=1, source_target_pairs={{0,2},{1,3},{2,0},{3,1},{4,6},{5,7},{6,4},{7,5},{8,10},{9,11},{10,... | collective-permute-start | bytes 3080 | tf_op jit(solution)/shard_map/ppermute | solution.py:431
  20.5 1.4 collective-permute-done.1
  21.9 2.0 %collective-permute-start.2 = (f32[2,128]{1,0:T(2,128)S(1)}, f32[2,128]{1,0:T(2,128)S(1)}, u32[]{:S(2)}, u32[]{:S(2)}) collective-permute-start(f32[2,128]{1,0:T(2,128)S(1)} %mul.90), channel_id=1, source_target_pairs={{0,4},{1,5},{2,6},{3,7},{4,0},{5,1},{6,2},{7,3},{8,12},{9,13},{10,... | collective-permute-start | bytes 3080 | tf_op jit(solution)/shard_map/ppermute | solution.py:431
  26.3 5.6 %shard_map.95 = (f32[2,64,64,128]{3,2,1,0:T(8,128)}, f32[4,64,128]{2,1,0:T(8,128)}) custom-call(s32[134]{0:T(256)} %pad_add_fusion.pos_ref, f32[2,64,64,128]{3,2,1,0:T(8,128)} %get-tuple-element.26.ba_ref.refs_2_, f32[2,64,128]{2,1,0:T(8,128)} %copy.30.sign_ref.refs_2_.refs_3_, f32[2,64,128]{2,1,0:T(8,128)} %get-tuple-element.27.here_ref.refs_4_.refs_6_, ...), custom_call_target="tpu_custom_call" | custom-call | tf_op jit(solution)/shard_map/pallas_call | solution.py:294
  32.0 2.7 %collective-permute-start.3 = (f32[4,64,128]{2,1,0:T(8,128)}, f32[4,64,128]{2,1,0:T(8,128)S(1)}, u32[]{:S(2)}, u32[]{:S(2)}) collective-permute-start(f32[4,64,128]{2,1,0:T(8,128)} %get-tuple-element.29), channel_id=1, source_target_pairs={{0,8},{8,0},{16,24},{24,16},{1,9},{9,1},{17,25},{25,17},{2,10},{10... | collective-permute-start | bytes 393224 | tf_op jit(solution)/shard_map/ppermute | solution.py:431
  34.6 3.2 %collective-permute-done.3 = f32[4,64,128]{2,1,0:T(8,128)S(1)} collective-permute-done((f32[4,64,128]{2,1,0:T(8,128)}, f32[4,64,128]{2,1,0:T(8,128)S(1)}, u32[]{:S(2)}, u32[]{:S(2)}) %collective-permute-start.3) | collective-permute-done | bytes 131104 | tf_op jit(solution)/shard_map/ppermute | solution.py:431
  37.8 0.9 add.80
  38.7 2.5 %collective-permute-start.4 = (f32[4,64,128]{2,1,0:T(8,128)S(1)}, f32[4,64,128]{2,1,0:T(8,128)S(1)}, u32[]{:S(2)}, u32[]{:S(2)}) collective-permute-start(f32[4,64,128]{2,1,0:T(8,128)S(1)} %add.80), channel_id=1, source_target_pairs={{0,16},{8,24},{16,0},{24,8},{1,17},{9,25},{17,1},{25,9},{2,18},{10... | collective-permute-start | bytes 393224 | tf_op jit(solution)/shard_map/ppermute | solution.py:431
  41.2 3.5 %collective-permute-done.4 = f32[4,64,128]{2,1,0:T(8,128)S(1)} collective-permute-done((f32[4,64,128]{2,1,0:T(8,128)S(1)}, f32[4,64,128]{2,1,0:T(8,128)S(1)}, u32[]{:S(2)}, u32[]{:S(2)}) %collective-permute-start.4) | collective-permute-done | bytes 131104 | tf_op jit(solution)/shard_map/ppermute | solution.py:431
  45.4 5.7 %shard_map.96 = (f32[2,64,64,128]{3,2,1,0:T(8,128)}, f32[2,64,128]{2,1,0:T(8,128)}, f32[4,64,128]{2,1,0:T(8,128)}, f32[2,64,128]{2,1,0:T(8,128)}) custom-call(s32[134]{0:T(256)} %pad_add_fusion.pos_ref, f32[4,64,128]{2,1,0:T(8,128)} %add_add_fusion.1.refs_0_, f32[2,64,64,128]{3,2,1,0:T(8,128)} %get-tuple-element.30.refs_1_, ...), custom_call_target="tpu_custom_call" | custom-call | tf_op jit(solution)/shard_map/pallas_call | solution.py:294
  51.1 1.5 %collective-permute-done.5 = f32[4,64,128]{2,1,0:T(8,128)S(1)} collective-permute-done((f32[4,64,128]{2,1,0:T(8,128)}, f32[4,64,128]{2,1,0:T(8,128)S(1)}, u32[]{:S(2)}, u32[]{:S(2)}) %collective-permute-start.5) | collective-permute-done | bytes 131104 | tf_op jit(solution)/shard_map/ppermute | solution.py:431
  52.7 0.9 mul.92
  53.6 3.9 %collective-permute-start.6 = (f32[4,64,128]{2,1,0:T(8,128)S(1)}, f32[4,64,128]{2,1,0:T(8,128)S(1)}, u32[]{:S(2)}, u32[]{:S(2)}) collective-permute-start(f32[4,64,128]{2,1,0:T(8,128)S(1)} %mul.92), channel_id=1, source_target_pairs={{0,2},{1,3},{2,0},{3,1},{4,6},{5,7},{6,4},{7,5},{8,10},{9,11},{10,... | collective-permute-start | bytes 393224 | tf_op jit(solution)/shard_map/ppermute | solution.py:431
  57.5 3.8 %collective-permute-done.6 = f32[4,64,128]{2,1,0:T(8,128)S(1)} collective-permute-done((f32[4,64,128]{2,1,0:T(8,128)S(1)}, f32[4,64,128]{2,1,0:T(8,128)S(1)}, u32[]{:S(2)}, u32[]{:S(2)}) %collective-permute-start.6) | collective-permute-done | bytes 131104 | tf_op jit(solution)/shard_map/ppermute | solution.py:431
  61.8 4.6 %collective-permute-done.7 = f32[4,64,128]{2,1,0:T(8,128)S(1)} collective-permute-done((f32[4,64,128]{2,1,0:T(8,128)S(1)}, f32[4,64,128]{2,1,0:T(8,128)S(1)}, u32[]{:S(2)}, u32[]{:S(2)}) %collective-permute-start.7) | collective-permute-done | bytes 131104 | tf_op jit(solution)/shard_map/ppermute | solution.py:431
  67.1 7.9 %shard_map.97 = (f32[2,64,64,128]{3,2,1,0:T(8,128)}, f32[2,64,64,128]{3,2,1,0:T(8,128)}, f32[2,64,128]{2,1,0:T(8,128)}, f32[4,64,128]{2,1,0:T(8,128)}, f32[4,64,128]{2,1,0:T(8,128)}) custom-call(s32[134]{0:T(256)} %pad_add_fusion.pos_ref, f32[4,64,128]{2,1,0:T(8,128)} %bitcast.15, f32[2,64,64,128]{3,2,1,0:T(8,128)} %get-tuple-element.31.refs_1_, ...), custom_call_target="tpu_custom_call" | custom-call | tf_op jit(solution)/shard_map/pallas_call | solution.py:294
  75.1 1.5 %collective-permute-done.10 = f32[4,64,128]{2,1,0:T(8,128)S(1)} collective-permute-done((f32[4,64,128]{2,1,0:T(8,128)}, f32[4,64,128]{2,1,0:T(8,128)S(1)}, u32[]{:S(2)}, u32[]{:S(2)}) %collective-permute-start.10) | collective-permute-done | bytes 131104 | tf_op jit(solution)/shard_map/ppermute | solution.py:431
  76.6 0.9 multiply_add_fusion.5
  77.6 1.6 %collective-permute-start.11 = (f32[4,64,128]{2,1,0:T(8,128)S(1)}, f32[4,64,128]{2,1,0:T(8,128)S(1)}, u32[]{:S(2)}, u32[]{:S(2)}) collective-permute-start(f32[4,64,128]{2,1,0:T(8,128)S(1)} %multiply_add_fusion.5), channel_id=1, source_target_pairs={{0,2},{1,3},{2,0},{3,1},{4,6},{5,7},{6,4},{7,5},{8,10},{9,11},{10,... | collective-permute-start | bytes 393224 | tf_op jit(solution)/shard_map/ppermute | solution.py:431
  79.2 4.0 %collective-permute-done.11 = f32[4,64,128]{2,1,0:T(8,128)S(1)} collective-permute-done((f32[4,64,128]{2,1,0:T(8,128)S(1)}, f32[4,64,128]{2,1,0:T(8,128)S(1)}, u32[]{:S(2)}, u32[]{:S(2)}) %collective-permute-start.11) | collective-permute-done | bytes 131104 | tf_op jit(solution)/shard_map/ppermute | solution.py:431
  83.7 4.6 %collective-permute-done.12 = f32[4,64,128]{2,1,0:T(8,128)S(1)} collective-permute-done((f32[4,64,128]{2,1,0:T(8,128)S(1)}, f32[4,64,128]{2,1,0:T(8,128)S(1)}, u32[]{:S(2)}, u32[]{:S(2)}) %collective-permute-start.12) | collective-permute-done | bytes 131104 | tf_op jit(solution)/shard_map/ppermute | solution.py:431
  89.0 7.3 %shard_map.98 = (f32[2,64,64,128]{3,2,1,0:T(8,128)}, f32[4,64,128]{2,1,0:T(8,128)}) custom-call(s32[134]{0:T(256)} %pad_add_fusion.pos_ref, f32[4,64,128]{2,1,0:T(8,128)} %add_add_fusion.1.refs_0_, f32[2,64,64,128]{3,2,1,0:T(8,128)} %get-tuple-element.30.refs_1_, f32[2,64,64,128]{3,2,1,0:T(8,128)} %broadcast_in_dim.91.refs_1_.ew_ref.refs_2_.refs_5_.refs_6_, ...), custom_call_target="tpu_custom_call" | custom-call | tf_op jit(solution)/shard_map/pallas_call | solution.py:294
  96.3 1.2 collective-permute-start.13
  97.5 4.1 %collective-permute-done.13 = f32[4,64,128]{2,1,0:T(8,128)S(1)} collective-permute-done((f32[4,64,128]{2,1,0:T(8,128)}, f32[4,64,128]{2,1,0:T(8,128)S(1)}, u32[]{:S(2)}, u32[]{:S(2)}) %collective-permute-start.13) | collective-permute-done | bytes 131104 | tf_op jit(solution)/shard_map/ppermute | solution.py:431
  101.5 0.9 add.91
  102.4 1.3 collective-permute-start.14
  103.7 6.1 %collective-permute-done.14 = f32[4,64,128]{2,1,0:T(8,128)S(1)} collective-permute-done((f32[4,64,128]{2,1,0:T(8,128)S(1)}, f32[4,64,128]{2,1,0:T(8,128)S(1)}, u32[]{:S(2)}, u32[]{:S(2)}) %collective-permute-start.14) | collective-permute-done | bytes 131104 | tf_op jit(solution)/shard_map/ppermute | solution.py:431
  110.5 9.6 %shard_map.99 = (f32[2,64,64,128]{3,2,1,0:T(8,128)}, f32[2,64,64,128]{3,2,1,0:T(8,128)}, f32[2,64,128]{2,1,0:T(8,128)}, f32[4,64,128]{2,1,0:T(8,128)}) custom-call(s32[134]{0:T(256)} %pad_add_fusion.pos_ref, f32[4,64,128]{2,1,0:T(8,128)} %get-tuple-element.48.refs_0_, f32[2,64,64,128]{3,2,1,0:T(8,128)} %get-tuple-element.40.refs_1_, ...), custom_call_target="tpu_custom_call" | custom-call | tf_op jit(solution)/shard_map/pallas_call | solution.py:294
  120.2 1.5 collective-permute-done.15
  121.7 1.0 multiply_add_fusion.2
  122.7 1.8 %collective-permute-start.16 = (f32[4,64,128]{2,1,0:T(8,128)S(1)}, f32[4,64,128]{2,1,0:T(8,128)S(1)}, u32[]{:S(2)}, u32[]{:S(2)}) collective-permute-start(f32[4,64,128]{2,1,0:T(8,128)S(1)} %multiply_add_fusion.2), channel_id=1, source_target_pairs={{0,2},{1,3},{2,0},{3,1},{4,6},{5,7},{6,4},{7,5},{8,10},{9,11},{10,... | collective-permute-start | bytes 393224 | tf_op jit(solution)/shard_map/ppermute | solution.py:431
  124.9 3.5 %collective-permute-done.16 = f32[4,64,128]{2,1,0:T(8,128)S(1)} collective-permute-done((f32[4,64,128]{2,1,0:T(8,128)S(1)}, f32[4,64,128]{2,1,0:T(8,128)S(1)}, u32[]{:S(2)}, u32[]{:S(2)}) %collective-permute-start.16) | collective-permute-done | bytes 131104 | tf_op jit(solution)/shard_map/ppermute | solution.py:431
  129.1 1.0 collective-permute-done.8
  130.1 1.8 %collective-permute-start.9 = (f32[4,64,128]{2,1,0:T(8,128)S(1)}, f32[4,64,128]{2,1,0:T(8,128)S(1)}, u32[]{:S(2)}, u32[]{:S(2)}) collective-permute-start(f32[4,64,128]{2,1,0:T(8,128)S(1)} %add.83), channel_id=1, source_target_pairs={{0,16},{8,24},{16,0},{24,8},{1,17},{9,25},{17,1},{25,9},{2,18},{10... | collective-permute-start | bytes 393224 | tf_op jit(solution)/shard_map/ppermute | solution.py:431
  131.8 1.7 %collective-permute-done.17 = f32[4,64,128]{2,1,0:T(8,128)S(1)} collective-permute-done((f32[4,64,128]{2,1,0:T(8,128)S(1)}, f32[4,64,128]{2,1,0:T(8,128)S(1)}, u32[]{:S(2)}, u32[]{:S(2)}) %collective-permute-start.17) | collective-permute-done | bytes 131104 | tf_op jit(solution)/shard_map/ppermute | solution.py:431
  133.5 0.9 multiply_add_fusion.refs_3_
  134.4 5.3 %shard_map.100 = f32[4,64,128]{2,1,0:T(8,128)} custom-call(s32[134]{0:T(256)} %pad_add_fusion.pos_ref, f32[4,64,128]{2,1,0:T(8,128)} %add.79.refs_0_, f32[2,64,64,128]{3,2,1,0:T(8,128)} %broadcast_in_dim.91.refs_1_.ew_ref.refs_2_.refs_5_.refs_6_, f32[2,64,64,128]{3,2,1,0:T(8,128)} %get-tuple-element.43.refs_2_, f32[4,64,128]{2,1,0:T(8,128)} %multiply_add_fusion.refs_3_, ...), custom_call_target="tpu_custom_call" | custom-call | tf_op jit(solution)/shard_map/pallas_call | solution.py:294
  139.7 1.0 reduce_sum.52
  140.8 1.1 collective-permute-start.18
  142.6 3.3 %reduce_sum.48 = f32[2,64,64]{2,1,0:T(8,128)S(1)} reduce(f32[2,64,64,128]{3,2,1,0:T(8,128)} %get-tuple-element.42, f32[]{:T(128)} %constant.7.clone.1), dimensions={3}, to_apply=%region_3.4 | reduce | flops 1040384 | bytes 4227076 | tf_op jit(solution)/shard_map/reduce_sum | solution.py:573
  146.0 2.4 %collective-permute-start.19 = (f32[2,128]{1,0:T(2,128)S(1)}, f32[2,128]{1,0:T(2,128)S(1)}, u32[]{:S(2)}, u32[]{:S(2)}) collective-permute-start(f32[2,128]{1,0:T(2,128)S(1)} %add.99), channel_id=1, source_target_pairs={{0,16},{8,24},{16,0},{24,8},{1,17},{9,25},{17,1},{25,9},{2,18},{10... | collective-permute-start | bytes 3080 | tf_op jit(solution)/shard_map/ppermute | solution.py:431
  149.3 1.2 collective-permute-done.19
  (69 shorter events, 15.2 us)
Async XLA Ops:
  7.0 9.7 %copy-start.3 = (s32[256,128]{1,0:T(8,128)S(1)}, s32[256,128]{1,0:T(8,128)}, u32[]{:S(2)}) copy-start(s32[256,128]{1,0:T(8,128)} %param.11) | copy-start | bytes 393220
  7.0 13.3 %copy-start.4 = (s32[1,1,2,2]{3,2,1,0:T(2,128)S(1)}, s32[1,1,2,2]{3,2,1,0:T(2,128)}, u32[]{:S(2)}) copy-start(s32[1,1,2,2]{3,2,1,0:T(2,128)} %param.8) | copy-start | bytes 52
  16.2 1.3 collective-permute-start
  17.6 4.3 %collective-permute-start.1 = (f32[2,128]{1,0:T(2,128)S(1)}, f32[2,128]{1,0:T(2,128)S(1)}, u32[]{:S(2)}, u32[]{:S(2)}) collective-permute-start(f32[2,128]{1,0:T(2,128)S(1)} %mul.88), channel_id=1, source_target_pairs={{0,2},{1,3},{2,0},{3,1},{4,6},{5,7},{6,4},{7,5},{8,10},{9,11},{10,... | collective-permute-start | bytes 3080 | tf_op jit(solution)/shard_map/ppermute | solution.py:431
  21.9 3.6 %collective-permute-start.2 = (f32[2,128]{1,0:T(2,128)S(1)}, f32[2,128]{1,0:T(2,128)S(1)}, u32[]{:S(2)}, u32[]{:S(2)}) collective-permute-start(f32[2,128]{1,0:T(2,128)S(1)} %mul.90), channel_id=1, source_target_pairs={{0,4},{1,5},{2,6},{3,7},{4,0},{5,1},{6,2},{7,3},{8,12},{9,13},{10,... | collective-permute-start | bytes 3080 | tf_op jit(solution)/shard_map/ppermute | solution.py:431
  32.0 5.8 %collective-permute-start.3 = (f32[4,64,128]{2,1,0:T(8,128)}, f32[4,64,128]{2,1,0:T(8,128)S(1)}, u32[]{:S(2)}, u32[]{:S(2)}) collective-permute-start(f32[4,64,128]{2,1,0:T(8,128)} %get-tuple-element.29), channel_id=1, source_target_pairs={{0,8},{8,0},{16,24},{24,16},{1,9},{9,1},{17,25},{25,17},{2,10},{10... | collective-permute-start | bytes 393224 | tf_op jit(solution)/shard_map/ppermute | solution.py:431
  38.7 5.9 %collective-permute-start.4 = (f32[4,64,128]{2,1,0:T(8,128)S(1)}, f32[4,64,128]{2,1,0:T(8,128)S(1)}, u32[]{:S(2)}, u32[]{:S(2)}) collective-permute-start(f32[4,64,128]{2,1,0:T(8,128)S(1)} %add.80), channel_id=1, source_target_pairs={{0,16},{8,24},{16,0},{24,8},{1,17},{9,25},{17,1},{25,9},{2,18},{10... | collective-permute-start | bytes 393224 | tf_op jit(solution)/shard_map/ppermute | solution.py:431
  51.1 1.6 %collective-permute-start.5 = (f32[4,64,128]{2,1,0:T(8,128)}, f32[4,64,128]{2,1,0:T(8,128)S(1)}, u32[]{:S(2)}, u32[]{:S(2)}) collective-permute-start(f32[4,64,128]{2,1,0:T(8,128)} %get-tuple-element.33), channel_id=1, source_target_pairs={{0,1},{1,0},{2,3},{3,2},{4,5},{5,4},{6,7},{7,6},{8,9},{9,8},{10,11... | collective-permute-start | bytes 393224 | tf_op jit(solution)/shard_map/ppermute | solution.py:431
  53.6 7.7 %collective-permute-start.6 = (f32[4,64,128]{2,1,0:T(8,128)S(1)}, f32[4,64,128]{2,1,0:T(8,128)S(1)}, u32[]{:S(2)}, u32[]{:S(2)}) collective-permute-start(f32[4,64,128]{2,1,0:T(8,128)S(1)} %mul.92), channel_id=1, source_target_pairs={{0,2},{1,3},{2,0},{3,1},{4,6},{5,7},{6,4},{7,5},{8,10},{9,11},{10,... | collective-permute-start | bytes 393224 | tf_op jit(solution)/shard_map/ppermute | solution.py:431
  61.3 5.1 %collective-permute-start.7 = (f32[4,64,128]{2,1,0:T(8,128)S(1)}, f32[4,64,128]{2,1,0:T(8,128)S(1)}, u32[]{:S(2)}, u32[]{:S(2)}) collective-permute-start(f32[4,64,128]{2,1,0:T(8,128)S(1)} %mul.94), channel_id=1, source_target_pairs={{0,4},{1,5},{2,6},{3,7},{4,0},{5,1},{6,2},{7,3},{8,12},{9,13},{10,... | collective-permute-start | bytes 393224 | tf_op jit(solution)/shard_map/ppermute | solution.py:431
  67.1 9.6 %copy-start.1 = (f32[4,64,128]{2,1,0:T(8,128)S(1)}, f32[4,64,128]{2,1,0:T(8,128)}, u32[]{:S(2)}) copy-start(f32[4,64,128]{2,1,0:T(8,128)} %get-tuple-element.33) | copy-start | bytes 393220
  75.0 1.6 %collective-permute-start.10 = (f32[4,64,128]{2,1,0:T(8,128)}, f32[4,64,128]{2,1,0:T(8,128)S(1)}, u32[]{:S(2)}, u32[]{:S(2)}) collective-permute-start(f32[4,64,128]{2,1,0:T(8,128)} %get-tuple-element.36), channel_id=1, source_target_pairs={{0,1},{1,0},{2,3},{3,2},{4,5},{5,4},{6,7},{7,6},{8,9},{9,8},{10,11... | collective-permute-start | bytes 393224 | tf_op jit(solution)/shard_map/ppermute | solution.py:431
  77.6 5.6 %collective-permute-start.11 = (f32[4,64,128]{2,1,0:T(8,128)S(1)}, f32[4,64,128]{2,1,0:T(8,128)S(1)}, u32[]{:S(2)}, u32[]{:S(2)}) collective-permute-start(f32[4,64,128]{2,1,0:T(8,128)S(1)} %multiply_add_fusion.5), channel_id=1, source_target_pairs={{0,2},{1,3},{2,0},{3,1},{4,6},{5,7},{6,4},{7,5},{8,10},{9,11},{10,... | collective-permute-start | bytes 393224 | tf_op jit(solution)/shard_map/ppermute | solution.py:431
  83.2 5.0 %collective-permute-start.12 = (f32[4,64,128]{2,1,0:T(8,128)S(1)}, f32[4,64,128]{2,1,0:T(8,128)S(1)}, u32[]{:S(2)}, u32[]{:S(2)}) collective-permute-start(f32[4,64,128]{2,1,0:T(8,128)S(1)} %multiply_add_fusion.4), channel_id=1, source_target_pairs={{0,4},{1,5},{2,6},{3,7},{4,0},{5,1},{6,2},{7,3},{8,12},{9,13},{10,... | collective-permute-start | bytes 393224 | tf_op jit(solution)/shard_map/ppermute | solution.py:431
  96.3 5.2 %collective-permute-start.13 = (f32[4,64,128]{2,1,0:T(8,128)}, f32[4,64,128]{2,1,0:T(8,128)S(1)}, u32[]{:S(2)}, u32[]{:S(2)}) collective-permute-start(f32[4,64,128]{2,1,0:T(8,128)} %get-tuple-element.39), channel_id=1, source_target_pairs={{0,8},{8,0},{16,24},{24,16},{1,9},{9,1},{17,25},{25,17},{2,10},{10... | collective-permute-start | bytes 393224 | tf_op jit(solution)/shard_map/ppermute | solution.py:431
  102.4 7.3 %collective-permute-start.14 = (f32[4,64,128]{2,1,0:T(8,128)S(1)}, f32[4,64,128]{2,1,0:T(8,128)S(1)}, u32[]{:S(2)}, u32[]{:S(2)}) collective-permute-start(f32[4,64,128]{2,1,0:T(8,128)S(1)} %add.91), channel_id=1, source_target_pairs={{0,16},{8,24},{16,0},{24,8},{1,17},{9,25},{17,1},{25,9},{2,18},{10... | collective-permute-start | bytes 393224 | tf_op jit(solution)/shard_map/ppermute | solution.py:431
  110.5 14.1 %copy-start = (f32[256,128]{1,0:T(8,128)S(1)}, f32[256,128]{1,0:T(8,128)}, u32[]{:S(2)}) copy-start(f32[256,128]{1,0:T(8,128)} %param.13) | copy-start | bytes 393220
  110.5 14.3 %copy-start.2 = (f32[4,64,128]{2,1,0:T(8,128)S(1)}, f32[4,64,128]{2,1,0:T(8,128)}, u32[]{:S(2)}) copy-start(f32[4,64,128]{2,1,0:T(8,128)} %get-tuple-element.34) | copy-start | bytes 393220
  120.1 1.6 %collective-permute-start.15 = (f32[4,64,128]{2,1,0:T(8,128)}, f32[4,64,128]{2,1,0:T(8,128)S(1)}, u32[]{:S(2)}, u32[]{:S(2)}) collective-permute-start(f32[4,64,128]{2,1,0:T(8,128)} %get-tuple-element.44), channel_id=1, source_target_pairs={{0,1},{1,0},{2,3},{3,2},{4,5},{5,4},{6,7},{7,6},{8,9},{9,8},{10,11... | collective-permute-start | bytes 393224 | tf_op jit(solution)/shard_map/ppermute | solution.py:431
  122.7 5.6 %collective-permute-start.16 = (f32[4,64,128]{2,1,0:T(8,128)S(1)}, f32[4,64,128]{2,1,0:T(8,128)S(1)}, u32[]{:S(2)}, u32[]{:S(2)}) collective-permute-start(f32[4,64,128]{2,1,0:T(8,128)S(1)} %multiply_add_fusion.2), channel_id=1, source_target_pairs={{0,2},{1,3},{2,0},{3,1},{4,6},{5,7},{6,4},{7,5},{8,10},{9,11},{10,... | collective-permute-start | bytes 393224 | tf_op jit(solution)/shard_map/ppermute | solution.py:431
  124.8 5.3 %collective-permute-start.8 = (f32[4,64,128]{2,1,0:T(8,128)S(1)}, f32[4,64,128]{2,1,0:T(8,128)S(1)}, u32[]{:S(2)}, u32[]{:S(2)}) collective-permute-start(f32[4,64,128]{2,1,0:T(8,128)S(1)} %copy-done.2), channel_id=1, source_target_pairs={{0,8},{8,0},{16,24},{24,16},{1,9},{9,1},{17,25},{25,17},{2,10},{10... | collective-permute-start | bytes 393224 | tf_op jit(solution)/shard_map/ppermute | solution.py:431
  128.5 5.0 %collective-permute-start.17 = (f32[4,64,128]{2,1,0:T(8,128)S(1)}, f32[4,64,128]{2,1,0:T(8,128)S(1)}, u32[]{:S(2)}, u32[]{:S(2)}) collective-permute-start(f32[4,64,128]{2,1,0:T(8,128)S(1)} %multiply_add_fusion.1), channel_id=1, source_target_pairs={{0,4},{1,5},{2,6},{3,7},{4,0},{5,1},{6,2},{7,3},{8,12},{9,13},{10,... | collective-permute-start | bytes 393224 | tf_op jit(solution)/shard_map/ppermute | solution.py:431
  130.1 11.8 %collective-permute-start.9 = (f32[4,64,128]{2,1,0:T(8,128)S(1)}, f32[4,64,128]{2,1,0:T(8,128)S(1)}, u32[]{:S(2)}, u32[]{:S(2)}) collective-permute-start(f32[4,64,128]{2,1,0:T(8,128)S(1)} %add.83), channel_id=1, source_target_pairs={{0,16},{8,24},{16,0},{24,8},{1,17},{9,25},{17,1},{25,9},{2,18},{10... | collective-permute-start | bytes 393224 | tf_op jit(solution)/shard_map/ppermute | solution.py:431
  140.8 5.2 %collective-permute-start.18 = (f32[2,128]{1,0:T(2,128)S(1)}, f32[2,128]{1,0:T(2,128)S(1)}, u32[]{:S(2)}, u32[]{:S(2)}) collective-permute-start(f32[2,128]{1,0:T(2,128)S(1)} %reshape.64), channel_id=1, source_target_pairs={{0,8},{8,0},{16,24},{24,16},{1,9},{9,1},{17,25},{25,17},{2,10},{10... | collective-permute-start | bytes 3080 | tf_op jit(solution)/shard_map/ppermute | solution.py:431
  146.0 4.5 %collective-permute-start.19 = (f32[2,128]{1,0:T(2,128)S(1)}, f32[2,128]{1,0:T(2,128)S(1)}, u32[]{:S(2)}, u32[]{:S(2)}) collective-permute-start(f32[2,128]{1,0:T(2,128)S(1)} %add.99), channel_id=1, source_target_pairs={{0,16},{8,24},{16,0},{24,8},{1,17},{9,25},{17,1},{25,9},{2,18},{10... | collective-permute-start | bytes 3080 | tf_op jit(solution)/shard_map/ppermute | solution.py:431

commit v12 on v11

--- a/solution.py
+++ b/solution.py
@@ -548,15 +548,17 @@
         spread_t, u_prev, ba, whole, others_here, others, trail = saved[step]
         prior_grad = prior_grad + jnp.sum(grad_total, axis=2)
         if step + 1 == ITERS:
-            acc, grad_ba, grad_here, grad_others, last_column = bwd_messages(
-                pos, grad_total, grad_m, ba, sign_slot, others_here, others, ew, acc, column_blocks
+            term, grad_ba, grad_here, grad_others, last_column = bwd_messages(
+                pos, grad_total, grad_m, ba, sign_slot, others_here, others, ew, None, column_blocks
             )
             total = prior_dev[:, :, None] + checks_total(last_column, n_chk)
             marginals = total.reshape(column_blocks * TILE, shots)
         else:
-            acc, grad_ba, grad_here, grad_others = bwd_messages(
-                pos, grad_total, grad_m, ba, sign_slot, others_here, others, ew, acc
+            term, grad_ba, grad_here, grad_others = bwd_messages(
+                pos, grad_total, grad_m, ba, sign_slot, others_here, others, ew, None
             )
+        term = jnp.sum(term, axis=3)
+        acc = term if acc is None else acc + term
         grad_rows = others_backward(trail, grad_others, check_blocks, n_var)
         grad_m, column = bwd_products(
             pos, spread_t, u_prev, ew, grad_ba, grad_rows, grad_here, whole, others_here,
@@ -570,7 +572,7 @@
     else:
         shot_sums = checks_total(shot_sums, n_chk)
     prior_grad = prior_grad + shot_sums
-    weight_grad = jnp.where(edge > 0, jnp.swapaxes(jnp.sum(acc, axis=3), 1, 2), 0.0)
+    weight_grad = jnp.where(edge > 0, jnp.swapaxes(acc, 1, 2), 0.0)
     return (
         marginals,
         weight_grad.reshape(1, 1, slot_total, TILE * TILE),

time: 152 us -> 153 us (level)
  waiting for transfers between devices: 48.5 us -> 37.5 us
  starting transfers between devices: 27 us -> 37.8 us
  other arithmetic: 16.5 us -> 19.8 us
    ppermute x20, waiting for transfers between devices: 48.5 us -> 37.5 us  [_swap(): return lax.ppermute(value, axis, perm)]
    ppermute x20, starting transfers between devices: 27 us -> 37.8 us  [_swap(): return lax.ppermute(value, axis, perm)]
    reduce_sum x1 -> x2, other arithmetic: 3.34 us -> 6.68 us  [body(): term = jnp.sum(term, axis=3)]
  transfers between devices with their start and end apart: 20 -> 20, of which waited for: 18 -> 16; matrix products, arithmetic and copies ran while one was open for 6% -> 8% of each run, Pallas kernels for 4% -> 3%
where the time goes in v12:
time: 153 us
  Pallas kernels  44.9 us (29%)
  starting transfers between devices  37.8 us (25%)
  waiting for transfers between devices  37.5 us (25%)
  other arithmetic  19.8 us (13%)
  local copies, waits for them, and re-layouts  11 us (7%)
    pallas_call x7, Pallas kernels, _call(): pl.pallas_call(kernel, grid_spec=grid_spec, out_shape=[o for kind, o in o...  44.9 us
    ppermute x20, starting transfers between devices, _swap(): return lax.ppermute(value, axis, perm)  37.8 us
    ppermute x20, waiting for transfers between devices, _swap(): return lax.ppermute(value, axis, perm)  37.5 us
    reduce_sum x2, other arithmetic, body(): term = jnp.sum(term, axis=3)  6.68 us
  transfers between devices with their start and end apart: 20, of which 16 were waited for; matrix products, arithmetic and copies ran while one was open for 8% of the time, Pallas kernels for 3%

profile of v12, /device:TPU:0, one launch (start us, length us, event | category | flops | bytes accessed | tf_op | source)
XLA Modules:
  0.0 152.8 jit_solution(4166787231941118115)
XLA Ops:
  2.7 1.0 sort.17
  7.0 2.5 %broadcast_in_dim.91.refs_1_.ew_ref.refs_2_.refs_5_.refs_6_ = f32[2,64,64,128]{3,2,1,0:T(8,128)} broadcast(f32[2,64,64]{2,1,0:T(8,128)S(1)} %multiply_bitcast_fusion), dimensions={0,1,2} | broadcast | bytes 4227072 | tf_op jit(solution)/shard_map/broadcast_in_dim | solution.py:526
  10.3 4.8 %shard_map.94 = (f32[2,64,64,128]{3,2,1,0:T(8,128)}, f32[2,64,128]{2,1,0:T(8,128)}, f32[4,64,128]{2,1,0:T(8,128)}, f32[2,64,128]{2,1,0:T(8,128)}) custom-call(s32[134]{0:T(256)} %pad_add_fusion.pos_ref, f32[4,64,128]{2,1,0:T(8,128)} %add.86.refs_0_, f32[2,64,64,128]{3,2,1,0:T(8,128)} %broadcast_in_dim.91.refs_1_.ew_ref.refs_2_.refs_5_.refs_6_), custom_call_target="tpu_custom_call" | custom-call | tf_op jit(solution)/shard_map/pallas_call | solution.py:294
  15.1 1.0 slice_reduce_fusion
  17.4 2.9 %collective-permute-start.1 = (f32[2,128]{1,0:T(2,128)S(1)}, f32[2,128]{1,0:T(2,128)S(1)}, u32[]{:S(2)}, u32[]{:S(2)}) collective-permute-start(f32[2,128]{1,0:T(2,128)S(1)} %mul.88), channel_id=1, source_target_pairs={{0,2},{1,3},{2,0},{3,1},{4,6},{5,7},{6,4},{7,5},{8,10},{9,11},{10,... | collective-permute-start | bytes 3080 | tf_op jit(solution)/shard_map/ppermute | solution.py:431
  20.4 1.4 collective-permute-done.1
  21.9 2.0 %collective-permute-start.2 = (f32[2,128]{1,0:T(2,128)S(1)}, f32[2,128]{1,0:T(2,128)S(1)}, u32[]{:S(2)}, u32[]{:S(2)}) collective-permute-start(f32[2,128]{1,0:T(2,128)S(1)} %mul.90), channel_id=1, source_target_pairs={{0,4},{1,5},{2,6},{3,7},{4,0},{5,1},{6,2},{7,3},{8,12},{9,13},{10,... | collective-permute-start | bytes 3080 | tf_op jit(solution)/shard_map/ppermute | solution.py:431
  26.3 5.7 %shard_map.95 = (f32[2,64,64,128]{3,2,1,0:T(8,128)}, f32[4,64,128]{2,1,0:T(8,128)}) custom-call(s32[134]{0:T(256)} %pad_add_fusion.pos_ref, f32[2,64,64,128]{3,2,1,0:T(8,128)} %get-tuple-element.26.ba_ref.refs_2_, f32[2,64,128]{2,1,0:T(8,128)} %copy.30.sign_ref.refs_2_.refs_3_, f32[2,64,128]{2,1,0:T(8,128)} %get-tuple-element.27.here_ref.refs_4_.refs_6_, ...), custom_call_target="tpu_custom_call" | custom-call | tf_op jit(solution)/shard_map/pallas_call | solution.py:294
  32.0 2.0 %collective-permute-start.3 = (f32[4,64,128]{2,1,0:T(8,128)}, f32[4,64,128]{2,1,0:T(8,128)S(1)}, u32[]{:S(2)}, u32[]{:S(2)}) collective-permute-start(f32[4,64,128]{2,1,0:T(8,128)} %get-tuple-element.29), channel_id=1, source_target_pairs={{0,8},{8,0},{16,24},{24,16},{1,9},{9,1},{17,25},{25,17},{2,10},{10... | collective-permute-start | bytes 393224 | tf_op jit(solution)/shard_map/ppermute | solution.py:431
  34.0 3.2 %collective-permute-done.3 = f32[4,64,128]{2,1,0:T(8,128)S(1)} collective-permute-done((f32[4,64,128]{2,1,0:T(8,128)}, f32[4,64,128]{2,1,0:T(8,128)S(1)}, u32[]{:S(2)}, u32[]{:S(2)}) %collective-permute-start.3) | collective-permute-done | bytes 131104 | tf_op jit(solution)/shard_map/ppermute | solution.py:431
  37.2 0.9 add.87
  38.1 3.2 %collective-permute-start.4 = (f32[4,64,128]{2,1,0:T(8,128)S(1)}, f32[4,64,128]{2,1,0:T(8,128)S(1)}, u32[]{:S(2)}, u32[]{:S(2)}) collective-permute-start(f32[4,64,128]{2,1,0:T(8,128)S(1)} %add.87), channel_id=1, source_target_pairs={{0,16},{8,24},{16,0},{24,8},{1,17},{9,25},{17,1},{25,9},{2,18},{10... | collective-permute-start | bytes 393224 | tf_op jit(solution)/shard_map/ppermute | solution.py:431
  41.3 2.9 %collective-permute-done.4 = f32[4,64,128]{2,1,0:T(8,128)S(1)} collective-permute-done((f32[4,64,128]{2,1,0:T(8,128)S(1)}, f32[4,64,128]{2,1,0:T(8,128)S(1)}, u32[]{:S(2)}, u32[]{:S(2)}) %collective-permute-start.4) | collective-permute-done | bytes 131104 | tf_op jit(solution)/shard_map/ppermute | solution.py:431
  45.0 5.6 %shard_map.96 = (f32[2,64,64,128]{3,2,1,0:T(8,128)}, f32[2,64,128]{2,1,0:T(8,128)}, f32[4,64,128]{2,1,0:T(8,128)}, f32[2,64,128]{2,1,0:T(8,128)}) custom-call(s32[134]{0:T(256)} %pad_add_fusion.pos_ref, f32[4,64,128]{2,1,0:T(8,128)} %add_add_fusion.1.refs_0_, f32[2,64,64,128]{3,2,1,0:T(8,128)} %get-tuple-element.30.refs_1_, ...), custom_call_target="tpu_custom_call" | custom-call | tf_op jit(solution)/shard_map/pallas_call | solution.py:294
  50.6 1.5 %collective-permute-done.5 = f32[4,64,128]{2,1,0:T(8,128)S(1)} collective-permute-done((f32[4,64,128]{2,1,0:T(8,128)}, f32[4,64,128]{2,1,0:T(8,128)S(1)}, u32[]{:S(2)}, u32[]{:S(2)}) %collective-permute-start.5) | collective-permute-done | bytes 131104 | tf_op jit(solution)/shard_map/ppermute | solution.py:431
  52.2 0.9 mul.92
  53.1 1.9 %collective-permute-start.6 = (f32[4,64,128]{2,1,0:T(8,128)S(1)}, f32[4,64,128]{2,1,0:T(8,128)S(1)}, u32[]{:S(2)}, u32[]{:S(2)}) collective-permute-start(f32[4,64,128]{2,1,0:T(8,128)S(1)} %mul.92), channel_id=1, source_target_pairs={{0,2},{1,3},{2,0},{3,1},{4,6},{5,7},{6,4},{7,5},{8,10},{9,11},{10,... | collective-permute-start | bytes 393224 | tf_op jit(solution)/shard_map/ppermute | solution.py:431
  55.1 3.8 %collective-permute-done.6 = f32[4,64,128]{2,1,0:T(8,128)S(1)} collective-permute-done((f32[4,64,128]{2,1,0:T(8,128)S(1)}, f32[4,64,128]{2,1,0:T(8,128)S(1)}, u32[]{:S(2)}, u32[]{:S(2)}) %collective-permute-start.6) | collective-permute-done | bytes 131104 | tf_op jit(solution)/shard_map/ppermute | solution.py:431
  58.9 1.8 %collective-permute-start.7 = (f32[4,64,128]{2,1,0:T(8,128)S(1)}, f32[4,64,128]{2,1,0:T(8,128)S(1)}, u32[]{:S(2)}, u32[]{:S(2)}) collective-permute-start(f32[4,64,128]{2,1,0:T(8,128)S(1)} %mul.94), channel_id=1, source_target_pairs={{0,4},{1,5},{2,6},{3,7},{4,0},{5,1},{6,2},{7,3},{8,12},{9,13},{10,... | collective-permute-start | bytes 393224 | tf_op jit(solution)/shard_map/ppermute | solution.py:431
  60.7 3.3 %collective-permute-done.7 = f32[4,64,128]{2,1,0:T(8,128)S(1)} collective-permute-done((f32[4,64,128]{2,1,0:T(8,128)S(1)}, f32[4,64,128]{2,1,0:T(8,128)S(1)}, u32[]{:S(2)}, u32[]{:S(2)}) %collective-permute-start.7) | collective-permute-done | bytes 131104 | tf_op jit(solution)/shard_map/ppermute | solution.py:431
  64.6 7.9 %shard_map.97 = (f32[2,64,64,128]{3,2,1,0:T(8,128)}, f32[2,64,64,128]{3,2,1,0:T(8,128)}, f32[2,64,128]{2,1,0:T(8,128)}, f32[4,64,128]{2,1,0:T(8,128)}, f32[4,64,128]{2,1,0:T(8,128)}) custom-call(s32[134]{0:T(256)} %pad_add_fusion.pos_ref, f32[4,64,128]{2,1,0:T(8,128)} %bitcast.15, f32[2,64,64,128]{3,2,1,0:T(8,128)} %get-tuple-element.31.refs_1_, ...), custom_call_target="tpu_custom_call" | custom-call | tf_op jit(solution)/shard_map/pallas_call | solution.py:294
  72.6 1.5 %collective-permute-done.10 = f32[4,64,128]{2,1,0:T(8,128)S(1)} collective-permute-done((f32[4,64,128]{2,1,0:T(8,128)}, f32[4,64,128]{2,1,0:T(8,128)S(1)}, u32[]{:S(2)}, u32[]{:S(2)}) %collective-permute-start.10) | collective-permute-done | bytes 131104 | tf_op jit(solution)/shard_map/ppermute | solution.py:431
  74.1 0.9 multiply_add_fusion.5
  75.1 1.8 %collective-permute-start.11 = (f32[4,64,128]{2,1,0:T(8,128)S(1)}, f32[4,64,128]{2,1,0:T(8,128)S(1)}, u32[]{:S(2)}, u32[]{:S(2)}) collective-permute-start(f32[4,64,128]{2,1,0:T(8,128)S(1)} %multiply_add_fusion.5), channel_id=1, source_target_pairs={{0,2},{1,3},{2,0},{3,1},{4,6},{5,7},{6,4},{7,5},{8,10},{9,11},{10,... | collective-permute-start | bytes 393224 | tf_op jit(solution)/shard_map/ppermute | solution.py:431
  76.9 3.8 %collective-permute-done.11 = f32[4,64,128]{2,1,0:T(8,128)S(1)} collective-permute-done((f32[4,64,128]{2,1,0:T(8,128)S(1)}, f32[4,64,128]{2,1,0:T(8,128)S(1)}, u32[]{:S(2)}, u32[]{:S(2)}) %collective-permute-start.11) | collective-permute-done | bytes 131104 | tf_op jit(solution)/shard_map/ppermute | solution.py:431
  80.8 1.7 %collective-permute-start.12 = (f32[4,64,128]{2,1,0:T(8,128)S(1)}, f32[4,64,128]{2,1,0:T(8,128)S(1)}, u32[]{:S(2)}, u32[]{:S(2)}) collective-permute-start(f32[4,64,128]{2,1,0:T(8,128)S(1)} %multiply_add_fusion.4), channel_id=1, source_target_pairs={{0,4},{1,5},{2,6},{3,7},{4,0},{5,1},{6,2},{7,3},{8,12},{9,13},{10,... | collective-permute-start | bytes 393224 | tf_op jit(solution)/shard_map/ppermute | solution.py:431
  82.5 3.3 %collective-permute-done.12 = f32[4,64,128]{2,1,0:T(8,128)S(1)} collective-permute-done((f32[4,64,128]{2,1,0:T(8,128)S(1)}, f32[4,64,128]{2,1,0:T(8,128)S(1)}, u32[]{:S(2)}, u32[]{:S(2)}) %collective-permute-start.12) | collective-permute-done | bytes 131104 | tf_op jit(solution)/shard_map/ppermute | solution.py:431
  86.5 7.3 %shard_map.98 = (f32[2,64,64,128]{3,2,1,0:T(8,128)}, f32[4,64,128]{2,1,0:T(8,128)}) custom-call(s32[134]{0:T(256)} %pad_add_fusion.pos_ref, f32[4,64,128]{2,1,0:T(8,128)} %add_add_fusion.1.refs_0_, f32[2,64,64,128]{3,2,1,0:T(8,128)} %get-tuple-element.30.refs_1_, f32[2,64,64,128]{3,2,1,0:T(8,128)} %broadcast_in_dim.91.refs_1_.ew_ref.refs_2_.refs_5_.refs_6_, ...), custom_call_target="tpu_custom_call" | custom-call | tf_op jit(solution)/shard_map/pallas_call | solution.py:294
  93.8 2.5 %collective-permute-start.13 = (f32[4,64,128]{2,1,0:T(8,128)}, f32[4,64,128]{2,1,0:T(8,128)S(1)}, u32[]{:S(2)}, u32[]{:S(2)}) collective-permute-start(f32[4,64,128]{2,1,0:T(8,128)} %get-tuple-element.40), channel_id=1, source_target_pairs={{0,8},{8,0},{16,24},{24,16},{1,9},{9,1},{17,25},{25,17},{2,10},{10... | collective-permute-start | bytes 393224 | tf_op jit(solution)/shard_map/ppermute | solution.py:431
  96.3 3.2 %collective-permute-done.13 = f32[4,64,128]{2,1,0:T(8,128)S(1)} collective-permute-done((f32[4,64,128]{2,1,0:T(8,128)}, f32[4,64,128]{2,1,0:T(8,128)S(1)}, u32[]{:S(2)}, u32[]{:S(2)}) %collective-permute-start.13) | collective-permute-done | bytes 131104 | tf_op jit(solution)/shard_map/ppermute | solution.py:431
  99.5 0.9 add.98
  100.4 4.3 %collective-permute-start.14 = (f32[4,64,128]{2,1,0:T(8,128)S(1)}, f32[4,64,128]{2,1,0:T(8,128)S(1)}, u32[]{:S(2)}, u32[]{:S(2)}) collective-permute-start(f32[4,64,128]{2,1,0:T(8,128)S(1)} %add.98), channel_id=1, source_target_pairs={{0,16},{8,24},{16,0},{24,8},{1,17},{9,25},{17,1},{25,9},{2,18},{10... | collective-permute-start | bytes 393224 | tf_op jit(solution)/shard_map/ppermute | solution.py:431
  104.7 2.9 %collective-permute-done.14 = f32[4,64,128]{2,1,0:T(8,128)S(1)} collective-permute-done((f32[4,64,128]{2,1,0:T(8,128)S(1)}, f32[4,64,128]{2,1,0:T(8,128)S(1)}, u32[]{:S(2)}, u32[]{:S(2)}) %collective-permute-start.14) | collective-permute-done | bytes 131104 | tf_op jit(solution)/shard_map/ppermute | solution.py:431
  108.3 8.3 %shard_map.99 = (f32[2,64,64,128]{3,2,1,0:T(8,128)}, f32[2,64,64,128]{3,2,1,0:T(8,128)}, f32[2,64,128]{2,1,0:T(8,128)}, f32[4,64,128]{2,1,0:T(8,128)}) custom-call(s32[134]{0:T(256)} %pad_add_fusion.pos_ref, f32[4,64,128]{2,1,0:T(8,128)} %get-tuple-element.48.refs_0_, f32[2,64,64,128]{3,2,1,0:T(8,128)} %get-tuple-element.41.refs_1_, ...), custom_call_target="tpu_custom_call" | custom-call | tf_op jit(solution)/shard_map/pallas_call | solution.py:294
  116.8 1.5 collective-permute-done.15
  118.3 1.0 multiply_add_fusion.2
  119.3 1.9 %collective-permute-start.16 = (f32[4,64,128]{2,1,0:T(8,128)S(1)}, f32[4,64,128]{2,1,0:T(8,128)S(1)}, u32[]{:S(2)}, u32[]{:S(2)}) collective-permute-start(f32[4,64,128]{2,1,0:T(8,128)S(1)} %multiply_add_fusion.2), channel_id=1, source_target_pairs={{0,2},{1,3},{2,0},{3,1},{4,6},{5,7},{6,4},{7,5},{8,10},{9,11},{10,... | collective-permute-start | bytes 393224 | tf_op jit(solution)/shard_map/ppermute | solution.py:431
  121.4 2.5 %collective-permute-start.8 = (f32[4,64,128]{2,1,0:T(8,128)S(1)}, f32[4,64,128]{2,1,0:T(8,128)S(1)}, u32[]{:S(2)}, u32[]{:S(2)}) collective-permute-start(f32[4,64,128]{2,1,0:T(8,128)S(1)} %copy-done.2), channel_id=1, source_target_pairs={{0,8},{8,0},{16,24},{24,16},{1,9},{9,1},{17,25},{25,17},{2,10},{10... | collective-permute-start | bytes 393224 | tf_op jit(solution)/shard_map/ppermute | solution.py:431
  123.9 1.1 collective-permute-done.16
  125.1 1.7 %collective-permute-start.17 = (f32[4,64,128]{2,1,0:T(8,128)S(1)}, f32[4,64,128]{2,1,0:T(8,128)S(1)}, u32[]{:S(2)}, u32[]{:S(2)}) collective-permute-start(f32[4,64,128]{2,1,0:T(8,128)S(1)} %multiply_add_fusion.1), channel_id=1, source_target_pairs={{0,4},{1,5},{2,6},{3,7},{4,0},{5,1},{6,2},{7,3},{8,12},{9,13},{10,... | collective-permute-start | bytes 393224 | tf_op jit(solution)/shard_map/ppermute | solution.py:431
  126.9 3.3 %reduce_sum.57 = f32[2,64,64]{2,1,0:T(8,128)S(1)} reduce(f32[2,64,64,128]{3,2,1,0:T(8,128)} %get-tuple-element.35, f32[]{:T(128)} %constant.7.clone.1), dimensions={3}, to_apply=%region_3.4 | reduce | flops 1040384 | bytes 4227076 | tf_op jit(solution)/shard_map/reduce_sum | solution.py:560
  130.3 3.3 %collective-permute-start.9 = (f32[4,64,128]{2,1,0:T(8,128)S(1)}, f32[4,64,128]{2,1,0:T(8,128)S(1)}, u32[]{:S(2)}, u32[]{:S(2)}) collective-permute-start(f32[4,64,128]{2,1,0:T(8,128)S(1)} %add.90), channel_id=1, source_target_pairs={{0,16},{8,24},{16,0},{24,8},{1,17},{9,25},{17,1},{25,9},{2,18},{10... | collective-permute-start | bytes 393224 | tf_op jit(solution)/shard_map/ppermute | solution.py:431
  134.5 5.3 %shard_map.100 = f32[4,64,128]{2,1,0:T(8,128)} custom-call(s32[134]{0:T(256)} %pad_add_fusion.pos_ref, f32[4,64,128]{2,1,0:T(8,128)} %add.86.refs_0_, f32[2,64,64,128]{3,2,1,0:T(8,128)} %broadcast_in_dim.91.refs_1_.ew_ref.refs_2_.refs_5_.refs_6_, f32[2,64,64,128]{3,2,1,0:T(8,128)} %get-tuple-element.43.refs_2_, f32[4,64,128]{2,1,0:T(8,128)} %multiply_add_fusion.refs_3_, ...), custom_call_target="tpu_custom_call" | custom-call | tf_op jit(solution)/shard_map/pallas_call | solution.py:294
  139.8 1.0 reduce_sum.62
  140.9 2.6 %collective-permute-start.18 = (f32[2,128]{1,0:T(2,128)S(1)}, f32[2,128]{1,0:T(2,128)S(1)}, u32[]{:S(2)}, u32[]{:S(2)}) collective-permute-start(f32[2,128]{1,0:T(2,128)S(1)} %reshape.64), channel_id=1, source_target_pairs={{0,8},{8,0},{16,24},{24,16},{1,9},{9,1},{17,25},{25,17},{2,10},{10... | collective-permute-start | bytes 3080 | tf_op jit(solution)/shard_map/ppermute | solution.py:431
  144.3 3.3 %reduce_sum.58 = f32[2,64,64]{2,1,0:T(8,128)S(1)} reduce(f32[2,64,64,128]{3,2,1,0:T(8,128)} %get-tuple-element.42, f32[]{:T(128)} %constant.7.clone.1), dimensions={3}, to_apply=%region_4.5 | reduce | flops 1040384 | bytes 4227076 | tf_op jit(solution)/shard_map/reduce_sum | solution.py:560
  147.7 1.0 collective-permute-start.19
  149.6 2.6 %collective-permute-done.19 = f32[2,128]{1,0:T(2,128)S(1)} collective-permute-done((f32[2,128]{1,0:T(2,128)S(1)}, f32[2,128]{1,0:T(2,128)S(1)}, u32[]{:S(2)}, u32[]{:S(2)}) %collective-permute-start.19) | collective-permute-done | bytes 1056 | tf_op jit(solution)/shard_map/ppermute | solution.py:431
  (70 shorter events, 16.1 us)
Async XLA Ops:
  7.0 9.6 %copy-start.3 = (s32[256,128]{1,0:T(8,128)S(1)}, s32[256,128]{1,0:T(8,128)}, u32[]{:S(2)}) copy-start(s32[256,128]{1,0:T(8,128)} %param.11) | copy-start | bytes 393220
  7.0 13.3 %copy-start.4 = (s32[1,1,2,2]{3,2,1,0:T(2,128)S(1)}, s32[1,1,2,2]{3,2,1,0:T(2,128)}, u32[]{:S(2)}) copy-start(s32[1,1,2,2]{3,2,1,0:T(2,128)} %param.8) | copy-start | bytes 52
  16.2 1.2 collective-permute-start
  17.4 4.5 %collective-permute-start.1 = (f32[2,128]{1,0:T(2,128)S(1)}, f32[2,128]{1,0:T(2,128)S(1)}, u32[]{:S(2)}, u32[]{:S(2)}) collective-permute-start(f32[2,128]{1,0:T(2,128)S(1)} %mul.88), channel_id=1, source_target_pairs={{0,2},{1,3},{2,0},{3,1},{4,6},{5,7},{6,4},{7,5},{8,10},{9,11},{10,... | collective-permute-start | bytes 3080 | tf_op jit(solution)/shard_map/ppermute | solution.py:431
  21.9 3.6 %collective-permute-start.2 = (f32[2,128]{1,0:T(2,128)S(1)}, f32[2,128]{1,0:T(2,128)S(1)}, u32[]{:S(2)}, u32[]{:S(2)}) collective-permute-start(f32[2,128]{1,0:T(2,128)S(1)} %mul.90), channel_id=1, source_target_pairs={{0,4},{1,5},{2,6},{3,7},{4,0},{5,1},{6,2},{7,3},{8,12},{9,13},{10,... | collective-permute-start | bytes 3080 | tf_op jit(solution)/shard_map/ppermute | solution.py:431
  32.0 5.2 %collective-permute-start.3 = (f32[4,64,128]{2,1,0:T(8,128)}, f32[4,64,128]{2,1,0:T(8,128)S(1)}, u32[]{:S(2)}, u32[]{:S(2)}) collective-permute-start(f32[4,64,128]{2,1,0:T(8,128)} %get-tuple-element.29), channel_id=1, source_target_pairs={{0,8},{8,0},{16,24},{24,16},{1,9},{9,1},{17,25},{25,17},{2,10},{10... | collective-permute-start | bytes 393224 | tf_op jit(solution)/shard_map/ppermute | solution.py:431
  38.1 6.1 %collective-permute-start.4 = (f32[4,64,128]{2,1,0:T(8,128)S(1)}, f32[4,64,128]{2,1,0:T(8,128)S(1)}, u32[]{:S(2)}, u32[]{:S(2)}) collective-permute-start(f32[4,64,128]{2,1,0:T(8,128)S(1)} %add.87), channel_id=1, source_target_pairs={{0,16},{8,24},{16,0},{24,8},{1,17},{9,25},{17,1},{25,9},{2,18},{10... | collective-permute-start | bytes 393224 | tf_op jit(solution)/shard_map/ppermute | solution.py:431
  50.6 1.6 %collective-permute-start.5 = (f32[4,64,128]{2,1,0:T(8,128)}, f32[4,64,128]{2,1,0:T(8,128)S(1)}, u32[]{:S(2)}, u32[]{:S(2)}) collective-permute-start(f32[4,64,128]{2,1,0:T(8,128)} %get-tuple-element.33), channel_id=1, source_target_pairs={{0,1},{1,0},{2,3},{3,2},{4,5},{5,4},{6,7},{7,6},{8,9},{9,8},{10,11... | collective-permute-start | bytes 393224 | tf_op jit(solution)/shard_map/ppermute | solution.py:431
  53.1 5.8 %collective-permute-start.6 = (f32[4,64,128]{2,1,0:T(8,128)S(1)}, f32[4,64,128]{2,1,0:T(8,128)S(1)}, u32[]{:S(2)}, u32[]{:S(2)}) collective-permute-start(f32[4,64,128]{2,1,0:T(8,128)S(1)} %mul.92), channel_id=1, source_target_pairs={{0,2},{1,3},{2,0},{3,1},{4,6},{5,7},{6,4},{7,5},{8,10},{9,11},{10,... | collective-permute-start | bytes 393224 | tf_op jit(solution)/shard_map/ppermute | solution.py:431
  58.9 5.0 %collective-permute-start.7 = (f32[4,64,128]{2,1,0:T(8,128)S(1)}, f32[4,64,128]{2,1,0:T(8,128)S(1)}, u32[]{:S(2)}, u32[]{:S(2)}) collective-permute-start(f32[4,64,128]{2,1,0:T(8,128)S(1)} %mul.94), channel_id=1, source_target_pairs={{0,4},{1,5},{2,6},{3,7},{4,0},{5,1},{6,2},{7,3},{8,12},{9,13},{10,... | collective-permute-start | bytes 393224 | tf_op jit(solution)/shard_map/ppermute | solution.py:431
  64.6 9.5 %copy-start.1 = (f32[4,64,128]{2,1,0:T(8,128)S(1)}, f32[4,64,128]{2,1,0:T(8,128)}, u32[]{:S(2)}) copy-start(f32[4,64,128]{2,1,0:T(8,128)} %get-tuple-element.33) | copy-start | bytes 393220
  72.5 1.6 %collective-permute-start.10 = (f32[4,64,128]{2,1,0:T(8,128)}, f32[4,64,128]{2,1,0:T(8,128)S(1)}, u32[]{:S(2)}, u32[]{:S(2)}) collective-permute-start(f32[4,64,128]{2,1,0:T(8,128)} %get-tuple-element.37), channel_id=1, source_target_pairs={{0,1},{1,0},{2,3},{3,2},{4,5},{5,4},{6,7},{7,6},{8,9},{9,8},{10,11... | collective-permute-start | bytes 393224 | tf_op jit(solution)/shard_map/ppermute | solution.py:431
  75.1 5.7 %collective-permute-start.11 = (f32[4,64,128]{2,1,0:T(8,128)S(1)}, f32[4,64,128]{2,1,0:T(8,128)S(1)}, u32[]{:S(2)}, u32[]{:S(2)}) collective-permute-start(f32[4,64,128]{2,1,0:T(8,128)S(1)} %multiply_add_fusion.5), channel_id=1, source_target_pairs={{0,2},{1,3},{2,0},{3,1},{4,6},{5,7},{6,4},{7,5},{8,10},{9,11},{10,... | collective-permute-start | bytes 393224 | tf_op jit(solution)/shard_map/ppermute | solution.py:431
  80.8 5.0 %collective-permute-start.12 = (f32[4,64,128]{2,1,0:T(8,128)S(1)}, f32[4,64,128]{2,1,0:T(8,128)S(1)}, u32[]{:S(2)}, u32[]{:S(2)}) collective-permute-start(f32[4,64,128]{2,1,0:T(8,128)S(1)} %multiply_add_fusion.4), channel_id=1, source_target_pairs={{0,4},{1,5},{2,6},{3,7},{4,0},{5,1},{6,2},{7,3},{8,12},{9,13},{10,... | collective-permute-start | bytes 393224 | tf_op jit(solution)/shard_map/ppermute | solution.py:431
  93.8 5.7 %collective-permute-start.13 = (f32[4,64,128]{2,1,0:T(8,128)}, f32[4,64,128]{2,1,0:T(8,128)S(1)}, u32[]{:S(2)}, u32[]{:S(2)}) collective-permute-start(f32[4,64,128]{2,1,0:T(8,128)} %get-tuple-element.40), channel_id=1, source_target_pairs={{0,8},{8,0},{16,24},{24,16},{1,9},{9,1},{17,25},{25,17},{2,10},{10... | collective-permute-start | bytes 393224 | tf_op jit(solution)/shard_map/ppermute | solution.py:431
  100.4 7.2 %collective-permute-start.14 = (f32[4,64,128]{2,1,0:T(8,128)S(1)}, f32[4,64,128]{2,1,0:T(8,128)S(1)}, u32[]{:S(2)}, u32[]{:S(2)}) collective-permute-start(f32[4,64,128]{2,1,0:T(8,128)S(1)} %add.98), channel_id=1, source_target_pairs={{0,16},{8,24},{16,0},{24,8},{1,17},{9,25},{17,1},{25,9},{2,18},{10... | collective-permute-start | bytes 393224 | tf_op jit(solution)/shard_map/ppermute | solution.py:431
  108.3 12.8 %copy-start = (f32[256,128]{1,0:T(8,128)S(1)}, f32[256,128]{1,0:T(8,128)}, u32[]{:S(2)}) copy-start(f32[256,128]{1,0:T(8,128)} %param.13) | copy-start | bytes 393220
  108.3 13.1 %copy-start.2 = (f32[4,64,128]{2,1,0:T(8,128)S(1)}, f32[4,64,128]{2,1,0:T(8,128)}, u32[]{:S(2)}) copy-start(f32[4,64,128]{2,1,0:T(8,128)} %get-tuple-element.34) | copy-start | bytes 393220
  116.6 1.6 %collective-permute-start.15 = (f32[4,64,128]{2,1,0:T(8,128)}, f32[4,64,128]{2,1,0:T(8,128)S(1)}, u32[]{:S(2)}, u32[]{:S(2)}) collective-permute-start(f32[4,64,128]{2,1,0:T(8,128)} %get-tuple-element.44), channel_id=1, source_target_pairs={{0,1},{1,0},{2,3},{3,2},{4,5},{5,4},{6,7},{7,6},{8,9},{9,8},{10,11... | collective-permute-start | bytes 393224 | tf_op jit(solution)/shard_map/ppermute | solution.py:431
  119.3 5.7 %collective-permute-start.16 = (f32[4,64,128]{2,1,0:T(8,128)S(1)}, f32[4,64,128]{2,1,0:T(8,128)S(1)}, u32[]{:S(2)}, u32[]{:S(2)}) collective-permute-start(f32[4,64,128]{2,1,0:T(8,128)S(1)} %multiply_add_fusion.2), channel_id=1, source_target_pairs={{0,2},{1,3},{2,0},{3,1},{4,6},{5,7},{6,4},{7,5},{8,10},{9,11},{10,... | collective-permute-start | bytes 393224 | tf_op jit(solution)/shard_map/ppermute | solution.py:431
  121.4 8.8 %collective-permute-start.8 = (f32[4,64,128]{2,1,0:T(8,128)S(1)}, f32[4,64,128]{2,1,0:T(8,128)S(1)}, u32[]{:S(2)}, u32[]{:S(2)}) collective-permute-start(f32[4,64,128]{2,1,0:T(8,128)S(1)} %copy-done.2), channel_id=1, source_target_pairs={{0,8},{8,0},{16,24},{24,16},{1,9},{9,1},{17,25},{25,17},{2,10},{10... | collective-permute-start | bytes 393224 | tf_op jit(solution)/shard_map/ppermute | solution.py:431
  125.1 8.5 %collective-permute-start.17 = (f32[4,64,128]{2,1,0:T(8,128)S(1)}, f32[4,64,128]{2,1,0:T(8,128)S(1)}, u32[]{:S(2)}, u32[]{:S(2)}) collective-permute-start(f32[4,64,128]{2,1,0:T(8,128)S(1)} %multiply_add_fusion.1), channel_id=1, source_target_pairs={{0,4},{1,5},{2,6},{3,7},{4,0},{5,1},{6,2},{7,3},{8,12},{9,13},{10,... | collective-permute-start | bytes 393224 | tf_op jit(solution)/shard_map/ppermute | solution.py:431
  130.3 13.3 %collective-permute-start.9 = (f32[4,64,128]{2,1,0:T(8,128)S(1)}, f32[4,64,128]{2,1,0:T(8,128)S(1)}, u32[]{:S(2)}, u32[]{:S(2)}) collective-permute-start(f32[4,64,128]{2,1,0:T(8,128)S(1)} %add.90), channel_id=1, source_target_pairs={{0,16},{8,24},{16,0},{24,8},{1,17},{9,25},{17,1},{25,9},{2,18},{10... | collective-permute-start | bytes 393224 | tf_op jit(solution)/shard_map/ppermute | solution.py:431
  140.9 6.7 %collective-permute-start.18 = (f32[2,128]{1,0:T(2,128)S(1)}, f32[2,128]{1,0:T(2,128)S(1)}, u32[]{:S(2)}, u32[]{:S(2)}) collective-permute-start(f32[2,128]{1,0:T(2,128)S(1)} %reshape.64), channel_id=1, source_target_pairs={{0,8},{8,0},{16,24},{24,16},{1,9},{9,1},{17,25},{25,17},{2,10},{10... | collective-permute-start | bytes 3080 | tf_op jit(solution)/shard_map/ppermute | solution.py:431
  147.7 4.5 %collective-permute-start.19 = (f32[2,128]{1,0:T(2,128)S(1)}, f32[2,128]{1,0:T(2,128)S(1)}, u32[]{:S(2)}, u32[]{:S(2)}) collective-permute-start(f32[2,128]{1,0:T(2,128)S(1)} %add.108), channel_id=1, source_target_pairs={{0,16},{8,24},{16,0},{24,8},{1,17},{9,25},{17,1},{25,9},{2,18},{10... | collective-permute-start | bytes 3080 | tf_op jit(solution)/shard_map/ppermute | solution.py:431

commit v13 on v11

--- a/solution.py
+++ b/solution.py
@@ -90,7 +90,7 @@
     refs = list(refs)
     spread_ref = refs.pop(0)
     u_ref = refs.pop(0) if has_u else None
-    ew_ref, ba_ref, whole_ref, rows_ref, here_ref, h_scr = refs
+    ew_ref, ba_ref, h_scr, whole_ref, rows_ref, here_ref = refs
     k = pl.program_id(0)
     n_c = ew_ref.shape[1]
     shape = ew_ref.shape[2:]
@@ -103,7 +103,7 @@
         if has_u:
             m = m - u_ref[0, c]
         h = jnp.where(ew_ref[0, c] > 0, jnp.tanh(0.5 * m), 1.0)
-        h_scr[c] = h
+        h_scr[0, c] = h
         ba_ref[0, c] = carry
         return carry * h
 
@@ -113,7 +113,7 @@
     def backward(i, carry):
         c = pos_ref[base + count - 1 - i]
         ba_ref[0, c] = ba_ref[0, c] * carry
-        return carry * h_scr[c]
+        return carry * h_scr[0, c]
 
     _loop(count, backward, jnp.ones(shape, F32))
 
@@ -210,17 +210,15 @@
     gothers_ref[p] = gothers_ref[p] + grad_factor * sign * here
 
 
-def _bwd_products_kernel(has_u, emit_gm, slots, pos_ref, *refs):
+def _bwd_products_kernel(emit_gm, slots, pos_ref, *refs):
     refs = list(refs)
-    spread_ref = refs.pop(0)
-    u_ref = refs.pop(0) if has_u else None
-    ew_ref, gba_ref, grows_ref, ghere_ref, whole_ref, here_ref = refs[:6]
+    h_ref, gba_ref, grows_ref, ghere_ref, whole_ref, here_ref = refs[:6]
     refs = refs[6:]
     gm_ref = refs.pop(0) if emit_gm else None
-    col_ref, h_scr, p_scr, q_scr = refs
+    col_ref, p_scr, q_scr = refs
     k = pl.program_id(0)
-    n_c = ew_ref.shape[1]
-    shape = ew_ref.shape[2:]
+    n_c = h_ref.shape[1]
+    shape = h_ref.shape[2:]
 
     @pl.when(k == 0)
     def _():
@@ -244,11 +242,7 @@
     def forward(i, carry):
         prod, grad = carry
         c = pos_ref[base + i]
-        m = _spread_row(spread_ref, c, shape)
-        if has_u:
-            m = m - u_ref[0, c]
-        h = jnp.where(ew_ref[0, c] > 0, jnp.tanh(0.5 * m), 1.0)
-        h_scr[c] = h
+        h = h_ref[0, c]
         p_scr[c] = prod
         q_scr[c] = grad
         return (prod * h, grad * h + gba_ref[0, c] * prod)
@@ -260,10 +254,10 @@
     def backward(i, carry):
         prod, grad = carry
         c = pos_ref[base + count - 1 - i]
-        h = h_scr[c]
+        h = h_ref[0, c]
         before = p_scr[c]
         gh = q_scr[c] * prod + before * (grad + gwh * prod)
-        gm = jnp.where(ew_ref[0, c] > 0, gh * (0.5 * (1.0 - h * h)), 0.0)
+        gm = gh * (0.5 * (1.0 - h * h))
         if emit_gm:
             gm_ref[0, c] = gm
         col_ref[q, pl.ds(c, 1), :] = col_ref[q, pl.ds(c, 1), :] + jnp.sum(gm, axis=0, keepdims=True)
@@ -310,17 +304,12 @@
     inputs = [("column", spread)] + ([("dense", u)] if has_u else []) + [("dense", ew)]
     outs = [
         ("dense", jax.ShapeDtypeStruct(ew.shape, F32)),
+        ("dense", jax.ShapeDtypeStruct(ew.shape, F32)),
         ("full", jax.ShapeDtypeStruct((k, r, s), F32)),
         ("full", jax.ShapeDtypeStruct((blocks, r, s), F32)),
         ("full", jax.ShapeDtypeStruct((k, r, s), F32)),
     ]
-    return _call(
-        functools.partial(_fwd_products_kernel, has_u, k, blocks),
-        pos,
-        inputs,
-        outs,
-        [_vmem((c, r, s))],
-    )
+    return _call(functools.partial(_fwd_products_kernel, has_u, k, blocks), pos, inputs, outs)
 
 
 def fwd_messages(pos, ba, sign, here, others, ew, col_blocks):
@@ -356,26 +345,25 @@
     )
 
 
-def bwd_products(pos, spread, u, ew, gba, grows, ghere, whole, here, col_blocks, emit_gm):
-    k, c, r, s = ew.shape
-    has_u = u is not None
-    inputs = [("column", spread)] + ([("dense", u)] if has_u else []) + [
-        ("dense", ew),
+def bwd_products(pos, h, gba, grows, ghere, whole, here, col_blocks, emit_gm):
+    k, c, r, s = h.shape
+    inputs = [
+        ("dense", h),
         ("dense", gba),
         ("full", grows),
         ("full", ghere),
         ("full", whole),
         ("full", here),
     ]
-    outs = ([("dense", jax.ShapeDtypeStruct(ew.shape, F32))] if emit_gm else []) + [
+    outs = ([("dense", jax.ShapeDtypeStruct(h.shape, F32))] if emit_gm else []) + [
         ("full", jax.ShapeDtypeStruct((col_blocks, c, s), F32))
     ]
     results = _call(
-        functools.partial(_bwd_products_kernel, has_u, emit_gm, k),
+        functools.partial(_bwd_products_kernel, emit_gm, k),
         pos,
         inputs,
         outs,
-        [_vmem((c, r, s)) for _ in range(3)],
+        [_vmem((c, r, s)) for _ in range(2)],
     )
     if emit_gm:
         return results[0], results[1]
@@ -532,9 +520,9 @@
     saved = []
     total = None
     for step in range(ITERS):
-        ba, whole, rows, others_here = fwd_products(pos, spread, u, ew, check_blocks)
+        ba, halves, whole, rows, others_here = fwd_products(pos, spread, u, ew, check_blocks)
         others, trail = others_forward(rows, check_blocks, n_var, uniform=(step == 0 and (check_blocks * TILE) % shots == 0))
-        saved.append((spread, u, ba, whole, others_here, others, trail))
+        saved.append((halves, ba, whole, others_here, others, trail))
         if step + 1 < ITERS:
             u, column = fwd_messages(pos, ba, sign_slot, others_here, others, ew, column_blocks)
             total = prior_dev[:, :, None] + checks_total(column, n_chk)
@@ -545,7 +533,7 @@
     grad_m = None
     acc = None
     for step in reversed(range(ITERS)):
-        spread_t, u_prev, ba, whole, others_here, others, trail = saved[step]
+        halves, ba, whole, others_here, others, trail = saved[step]
         prior_grad = prior_grad + jnp.sum(grad_total, axis=2)
         if step + 1 == ITERS:
             acc, grad_ba, grad_here, grad_others, last_column = bwd_messages(
@@ -559,7 +547,7 @@
             )
         grad_rows = others_backward(trail, grad_others, check_blocks, n_var)
         grad_m, column = bwd_products(
-            pos, spread_t, u_prev, ew, grad_ba, grad_rows, grad_here, whole, others_here,
+            pos, halves, grad_ba, grad_rows, grad_here, whole, others_here,
             column_blocks, step > 0,
         )
         if step > 0:

time: 152 us -> 152 us (level)
  starting transfers between devices: 27 us -> 33.4 us
  waiting for transfers between devices: 48.5 us -> 42.5 us
    ppermute x20, starting transfers between devices: 27 us -> 33.4 us  [_swap(): return lax.ppermute(value, axis, perm)]
    ppermute x20, waiting for transfers between devices: 48.5 us -> 42.5 us  [_swap(): return lax.ppermute(value, axis, perm)]
  transfers between devices with their start and end apart: 20 -> 20, of which waited for: 18 -> 17; matrix products, arithmetic and copies ran while one was open for 6% -> 6% of each run, Pallas kernels for 4% -> 3%
where the time goes in v13:
time: 152 us; the launch traced here: 151 us
  Pallas kernels  46.2 us (30%)
  waiting for transfers between devices  42.5 us (28%)
  starting transfers between devices  33.4 us (22%)
  other arithmetic  16.5 us (11%)
  local copies, waits for them, and re-layouts  11.1 us (7%)
    pallas_call x7, Pallas kernels, _call(): pl.pallas_call(kernel, grid_spec=grid_spec, out_shape=[o for kind, o in o...  46.2 us
    ppermute x20, waiting for transfers between devices, _swap(): return lax.ppermute(value, axis, perm)  42.5 us
    ppermute x20, starting transfers between devices, _swap(): return lax.ppermute(value, axis, perm)  33.4 us
    reduce_sum x1, other arithmetic, body(): jnp.sum(acc, axis=3)  3.34 us
  transfers between devices with their start and end apart: 20, of which 17 were waited for; matrix products, arithmetic and copies ran while one was open for 6% of the time, Pallas kernels for 3%

profile of v13, /device:TPU:0, one launch (start us, length us, event | category | flops | bytes accessed | tf_op | source)
XLA Modules:
  0.0 151.4 jit_solution(11562486760371280580)
XLA Ops:
  2.7 1.0 sort.17
  7.0 2.6 %broadcast_in_dim.91.refs_1_.ew_ref.refs_2_.refs_5_.refs_6_ = f32[2,64,64,128]{3,2,1,0:T(8,128)} broadcast(f32[2,64,64]{2,1,0:T(8,128)S(1)} %multiply_bitcast_fusion), dimensions={0,1,2} | broadcast | bytes 4227072 | tf_op jit(solution)/shard_map/broadcast_in_dim | solution.py:514
  10.4 6.1 %shard_map.94 = (f32[2,64,64,128]{3,2,1,0:T(8,128)}, f32[2,64,64,128]{3,2,1,0:T(8,128)}, f32[2,64,128]{2,1,0:T(8,128)}, f32[4,64,128]{2,1,0:T(8,128)}, f32[2,64,128]{2,1,0:T(8,128)}) custom-call(s32[134]{0:T(256)} %pad_add_fusion.pos_ref, f32[4,64,128]{2,1,0:T(8,128)} %add.79.refs_0_, f32[2,64,64,128]{3,2,1,0:T(8,128)} %broadcast_in_dim.91.refs_1_.ew_ref.refs_2_.refs_5_.refs_6_), custom_call_target="tpu_custom_call" | custom-call | tf_op jit(solution)/shard_map/pallas_call | solution.py:288
  16.4 1.0 slice_reduce_fusion
  18.9 2.7 %collective-permute-start.1 = (f32[2,128]{1,0:T(2,128)S(1)}, f32[2,128]{1,0:T(2,128)S(1)}, u32[]{:S(2)}, u32[]{:S(2)}) collective-permute-start(f32[2,128]{1,0:T(2,128)S(1)} %mul.88), channel_id=1, source_target_pairs={{0,2},{1,3},{2,0},{3,1},{4,6},{5,7},{6,4},{7,5},{8,10},{9,11},{10,... | collective-permute-start | bytes 3080 | tf_op jit(solution)/shard_map/ppermute | solution.py:419
  21.8 1.4 collective-permute-done.1
  23.2 2.1 %collective-permute-start.2 = (f32[2,128]{1,0:T(2,128)S(1)}, f32[2,128]{1,0:T(2,128)S(1)}, u32[]{:S(2)}, u32[]{:S(2)}) collective-permute-start(f32[2,128]{1,0:T(2,128)S(1)} %mul.90), channel_id=1, source_target_pairs={{0,4},{1,5},{2,6},{3,7},{4,0},{5,1},{6,2},{7,3},{8,12},{9,13},{10,... | collective-permute-start | bytes 3080 | tf_op jit(solution)/shard_map/ppermute | solution.py:419
  27.7 5.6 %shard_map.95 = (f32[2,64,64,128]{3,2,1,0:T(8,128)}, f32[4,64,128]{2,1,0:T(8,128)}) custom-call(s32[134]{0:T(256)} %pad_add_fusion.pos_ref, f32[2,64,64,128]{3,2,1,0:T(8,128)} %get-tuple-element.28.ba_ref.refs_2_, f32[2,64,128]{2,1,0:T(8,128)} %copy.30.sign_ref.refs_2_.refs_3_, f32[2,64,128]{2,1,0:T(8,128)} %get-tuple-element.29.here_ref.refs_4_.refs_5_, ...), custom_call_target="tpu_custom_call" | custom-call | tf_op jit(solution)/shard_map/pallas_call | solution.py:288
  33.3 2.6 %collective-permute-start.3 = (f32[4,64,128]{2,1,0:T(8,128)}, f32[4,64,128]{2,1,0:T(8,128)S(1)}, u32[]{:S(2)}, u32[]{:S(2)}) collective-permute-start(f32[4,64,128]{2,1,0:T(8,128)} %get-tuple-element.31), channel_id=1, source_target_pairs={{0,8},{8,0},{16,24},{24,16},{1,9},{9,1},{17,25},{25,17},{2,10},{10... | collective-permute-start | bytes 393224 | tf_op jit(solution)/shard_map/ppermute | solution.py:419
  35.8 3.2 %collective-permute-done.3 = f32[4,64,128]{2,1,0:T(8,128)S(1)} collective-permute-done((f32[4,64,128]{2,1,0:T(8,128)}, f32[4,64,128]{2,1,0:T(8,128)S(1)}, u32[]{:S(2)}, u32[]{:S(2)}) %collective-permute-start.3) | collective-permute-done | bytes 131104 | tf_op jit(solution)/shard_map/ppermute | solution.py:419
  39.0 0.9 add.80
  39.9 2.6 %collective-permute-start.4 = (f32[4,64,128]{2,1,0:T(8,128)S(1)}, f32[4,64,128]{2,1,0:T(8,128)S(1)}, u32[]{:S(2)}, u32[]{:S(2)}) collective-permute-start(f32[4,64,128]{2,1,0:T(8,128)S(1)} %add.80), channel_id=1, source_target_pairs={{0,16},{8,24},{16,0},{24,8},{1,17},{9,25},{17,1},{25,9},{2,18},{10... | collective-permute-start | bytes 393224 | tf_op jit(solution)/shard_map/ppermute | solution.py:419
  42.5 3.3 %collective-permute-done.4 = f32[4,64,128]{2,1,0:T(8,128)S(1)} collective-permute-done((f32[4,64,128]{2,1,0:T(8,128)S(1)}, f32[4,64,128]{2,1,0:T(8,128)S(1)}, u32[]{:S(2)}, u32[]{:S(2)}) %collective-permute-start.4) | collective-permute-done | bytes 131104 | tf_op jit(solution)/shard_map/ppermute | solution.py:419
  46.6 6.7 %shard_map.96 = (f32[2,64,64,128]{3,2,1,0:T(8,128)}, f32[2,64,64,128]{3,2,1,0:T(8,128)}, f32[2,64,128]{2,1,0:T(8,128)}, f32[4,64,128]{2,1,0:T(8,128)}, f32[2,64,128]{2,1,0:T(8,128)}) custom-call(s32[134]{0:T(256)} %pad_add_fusion.pos_ref, f32[4,64,128]{2,1,0:T(8,128)} %add_add_fusion.1.refs_0_, f32[2,64,64,128]{3,2,1,0:T(8,128)} %get-tuple-element.32.refs_1_, ...), custom_call_target="tpu_custom_call" | custom-call | tf_op jit(solution)/shard_map/pallas_call | solution.py:288
  53.4 1.5 %collective-permute-done.5 = f32[4,64,128]{2,1,0:T(8,128)S(1)} collective-permute-done((f32[4,64,128]{2,1,0:T(8,128)}, f32[4,64,128]{2,1,0:T(8,128)S(1)}, u32[]{:S(2)}, u32[]{:S(2)}) %collective-permute-start.5) | collective-permute-done | bytes 131104 | tf_op jit(solution)/shard_map/ppermute | solution.py:419
  54.9 0.9 mul.92
  55.9 3.6 %collective-permute-start.6 = (f32[4,64,128]{2,1,0:T(8,128)S(1)}, f32[4,64,128]{2,1,0:T(8,128)S(1)}, u32[]{:S(2)}, u32[]{:S(2)}) collective-permute-start(f32[4,64,128]{2,1,0:T(8,128)S(1)} %mul.92), channel_id=1, source_target_pairs={{0,2},{1,3},{2,0},{3,1},{4,6},{5,7},{6,4},{7,5},{8,10},{9,11},{10,... | collective-permute-start | bytes 393224 | tf_op jit(solution)/shard_map/ppermute | solution.py:419
  59.5 3.8 %collective-permute-done.6 = f32[4,64,128]{2,1,0:T(8,128)S(1)} collective-permute-done((f32[4,64,128]{2,1,0:T(8,128)S(1)}, f32[4,64,128]{2,1,0:T(8,128)S(1)}, u32[]{:S(2)}, u32[]{:S(2)}) %collective-permute-start.6) | collective-permute-done | bytes 131104 | tf_op jit(solution)/shard_map/ppermute | solution.py:419
  63.3 1.8 %collective-permute-start.7 = (f32[4,64,128]{2,1,0:T(8,128)S(1)}, f32[4,64,128]{2,1,0:T(8,128)S(1)}, u32[]{:S(2)}, u32[]{:S(2)}) collective-permute-start(f32[4,64,128]{2,1,0:T(8,128)S(1)} %mul.94), channel_id=1, source_target_pairs={{0,4},{1,5},{2,6},{3,7},{4,0},{5,1},{6,2},{7,3},{8,12},{9,13},{10,... | collective-permute-start | bytes 393224 | tf_op jit(solution)/shard_map/ppermute | solution.py:419
  65.1 3.3 %collective-permute-done.7 = f32[4,64,128]{2,1,0:T(8,128)S(1)} collective-permute-done((f32[4,64,128]{2,1,0:T(8,128)S(1)}, f32[4,64,128]{2,1,0:T(8,128)S(1)}, u32[]{:S(2)}, u32[]{:S(2)}) %collective-permute-start.7) | collective-permute-done | bytes 131104 | tf_op jit(solution)/shard_map/ppermute | solution.py:419
  69.1 7.7 %shard_map.97 = (f32[2,64,64,128]{3,2,1,0:T(8,128)}, f32[2,64,64,128]{3,2,1,0:T(8,128)}, f32[2,64,128]{2,1,0:T(8,128)}, f32[4,64,128]{2,1,0:T(8,128)}, f32[4,64,128]{2,1,0:T(8,128)}) custom-call(s32[134]{0:T(256)} %pad_add_fusion.pos_ref, f32[4,64,128]{2,1,0:T(8,128)} %bitcast.15, f32[2,64,64,128]{3,2,1,0:T(8,128)} %get-tuple-element.33.refs_1_, ...), custom_call_target="tpu_custom_call" | custom-call | tf_op jit(solution)/shard_map/pallas_call | solution.py:288
  76.9 1.5 %collective-permute-done.10 = f32[4,64,128]{2,1,0:T(8,128)S(1)} collective-permute-done((f32[4,64,128]{2,1,0:T(8,128)}, f32[4,64,128]{2,1,0:T(8,128)S(1)}, u32[]{:S(2)}, u32[]{:S(2)}) %collective-permute-start.10) | collective-permute-done | bytes 131104 | tf_op jit(solution)/shard_map/ppermute | solution.py:419
  78.5 0.9 multiply_add_fusion.5
  79.4 1.8 %collective-permute-start.11 = (f32[4,64,128]{2,1,0:T(8,128)S(1)}, f32[4,64,128]{2,1,0:T(8,128)S(1)}, u32[]{:S(2)}, u32[]{:S(2)}) collective-permute-start(f32[4,64,128]{2,1,0:T(8,128)S(1)} %multiply_add_fusion.5), channel_id=1, source_target_pairs={{0,2},{1,3},{2,0},{3,1},{4,6},{5,7},{6,4},{7,5},{8,10},{9,11},{10,... | collective-permute-start | bytes 393224 | tf_op jit(solution)/shard_map/ppermute | solution.py:419
  81.2 3.8 %collective-permute-done.11 = f32[4,64,128]{2,1,0:T(8,128)S(1)} collective-permute-done((f32[4,64,128]{2,1,0:T(8,128)S(1)}, f32[4,64,128]{2,1,0:T(8,128)S(1)}, u32[]{:S(2)}, u32[]{:S(2)}) %collective-permute-start.11) | collective-permute-done | bytes 131104 | tf_op jit(solution)/shard_map/ppermute | solution.py:419
  85.0 1.8 %collective-permute-start.12 = (f32[4,64,128]{2,1,0:T(8,128)S(1)}, f32[4,64,128]{2,1,0:T(8,128)S(1)}, u32[]{:S(2)}, u32[]{:S(2)}) collective-permute-start(f32[4,64,128]{2,1,0:T(8,128)S(1)} %multiply_add_fusion.4), channel_id=1, source_target_pairs={{0,4},{1,5},{2,6},{3,7},{4,0},{5,1},{6,2},{7,3},{8,12},{9,13},{10,... | collective-permute-start | bytes 393224 | tf_op jit(solution)/shard_map/ppermute | solution.py:419
  86.9 3.2 %collective-permute-done.12 = f32[4,64,128]{2,1,0:T(8,128)S(1)} collective-permute-done((f32[4,64,128]{2,1,0:T(8,128)S(1)}, f32[4,64,128]{2,1,0:T(8,128)S(1)}, u32[]{:S(2)}, u32[]{:S(2)}) %collective-permute-start.12) | collective-permute-done | bytes 131104 | tf_op jit(solution)/shard_map/ppermute | solution.py:419
  90.8 5.7 %shard_map.98 = (f32[2,64,64,128]{3,2,1,0:T(8,128)}, f32[4,64,128]{2,1,0:T(8,128)}) custom-call(s32[134]{0:T(256)} %pad_add_fusion.pos_ref, f32[2,64,64,128]{3,2,1,0:T(8,128)} %get-tuple-element.37.refs_0_, f32[2,64,64,128]{3,2,1,0:T(8,128)} %get-tuple-element.38.refs_1_, f32[4,64,128]{2,1,0:T(8,128)} %multiply_add_fusion.3.refs_2_, ...), custom_call_target="tpu_custom_call" | custom-call | tf_op jit(solution)/shard_map/pallas_call | solution.py:288
  96.5 1.1 collective-permute-start.13
  97.6 4.1 %collective-permute-done.13 = f32[4,64,128]{2,1,0:T(8,128)S(1)} collective-permute-done((f32[4,64,128]{2,1,0:T(8,128)}, f32[4,64,128]{2,1,0:T(8,128)S(1)}, u32[]{:S(2)}, u32[]{:S(2)}) %collective-permute-start.13) | collective-permute-done | bytes 131104 | tf_op jit(solution)/shard_map/ppermute | solution.py:419
  101.7 0.9 add.91
  102.6 2.2 %collective-permute-start.14 = (f32[4,64,128]{2,1,0:T(8,128)S(1)}, f32[4,64,128]{2,1,0:T(8,128)S(1)}, u32[]{:S(2)}, u32[]{:S(2)}) collective-permute-start(f32[4,64,128]{2,1,0:T(8,128)S(1)} %add.91), channel_id=1, source_target_pairs={{0,16},{8,24},{16,0},{24,8},{1,17},{9,25},{17,1},{25,9},{2,18},{10... | collective-permute-start | bytes 393224 | tf_op jit(solution)/shard_map/ppermute | solution.py:419
  104.8 5.1 %collective-permute-done.14 = f32[4,64,128]{2,1,0:T(8,128)S(1)} collective-permute-done((f32[4,64,128]{2,1,0:T(8,128)S(1)}, f32[4,64,128]{2,1,0:T(8,128)S(1)}, u32[]{:S(2)}, u32[]{:S(2)}) %collective-permute-start.14) | collective-permute-done | bytes 131104 | tf_op jit(solution)/shard_map/ppermute | solution.py:419
  110.7 9.5 %shard_map.99 = (f32[2,64,64,128]{3,2,1,0:T(8,128)}, f32[2,64,64,128]{3,2,1,0:T(8,128)}, f32[2,64,128]{2,1,0:T(8,128)}, f32[4,64,128]{2,1,0:T(8,128)}) custom-call(s32[134]{0:T(256)} %pad_add_fusion.pos_ref, f32[4,64,128]{2,1,0:T(8,128)} %get-tuple-element.52.refs_0_, f32[2,64,64,128]{3,2,1,0:T(8,128)} %get-tuple-element.43.refs_1_, ...), custom_call_target="tpu_custom_call" | custom-call | tf_op jit(solution)/shard_map/pallas_call | solution.py:288
  120.3 1.5 collective-permute-done.15
  121.7 1.0 multiply_add_fusion.2
  122.8 1.9 %collective-permute-start.16 = (f32[4,64,128]{2,1,0:T(8,128)S(1)}, f32[4,64,128]{2,1,0:T(8,128)S(1)}, u32[]{:S(2)}, u32[]{:S(2)}) collective-permute-start(f32[4,64,128]{2,1,0:T(8,128)S(1)} %multiply_add_fusion.2), channel_id=1, source_target_pairs={{0,2},{1,3},{2,0},{3,1},{4,6},{5,7},{6,4},{7,5},{8,10},{9,11},{10,... | collective-permute-start | bytes 393224 | tf_op jit(solution)/shard_map/ppermute | solution.py:419
  125.5 3.1 %collective-permute-done.16 = f32[4,64,128]{2,1,0:T(8,128)S(1)} collective-permute-done((f32[4,64,128]{2,1,0:T(8,128)S(1)}, f32[4,64,128]{2,1,0:T(8,128)S(1)}, u32[]{:S(2)}, u32[]{:S(2)}) %collective-permute-start.16) | collective-permute-done | bytes 131104 | tf_op jit(solution)/shard_map/ppermute | solution.py:419
  128.7 2.2 %collective-permute-start.17 = (f32[4,64,128]{2,1,0:T(8,128)S(1)}, f32[4,64,128]{2,1,0:T(8,128)S(1)}, u32[]{:S(2)}, u32[]{:S(2)}) collective-permute-start(f32[4,64,128]{2,1,0:T(8,128)S(1)} %multiply_add_fusion.1), channel_id=1, source_target_pairs={{0,4},{1,5},{2,6},{3,7},{4,0},{5,1},{6,2},{7,3},{8,12},{9,13},{10,... | collective-permute-start | bytes 393224 | tf_op jit(solution)/shard_map/ppermute | solution.py:419
  131.1 1.6 %collective-permute-start.9 = (f32[4,64,128]{2,1,0:T(8,128)S(1)}, f32[4,64,128]{2,1,0:T(8,128)S(1)}, u32[]{:S(2)}, u32[]{:S(2)}) collective-permute-start(f32[4,64,128]{2,1,0:T(8,128)S(1)} %add.83), channel_id=1, source_target_pairs={{0,16},{8,24},{16,0},{24,8},{1,17},{9,25},{17,1},{25,9},{2,18},{10... | collective-permute-start | bytes 393224 | tf_op jit(solution)/shard_map/ppermute | solution.py:419
  132.7 1.2 collective-permute-done.17
  133.9 0.9 multiply_add_fusion.refs_2_
  134.7 4.9 %shard_map.100 = f32[4,64,128]{2,1,0:T(8,128)} custom-call(s32[134]{0:T(256)} %pad_add_fusion.pos_ref, f32[2,64,64,128]{3,2,1,0:T(8,128)} %get-tuple-element.46.refs_0_, f32[2,64,64,128]{3,2,1,0:T(8,128)} %get-tuple-element.47.refs_1_, f32[4,64,128]{2,1,0:T(8,128)} %multiply_add_fusion.refs_2_, f32[2,64,128]{2,1,0:T(8,128)} %get-tuple-element.49.refs_3_, ...), custom_call_target="tpu_custom_call" | custom-call | tf_op jit(solution)/shard_map/pallas_call | solution.py:288
  139.7 1.0 reduce_sum.52
  140.8 1.4 collective-permute-start.18
  142.9 3.3 %reduce_sum.48 = f32[2,64,64]{2,1,0:T(8,128)S(1)} reduce(f32[2,64,64,128]{3,2,1,0:T(8,128)} %get-tuple-element.45, f32[]{:T(128)} %constant.7.clone.1), dimensions={3}, to_apply=%region_3.4 | reduce | flops 1040384 | bytes 4227076 | tf_op jit(solution)/shard_map/reduce_sum | solution.py:561
  146.3 2.6 %collective-permute-start.19 = (f32[2,128]{1,0:T(2,128)S(1)}, f32[2,128]{1,0:T(2,128)S(1)}, u32[]{:S(2)}, u32[]{:S(2)}) collective-permute-start(f32[2,128]{1,0:T(2,128)S(1)} %add.99), channel_id=1, source_target_pairs={{0,16},{8,24},{16,0},{24,8},{1,17},{9,25},{17,1},{25,9},{2,18},{10... | collective-permute-start | bytes 3080 | tf_op jit(solution)/shard_map/ppermute | solution.py:419
  149.8 1.0 collective-permute-done.19
  (69 shorter events, 15.9 us)
Async XLA Ops:
  7.0 11.1 %copy-start.3 = (s32[256,128]{1,0:T(8,128)S(1)}, s32[256,128]{1,0:T(8,128)}, u32[]{:S(2)}) copy-start(s32[256,128]{1,0:T(8,128)} %param.11) | copy-start | bytes 393220
  7.0 14.6 %copy-start.4 = (s32[1,1,2,2]{3,2,1,0:T(2,128)S(1)}, s32[1,1,2,2]{3,2,1,0:T(2,128)}, u32[]{:S(2)}) copy-start(s32[1,1,2,2]{3,2,1,0:T(2,128)} %param.8) | copy-start | bytes 52
  17.5 1.4 collective-permute-start
  18.9 4.3 %collective-permute-start.1 = (f32[2,128]{1,0:T(2,128)S(1)}, f32[2,128]{1,0:T(2,128)S(1)}, u32[]{:S(2)}, u32[]{:S(2)}) collective-permute-start(f32[2,128]{1,0:T(2,128)S(1)} %mul.88), channel_id=1, source_target_pairs={{0,2},{1,3},{2,0},{3,1},{4,6},{5,7},{6,4},{7,5},{8,10},{9,11},{10,... | collective-permute-start | bytes 3080 | tf_op jit(solution)/shard_map/ppermute | solution.py:419
  23.2 3.6 %collective-permute-start.2 = (f32[2,128]{1,0:T(2,128)S(1)}, f32[2,128]{1,0:T(2,128)S(1)}, u32[]{:S(2)}, u32[]{:S(2)}) collective-permute-start(f32[2,128]{1,0:T(2,128)S(1)} %mul.90), channel_id=1, source_target_pairs={{0,4},{1,5},{2,6},{3,7},{4,0},{5,1},{6,2},{7,3},{8,12},{9,13},{10,... | collective-permute-start | bytes 3080 | tf_op jit(solution)/shard_map/ppermute | solution.py:419
  33.3 5.7 %collective-permute-start.3 = (f32[4,64,128]{2,1,0:T(8,128)}, f32[4,64,128]{2,1,0:T(8,128)S(1)}, u32[]{:S(2)}, u32[]{:S(2)}) collective-permute-start(f32[4,64,128]{2,1,0:T(8,128)} %get-tuple-element.31), channel_id=1, source_target_pairs={{0,8},{8,0},{16,24},{24,16},{1,9},{9,1},{17,25},{25,17},{2,10},{10... | collective-permute-start | bytes 393224 | tf_op jit(solution)/shard_map/ppermute | solution.py:419
  39.9 5.9 %collective-permute-start.4 = (f32[4,64,128]{2,1,0:T(8,128)S(1)}, f32[4,64,128]{2,1,0:T(8,128)S(1)}, u32[]{:S(2)}, u32[]{:S(2)}) collective-permute-start(f32[4,64,128]{2,1,0:T(8,128)S(1)} %add.80), channel_id=1, source_target_pairs={{0,16},{8,24},{16,0},{24,8},{1,17},{9,25},{17,1},{25,9},{2,18},{10... | collective-permute-start | bytes 393224 | tf_op jit(solution)/shard_map/ppermute | solution.py:419
  53.3 1.6 %collective-permute-start.5 = (f32[4,64,128]{2,1,0:T(8,128)}, f32[4,64,128]{2,1,0:T(8,128)S(1)}, u32[]{:S(2)}, u32[]{:S(2)}) collective-permute-start(f32[4,64,128]{2,1,0:T(8,128)} %get-tuple-element.35), channel_id=1, source_target_pairs={{0,1},{1,0},{2,3},{3,2},{4,5},{5,4},{6,7},{7,6},{8,9},{9,8},{10,11... | collective-permute-start | bytes 393224 | tf_op jit(solution)/shard_map/ppermute | solution.py:419
  55.9 7.4 %collective-permute-start.6 = (f32[4,64,128]{2,1,0:T(8,128)S(1)}, f32[4,64,128]{2,1,0:T(8,128)S(1)}, u32[]{:S(2)}, u32[]{:S(2)}) collective-permute-start(f32[4,64,128]{2,1,0:T(8,128)S(1)} %mul.92), channel_id=1, source_target_pairs={{0,2},{1,3},{2,0},{3,1},{4,6},{5,7},{6,4},{7,5},{8,10},{9,11},{10,... | collective-permute-start | bytes 393224 | tf_op jit(solution)/shard_map/ppermute | solution.py:419
  63.3 5.1 %collective-permute-start.7 = (f32[4,64,128]{2,1,0:T(8,128)S(1)}, f32[4,64,128]{2,1,0:T(8,128)S(1)}, u32[]{:S(2)}, u32[]{:S(2)}) collective-permute-start(f32[4,64,128]{2,1,0:T(8,128)S(1)} %mul.94), channel_id=1, source_target_pairs={{0,4},{1,5},{2,6},{3,7},{4,0},{5,1},{6,2},{7,3},{8,12},{9,13},{10,... | collective-permute-start | bytes 393224 | tf_op jit(solution)/shard_map/ppermute | solution.py:419
  69.1 9.4 %copy-start.1 = (f32[4,64,128]{2,1,0:T(8,128)S(1)}, f32[4,64,128]{2,1,0:T(8,128)}, u32[]{:S(2)}) copy-start(f32[4,64,128]{2,1,0:T(8,128)} %get-tuple-element.35) | copy-start | bytes 393220
  76.8 1.6 %collective-permute-start.10 = (f32[4,64,128]{2,1,0:T(8,128)}, f32[4,64,128]{2,1,0:T(8,128)S(1)}, u32[]{:S(2)}, u32[]{:S(2)}) collective-permute-start(f32[4,64,128]{2,1,0:T(8,128)} %get-tuple-element.39), channel_id=1, source_target_pairs={{0,1},{1,0},{2,3},{3,2},{4,5},{5,4},{6,7},{7,6},{8,9},{9,8},{10,11... | collective-permute-start | bytes 393224 | tf_op jit(solution)/shard_map/ppermute | solution.py:419
  79.4 5.6 %collective-permute-start.11 = (f32[4,64,128]{2,1,0:T(8,128)S(1)}, f32[4,64,128]{2,1,0:T(8,128)S(1)}, u32[]{:S(2)}, u32[]{:S(2)}) collective-permute-start(f32[4,64,128]{2,1,0:T(8,128)S(1)} %multiply_add_fusion.5), channel_id=1, source_target_pairs={{0,2},{1,3},{2,0},{3,1},{4,6},{5,7},{6,4},{7,5},{8,10},{9,11},{10,... | collective-permute-start | bytes 393224 | tf_op jit(solution)/shard_map/ppermute | solution.py:419
  85.0 5.0 %collective-permute-start.12 = (f32[4,64,128]{2,1,0:T(8,128)S(1)}, f32[4,64,128]{2,1,0:T(8,128)S(1)}, u32[]{:S(2)}, u32[]{:S(2)}) collective-permute-start(f32[4,64,128]{2,1,0:T(8,128)S(1)} %multiply_add_fusion.4), channel_id=1, source_target_pairs={{0,4},{1,5},{2,6},{3,7},{4,0},{5,1},{6,2},{7,3},{8,12},{9,13},{10,... | collective-permute-start | bytes 393224 | tf_op jit(solution)/shard_map/ppermute | solution.py:419
  96.5 5.2 %collective-permute-start.13 = (f32[4,64,128]{2,1,0:T(8,128)}, f32[4,64,128]{2,1,0:T(8,128)S(1)}, u32[]{:S(2)}, u32[]{:S(2)}) collective-permute-start(f32[4,64,128]{2,1,0:T(8,128)} %get-tuple-element.42), channel_id=1, source_target_pairs={{0,8},{8,0},{16,24},{24,16},{1,9},{9,1},{17,25},{25,17},{2,10},{10... | collective-permute-start | bytes 393224 | tf_op jit(solution)/shard_map/ppermute | solution.py:419
  102.6 7.3 %collective-permute-start.14 = (f32[4,64,128]{2,1,0:T(8,128)S(1)}, f32[4,64,128]{2,1,0:T(8,128)S(1)}, u32[]{:S(2)}, u32[]{:S(2)}) collective-permute-start(f32[4,64,128]{2,1,0:T(8,128)S(1)} %add.91), channel_id=1, source_target_pairs={{0,16},{8,24},{16,0},{24,8},{1,17},{9,25},{17,1},{25,9},{2,18},{10... | collective-permute-start | bytes 393224 | tf_op jit(solution)/shard_map/ppermute | solution.py:419
  110.7 14.1 %copy-start = (f32[256,128]{1,0:T(8,128)S(1)}, f32[256,128]{1,0:T(8,128)}, u32[]{:S(2)}) copy-start(f32[256,128]{1,0:T(8,128)} %param.13) | copy-start | bytes 393220
  110.7 14.4 %copy-start.2 = (f32[4,64,128]{2,1,0:T(8,128)S(1)}, f32[4,64,128]{2,1,0:T(8,128)}, u32[]{:S(2)}) copy-start(f32[4,64,128]{2,1,0:T(8,128)} %get-tuple-element.36) | copy-start | bytes 393220
  120.1 1.6 %collective-permute-start.15 = (f32[4,64,128]{2,1,0:T(8,128)}, f32[4,64,128]{2,1,0:T(8,128)S(1)}, u32[]{:S(2)}, u32[]{:S(2)}) collective-permute-start(f32[4,64,128]{2,1,0:T(8,128)} %get-tuple-element.48), channel_id=1, source_target_pairs={{0,1},{1,0},{2,3},{3,2},{4,5},{5,4},{6,7},{7,6},{8,9},{9,8},{10,11... | collective-permute-start | bytes 393224 | tf_op jit(solution)/shard_map/ppermute | solution.py:419
  122.8 5.8 %collective-permute-start.16 = (f32[4,64,128]{2,1,0:T(8,128)S(1)}, f32[4,64,128]{2,1,0:T(8,128)S(1)}, u32[]{:S(2)}, u32[]{:S(2)}) collective-permute-start(f32[4,64,128]{2,1,0:T(8,128)S(1)} %multiply_add_fusion.2), channel_id=1, source_target_pairs={{0,2},{1,3},{2,0},{3,1},{4,6},{5,7},{6,4},{7,5},{8,10},{9,11},{10,... | collective-permute-start | bytes 393224 | tf_op jit(solution)/shard_map/ppermute | solution.py:419
  125.0 6.0 %collective-permute-start.8 = (f32[4,64,128]{2,1,0:T(8,128)S(1)}, f32[4,64,128]{2,1,0:T(8,128)S(1)}, u32[]{:S(2)}, u32[]{:S(2)}) collective-permute-start(f32[4,64,128]{2,1,0:T(8,128)S(1)} %copy-done.2), channel_id=1, source_target_pairs={{0,8},{8,0},{16,24},{24,16},{1,9},{9,1},{17,25},{25,17},{2,10},{10... | collective-permute-start | bytes 393224 | tf_op jit(solution)/shard_map/ppermute | solution.py:419
  128.7 5.2 %collective-permute-start.17 = (f32[4,64,128]{2,1,0:T(8,128)S(1)}, f32[4,64,128]{2,1,0:T(8,128)S(1)}, u32[]{:S(2)}, u32[]{:S(2)}) collective-permute-start(f32[4,64,128]{2,1,0:T(8,128)S(1)} %multiply_add_fusion.1), channel_id=1, source_target_pairs={{0,4},{1,5},{2,6},{3,7},{4,0},{5,1},{6,2},{7,3},{8,12},{9,13},{10,... | collective-permute-start | bytes 393224 | tf_op jit(solution)/shard_map/ppermute | solution.py:419
  131.1 11.1 %collective-permute-start.9 = (f32[4,64,128]{2,1,0:T(8,128)S(1)}, f32[4,64,128]{2,1,0:T(8,128)S(1)}, u32[]{:S(2)}, u32[]{:S(2)}) collective-permute-start(f32[4,64,128]{2,1,0:T(8,128)S(1)} %add.83), channel_id=1, source_target_pairs={{0,16},{8,24},{16,0},{24,8},{1,17},{9,25},{17,1},{25,9},{2,18},{10... | collective-permute-start | bytes 393224 | tf_op jit(solution)/shard_map/ppermute | solution.py:419
  140.8 5.5 %collective-permute-start.18 = (f32[2,128]{1,0:T(2,128)S(1)}, f32[2,128]{1,0:T(2,128)S(1)}, u32[]{:S(2)}, u32[]{:S(2)}) collective-permute-start(f32[2,128]{1,0:T(2,128)S(1)} %reshape.64), channel_id=1, source_target_pairs={{0,8},{8,0},{16,24},{24,16},{1,9},{9,1},{17,25},{25,17},{2,10},{10... | collective-permute-start | bytes 3080 | tf_op jit(solution)/shard_map/ppermute | solution.py:419
  146.3 4.5 %collective-permute-start.19 = (f32[2,128]{1,0:T(2,128)S(1)}, f32[2,128]{1,0:T(2,128)S(1)}, u32[]{:S(2)}, u32[]{:S(2)}) collective-permute-start(f32[2,128]{1,0:T(2,128)S(1)} %add.99), channel_id=1, source_target_pairs={{0,16},{8,24},{16,0},{24,8},{1,17},{9,25},{17,1},{25,9},{2,18},{10... | collective-permute-start | bytes 3080 | tf_op jit(solution)/shard_map/ppermute | solution.py:419

commit v14 on v13

--- a/solution.py
+++ b/solution.py
@@ -76,14 +76,22 @@
     return pos_ref[2 * slots + k], 3 * slots + k * n_c
 
 
-def _loop(count, body, init):
+def _loop(count, body, init, start=0):
     def group(j, carry):
         for t in range(UNROLL):
-            carry = body(UNROLL * j + t, carry)
+            carry = body(start + UNROLL * j + t, carry)
         return carry
 
     carry = lax.fori_loop(0, count // UNROLL, group, init)
-    return lax.fori_loop(UNROLL * (count // UNROLL), count, body, carry)
+    return lax.fori_loop(start + UNROLL * (count // UNROLL), start + count, body, carry)
+
+
+def _half_range(pos_ref, k, h, slots, n_c):
+    count, base = _columns(pos_ref, k, slots, n_c)
+    low = pos_ref[3 * slots + slots * n_c + k]
+    start = jnp.where(h == 0, 0, low)
+    stop = jnp.where(h == 0, low, count)
+    return start, stop - start, base
 
 
 def _fwd_products_kernel(has_u, slots, blocks, pos_ref, *refs):
@@ -136,10 +144,12 @@
 
 def _fwd_messages_kernel(slots, pos_ref, ba_ref, sign_ref, here_ref, others_ref, ew_ref, u_ref, col_ref):
     k = pl.program_id(0)
-    n_c = ba_ref.shape[1]
-    count, base = _columns(pos_ref, k, slots, n_c)
-
-    @pl.when(k == 0)
+    h = pl.program_id(1)
+    width = ba_ref.shape[1]
+    n_c = width * 2
+    start, count, base = _half_range(pos_ref, k, h, slots, n_c)
+
+    @pl.when((k == 0) & (h == 0))
     def _():
         col_ref[...] = jnp.zeros(col_ref.shape, F32)
 
@@ -148,13 +158,14 @@
 
     def body(i, carry):
         c = pos_ref[base + i]
-        x = ba_ref[0, c] * f
-        u = ew_ref[0, c] * jnp.log((1.0 + DAMP * x) / (1.0 - DAMP * x))
-        u_ref[0, c] = u
+        local = c - h * width
+        x = ba_ref[0, local] * f
+        u = ew_ref[0, local] * jnp.log((1.0 + DAMP * x) / (1.0 - DAMP * x))
+        u_ref[0, local] = u
         col_ref[q, pl.ds(c, 1), :] = col_ref[q, pl.ds(c, 1), :] + jnp.sum(u, axis=0, keepdims=True)
         return carry
 
-    _loop(count, body, 0)
+    _loop(count, body, 0, start)
 
 
 def _bwd_messages_kernel(has_next, has_acc, emit_column, slots, pos_ref, *refs):
@@ -166,12 +177,15 @@
     acc_ref = refs.pop(0) if has_acc else None
     gw_ref, gba_ref, ghere_ref, gothers_ref = refs[:4]
     col_ref = refs[4] if emit_column else None
+    d1_scr = refs[-1]
     k = pl.program_id(0)
-    n_c = ba_ref.shape[1]
+    h = pl.program_id(1)
+    width = ba_ref.shape[1]
+    n_c = width * 2
     shape = ba_ref.shape[2:]
     q = _col_block(pos_ref, k)
 
-    @pl.when(k == 0)
+    @pl.when((k == 0) & (h == 0))
     def _():
         gothers_ref[...] = jnp.zeros(gothers_ref.shape, F32)
         if emit_column:
@@ -182,32 +196,38 @@
     here = here_ref[k]
     others = others_ref[p]
     f = sign * here * others
-    count, base = _columns(pos_ref, k, slots, n_c)
+    start, count, base = _half_range(pos_ref, k, h, slots, n_c)
 
     def body(i, total):
         c = pos_ref[base + i]
+        local = c - h * width
         gu = _spread_row(gsp_ref, c, shape)
         if has_next:
-            gu = gu - gm_ref[0, c]
-        ba = ba_ref[0, c]
+            gu = gu - gm_ref[0, local]
+        ba = ba_ref[0, local]
         x = ba * f
         low = 1.0 - DAMP * x
         high = 1.0 + DAMP * x
         ratio = jnp.log(high / low)
         if emit_column:
-            u = ew_ref[0, c] * ratio
+            u = ew_ref[0, local] * ratio
             col_ref[q, pl.ds(c, 1), :] = col_ref[q, pl.ds(c, 1), :] + jnp.sum(u, axis=0, keepdims=True)
         gw = gu * ratio
         if has_acc:
-            gw = gw + acc_ref[0, c]
-        gw_ref[0, c] = gw
-        gx = gu * ew_ref[0, c] * ((2.0 * DAMP) / (low * high))
-        gba_ref[0, c] = gx * f
+            gw = gw + acc_ref[0, local]
+        gw_ref[0, local] = gw
+        gx = gu * ew_ref[0, local] * ((2.0 * DAMP) / (low * high))
+        gba_ref[0, local] = gx * f
         return total + gx * ba
 
-    grad_factor = _loop(count, body, jnp.zeros(shape, F32))
-    ghere_ref[k] = grad_factor * sign * others
-    gothers_ref[p] = gothers_ref[p] + grad_factor * sign * here
+    begin = jnp.where(h == 0, jnp.zeros(shape, F32), d1_scr[...])
+    grad_factor = _loop(count, body, begin, start)
+    d1_scr[...] = grad_factor
+
+    @pl.when(h == 1)
+    def _():
+        ghere_ref[k] = grad_factor * sign * others
+        gothers_ref[p] = gothers_ref[p] + grad_factor * sign * here
 
 
 def _bwd_products_kernel(emit_gm, slots, pos_ref, *refs):
@@ -266,7 +286,14 @@
     _loop(count, backward, (ones, zeros))
 
 
-def _spec(kind, shape):
+def _spec(kind, shape, halves):
+    if halves > 1:
+        if kind == "dense":
+            block = (1, shape[1] // halves) + tuple(shape[2:])
+            return pl.BlockSpec(block, lambda k, h, pos: (k, h, 0, 0))
+        if kind == "column":
+            return pl.BlockSpec((1,) + tuple(shape[1:]), lambda k, h, pos: (pos[2 * k + 1], 0, 0))
+        return pl.BlockSpec(tuple(shape), lambda k, h, pos: (0,) * len(shape))
     if kind == "dense":
         return pl.BlockSpec((1,) + tuple(shape[1:]), lambda k, pos: (k, 0, 0, 0))
     if kind == "column":
@@ -274,15 +301,16 @@
     return pl.BlockSpec(tuple(shape), lambda k, pos: (0,) * len(shape))
 
 
-def _call(kernel, pos, inputs, outputs, scratch=()):
+def _call(kernel, pos, inputs, outputs, scratch=(), halves=1):
     from jax.experimental.pallas import tpu as pltpu
 
     dense = [a for kind, a in inputs if kind == "dense"][0]
+    grid = (dense.shape[0],) if halves == 1 else (dense.shape[0], halves)
     grid_spec = pltpu.PrefetchScalarGridSpec(
         num_scalar_prefetch=1,
-        grid=(dense.shape[0],),
-        in_specs=[_spec(kind, a.shape) for kind, a in inputs],
-        out_specs=[_spec(kind, o.shape) for kind, o in outputs],
+        grid=grid,
+        in_specs=[_spec(kind, a.shape, halves) for kind, a in inputs],
+        out_specs=[_spec(kind, o.shape, halves) for kind, o in outputs],
         scratch_shapes=list(scratch),
     )
     return pl.pallas_call(
@@ -319,7 +347,7 @@
         ("dense", jax.ShapeDtypeStruct(ba.shape, F32)),
         ("full", jax.ShapeDtypeStruct((col_blocks, c, s), F32)),
     ]
-    return _call(functools.partial(_fwd_messages_kernel, k), pos, inputs, outs)
+    return _call(functools.partial(_fwd_messages_kernel, k), pos, inputs, outs, halves=2)
 
 
 def bwd_messages(pos, gsp, gm, ba, sign, here, others, ew, acc, col_blocks=0):
@@ -341,7 +369,12 @@
     if col_blocks:
         outs.append(("full", jax.ShapeDtypeStruct((col_blocks, c, s), F32)))
     return _call(
-        functools.partial(_bwd_messages_kernel, has_next, has_acc, col_blocks > 0, k), pos, inputs, outs
+        functools.partial(_bwd_messages_kernel, has_next, has_acc, col_blocks > 0, k),
+        pos,
+        inputs,
+        outs,
+        [_vmem((r, s))],
+        halves=2,
     )
 
 
@@ -508,6 +541,7 @@
             tile_pos[0, 0].reshape(slot_total * 2),
             jnp.sum(filled.astype(jnp.int32), axis=1),
             order.astype(jnp.int32).reshape(slot_total * TILE),
+            jnp.sum(filled[:, : TILE // 2].astype(jnp.int32), axis=1),
         ]
     )
     dense = (slot_total, TILE, TILE, shots)

time: 152 us -> 155 us (1.020)
  starting transfers between devices: 33.4 us -> 27.4 us
  waiting for transfers between devices: 42.5 us -> 46.9 us
  Pallas kernels: 46.2 us -> 50.5 us
    ppermute x20, starting transfers between devices: 33.4 us -> 27.4 us  [_swap(): return lax.ppermute(value, axis, perm)]
    ppermute x20, waiting for transfers between devices: 42.5 us -> 46.9 us  [_swap(): return lax.ppermute(value, axis, perm)]
    pallas_call x7, Pallas kernels: 46.2 us -> 50.5 us  [_call(): pl.pallas_call(kernel, grid_spec=grid_spec, out_shape=[o for kind, o in o...]
  transfers between devices with their start and end apart: 20 -> 20, of which waited for: 17 -> 17; matrix products, arithmetic and copies ran while one was open for 6% -> 6% of each run, Pallas kernels for 3% -> 4%
where the time goes in v14:
time: 155 us; the launch traced here: 154 us
  Pallas kernels  50.5 us (33%)
  waiting for transfers between devices  46.9 us (30%)
  starting transfers between devices  27.4 us (18%)
  other arithmetic  16.6 us (11%)
  local copies, waits for them, and re-layouts  11 us (7%)
    pallas_call x7, Pallas kernels, _call(): pl.pallas_call(kernel, grid_spec=grid_spec, out_shape=[o for kind, o in o...  50.5 us
    ppermute x20, waiting for transfers between devices, _swap(): return lax.ppermute(value, axis, perm)  46.9 us
    ppermute x20, starting transfers between devices, _swap(): return lax.ppermute(value, axis, perm)  27.4 us
    reduce_sum x1, other arithmetic, body(): jnp.sum(acc, axis=3)  3.34 us
  transfers between devices with their start and end apart: 20, of which 17 were waited for; matrix products, arithmetic and copies ran while one was open for 6% of the time, Pallas kernels for 4%

profile of v14, /device:TPU:0, one launch (start us, length us, event | category | flops | bytes accessed | tf_op | source)
XLA Modules:
  0.0 154.4 jit_solution(13093022843380837320)
XLA Ops:
  0.6 0.9 squeeze.10
  2.8 1.0 sort.17
  4.7 0.9 reshape_squeeze.10
  7.2 2.6 %broadcast_in_dim.91.refs_1_.ew_ref.refs_2_.refs_5_.refs_6_ = f32[2,64,64,128]{3,2,1,0:T(8,128)} broadcast(f32[2,64,64]{2,1,0:T(8,128)S(1)} %multiply_bitcast_fusion), dimensions={0,1,2} | broadcast | bytes 4227072 | tf_op jit(solution)/shard_map/broadcast_in_dim | solution.py:548
  10.5 6.0 %shard_map.94 = (f32[2,64,64,128]{3,2,1,0:T(8,128)}, f32[2,64,64,128]{3,2,1,0:T(8,128)}, f32[2,64,128]{2,1,0:T(8,128)}, f32[4,64,128]{2,1,0:T(8,128)}, f32[2,64,128]{2,1,0:T(8,128)}) custom-call(s32[136]{0:T(256)} %pad_add_fusion.pos_ref, f32[4,64,128]{2,1,0:T(8,128)} %add.79.refs_0_, f32[2,64,64,128]{3,2,1,0:T(8,128)} %broadcast_in_dim.91.refs_1_.ew_ref.refs_2_.refs_5_.refs_6_), custom_call_target="tpu_custom_call" | custom-call | tf_op jit(solution)/shard_map/pallas_call | solution.py:316
  16.5 1.0 slice_reduce_fusion
  18.1 0.8 collective-permute-done
  18.9 2.8 %collective-permute-start.1 = (f32[2,128]{1,0:T(2,128)S(1)}, f32[2,128]{1,0:T(2,128)S(1)}, u32[]{:S(2)}, u32[]{:S(2)}) collective-permute-start(f32[2,128]{1,0:T(2,128)S(1)} %mul.88), channel_id=1, source_target_pairs={{0,2},{1,3},{2,0},{3,1},{4,6},{5,7},{6,4},{7,5},{8,10},{9,11},{10,... | collective-permute-start | bytes 3080 | tf_op jit(solution)/shard_map/ppermute | solution.py:452
  21.8 1.4 collective-permute-done.1
  23.3 2.1 %collective-permute-start.2 = (f32[2,128]{1,0:T(2,128)S(1)}, f32[2,128]{1,0:T(2,128)S(1)}, u32[]{:S(2)}, u32[]{:S(2)}) collective-permute-start(f32[2,128]{1,0:T(2,128)S(1)} %mul.90), channel_id=1, source_target_pairs={{0,4},{1,5},{2,6},{3,7},{4,0},{5,1},{6,2},{7,3},{8,12},{9,13},{10,... | collective-permute-start | bytes 3080 | tf_op jit(solution)/shard_map/ppermute | solution.py:452
  27.8 6.7 %shard_map.95 = (f32[2,64,64,128]{3,2,1,0:T(8,128)}, f32[4,64,128]{2,1,0:T(8,128)}) custom-call(s32[136]{0:T(256)} %pad_add_fusion.pos_ref, f32[2,64,64,128]{3,2,1,0:T(8,128)} %get-tuple-element.28.ba_ref.refs_2_, f32[2,64,128]{2,1,0:T(8,128)} %copy.30.sign_ref.refs_2_.refs_3_, f32[2,64,128]{2,1,0:T(8,128)} %get-tuple-element.29.here_ref.refs_4_.refs_5_, ...), custom_call_target="tpu_custom_call" | custom-call | tf_op jit(solution)/shard_map/pallas_call | solution.py:316
  34.5 2.3 %collective-permute-start.3 = (f32[4,64,128]{2,1,0:T(8,128)}, f32[4,64,128]{2,1,0:T(8,128)S(1)}, u32[]{:S(2)}, u32[]{:S(2)}) collective-permute-start(f32[4,64,128]{2,1,0:T(8,128)} %get-tuple-element.31), channel_id=1, source_target_pairs={{0,8},{8,0},{16,24},{24,16},{1,9},{9,1},{17,25},{25,17},{2,10},{10... | collective-permute-start | bytes 393224 | tf_op jit(solution)/shard_map/ppermute | solution.py:452
  36.8 3.2 %collective-permute-done.3 = f32[4,64,128]{2,1,0:T(8,128)S(1)} collective-permute-done((f32[4,64,128]{2,1,0:T(8,128)}, f32[4,64,128]{2,1,0:T(8,128)S(1)}, u32[]{:S(2)}, u32[]{:S(2)}) %collective-permute-start.3) | collective-permute-done | bytes 131104 | tf_op jit(solution)/shard_map/ppermute | solution.py:452
  39.9 0.9 add.80
  40.8 3.3 %collective-permute-start.4 = (f32[4,64,128]{2,1,0:T(8,128)S(1)}, f32[4,64,128]{2,1,0:T(8,128)S(1)}, u32[]{:S(2)}, u32[]{:S(2)}) collective-permute-start(f32[4,64,128]{2,1,0:T(8,128)S(1)} %add.80), channel_id=1, source_target_pairs={{0,16},{8,24},{16,0},{24,8},{1,17},{9,25},{17,1},{25,9},{2,18},{10... | collective-permute-start | bytes 393224 | tf_op jit(solution)/shard_map/ppermute | solution.py:452
  44.1 4.4 %collective-permute-done.4 = f32[4,64,128]{2,1,0:T(8,128)S(1)} collective-permute-done((f32[4,64,128]{2,1,0:T(8,128)S(1)}, f32[4,64,128]{2,1,0:T(8,128)S(1)}, u32[]{:S(2)}, u32[]{:S(2)}) %collective-permute-start.4) | collective-permute-done | bytes 131104 | tf_op jit(solution)/shard_map/ppermute | solution.py:452
  49.2 6.6 %shard_map.96 = (f32[2,64,64,128]{3,2,1,0:T(8,128)}, f32[2,64,64,128]{3,2,1,0:T(8,128)}, f32[2,64,128]{2,1,0:T(8,128)}, f32[4,64,128]{2,1,0:T(8,128)}, f32[2,64,128]{2,1,0:T(8,128)}) custom-call(s32[136]{0:T(256)} %pad_add_fusion.pos_ref, f32[4,64,128]{2,1,0:T(8,128)} %add_add_fusion.1.refs_0_, f32[2,64,64,128]{3,2,1,0:T(8,128)} %get-tuple-element.32.refs_1_, ...), custom_call_target="tpu_custom_call" | custom-call | tf_op jit(solution)/shard_map/pallas_call | solution.py:316
  55.9 1.5 %collective-permute-done.5 = f32[4,64,128]{2,1,0:T(8,128)S(1)} collective-permute-done((f32[4,64,128]{2,1,0:T(8,128)}, f32[4,64,128]{2,1,0:T(8,128)S(1)}, u32[]{:S(2)}, u32[]{:S(2)}) %collective-permute-start.5) | collective-permute-done | bytes 131104 | tf_op jit(solution)/shard_map/ppermute | solution.py:452
  57.5 0.9 mul.92
  58.5 5.5 %collective-permute-done.6 = f32[4,64,128]{2,1,0:T(8,128)S(1)} collective-permute-done((f32[4,64,128]{2,1,0:T(8,128)S(1)}, f32[4,64,128]{2,1,0:T(8,128)S(1)}, u32[]{:S(2)}, u32[]{:S(2)}) %collective-permute-start.6) | collective-permute-done | bytes 131104 | tf_op jit(solution)/shard_map/ppermute | solution.py:452
  64.0 1.9 %collective-permute-start.7 = (f32[4,64,128]{2,1,0:T(8,128)S(1)}, f32[4,64,128]{2,1,0:T(8,128)S(1)}, u32[]{:S(2)}, u32[]{:S(2)}) collective-permute-start(f32[4,64,128]{2,1,0:T(8,128)S(1)} %mul.94), channel_id=1, source_target_pairs={{0,4},{1,5},{2,6},{3,7},{4,0},{5,1},{6,2},{7,3},{8,12},{9,13},{10,... | collective-permute-start | bytes 393224 | tf_op jit(solution)/shard_map/ppermute | solution.py:452
  65.9 3.1 %collective-permute-done.7 = f32[4,64,128]{2,1,0:T(8,128)S(1)} collective-permute-done((f32[4,64,128]{2,1,0:T(8,128)S(1)}, f32[4,64,128]{2,1,0:T(8,128)S(1)}, u32[]{:S(2)}, u32[]{:S(2)}) %collective-permute-start.7) | collective-permute-done | bytes 131104 | tf_op jit(solution)/shard_map/ppermute | solution.py:452
  69.8 8.7 %shard_map.97 = (f32[2,64,64,128]{3,2,1,0:T(8,128)}, f32[2,64,64,128]{3,2,1,0:T(8,128)}, f32[2,64,128]{2,1,0:T(8,128)}, f32[4,64,128]{2,1,0:T(8,128)}, f32[4,64,128]{2,1,0:T(8,128)}) custom-call(s32[136]{0:T(256)} %pad_add_fusion.pos_ref, f32[4,64,128]{2,1,0:T(8,128)} %bitcast.15, f32[2,64,64,128]{3,2,1,0:T(8,128)} %get-tuple-element.33.refs_1_, ...), custom_call_target="tpu_custom_call" | custom-call | tf_op jit(solution)/shard_map/pallas_call | solution.py:316
  78.5 1.5 %collective-permute-done.10 = f32[4,64,128]{2,1,0:T(8,128)S(1)} collective-permute-done((f32[4,64,128]{2,1,0:T(8,128)}, f32[4,64,128]{2,1,0:T(8,128)S(1)}, u32[]{:S(2)}, u32[]{:S(2)}) %collective-permute-start.10) | collective-permute-done | bytes 131104 | tf_op jit(solution)/shard_map/ppermute | solution.py:452
  80.1 0.9 multiply_add_fusion.5
  81.0 1.1 collective-permute-start.11
  82.1 4.6 %collective-permute-done.11 = f32[4,64,128]{2,1,0:T(8,128)S(1)} collective-permute-done((f32[4,64,128]{2,1,0:T(8,128)S(1)}, f32[4,64,128]{2,1,0:T(8,128)S(1)}, u32[]{:S(2)}, u32[]{:S(2)}) %collective-permute-start.11) | collective-permute-done | bytes 131104 | tf_op jit(solution)/shard_map/ppermute | solution.py:452
  86.7 2.1 %collective-permute-start.12 = (f32[4,64,128]{2,1,0:T(8,128)S(1)}, f32[4,64,128]{2,1,0:T(8,128)S(1)}, u32[]{:S(2)}, u32[]{:S(2)}) collective-permute-start(f32[4,64,128]{2,1,0:T(8,128)S(1)} %multiply_add_fusion.4), channel_id=1, source_target_pairs={{0,4},{1,5},{2,6},{3,7},{4,0},{5,1},{6,2},{7,3},{8,12},{9,13},{10,... | collective-permute-start | bytes 393224 | tf_op jit(solution)/shard_map/ppermute | solution.py:452
  88.8 3.0 %collective-permute-done.12 = f32[4,64,128]{2,1,0:T(8,128)S(1)} collective-permute-done((f32[4,64,128]{2,1,0:T(8,128)S(1)}, f32[4,64,128]{2,1,0:T(8,128)S(1)}, u32[]{:S(2)}, u32[]{:S(2)}) %collective-permute-start.12) | collective-permute-done | bytes 131104 | tf_op jit(solution)/shard_map/ppermute | solution.py:452
  92.5 6.3 %shard_map.98 = (f32[2,64,64,128]{3,2,1,0:T(8,128)}, f32[4,64,128]{2,1,0:T(8,128)}) custom-call(s32[136]{0:T(256)} %pad_add_fusion.pos_ref, f32[2,64,64,128]{3,2,1,0:T(8,128)} %get-tuple-element.37.refs_0_, f32[2,64,64,128]{3,2,1,0:T(8,128)} %get-tuple-element.38.refs_1_, f32[4,64,128]{2,1,0:T(8,128)} %multiply_add_fusion.3.refs_2_, ...), custom_call_target="tpu_custom_call" | custom-call | tf_op jit(solution)/shard_map/pallas_call | solution.py:316
  98.8 1.1 collective-permute-start.13
  99.9 4.0 %collective-permute-done.13 = f32[4,64,128]{2,1,0:T(8,128)S(1)} collective-permute-done((f32[4,64,128]{2,1,0:T(8,128)}, f32[4,64,128]{2,1,0:T(8,128)S(1)}, u32[]{:S(2)}, u32[]{:S(2)}) %collective-permute-start.13) | collective-permute-done | bytes 131104 | tf_op jit(solution)/shard_map/ppermute | solution.py:452
  104.0 0.9 add.91
  104.9 2.4 %collective-permute-start.14 = (f32[4,64,128]{2,1,0:T(8,128)S(1)}, f32[4,64,128]{2,1,0:T(8,128)S(1)}, u32[]{:S(2)}, u32[]{:S(2)}) collective-permute-start(f32[4,64,128]{2,1,0:T(8,128)S(1)} %add.91), channel_id=1, source_target_pairs={{0,16},{8,24},{16,0},{24,8},{1,17},{9,25},{17,1},{25,9},{2,18},{10... | collective-permute-start | bytes 393224 | tf_op jit(solution)/shard_map/ppermute | solution.py:452
  107.3 5.0 %collective-permute-done.14 = f32[4,64,128]{2,1,0:T(8,128)S(1)} collective-permute-done((f32[4,64,128]{2,1,0:T(8,128)S(1)}, f32[4,64,128]{2,1,0:T(8,128)S(1)}, u32[]{:S(2)}, u32[]{:S(2)}) %collective-permute-start.14) | collective-permute-done | bytes 131104 | tf_op jit(solution)/shard_map/ppermute | solution.py:452
  112.9 10.6 %shard_map.99 = (f32[2,64,64,128]{3,2,1,0:T(8,128)}, f32[2,64,64,128]{3,2,1,0:T(8,128)}, f32[2,64,128]{2,1,0:T(8,128)}, f32[4,64,128]{2,1,0:T(8,128)}) custom-call(s32[136]{0:T(256)} %pad_add_fusion.pos_ref, f32[4,64,128]{2,1,0:T(8,128)} %get-tuple-element.52.refs_0_, f32[2,64,64,128]{3,2,1,0:T(8,128)} %get-tuple-element.43.refs_1_, ...), custom_call_target="tpu_custom_call" | custom-call | tf_op jit(solution)/shard_map/pallas_call | solution.py:316
  123.7 1.5 collective-permute-done.15
  125.2 1.0 multiply_add_fusion.2
  126.6 1.9 %collective-permute-start.8 = (f32[4,64,128]{2,1,0:T(8,128)S(1)}, f32[4,64,128]{2,1,0:T(8,128)S(1)}, u32[]{:S(2)}, u32[]{:S(2)}) collective-permute-start(f32[4,64,128]{2,1,0:T(8,128)S(1)} %copy-done.2), channel_id=1, source_target_pairs={{0,8},{8,0},{16,24},{24,16},{1,9},{9,1},{17,25},{25,17},{2,10},{10... | collective-permute-start | bytes 393224 | tf_op jit(solution)/shard_map/ppermute | solution.py:452
  128.4 3.4 %collective-permute-done.16 = f32[4,64,128]{2,1,0:T(8,128)S(1)} collective-permute-done((f32[4,64,128]{2,1,0:T(8,128)S(1)}, f32[4,64,128]{2,1,0:T(8,128)S(1)}, u32[]{:S(2)}, u32[]{:S(2)}) %collective-permute-start.16) | collective-permute-done | bytes 131104 | tf_op jit(solution)/shard_map/ppermute | solution.py:452
  131.9 2.0 %collective-permute-start.17 = (f32[4,64,128]{2,1,0:T(8,128)S(1)}, f32[4,64,128]{2,1,0:T(8,128)S(1)}, u32[]{:S(2)}, u32[]{:S(2)}) collective-permute-start(f32[4,64,128]{2,1,0:T(8,128)S(1)} %multiply_add_fusion.1), channel_id=1, source_target_pairs={{0,4},{1,5},{2,6},{3,7},{4,0},{5,1},{6,2},{7,3},{8,12},{9,13},{10,... | collective-permute-start | bytes 393224 | tf_op jit(solution)/shard_map/ppermute | solution.py:452
  134.5 2.5 %collective-permute-done.17 = f32[4,64,128]{2,1,0:T(8,128)S(1)} collective-permute-done((f32[4,64,128]{2,1,0:T(8,128)S(1)}, f32[4,64,128]{2,1,0:T(8,128)S(1)}, u32[]{:S(2)}, u32[]{:S(2)}) %collective-permute-start.17) | collective-permute-done | bytes 131104 | tf_op jit(solution)/shard_map/ppermute | solution.py:452
  137.0 0.9 multiply_add_fusion.refs_2_
  137.9 5.6 %shard_map.100 = f32[4,64,128]{2,1,0:T(8,128)} custom-call(s32[136]{0:T(256)} %pad_add_fusion.pos_ref, f32[2,64,64,128]{3,2,1,0:T(8,128)} %get-tuple-element.46.refs_0_, f32[2,64,64,128]{3,2,1,0:T(8,128)} %get-tuple-element.47.refs_1_, f32[4,64,128]{2,1,0:T(8,128)} %multiply_add_fusion.refs_2_, f32[2,64,128]{2,1,0:T(8,128)} %get-tuple-element.49.refs_3_, ...), custom_call_target="tpu_custom_call" | custom-call | tf_op jit(solution)/shard_map/pallas_call | solution.py:316
  143.4 1.0 reduce_sum.62
  145.9 3.3 %reduce_sum.58 = f32[2,64,64]{2,1,0:T(8,128)S(1)} reduce(f32[2,64,64,128]{3,2,1,0:T(8,128)} %get-tuple-element.45, f32[]{:T(128)} %constant.7.clone.1), dimensions={3}, to_apply=%region_4.5 | reduce | flops 1040384 | bytes 4227076 | tf_op jit(solution)/shard_map/reduce_sum | solution.py:595
  149.3 2.7 %collective-permute-start.19 = (f32[2,128]{1,0:T(2,128)S(1)}, f32[2,128]{1,0:T(2,128)S(1)}, u32[]{:S(2)}, u32[]{:S(2)}) collective-permute-start(f32[2,128]{1,0:T(2,128)S(1)} %add.99), channel_id=1, source_target_pairs={{0,16},{8,24},{16,0},{24,8},{1,17},{9,25},{17,1},{25,9},{2,18},{10... | collective-permute-start | bytes 3080 | tf_op jit(solution)/shard_map/ppermute | solution.py:452
  152.9 0.9 collective-permute-done.19
  (70 shorter events, 14.0 us)
Async XLA Ops:
  7.1 10.9 %copy-start.3 = (s32[256,128]{1,0:T(8,128)S(1)}, s32[256,128]{1,0:T(8,128)}, u32[]{:S(2)}) copy-start(s32[256,128]{1,0:T(8,128)} %param.11) | copy-start | bytes 393220
  7.2 14.6 %copy-start.4 = (s32[1,1,2,2]{3,2,1,0:T(2,128)S(1)}, s32[1,1,2,2]{3,2,1,0:T(2,128)}, u32[]{:S(2)}) copy-start(s32[1,1,2,2]{3,2,1,0:T(2,128)} %param.8) | copy-start | bytes 52
  17.6 1.3 collective-permute-start
  18.9 4.4 %collective-permute-start.1 = (f32[2,128]{1,0:T(2,128)S(1)}, f32[2,128]{1,0:T(2,128)S(1)}, u32[]{:S(2)}, u32[]{:S(2)}) collective-permute-start(f32[2,128]{1,0:T(2,128)S(1)} %mul.88), channel_id=1, source_target_pairs={{0,2},{1,3},{2,0},{3,1},{4,6},{5,7},{6,4},{7,5},{8,10},{9,11},{10,... | collective-permute-start | bytes 3080 | tf_op jit(solution)/shard_map/ppermute | solution.py:452
  23.3 3.7 %collective-permute-start.2 = (f32[2,128]{1,0:T(2,128)S(1)}, f32[2,128]{1,0:T(2,128)S(1)}, u32[]{:S(2)}, u32[]{:S(2)}) collective-permute-start(f32[2,128]{1,0:T(2,128)S(1)} %mul.90), channel_id=1, source_target_pairs={{0,4},{1,5},{2,6},{3,7},{4,0},{5,1},{6,2},{7,3},{8,12},{9,13},{10,... | collective-permute-start | bytes 3080 | tf_op jit(solution)/shard_map/ppermute | solution.py:452
  34.5 5.4 %collective-permute-start.3 = (f32[4,64,128]{2,1,0:T(8,128)}, f32[4,64,128]{2,1,0:T(8,128)S(1)}, u32[]{:S(2)}, u32[]{:S(2)}) collective-permute-start(f32[4,64,128]{2,1,0:T(8,128)} %get-tuple-element.31), channel_id=1, source_target_pairs={{0,8},{8,0},{16,24},{24,16},{1,9},{9,1},{17,25},{25,17},{2,10},{10... | collective-permute-start | bytes 393224 | tf_op jit(solution)/shard_map/ppermute | solution.py:452
  40.8 7.6 %collective-permute-start.4 = (f32[4,64,128]{2,1,0:T(8,128)S(1)}, f32[4,64,128]{2,1,0:T(8,128)S(1)}, u32[]{:S(2)}, u32[]{:S(2)}) collective-permute-start(f32[4,64,128]{2,1,0:T(8,128)S(1)} %add.80), channel_id=1, source_target_pairs={{0,16},{8,24},{16,0},{24,8},{1,17},{9,25},{17,1},{25,9},{2,18},{10... | collective-permute-start | bytes 393224 | tf_op jit(solution)/shard_map/ppermute | solution.py:452
  55.9 1.6 %collective-permute-start.5 = (f32[4,64,128]{2,1,0:T(8,128)}, f32[4,64,128]{2,1,0:T(8,128)S(1)}, u32[]{:S(2)}, u32[]{:S(2)}) collective-permute-start(f32[4,64,128]{2,1,0:T(8,128)} %get-tuple-element.35), channel_id=1, source_target_pairs={{0,1},{1,0},{2,3},{3,2},{4,5},{5,4},{6,7},{7,6},{8,9},{9,8},{10,11... | collective-permute-start | bytes 393224 | tf_op jit(solution)/shard_map/ppermute | solution.py:452
  58.4 5.6 %collective-permute-start.6 = (f32[4,64,128]{2,1,0:T(8,128)S(1)}, f32[4,64,128]{2,1,0:T(8,128)S(1)}, u32[]{:S(2)}, u32[]{:S(2)}) collective-permute-start(f32[4,64,128]{2,1,0:T(8,128)S(1)} %mul.92), channel_id=1, source_target_pairs={{0,2},{1,3},{2,0},{3,1},{4,6},{5,7},{6,4},{7,5},{8,10},{9,11},{10,... | collective-permute-start | bytes 393224 | tf_op jit(solution)/shard_map/ppermute | solution.py:452
  64.0 5.0 %collective-permute-start.7 = (f32[4,64,128]{2,1,0:T(8,128)S(1)}, f32[4,64,128]{2,1,0:T(8,128)S(1)}, u32[]{:S(2)}, u32[]{:S(2)}) collective-permute-start(f32[4,64,128]{2,1,0:T(8,128)S(1)} %mul.94), channel_id=1, source_target_pairs={{0,4},{1,5},{2,6},{3,7},{4,0},{5,1},{6,2},{7,3},{8,12},{9,13},{10,... | collective-permute-start | bytes 393224 | tf_op jit(solution)/shard_map/ppermute | solution.py:452
  69.8 10.3 %copy-start.1 = (f32[4,64,128]{2,1,0:T(8,128)S(1)}, f32[4,64,128]{2,1,0:T(8,128)}, u32[]{:S(2)}) copy-start(f32[4,64,128]{2,1,0:T(8,128)} %get-tuple-element.35) | copy-start | bytes 393220
  78.4 1.6 %collective-permute-start.10 = (f32[4,64,128]{2,1,0:T(8,128)}, f32[4,64,128]{2,1,0:T(8,128)S(1)}, u32[]{:S(2)}, u32[]{:S(2)}) collective-permute-start(f32[4,64,128]{2,1,0:T(8,128)} %get-tuple-element.39), channel_id=1, source_target_pairs={{0,1},{1,0},{2,3},{3,2},{4,5},{5,4},{6,7},{7,6},{8,9},{9,8},{10,11... | collective-permute-start | bytes 393224 | tf_op jit(solution)/shard_map/ppermute | solution.py:452
  81.0 5.6 %collective-permute-start.11 = (f32[4,64,128]{2,1,0:T(8,128)S(1)}, f32[4,64,128]{2,1,0:T(8,128)S(1)}, u32[]{:S(2)}, u32[]{:S(2)}) collective-permute-start(f32[4,64,128]{2,1,0:T(8,128)S(1)} %multiply_add_fusion.5), channel_id=1, source_target_pairs={{0,2},{1,3},{2,0},{3,1},{4,6},{5,7},{6,4},{7,5},{8,10},{9,11},{10,... | collective-permute-start | bytes 393224 | tf_op jit(solution)/shard_map/ppermute | solution.py:452
  86.7 5.1 %collective-permute-start.12 = (f32[4,64,128]{2,1,0:T(8,128)S(1)}, f32[4,64,128]{2,1,0:T(8,128)S(1)}, u32[]{:S(2)}, u32[]{:S(2)}) collective-permute-start(f32[4,64,128]{2,1,0:T(8,128)S(1)} %multiply_add_fusion.4), channel_id=1, source_target_pairs={{0,4},{1,5},{2,6},{3,7},{4,0},{5,1},{6,2},{7,3},{8,12},{9,13},{10,... | collective-permute-start | bytes 393224 | tf_op jit(solution)/shard_map/ppermute | solution.py:452
  98.8 5.2 %collective-permute-start.13 = (f32[4,64,128]{2,1,0:T(8,128)}, f32[4,64,128]{2,1,0:T(8,128)S(1)}, u32[]{:S(2)}, u32[]{:S(2)}) collective-permute-start(f32[4,64,128]{2,1,0:T(8,128)} %get-tuple-element.42), channel_id=1, source_target_pairs={{0,8},{8,0},{16,24},{24,16},{1,9},{9,1},{17,25},{25,17},{2,10},{10... | collective-permute-start | bytes 393224 | tf_op jit(solution)/shard_map/ppermute | solution.py:452
  104.9 7.3 %collective-permute-start.14 = (f32[4,64,128]{2,1,0:T(8,128)S(1)}, f32[4,64,128]{2,1,0:T(8,128)S(1)}, u32[]{:S(2)}, u32[]{:S(2)}) collective-permute-start(f32[4,64,128]{2,1,0:T(8,128)S(1)} %add.91), channel_id=1, source_target_pairs={{0,16},{8,24},{16,0},{24,8},{1,17},{9,25},{17,1},{25,9},{2,18},{10... | collective-permute-start | bytes 393224 | tf_op jit(solution)/shard_map/ppermute | solution.py:452
  112.9 13.4 %copy-start = (f32[256,128]{1,0:T(8,128)S(1)}, f32[256,128]{1,0:T(8,128)}, u32[]{:S(2)}) copy-start(f32[256,128]{1,0:T(8,128)} %param.13) | copy-start | bytes 393220
  112.9 13.7 %copy-start.2 = (f32[4,64,128]{2,1,0:T(8,128)S(1)}, f32[4,64,128]{2,1,0:T(8,128)}, u32[]{:S(2)}) copy-start(f32[4,64,128]{2,1,0:T(8,128)} %get-tuple-element.36) | copy-start | bytes 393220
  123.5 1.6 %collective-permute-start.15 = (f32[4,64,128]{2,1,0:T(8,128)}, f32[4,64,128]{2,1,0:T(8,128)S(1)}, u32[]{:S(2)}, u32[]{:S(2)}) collective-permute-start(f32[4,64,128]{2,1,0:T(8,128)} %get-tuple-element.48), channel_id=1, source_target_pairs={{0,1},{1,0},{2,3},{3,2},{4,5},{5,4},{6,7},{7,6},{8,9},{9,8},{10,11... | collective-permute-start | bytes 393224 | tf_op jit(solution)/shard_map/ppermute | solution.py:452
  126.2 5.6 %collective-permute-start.16 = (f32[4,64,128]{2,1,0:T(8,128)S(1)}, f32[4,64,128]{2,1,0:T(8,128)S(1)}, u32[]{:S(2)}, u32[]{:S(2)}) collective-permute-start(f32[4,64,128]{2,1,0:T(8,128)S(1)} %multiply_add_fusion.2), channel_id=1, source_target_pairs={{0,2},{1,3},{2,0},{3,1},{4,6},{5,7},{6,4},{7,5},{8,10},{9,11},{10,... | collective-permute-start | bytes 393224 | tf_op jit(solution)/shard_map/ppermute | solution.py:452
  126.6 7.5 %collective-permute-start.8 = (f32[4,64,128]{2,1,0:T(8,128)S(1)}, f32[4,64,128]{2,1,0:T(8,128)S(1)}, u32[]{:S(2)}, u32[]{:S(2)}) collective-permute-start(f32[4,64,128]{2,1,0:T(8,128)S(1)} %copy-done.2), channel_id=1, source_target_pairs={{0,8},{8,0},{16,24},{24,16},{1,9},{9,1},{17,25},{25,17},{2,10},{10... | collective-permute-start | bytes 393224 | tf_op jit(solution)/shard_map/ppermute | solution.py:452
  131.9 5.0 %collective-permute-start.17 = (f32[4,64,128]{2,1,0:T(8,128)S(1)}, f32[4,64,128]{2,1,0:T(8,128)S(1)}, u32[]{:S(2)}, u32[]{:S(2)}) collective-permute-start(f32[4,64,128]{2,1,0:T(8,128)S(1)} %multiply_add_fusion.1), channel_id=1, source_target_pairs={{0,4},{1,5},{2,6},{3,7},{4,0},{5,1},{6,2},{7,3},{8,12},{9,13},{10,... | collective-permute-start | bytes 393224 | tf_op jit(solution)/shard_map/ppermute | solution.py:452
  134.1 11.0 %collective-permute-start.9 = (f32[4,64,128]{2,1,0:T(8,128)S(1)}, f32[4,64,128]{2,1,0:T(8,128)S(1)}, u32[]{:S(2)}, u32[]{:S(2)}) collective-permute-start(f32[4,64,128]{2,1,0:T(8,128)S(1)} %add.83), channel_id=1, source_target_pairs={{0,16},{8,24},{16,0},{24,8},{1,17},{9,25},{17,1},{25,9},{2,18},{10... | collective-permute-start | bytes 393224 | tf_op jit(solution)/shard_map/ppermute | solution.py:452
  144.5 4.7 %collective-permute-start.18 = (f32[2,128]{1,0:T(2,128)S(1)}, f32[2,128]{1,0:T(2,128)S(1)}, u32[]{:S(2)}, u32[]{:S(2)}) collective-permute-start(f32[2,128]{1,0:T(2,128)S(1)} %reshape.64), channel_id=1, source_target_pairs={{0,8},{8,0},{16,24},{24,16},{1,9},{9,1},{17,25},{25,17},{2,10},{10... | collective-permute-start | bytes 3080 | tf_op jit(solution)/shard_map/ppermute | solution.py:452
  149.3 4.5 %collective-permute-start.19 = (f32[2,128]{1,0:T(2,128)S(1)}, f32[2,128]{1,0:T(2,128)S(1)}, u32[]{:S(2)}, u32[]{:S(2)}) collective-permute-start(f32[2,128]{1,0:T(2,128)S(1)} %add.99), channel_id=1, source_target_pairs={{0,16},{8,24},{16,0},{24,8},{1,17},{9,25},{17,1},{25,9},{2,18},{10... | collective-permute-start | bytes 3080 | tf_op jit(solution)/shard_map/ppermute | solution.py:452

commit v15 on v13

--- a/solution.py
+++ b/solution.py
@@ -90,10 +90,11 @@
     refs = list(refs)
     spread_ref = refs.pop(0)
     u_ref = refs.pop(0) if has_u else None
-    ew_ref, ba_ref, h_scr, whole_ref, rows_ref, here_ref = refs
+    ew_ref = None if has_u else refs.pop(0)
+    ba_ref, h_scr, whole_ref, rows_ref, here_ref = refs
     k = pl.program_id(0)
-    n_c = ew_ref.shape[1]
-    shape = ew_ref.shape[2:]
+    n_c = ba_ref.shape[1]
+    shape = ba_ref.shape[2:]
 
     count, base = _columns(pos_ref, k, slots, n_c)
 
@@ -101,8 +102,10 @@
         c = pos_ref[base + i]
         m = _spread_row(spread_ref, c, shape)
         if has_u:
-            m = m - u_ref[0, c]
-        h = jnp.where(ew_ref[0, c] > 0, jnp.tanh(0.5 * m), 1.0)
+            u = u_ref[0, c]
+            h = jnp.where(u == u, jnp.tanh(0.5 * (m - u)), 1.0)
+        else:
+            h = jnp.where(ew_ref[0, c] > 0, jnp.tanh(0.5 * m), 1.0)
         h_scr[0, c] = h
         ba_ref[0, c] = carry
         return carry * h
@@ -150,7 +153,7 @@
         c = pos_ref[base + i]
         x = ba_ref[0, c] * f
         u = ew_ref[0, c] * jnp.log((1.0 + DAMP * x) / (1.0 - DAMP * x))
-        u_ref[0, c] = u
+        u_ref[0, c] = jnp.where(ew_ref[0, c] > 0, u, jnp.nan)
         col_ref[q, pl.ds(c, 1), :] = col_ref[q, pl.ds(c, 1), :] + jnp.sum(u, axis=0, keepdims=True)
         return carry
 
@@ -301,7 +304,7 @@
 def fwd_products(pos, spread, u, ew, blocks):
     k, c, r, s = ew.shape
     has_u = u is not None
-    inputs = [("column", spread)] + ([("dense", u)] if has_u else []) + [("dense", ew)]
+    inputs = [("column", spread)] + ([("dense", u)] if has_u else [("dense", ew)])
     outs = [
         ("dense", jax.ShapeDtypeStruct(ew.shape, F32)),
         ("dense", jax.ShapeDtypeStruct(ew.shape, F32)),

time: 152 us -> 151 us (level)
  starting transfers between devices: 33.4 us -> 25.2 us
  waiting for transfers between devices: 42.5 us -> 47.9 us
  Pallas kernels: 46.2 us -> 48.2 us
    ppermute x20, starting transfers between devices: 33.4 us -> 25.2 us  [_swap(): return lax.ppermute(value, axis, perm)]
    ppermute x20, waiting for transfers between devices: 42.5 us -> 47.9 us  [_swap(): return lax.ppermute(value, axis, perm)]
    pallas_call x7, Pallas kernels: 46.2 us -> 48.2 us  [_call(): pl.pallas_call(kernel, grid_spec=grid_spec, out_shape=[o for kind, o in o...]
  transfers between devices with their start and end apart: 20 -> 20, of which waited for: 17 -> 18; matrix products, arithmetic and copies ran while one was open for 6% -> 6% of each run, Pallas kernels for 3% -> 4%
where the time goes in v15:
time: 151 us
  Pallas kernels  48.2 us (32%)
  waiting for transfers between devices  47.9 us (32%)
  starting transfers between devices  25.2 us (17%)
  other arithmetic  16.5 us (11%)
  local copies, waits for them, and re-layouts  11.1 us (7%)
    pallas_call x7, Pallas kernels, _call(): pl.pallas_call(kernel, grid_spec=grid_spec, out_shape=[o for kind, o in o...  48.2 us
    ppermute x20, waiting for transfers between devices, _swap(): return lax.ppermute(value, axis, perm)  47.9 us
    ppermute x20, starting transfers between devices, _swap(): return lax.ppermute(value, axis, perm)  25.2 us
    reduce_sum x1, other arithmetic, body(): jnp.sum(acc, axis=3)  3.34 us
  transfers between devices with their start and end apart: 20, of which 18 were waited for; matrix products, arithmetic and copies ran while one was open for 6% of the time, Pallas kernels for 4%

profile of v15, /device:TPU:0, one launch (start us, length us, event | category | flops | bytes accessed | tf_op | source)
XLA Modules:
  0.0 150.6 jit_solution(6262128217844365515)
XLA Ops:
  0.6 0.9 squeeze.10
  2.7 1.0 sort.17
  4.6 0.9 reshape_squeeze.10
  7.0 2.6 %broadcast_in_dim.91.refs_1_.ew_ref.refs_5_.refs_6_ = f32[2,64,64,128]{3,2,1,0:T(8,128)} broadcast(f32[2,64,64]{2,1,0:T(8,128)S(1)} %multiply_bitcast_fusion), dimensions={0,1,2} | broadcast | bytes 4227072 | tf_op jit(solution)/shard_map/broadcast_in_dim | solution.py:517
  10.4 6.1 %shard_map.94 = (f32[2,64,64,128]{3,2,1,0:T(8,128)}, f32[2,64,64,128]{3,2,1,0:T(8,128)}, f32[2,64,128]{2,1,0:T(8,128)}, f32[4,64,128]{2,1,0:T(8,128)}, f32[2,64,128]{2,1,0:T(8,128)}) custom-call(s32[134]{0:T(256)} %pad_add_fusion.pos_ref, f32[4,64,128]{2,1,0:T(8,128)} %add.79.refs_0_, f32[2,64,64,128]{3,2,1,0:T(8,128)} %broadcast_in_dim.91.refs_1_.ew_ref.refs_5_.refs_6_), custom_call_target="tpu_custom_call" | custom-call | tf_op jit(solution)/shard_map/pallas_call | solution.py:291
  16.5 1.0 slice_reduce_fusion
  18.1 0.8 collective-permute-done
  18.9 2.8 %collective-permute-start.1 = (f32[2,128]{1,0:T(2,128)S(1)}, f32[2,128]{1,0:T(2,128)S(1)}, u32[]{:S(2)}, u32[]{:S(2)}) collective-permute-start(f32[2,128]{1,0:T(2,128)S(1)} %mul.88), channel_id=1, source_target_pairs={{0,2},{1,3},{2,0},{3,1},{4,6},{5,7},{6,4},{7,5},{8,10},{9,11},{10,... | collective-permute-start | bytes 3080 | tf_op jit(solution)/shard_map/ppermute | solution.py:422
  21.8 1.4 collective-permute-done.1
  23.3 2.0 %collective-permute-start.2 = (f32[2,128]{1,0:T(2,128)S(1)}, f32[2,128]{1,0:T(2,128)S(1)}, u32[]{:S(2)}, u32[]{:S(2)}) collective-permute-start(f32[2,128]{1,0:T(2,128)S(1)} %mul.90), channel_id=1, source_target_pairs={{0,4},{1,5},{2,6},{3,7},{4,0},{5,1},{6,2},{7,3},{8,12},{9,13},{10,... | collective-permute-start | bytes 3080 | tf_op jit(solution)/shard_map/ppermute | solution.py:422
  27.7 6.2 %shard_map.95 = (f32[2,64,64,128]{3,2,1,0:T(8,128)}, f32[4,64,128]{2,1,0:T(8,128)}) custom-call(s32[134]{0:T(256)} %pad_add_fusion.pos_ref, f32[2,64,64,128]{3,2,1,0:T(8,128)} %get-tuple-element.28.ba_ref.refs_2_, f32[2,64,128]{2,1,0:T(8,128)} %copy.30.sign_ref.refs_2_.refs_3_, f32[2,64,128]{2,1,0:T(8,128)} %get-tuple-element.29.here_ref.refs_4_.refs_5_, ...), custom_call_target="tpu_custom_call" | custom-call | tf_op jit(solution)/shard_map/pallas_call | solution.py:291
  33.9 1.9 %collective-permute-start.3 = (f32[4,64,128]{2,1,0:T(8,128)}, f32[4,64,128]{2,1,0:T(8,128)S(1)}, u32[]{:S(2)}, u32[]{:S(2)}) collective-permute-start(f32[4,64,128]{2,1,0:T(8,128)} %get-tuple-element.31), channel_id=1, source_target_pairs={{0,8},{8,0},{16,24},{24,16},{1,9},{9,1},{17,25},{25,17},{2,10},{10... | collective-permute-start | bytes 393224 | tf_op jit(solution)/shard_map/ppermute | solution.py:422
  35.8 3.3 %collective-permute-done.3 = f32[4,64,128]{2,1,0:T(8,128)S(1)} collective-permute-done((f32[4,64,128]{2,1,0:T(8,128)}, f32[4,64,128]{2,1,0:T(8,128)S(1)}, u32[]{:S(2)}, u32[]{:S(2)}) %collective-permute-start.3) | collective-permute-done | bytes 131104 | tf_op jit(solution)/shard_map/ppermute | solution.py:422
  39.0 0.9 add.80
  40.0 2.5 %collective-permute-start.4 = (f32[4,64,128]{2,1,0:T(8,128)S(1)}, f32[4,64,128]{2,1,0:T(8,128)S(1)}, u32[]{:S(2)}, u32[]{:S(2)}) collective-permute-start(f32[4,64,128]{2,1,0:T(8,128)S(1)} %add.80), channel_id=1, source_target_pairs={{0,16},{8,24},{16,0},{24,8},{1,17},{9,25},{17,1},{25,9},{2,18},{10... | collective-permute-start | bytes 393224 | tf_op jit(solution)/shard_map/ppermute | solution.py:422
  42.5 3.4 %collective-permute-done.4 = f32[4,64,128]{2,1,0:T(8,128)S(1)} collective-permute-done((f32[4,64,128]{2,1,0:T(8,128)S(1)}, f32[4,64,128]{2,1,0:T(8,128)S(1)}, u32[]{:S(2)}, u32[]{:S(2)}) %collective-permute-start.4) | collective-permute-done | bytes 131104 | tf_op jit(solution)/shard_map/ppermute | solution.py:422
  46.7 6.2 %shard_map.96 = (f32[2,64,64,128]{3,2,1,0:T(8,128)}, f32[2,64,64,128]{3,2,1,0:T(8,128)}, f32[2,64,128]{2,1,0:T(8,128)}, f32[4,64,128]{2,1,0:T(8,128)}, f32[2,64,128]{2,1,0:T(8,128)}) custom-call(s32[134]{0:T(256)} %pad_add_fusion.pos_ref, f32[4,64,128]{2,1,0:T(8,128)} %add_add_fusion.1.refs_0_, f32[2,64,64,128]{3,2,1,0:T(8,128)} %get-tuple-element.32.refs_1_), custom_call_target="tpu_custom_call" | custom-call | tf_op jit(solution)/shard_map/pallas_call | solution.py:291
  52.9 1.5 %collective-permute-done.5 = f32[4,64,128]{2,1,0:T(8,128)S(1)} collective-permute-done((f32[4,64,128]{2,1,0:T(8,128)}, f32[4,64,128]{2,1,0:T(8,128)S(1)}, u32[]{:S(2)}, u32[]{:S(2)}) %collective-permute-start.5) | collective-permute-done | bytes 131104 | tf_op jit(solution)/shard_map/ppermute | solution.py:422
  54.5 0.9 mul.92
  55.4 3.6 %collective-permute-start.6 = (f32[4,64,128]{2,1,0:T(8,128)S(1)}, f32[4,64,128]{2,1,0:T(8,128)S(1)}, u32[]{:S(2)}, u32[]{:S(2)}) collective-permute-start(f32[4,64,128]{2,1,0:T(8,128)S(1)} %mul.92), channel_id=1, source_target_pairs={{0,2},{1,3},{2,0},{3,1},{4,6},{5,7},{6,4},{7,5},{8,10},{9,11},{10,... | collective-permute-start | bytes 393224 | tf_op jit(solution)/shard_map/ppermute | solution.py:422
  59.0 3.8 %collective-permute-done.6 = f32[4,64,128]{2,1,0:T(8,128)S(1)} collective-permute-done((f32[4,64,128]{2,1,0:T(8,128)S(1)}, f32[4,64,128]{2,1,0:T(8,128)S(1)}, u32[]{:S(2)}, u32[]{:S(2)}) %collective-permute-start.6) | collective-permute-done | bytes 131104 | tf_op jit(solution)/shard_map/ppermute | solution.py:422
  62.8 1.6 %collective-permute-start.7 = (f32[4,64,128]{2,1,0:T(8,128)S(1)}, f32[4,64,128]{2,1,0:T(8,128)S(1)}, u32[]{:S(2)}, u32[]{:S(2)}) collective-permute-start(f32[4,64,128]{2,1,0:T(8,128)S(1)} %mul.94), channel_id=1, source_target_pairs={{0,4},{1,5},{2,6},{3,7},{4,0},{5,1},{6,2},{7,3},{8,12},{9,13},{10,... | collective-permute-start | bytes 393224 | tf_op jit(solution)/shard_map/ppermute | solution.py:422
  64.4 3.5 %collective-permute-done.7 = f32[4,64,128]{2,1,0:T(8,128)S(1)} collective-permute-done((f32[4,64,128]{2,1,0:T(8,128)S(1)}, f32[4,64,128]{2,1,0:T(8,128)S(1)}, u32[]{:S(2)}, u32[]{:S(2)}) %collective-permute-start.7) | collective-permute-done | bytes 131104 | tf_op jit(solution)/shard_map/ppermute | solution.py:422
  68.6 7.9 %shard_map.97 = (f32[2,64,64,128]{3,2,1,0:T(8,128)}, f32[2,64,64,128]{3,2,1,0:T(8,128)}, f32[2,64,128]{2,1,0:T(8,128)}, f32[4,64,128]{2,1,0:T(8,128)}, f32[4,64,128]{2,1,0:T(8,128)}) custom-call(s32[134]{0:T(256)} %pad_add_fusion.pos_ref, f32[4,64,128]{2,1,0:T(8,128)} %bitcast.15, f32[2,64,64,128]{3,2,1,0:T(8,128)} %get-tuple-element.33.refs_1_, ...), custom_call_target="tpu_custom_call" | custom-call | tf_op jit(solution)/shard_map/pallas_call | solution.py:291
  76.5 1.5 %collective-permute-done.10 = f32[4,64,128]{2,1,0:T(8,128)S(1)} collective-permute-done((f32[4,64,128]{2,1,0:T(8,128)}, f32[4,64,128]{2,1,0:T(8,128)S(1)}, u32[]{:S(2)}, u32[]{:S(2)}) %collective-permute-start.10) | collective-permute-done | bytes 131104 | tf_op jit(solution)/shard_map/ppermute | solution.py:422
  78.1 0.9 multiply_add_fusion.5
  79.0 1.8 %collective-permute-start.11 = (f32[4,64,128]{2,1,0:T(8,128)S(1)}, f32[4,64,128]{2,1,0:T(8,128)S(1)}, u32[]{:S(2)}, u32[]{:S(2)}) collective-permute-start(f32[4,64,128]{2,1,0:T(8,128)S(1)} %multiply_add_fusion.5), channel_id=1, source_target_pairs={{0,2},{1,3},{2,0},{3,1},{4,6},{5,7},{6,4},{7,5},{8,10},{9,11},{10,... | collective-permute-start | bytes 393224 | tf_op jit(solution)/shard_map/ppermute | solution.py:422
  80.8 3.8 %collective-permute-done.11 = f32[4,64,128]{2,1,0:T(8,128)S(1)} collective-permute-done((f32[4,64,128]{2,1,0:T(8,128)S(1)}, f32[4,64,128]{2,1,0:T(8,128)S(1)}, u32[]{:S(2)}, u32[]{:S(2)}) %collective-permute-start.11) | collective-permute-done | bytes 131104 | tf_op jit(solution)/shard_map/ppermute | solution.py:422
  84.7 1.5 collective-permute-start.12
  86.2 3.5 %collective-permute-done.12 = f32[4,64,128]{2,1,0:T(8,128)S(1)} collective-permute-done((f32[4,64,128]{2,1,0:T(8,128)S(1)}, f32[4,64,128]{2,1,0:T(8,128)S(1)}, u32[]{:S(2)}, u32[]{:S(2)}) %collective-permute-start.12) | collective-permute-done | bytes 131104 | tf_op jit(solution)/shard_map/ppermute | solution.py:422
  90.4 6.5 %shard_map.98 = (f32[2,64,64,128]{3,2,1,0:T(8,128)}, f32[4,64,128]{2,1,0:T(8,128)}) custom-call(s32[134]{0:T(256)} %pad_add_fusion.pos_ref, f32[2,64,64,128]{3,2,1,0:T(8,128)} %get-tuple-element.37.refs_0_, f32[2,64,64,128]{3,2,1,0:T(8,128)} %get-tuple-element.38.refs_1_, f32[4,64,128]{2,1,0:T(8,128)} %multiply_add_fusion.3.refs_2_, ...), custom_call_target="tpu_custom_call" | custom-call | tf_op jit(solution)/shard_map/pallas_call | solution.py:291
  96.9 5.2 %collective-permute-done.13 = f32[4,64,128]{2,1,0:T(8,128)S(1)} collective-permute-done((f32[4,64,128]{2,1,0:T(8,128)}, f32[4,64,128]{2,1,0:T(8,128)S(1)}, u32[]{:S(2)}, u32[]{:S(2)}) %collective-permute-start.13) | collective-permute-done | bytes 131104 | tf_op jit(solution)/shard_map/ppermute | solution.py:422
  102.1 0.9 add.91
  103.8 6.0 %collective-permute-done.14 = f32[4,64,128]{2,1,0:T(8,128)S(1)} collective-permute-done((f32[4,64,128]{2,1,0:T(8,128)S(1)}, f32[4,64,128]{2,1,0:T(8,128)S(1)}, u32[]{:S(2)}, u32[]{:S(2)}) %collective-permute-start.14) | collective-permute-done | bytes 131104 | tf_op jit(solution)/shard_map/ppermute | solution.py:422
  110.5 9.6 %shard_map.99 = (f32[2,64,64,128]{3,2,1,0:T(8,128)}, f32[2,64,64,128]{3,2,1,0:T(8,128)}, f32[2,64,128]{2,1,0:T(8,128)}, f32[4,64,128]{2,1,0:T(8,128)}) custom-call(s32[134]{0:T(256)} %pad_add_fusion.pos_ref, f32[4,64,128]{2,1,0:T(8,128)} %get-tuple-element.52.refs_0_, f32[2,64,64,128]{3,2,1,0:T(8,128)} %get-tuple-element.43.refs_1_, ...), custom_call_target="tpu_custom_call" | custom-call | tf_op jit(solution)/shard_map/pallas_call | solution.py:291
  120.3 1.5 collective-permute-done.15
  121.7 1.0 multiply_add_fusion.2
  122.8 1.9 %collective-permute-start.16 = (f32[4,64,128]{2,1,0:T(8,128)S(1)}, f32[4,64,128]{2,1,0:T(8,128)S(1)}, u32[]{:S(2)}, u32[]{:S(2)}) collective-permute-start(f32[4,64,128]{2,1,0:T(8,128)S(1)} %multiply_add_fusion.2), channel_id=1, source_target_pairs={{0,2},{1,3},{2,0},{3,1},{4,6},{5,7},{6,4},{7,5},{8,10},{9,11},{10,... | collective-permute-start | bytes 393224 | tf_op jit(solution)/shard_map/ppermute | solution.py:422
  124.9 3.5 %collective-permute-done.16 = f32[4,64,128]{2,1,0:T(8,128)S(1)} collective-permute-done((f32[4,64,128]{2,1,0:T(8,128)S(1)}, f32[4,64,128]{2,1,0:T(8,128)S(1)}, u32[]{:S(2)}, u32[]{:S(2)}) %collective-permute-start.16) | collective-permute-done | bytes 131104 | tf_op jit(solution)/shard_map/ppermute | solution.py:422
  128.6 1.3 collective-permute-start.17
  130.2 0.8 collective-permute-start.9
  131.1 2.6 %collective-permute-done.17 = f32[4,64,128]{2,1,0:T(8,128)S(1)} collective-permute-done((f32[4,64,128]{2,1,0:T(8,128)S(1)}, f32[4,64,128]{2,1,0:T(8,128)S(1)}, u32[]{:S(2)}, u32[]{:S(2)}) %collective-permute-start.17) | collective-permute-done | bytes 131104 | tf_op jit(solution)/shard_map/ppermute | solution.py:422
  133.6 0.9 multiply_add_fusion.refs_2_
  134.5 5.7 %shard_map.100 = f32[4,64,128]{2,1,0:T(8,128)} custom-call(s32[134]{0:T(256)} %pad_add_fusion.pos_ref, f32[2,64,64,128]{3,2,1,0:T(8,128)} %get-tuple-element.46.refs_0_, f32[2,64,64,128]{3,2,1,0:T(8,128)} %get-tuple-element.47.refs_1_, f32[4,64,128]{2,1,0:T(8,128)} %multiply_add_fusion.refs_2_, f32[2,64,128]{2,1,0:T(8,128)} %get-tuple-element.49.refs_3_, ...), custom_call_target="tpu_custom_call" | custom-call | tf_op jit(solution)/shard_map/pallas_call | solution.py:291
  140.3 1.0 reduce_sum.52
  142.1 3.3 %reduce_sum.48 = f32[2,64,64]{2,1,0:T(8,128)S(1)} reduce(f32[2,64,64,128]{3,2,1,0:T(8,128)} %get-tuple-element.45, f32[]{:T(128)} %constant.7.clone.1), dimensions={3}, to_apply=%region_3.4 | reduce | flops 1040384 | bytes 4227076 | tf_op jit(solution)/shard_map/reduce_sum | solution.py:564
  145.5 1.9 %collective-permute-start.19 = (f32[2,128]{1,0:T(2,128)S(1)}, f32[2,128]{1,0:T(2,128)S(1)}, u32[]{:S(2)}, u32[]{:S(2)}) collective-permute-start(f32[2,128]{1,0:T(2,128)S(1)} %add.99), channel_id=1, source_target_pairs={{0,16},{8,24},{16,0},{24,8},{1,17},{9,25},{17,1},{25,9},{2,18},{10... | collective-permute-start | bytes 3080 | tf_op jit(solution)/shard_map/ppermute | solution.py:422
  148.3 1.8 %collective-permute-done.19 = f32[2,128]{1,0:T(2,128)S(1)} collective-permute-done((f32[2,128]{1,0:T(2,128)S(1)}, f32[2,128]{1,0:T(2,128)S(1)}, u32[]{:S(2)}, u32[]{:S(2)}) %collective-permute-start.19) | collective-permute-done | bytes 1056 | tf_op jit(solution)/shard_map/ppermute | solution.py:422
  (69 shorter events, 13.8 us)
Async XLA Ops:
  7.0 11.1 %copy-start.3 = (s32[256,128]{1,0:T(8,128)S(1)}, s32[256,128]{1,0:T(8,128)}, u32[]{:S(2)}) copy-start(s32[256,128]{1,0:T(8,128)} %param.11) | copy-start | bytes 393220
  7.0 14.7 %copy-start.4 = (s32[1,1,2,2]{3,2,1,0:T(2,128)S(1)}, s32[1,1,2,2]{3,2,1,0:T(2,128)}, u32[]{:S(2)}) copy-start(s32[1,1,2,2]{3,2,1,0:T(2,128)} %param.8) | copy-start | bytes 52
  17.6 1.3 collective-permute-start
  18.9 4.4 %collective-permute-start.1 = (f32[2,128]{1,0:T(2,128)S(1)}, f32[2,128]{1,0:T(2,128)S(1)}, u32[]{:S(2)}, u32[]{:S(2)}) collective-permute-start(f32[2,128]{1,0:T(2,128)S(1)} %mul.88), channel_id=1, source_target_pairs={{0,2},{1,3},{2,0},{3,1},{4,6},{5,7},{6,4},{7,5},{8,10},{9,11},{10,... | collective-permute-start | bytes 3080 | tf_op jit(solution)/shard_map/ppermute | solution.py:422
  23.3 3.6 %collective-permute-start.2 = (f32[2,128]{1,0:T(2,128)S(1)}, f32[2,128]{1,0:T(2,128)S(1)}, u32[]{:S(2)}, u32[]{:S(2)}) collective-permute-start(f32[2,128]{1,0:T(2,128)S(1)} %mul.90), channel_id=1, source_target_pairs={{0,4},{1,5},{2,6},{3,7},{4,0},{5,1},{6,2},{7,3},{8,12},{9,13},{10,... | collective-permute-start | bytes 3080 | tf_op jit(solution)/shard_map/ppermute | solution.py:422
  33.9 5.2 %collective-permute-start.3 = (f32[4,64,128]{2,1,0:T(8,128)}, f32[4,64,128]{2,1,0:T(8,128)S(1)}, u32[]{:S(2)}, u32[]{:S(2)}) collective-permute-start(f32[4,64,128]{2,1,0:T(8,128)} %get-tuple-element.31), channel_id=1, source_target_pairs={{0,8},{8,0},{16,24},{24,16},{1,9},{9,1},{17,25},{25,17},{2,10},{10... | collective-permute-start | bytes 393224 | tf_op jit(solution)/shard_map/ppermute | solution.py:422
  40.0 5.9 %collective-permute-start.4 = (f32[4,64,128]{2,1,0:T(8,128)S(1)}, f32[4,64,128]{2,1,0:T(8,128)S(1)}, u32[]{:S(2)}, u32[]{:S(2)}) collective-permute-start(f32[4,64,128]{2,1,0:T(8,128)S(1)} %add.80), channel_id=1, source_target_pairs={{0,16},{8,24},{16,0},{24,8},{1,17},{9,25},{17,1},{25,9},{2,18},{10... | collective-permute-start | bytes 393224 | tf_op jit(solution)/shard_map/ppermute | solution.py:422
  52.8 1.6 %collective-permute-start.5 = (f32[4,64,128]{2,1,0:T(8,128)}, f32[4,64,128]{2,1,0:T(8,128)S(1)}, u32[]{:S(2)}, u32[]{:S(2)}) collective-permute-start(f32[4,64,128]{2,1,0:T(8,128)} %get-tuple-element.35), channel_id=1, source_target_pairs={{0,1},{1,0},{2,3},{3,2},{4,5},{5,4},{6,7},{7,6},{8,9},{9,8},{10,11... | collective-permute-start | bytes 393224 | tf_op jit(solution)/shard_map/ppermute | solution.py:422
  55.4 7.4 %collective-permute-start.6 = (f32[4,64,128]{2,1,0:T(8,128)S(1)}, f32[4,64,128]{2,1,0:T(8,128)S(1)}, u32[]{:S(2)}, u32[]{:S(2)}) collective-permute-start(f32[4,64,128]{2,1,0:T(8,128)S(1)} %mul.92), channel_id=1, source_target_pairs={{0,2},{1,3},{2,0},{3,1},{4,6},{5,7},{6,4},{7,5},{8,10},{9,11},{10,... | collective-permute-start | bytes 393224 | tf_op jit(solution)/shard_map/ppermute | solution.py:422
  62.8 5.1 %collective-permute-start.7 = (f32[4,64,128]{2,1,0:T(8,128)S(1)}, f32[4,64,128]{2,1,0:T(8,128)S(1)}, u32[]{:S(2)}, u32[]{:S(2)}) collective-permute-start(f32[4,64,128]{2,1,0:T(8,128)S(1)} %mul.94), channel_id=1, source_target_pairs={{0,4},{1,5},{2,6},{3,7},{4,0},{5,1},{6,2},{7,3},{8,12},{9,13},{10,... | collective-permute-start | bytes 393224 | tf_op jit(solution)/shard_map/ppermute | solution.py:422
  68.6 9.5 %copy-start.1 = (f32[4,64,128]{2,1,0:T(8,128)S(1)}, f32[4,64,128]{2,1,0:T(8,128)}, u32[]{:S(2)}) copy-start(f32[4,64,128]{2,1,0:T(8,128)} %get-tuple-element.35) | copy-start | bytes 393220
  76.4 1.6 %collective-permute-start.10 = (f32[4,64,128]{2,1,0:T(8,128)}, f32[4,64,128]{2,1,0:T(8,128)S(1)}, u32[]{:S(2)}, u32[]{:S(2)}) collective-permute-start(f32[4,64,128]{2,1,0:T(8,128)} %get-tuple-element.39), channel_id=1, source_target_pairs={{0,1},{1,0},{2,3},{3,2},{4,5},{5,4},{6,7},{7,6},{8,9},{9,8},{10,11... | collective-permute-start | bytes 393224 | tf_op jit(solution)/shard_map/ppermute | solution.py:422
  79.0 5.6 %collective-permute-start.11 = (f32[4,64,128]{2,1,0:T(8,128)S(1)}, f32[4,64,128]{2,1,0:T(8,128)S(1)}, u32[]{:S(2)}, u32[]{:S(2)}) collective-permute-start(f32[4,64,128]{2,1,0:T(8,128)S(1)} %multiply_add_fusion.5), channel_id=1, source_target_pairs={{0,2},{1,3},{2,0},{3,1},{4,6},{5,7},{6,4},{7,5},{8,10},{9,11},{10,... | collective-permute-start | bytes 393224 | tf_op jit(solution)/shard_map/ppermute | solution.py:422
  84.7 5.0 %collective-permute-start.12 = (f32[4,64,128]{2,1,0:T(8,128)S(1)}, f32[4,64,128]{2,1,0:T(8,128)S(1)}, u32[]{:S(2)}, u32[]{:S(2)}) collective-permute-start(f32[4,64,128]{2,1,0:T(8,128)S(1)} %multiply_add_fusion.4), channel_id=1, source_target_pairs={{0,4},{1,5},{2,6},{3,7},{4,0},{5,1},{6,2},{7,3},{8,12},{9,13},{10,... | collective-permute-start | bytes 393224 | tf_op jit(solution)/shard_map/ppermute | solution.py:422
  96.9 5.2 %collective-permute-start.13 = (f32[4,64,128]{2,1,0:T(8,128)}, f32[4,64,128]{2,1,0:T(8,128)S(1)}, u32[]{:S(2)}, u32[]{:S(2)}) collective-permute-start(f32[4,64,128]{2,1,0:T(8,128)} %get-tuple-element.42), channel_id=1, source_target_pairs={{0,8},{8,0},{16,24},{24,16},{1,9},{9,1},{17,25},{25,17},{2,10},{10... | collective-permute-start | bytes 393224 | tf_op jit(solution)/shard_map/ppermute | solution.py:422
  103.0 6.8 %collective-permute-start.14 = (f32[4,64,128]{2,1,0:T(8,128)S(1)}, f32[4,64,128]{2,1,0:T(8,128)S(1)}, u32[]{:S(2)}, u32[]{:S(2)}) collective-permute-start(f32[4,64,128]{2,1,0:T(8,128)S(1)} %add.91), channel_id=1, source_target_pairs={{0,16},{8,24},{16,0},{24,8},{1,17},{9,25},{17,1},{25,9},{2,18},{10... | collective-permute-start | bytes 393224 | tf_op jit(solution)/shard_map/ppermute | solution.py:422
  110.5 14.2 %copy-start = (f32[256,128]{1,0:T(8,128)S(1)}, f32[256,128]{1,0:T(8,128)}, u32[]{:S(2)}) copy-start(f32[256,128]{1,0:T(8,128)} %param.13) | copy-start | bytes 393220
  110.5 14.4 %copy-start.2 = (f32[4,64,128]{2,1,0:T(8,128)S(1)}, f32[4,64,128]{2,1,0:T(8,128)}, u32[]{:S(2)}) copy-start(f32[4,64,128]{2,1,0:T(8,128)} %get-tuple-element.36) | copy-start | bytes 393220
  120.1 1.6 %collective-permute-start.15 = (f32[4,64,128]{2,1,0:T(8,128)}, f32[4,64,128]{2,1,0:T(8,128)S(1)}, u32[]{:S(2)}, u32[]{:S(2)}) collective-permute-start(f32[4,64,128]{2,1,0:T(8,128)} %get-tuple-element.48), channel_id=1, source_target_pairs={{0,1},{1,0},{2,3},{3,2},{4,5},{5,4},{6,7},{7,6},{8,9},{9,8},{10,11... | collective-permute-start | bytes 393224 | tf_op jit(solution)/shard_map/ppermute | solution.py:422
  122.8 5.7 %collective-permute-start.16 = (f32[4,64,128]{2,1,0:T(8,128)S(1)}, f32[4,64,128]{2,1,0:T(8,128)S(1)}, u32[]{:S(2)}, u32[]{:S(2)}) collective-permute-start(f32[4,64,128]{2,1,0:T(8,128)S(1)} %multiply_add_fusion.2), channel_id=1, source_target_pairs={{0,2},{1,3},{2,0},{3,1},{4,6},{5,7},{6,4},{7,5},{8,10},{9,11},{10,... | collective-permute-start | bytes 393224 | tf_op jit(solution)/shard_map/ppermute | solution.py:422
  124.9 5.3 %collective-permute-start.8 = (f32[4,64,128]{2,1,0:T(8,128)S(1)}, f32[4,64,128]{2,1,0:T(8,128)S(1)}, u32[]{:S(2)}, u32[]{:S(2)}) collective-permute-start(f32[4,64,128]{2,1,0:T(8,128)S(1)} %copy-done.2), channel_id=1, source_target_pairs={{0,8},{8,0},{16,24},{24,16},{1,9},{9,1},{17,25},{25,17},{2,10},{10... | collective-permute-start | bytes 393224 | tf_op jit(solution)/shard_map/ppermute | solution.py:422
  128.6 5.0 %collective-permute-start.17 = (f32[4,64,128]{2,1,0:T(8,128)S(1)}, f32[4,64,128]{2,1,0:T(8,128)S(1)}, u32[]{:S(2)}, u32[]{:S(2)}) collective-permute-start(f32[4,64,128]{2,1,0:T(8,128)S(1)} %multiply_add_fusion.1), channel_id=1, source_target_pairs={{0,4},{1,5},{2,6},{3,7},{4,0},{5,1},{6,2},{7,3},{8,12},{9,13},{10,... | collective-permute-start | bytes 393224 | tf_op jit(solution)/shard_map/ppermute | solution.py:422
  130.2 11.2 %collective-permute-start.9 = (f32[4,64,128]{2,1,0:T(8,128)S(1)}, f32[4,64,128]{2,1,0:T(8,128)S(1)}, u32[]{:S(2)}, u32[]{:S(2)}) collective-permute-start(f32[4,64,128]{2,1,0:T(8,128)S(1)} %add.83), channel_id=1, source_target_pairs={{0,16},{8,24},{16,0},{24,8},{1,17},{9,25},{17,1},{25,9},{2,18},{10... | collective-permute-start | bytes 393224 | tf_op jit(solution)/shard_map/ppermute | solution.py:422
  141.4 4.1 %collective-permute-start.18 = (f32[2,128]{1,0:T(2,128)S(1)}, f32[2,128]{1,0:T(2,128)S(1)}, u32[]{:S(2)}, u32[]{:S(2)}) collective-permute-start(f32[2,128]{1,0:T(2,128)S(1)} %reshape.64), channel_id=1, source_target_pairs={{0,8},{8,0},{16,24},{24,16},{1,9},{9,1},{17,25},{25,17},{2,10},{10... | collective-permute-start | bytes 3080 | tf_op jit(solution)/shard_map/ppermute | solution.py:422
  145.5 4.5 %collective-permute-start.19 = (f32[2,128]{1,0:T(2,128)S(1)}, f32[2,128]{1,0:T(2,128)S(1)}, u32[]{:S(2)}, u32[]{:S(2)}) collective-permute-start(f32[2,128]{1,0:T(2,128)S(1)} %add.99), channel_id=1, source_target_pairs={{0,16},{8,24},{16,0},{24,8},{1,17},{9,25},{17,1},{25,9},{2,18},{10... | collective-permute-start | bytes 3080 | tf_op jit(solution)/shard_map/ppermute | solution.py:422

commit v16 on v13

--- a/solution.py
+++ b/solution.py
@@ -99,10 +99,12 @@
 
     def forward(i, carry):
         c = pos_ref[base + i]
-        m = _spread_row(spread_ref, c, shape)
         if has_u:
-            m = m - u_ref[0, c]
-        h = jnp.where(ew_ref[0, c] > 0, jnp.tanh(0.5 * m), 1.0)
+            m = _spread_row(spread_ref, c, shape) - u_ref[0, c]
+            h = jnp.where(ew_ref[0, c] > 0, jnp.tanh(0.5 * m), 1.0)
+        else:
+            t = jnp.broadcast_to(jnp.tanh(0.5 * spread_ref[0, pl.ds(c, 1), :]), shape)
+            h = jnp.where(ew_ref[0, c] > 0, t, 1.0)
         h_scr[0, c] = h
         ba_ref[0, c] = carry
         return carry * h

time: 152 us -> 152 us (level)
  starting transfers between devices: 33.4 us -> 28.5 us
  Pallas kernels: 46.2 us -> 48.4 us
  waiting for transfers between devices: 42.5 us -> 44.6 us
    ppermute x20, starting transfers between devices: 33.4 us -> 28.5 us  [_swap(): return lax.ppermute(value, axis, perm)]
    pallas_call x7, Pallas kernels: 46.2 us -> 48.4 us  [_call(): pl.pallas_call(kernel, grid_spec=grid_spec, out_shape=[o for kind, o in o...]
    ppermute x20, waiting for transfers between devices: 42.5 us -> 44.6 us  [_swap(): return lax.ppermute(value, axis, perm)]
  transfers between devices with their start and end apart: 20 -> 20, of which waited for: 17 -> 17; matrix products, arithmetic and copies ran while one was open for 6% -> 6% of each run, Pallas kernels for 3% -> 4%
where the time goes in v16:
time: 152 us; the launch traced here: 151 us
  Pallas kernels  48.4 us (32%)
  waiting for transfers between devices  44.6 us (29%)
  starting transfers between devices  28.5 us (19%)
  other arithmetic  16.5 us (11%)
  local copies, waits for them, and re-layouts  11.1 us (7%)
    pallas_call x7, Pallas kernels, _call(): pl.pallas_call(kernel, grid_spec=grid_spec, out_shape=[o for kind, o in o...  48.4 us
    ppermute x20, waiting for transfers between devices, _swap(): return lax.ppermute(value, axis, perm)  44.6 us
    ppermute x20, starting transfers between devices, _swap(): return lax.ppermute(value, axis, perm)  28.5 us
    reduce_sum x1, other arithmetic, body(): jnp.sum(acc, axis=3)  3.34 us
  transfers between devices with their start and end apart: 20, of which 17 were waited for; matrix products, arithmetic and copies ran while one was open for 6% of the time, Pallas kernels for 4%

profile of v16, /device:TPU:0, one launch (start us, length us, event | category | flops | bytes accessed | tf_op | source)
XLA Modules:
  0.0 150.9 jit_solution(2783052188709544426)
XLA Ops:
  0.6 0.9 squeeze.10
  2.7 1.0 sort.17
  4.6 0.9 reshape_squeeze.10
  7.0 2.6 %broadcast_in_dim.91.refs_1_.ew_ref.refs_2_.refs_5_.refs_6_ = f32[2,64,64,128]{3,2,1,0:T(8,128)} broadcast(f32[2,64,64]{2,1,0:T(8,128)S(1)} %multiply_bitcast_fusion), dimensions={0,1,2} | broadcast | bytes 4227072 | tf_op jit(solution)/shard_map/broadcast_in_dim | solution.py:516
  10.4 6.1 %shard_map.94 = (f32[2,64,64,128]{3,2,1,0:T(8,128)}, f32[2,64,64,128]{3,2,1,0:T(8,128)}, f32[2,64,128]{2,1,0:T(8,128)}, f32[4,64,128]{2,1,0:T(8,128)}, f32[2,64,128]{2,1,0:T(8,128)}) custom-call(s32[134]{0:T(256)} %pad_add_fusion.pos_ref, f32[4,64,128]{2,1,0:T(8,128)} %add.79.refs_0_, f32[2,64,64,128]{3,2,1,0:T(8,128)} %broadcast_in_dim.91.refs_1_.ew_ref.refs_2_.refs_5_.refs_6_), custom_call_target="tpu_custom_call" | custom-call | tf_op jit(solution)/shard_map/pallas_call | solution.py:290
  16.5 1.0 slice_reduce_fusion
  18.8 2.8 %collective-permute-start.1 = (f32[2,128]{1,0:T(2,128)S(1)}, f32[2,128]{1,0:T(2,128)S(1)}, u32[]{:S(2)}, u32[]{:S(2)}) collective-permute-start(f32[2,128]{1,0:T(2,128)S(1)} %mul.88), channel_id=1, source_target_pairs={{0,2},{1,3},{2,0},{3,1},{4,6},{5,7},{6,4},{7,5},{8,10},{9,11},{10,... | collective-permute-start | bytes 3080 | tf_op jit(solution)/shard_map/ppermute | solution.py:421
  21.7 1.4 collective-permute-done.1
  23.2 2.1 %collective-permute-start.2 = (f32[2,128]{1,0:T(2,128)S(1)}, f32[2,128]{1,0:T(2,128)S(1)}, u32[]{:S(2)}, u32[]{:S(2)}) collective-permute-start(f32[2,128]{1,0:T(2,128)S(1)} %mul.90), channel_id=1, source_target_pairs={{0,4},{1,5},{2,6},{3,7},{4,0},{5,1},{6,2},{7,3},{8,12},{9,13},{10,... | collective-permute-start | bytes 3080 | tf_op jit(solution)/shard_map/ppermute | solution.py:421
  27.7 6.0 %shard_map.95 = (f32[2,64,64,128]{3,2,1,0:T(8,128)}, f32[4,64,128]{2,1,0:T(8,128)}) custom-call(s32[134]{0:T(256)} %pad_add_fusion.pos_ref, f32[2,64,64,128]{3,2,1,0:T(8,128)} %get-tuple-element.28.ba_ref.refs_2_, f32[2,64,128]{2,1,0:T(8,128)} %copy.30.sign_ref.refs_2_.refs_3_, f32[2,64,128]{2,1,0:T(8,128)} %get-tuple-element.29.here_ref.refs_4_.refs_5_, ...), custom_call_target="tpu_custom_call" | custom-call | tf_op jit(solution)/shard_map/pallas_call | solution.py:290
  33.7 2.0 %collective-permute-start.3 = (f32[4,64,128]{2,1,0:T(8,128)}, f32[4,64,128]{2,1,0:T(8,128)S(1)}, u32[]{:S(2)}, u32[]{:S(2)}) collective-permute-start(f32[4,64,128]{2,1,0:T(8,128)} %get-tuple-element.31), channel_id=1, source_target_pairs={{0,8},{8,0},{16,24},{24,16},{1,9},{9,1},{17,25},{25,17},{2,10},{10... | collective-permute-start | bytes 393224 | tf_op jit(solution)/shard_map/ppermute | solution.py:421
  35.8 3.2 %collective-permute-done.3 = f32[4,64,128]{2,1,0:T(8,128)S(1)} collective-permute-done((f32[4,64,128]{2,1,0:T(8,128)}, f32[4,64,128]{2,1,0:T(8,128)S(1)}, u32[]{:S(2)}, u32[]{:S(2)}) %collective-permute-start.3) | collective-permute-done | bytes 131104 | tf_op jit(solution)/shard_map/ppermute | solution.py:421
  38.9 0.9 add.80
  39.9 2.8 %collective-permute-start.4 = (f32[4,64,128]{2,1,0:T(8,128)S(1)}, f32[4,64,128]{2,1,0:T(8,128)S(1)}, u32[]{:S(2)}, u32[]{:S(2)}) collective-permute-start(f32[4,64,128]{2,1,0:T(8,128)S(1)} %add.80), channel_id=1, source_target_pairs={{0,16},{8,24},{16,0},{24,8},{1,17},{9,25},{17,1},{25,9},{2,18},{10... | collective-permute-start | bytes 393224 | tf_op jit(solution)/shard_map/ppermute | solution.py:421
  42.6 3.1 %collective-permute-done.4 = f32[4,64,128]{2,1,0:T(8,128)S(1)} collective-permute-done((f32[4,64,128]{2,1,0:T(8,128)S(1)}, f32[4,64,128]{2,1,0:T(8,128)S(1)}, u32[]{:S(2)}, u32[]{:S(2)}) %collective-permute-start.4) | collective-permute-done | bytes 131104 | tf_op jit(solution)/shard_map/ppermute | solution.py:421
  46.5 6.8 %shard_map.96 = (f32[2,64,64,128]{3,2,1,0:T(8,128)}, f32[2,64,64,128]{3,2,1,0:T(8,128)}, f32[2,64,128]{2,1,0:T(8,128)}, f32[4,64,128]{2,1,0:T(8,128)}, f32[2,64,128]{2,1,0:T(8,128)}) custom-call(s32[134]{0:T(256)} %pad_add_fusion.pos_ref, f32[4,64,128]{2,1,0:T(8,128)} %add_add_fusion.1.refs_0_, f32[2,64,64,128]{3,2,1,0:T(8,128)} %get-tuple-element.32.refs_1_, ...), custom_call_target="tpu_custom_call" | custom-call | tf_op jit(solution)/shard_map/pallas_call | solution.py:290
  53.4 1.5 %collective-permute-done.5 = f32[4,64,128]{2,1,0:T(8,128)S(1)} collective-permute-done((f32[4,64,128]{2,1,0:T(8,128)}, f32[4,64,128]{2,1,0:T(8,128)S(1)}, u32[]{:S(2)}, u32[]{:S(2)}) %collective-permute-start.5) | collective-permute-done | bytes 131104 | tf_op jit(solution)/shard_map/ppermute | solution.py:421
  54.9 0.9 mul.92
  55.9 2.8 %collective-permute-start.6 = (f32[4,64,128]{2,1,0:T(8,128)S(1)}, f32[4,64,128]{2,1,0:T(8,128)S(1)}, u32[]{:S(2)}, u32[]{:S(2)}) collective-permute-start(f32[4,64,128]{2,1,0:T(8,128)S(1)} %mul.92), channel_id=1, source_target_pairs={{0,2},{1,3},{2,0},{3,1},{4,6},{5,7},{6,4},{7,5},{8,10},{9,11},{10,... | collective-permute-start | bytes 393224 | tf_op jit(solution)/shard_map/ppermute | solution.py:421
  58.7 3.8 %collective-permute-done.6 = f32[4,64,128]{2,1,0:T(8,128)S(1)} collective-permute-done((f32[4,64,128]{2,1,0:T(8,128)S(1)}, f32[4,64,128]{2,1,0:T(8,128)S(1)}, u32[]{:S(2)}, u32[]{:S(2)}) %collective-permute-start.6) | collective-permute-done | bytes 131104 | tf_op jit(solution)/shard_map/ppermute | solution.py:421
  62.5 2.5 %collective-permute-start.7 = (f32[4,64,128]{2,1,0:T(8,128)S(1)}, f32[4,64,128]{2,1,0:T(8,128)S(1)}, u32[]{:S(2)}, u32[]{:S(2)}) collective-permute-start(f32[4,64,128]{2,1,0:T(8,128)S(1)} %mul.94), channel_id=1, source_target_pairs={{0,4},{1,5},{2,6},{3,7},{4,0},{5,1},{6,2},{7,3},{8,12},{9,13},{10,... | collective-permute-start | bytes 393224 | tf_op jit(solution)/shard_map/ppermute | solution.py:421
  65.0 3.0 %collective-permute-done.7 = f32[4,64,128]{2,1,0:T(8,128)S(1)} collective-permute-done((f32[4,64,128]{2,1,0:T(8,128)S(1)}, f32[4,64,128]{2,1,0:T(8,128)S(1)}, u32[]{:S(2)}, u32[]{:S(2)}) %collective-permute-start.7) | collective-permute-done | bytes 131104 | tf_op jit(solution)/shard_map/ppermute | solution.py:421
  68.7 7.8 %shard_map.97 = (f32[2,64,64,128]{3,2,1,0:T(8,128)}, f32[2,64,64,128]{3,2,1,0:T(8,128)}, f32[2,64,128]{2,1,0:T(8,128)}, f32[4,64,128]{2,1,0:T(8,128)}, f32[4,64,128]{2,1,0:T(8,128)}) custom-call(s32[134]{0:T(256)} %pad_add_fusion.pos_ref, f32[4,64,128]{2,1,0:T(8,128)} %bitcast.15, f32[2,64,64,128]{3,2,1,0:T(8,128)} %get-tuple-element.33.refs_1_, ...), custom_call_target="tpu_custom_call" | custom-call | tf_op jit(solution)/shard_map/pallas_call | solution.py:290
  76.6 1.5 %collective-permute-done.10 = f32[4,64,128]{2,1,0:T(8,128)S(1)} collective-permute-done((f32[4,64,128]{2,1,0:T(8,128)}, f32[4,64,128]{2,1,0:T(8,128)S(1)}, u32[]{:S(2)}, u32[]{:S(2)}) %collective-permute-start.10) | collective-permute-done | bytes 131104 | tf_op jit(solution)/shard_map/ppermute | solution.py:421
  78.1 0.9 multiply_add_fusion.5
  79.1 1.3 collective-permute-start.11
  80.3 4.3 %collective-permute-done.11 = f32[4,64,128]{2,1,0:T(8,128)S(1)} collective-permute-done((f32[4,64,128]{2,1,0:T(8,128)S(1)}, f32[4,64,128]{2,1,0:T(8,128)S(1)}, u32[]{:S(2)}, u32[]{:S(2)}) %collective-permute-start.11) | collective-permute-done | bytes 131104 | tf_op jit(solution)/shard_map/ppermute | solution.py:421
  84.7 2.1 %collective-permute-start.12 = (f32[4,64,128]{2,1,0:T(8,128)S(1)}, f32[4,64,128]{2,1,0:T(8,128)S(1)}, u32[]{:S(2)}, u32[]{:S(2)}) collective-permute-start(f32[4,64,128]{2,1,0:T(8,128)S(1)} %multiply_add_fusion.4), channel_id=1, source_target_pairs={{0,4},{1,5},{2,6},{3,7},{4,0},{5,1},{6,2},{7,3},{8,12},{9,13},{10,... | collective-permute-start | bytes 393224 | tf_op jit(solution)/shard_map/ppermute | solution.py:421
  86.8 3.0 %collective-permute-done.12 = f32[4,64,128]{2,1,0:T(8,128)S(1)} collective-permute-done((f32[4,64,128]{2,1,0:T(8,128)S(1)}, f32[4,64,128]{2,1,0:T(8,128)S(1)}, u32[]{:S(2)}, u32[]{:S(2)}) %collective-permute-start.12) | collective-permute-done | bytes 131104 | tf_op jit(solution)/shard_map/ppermute | solution.py:421
  90.5 6.4 %shard_map.98 = (f32[2,64,64,128]{3,2,1,0:T(8,128)}, f32[4,64,128]{2,1,0:T(8,128)}) custom-call(s32[134]{0:T(256)} %pad_add_fusion.pos_ref, f32[2,64,64,128]{3,2,1,0:T(8,128)} %get-tuple-element.37.refs_0_, f32[2,64,64,128]{3,2,1,0:T(8,128)} %get-tuple-element.38.refs_1_, f32[4,64,128]{2,1,0:T(8,128)} %multiply_add_fusion.3.refs_2_, ...), custom_call_target="tpu_custom_call" | custom-call | tf_op jit(solution)/shard_map/pallas_call | solution.py:290
  97.6 4.5 %collective-permute-done.13 = f32[4,64,128]{2,1,0:T(8,128)S(1)} collective-permute-done((f32[4,64,128]{2,1,0:T(8,128)}, f32[4,64,128]{2,1,0:T(8,128)S(1)}, u32[]{:S(2)}, u32[]{:S(2)}) %collective-permute-start.13) | collective-permute-done | bytes 131104 | tf_op jit(solution)/shard_map/ppermute | solution.py:421
  102.1 0.9 add.91
  103.0 1.9 %collective-permute-start.14 = (f32[4,64,128]{2,1,0:T(8,128)S(1)}, f32[4,64,128]{2,1,0:T(8,128)S(1)}, u32[]{:S(2)}, u32[]{:S(2)}) collective-permute-start(f32[4,64,128]{2,1,0:T(8,128)S(1)} %add.91), channel_id=1, source_target_pairs={{0,16},{8,24},{16,0},{24,8},{1,17},{9,25},{17,1},{25,9},{2,18},{10... | collective-permute-start | bytes 393224 | tf_op jit(solution)/shard_map/ppermute | solution.py:421
  104.9 5.5 %collective-permute-done.14 = f32[4,64,128]{2,1,0:T(8,128)S(1)} collective-permute-done((f32[4,64,128]{2,1,0:T(8,128)S(1)}, f32[4,64,128]{2,1,0:T(8,128)S(1)}, u32[]{:S(2)}, u32[]{:S(2)}) %collective-permute-start.14) | collective-permute-done | bytes 131104 | tf_op jit(solution)/shard_map/ppermute | solution.py:421
  111.0 9.6 %shard_map.99 = (f32[2,64,64,128]{3,2,1,0:T(8,128)}, f32[2,64,64,128]{3,2,1,0:T(8,128)}, f32[2,64,128]{2,1,0:T(8,128)}, f32[4,64,128]{2,1,0:T(8,128)}) custom-call(s32[134]{0:T(256)} %pad_add_fusion.pos_ref, f32[4,64,128]{2,1,0:T(8,128)} %get-tuple-element.52.refs_0_, f32[2,64,64,128]{3,2,1,0:T(8,128)} %get-tuple-element.43.refs_1_, ...), custom_call_target="tpu_custom_call" | custom-call | tf_op jit(solution)/shard_map/pallas_call | solution.py:290
  120.7 1.5 collective-permute-done.15
  122.2 1.0 multiply_add_fusion.2
  123.6 1.3 collective-permute-start.8
  125.0 3.9 %collective-permute-done.16 = f32[4,64,128]{2,1,0:T(8,128)S(1)} collective-permute-done((f32[4,64,128]{2,1,0:T(8,128)S(1)}, f32[4,64,128]{2,1,0:T(8,128)S(1)}, u32[]{:S(2)}, u32[]{:S(2)}) %collective-permute-start.16) | collective-permute-done | bytes 131104 | tf_op jit(solution)/shard_map/ppermute | solution.py:421
  129.0 1.4 collective-permute-start.17
  130.5 1.6 %collective-permute-start.9 = (f32[4,64,128]{2,1,0:T(8,128)S(1)}, f32[4,64,128]{2,1,0:T(8,128)S(1)}, u32[]{:S(2)}, u32[]{:S(2)}) collective-permute-start(f32[4,64,128]{2,1,0:T(8,128)S(1)} %add.83), channel_id=1, source_target_pairs={{0,16},{8,24},{16,0},{24,8},{1,17},{9,25},{17,1},{25,9},{2,18},{10... | collective-permute-start | bytes 393224 | tf_op jit(solution)/shard_map/ppermute | solution.py:421
  132.1 1.9 %collective-permute-done.17 = f32[4,64,128]{2,1,0:T(8,128)S(1)} collective-permute-done((f32[4,64,128]{2,1,0:T(8,128)S(1)}, f32[4,64,128]{2,1,0:T(8,128)S(1)}, u32[]{:S(2)}, u32[]{:S(2)}) %collective-permute-start.17) | collective-permute-done | bytes 131104 | tf_op jit(solution)/shard_map/ppermute | solution.py:421
  134.0 0.9 multiply_add_fusion.refs_2_
  134.9 5.7 %shard_map.100 = f32[4,64,128]{2,1,0:T(8,128)} custom-call(s32[134]{0:T(256)} %pad_add_fusion.pos_ref, f32[2,64,64,128]{3,2,1,0:T(8,128)} %get-tuple-element.46.refs_0_, f32[2,64,64,128]{3,2,1,0:T(8,128)} %get-tuple-element.47.refs_1_, f32[4,64,128]{2,1,0:T(8,128)} %multiply_add_fusion.refs_2_, f32[2,64,128]{2,1,0:T(8,128)} %get-tuple-element.49.refs_3_, ...), custom_call_target="tpu_custom_call" | custom-call | tf_op jit(solution)/shard_map/pallas_call | solution.py:290
  140.6 1.0 reduce_sum.52
  142.5 3.3 %reduce_sum.48 = f32[2,64,64]{2,1,0:T(8,128)S(1)} reduce(f32[2,64,64,128]{3,2,1,0:T(8,128)} %get-tuple-element.45, f32[]{:T(128)} %constant.7.clone.1), dimensions={3}, to_apply=%region_3.4 | reduce | flops 1040384 | bytes 4227076 | tf_op jit(solution)/shard_map/reduce_sum | solution.py:563
  145.8 2.7 %collective-permute-start.19 = (f32[2,128]{1,0:T(2,128)S(1)}, f32[2,128]{1,0:T(2,128)S(1)}, u32[]{:S(2)}, u32[]{:S(2)}) collective-permute-start(f32[2,128]{1,0:T(2,128)S(1)} %add.99), channel_id=1, source_target_pairs={{0,16},{8,24},{16,0},{24,8},{1,17},{9,25},{17,1},{25,9},{2,18},{10... | collective-permute-start | bytes 3080 | tf_op jit(solution)/shard_map/ppermute | solution.py:421
  149.4 1.0 collective-permute-done.19
  (69 shorter events, 14.3 us)
Async XLA Ops:
  7.0 11.0 %copy-start.3 = (s32[256,128]{1,0:T(8,128)S(1)}, s32[256,128]{1,0:T(8,128)}, u32[]{:S(2)}) copy-start(s32[256,128]{1,0:T(8,128)} %param.11) | copy-start | bytes 393220
  7.0 14.6 %copy-start.4 = (s32[1,1,2,2]{3,2,1,0:T(2,128)S(1)}, s32[1,1,2,2]{3,2,1,0:T(2,128)}, u32[]{:S(2)}) copy-start(s32[1,1,2,2]{3,2,1,0:T(2,128)} %param.8) | copy-start | bytes 52
  17.6 1.2 collective-permute-start
  18.8 4.3 %collective-permute-start.1 = (f32[2,128]{1,0:T(2,128)S(1)}, f32[2,128]{1,0:T(2,128)S(1)}, u32[]{:S(2)}, u32[]{:S(2)}) collective-permute-start(f32[2,128]{1,0:T(2,128)S(1)} %mul.88), channel_id=1, source_target_pairs={{0,2},{1,3},{2,0},{3,1},{4,6},{5,7},{6,4},{7,5},{8,10},{9,11},{10,... | collective-permute-start | bytes 3080 | tf_op jit(solution)/shard_map/ppermute | solution.py:421
  23.2 3.7 %collective-permute-start.2 = (f32[2,128]{1,0:T(2,128)S(1)}, f32[2,128]{1,0:T(2,128)S(1)}, u32[]{:S(2)}, u32[]{:S(2)}) collective-permute-start(f32[2,128]{1,0:T(2,128)S(1)} %mul.90), channel_id=1, source_target_pairs={{0,4},{1,5},{2,6},{3,7},{4,0},{5,1},{6,2},{7,3},{8,12},{9,13},{10,... | collective-permute-start | bytes 3080 | tf_op jit(solution)/shard_map/ppermute | solution.py:421
  33.7 5.2 %collective-permute-start.3 = (f32[4,64,128]{2,1,0:T(8,128)}, f32[4,64,128]{2,1,0:T(8,128)S(1)}, u32[]{:S(2)}, u32[]{:S(2)}) collective-permute-start(f32[4,64,128]{2,1,0:T(8,128)} %get-tuple-element.31), channel_id=1, source_target_pairs={{0,8},{8,0},{16,24},{24,16},{1,9},{9,1},{17,25},{25,17},{2,10},{10... | collective-permute-start | bytes 393224 | tf_op jit(solution)/shard_map/ppermute | solution.py:421
  39.9 5.9 %collective-permute-start.4 = (f32[4,64,128]{2,1,0:T(8,128)S(1)}, f32[4,64,128]{2,1,0:T(8,128)S(1)}, u32[]{:S(2)}, u32[]{:S(2)}) collective-permute-start(f32[4,64,128]{2,1,0:T(8,128)S(1)} %add.80), channel_id=1, source_target_pairs={{0,16},{8,24},{16,0},{24,8},{1,17},{9,25},{17,1},{25,9},{2,18},{10... | collective-permute-start | bytes 393224 | tf_op jit(solution)/shard_map/ppermute | solution.py:421
  53.3 1.6 %collective-permute-start.5 = (f32[4,64,128]{2,1,0:T(8,128)}, f32[4,64,128]{2,1,0:T(8,128)S(1)}, u32[]{:S(2)}, u32[]{:S(2)}) collective-permute-start(f32[4,64,128]{2,1,0:T(8,128)} %get-tuple-element.35), channel_id=1, source_target_pairs={{0,1},{1,0},{2,3},{3,2},{4,5},{5,4},{6,7},{7,6},{8,9},{9,8},{10,11... | collective-permute-start | bytes 393224 | tf_op jit(solution)/shard_map/ppermute | solution.py:421
  55.9 6.6 %collective-permute-start.6 = (f32[4,64,128]{2,1,0:T(8,128)S(1)}, f32[4,64,128]{2,1,0:T(8,128)S(1)}, u32[]{:S(2)}, u32[]{:S(2)}) collective-permute-start(f32[4,64,128]{2,1,0:T(8,128)S(1)} %mul.92), channel_id=1, source_target_pairs={{0,2},{1,3},{2,0},{3,1},{4,6},{5,7},{6,4},{7,5},{8,10},{9,11},{10,... | collective-permute-start | bytes 393224 | tf_op jit(solution)/shard_map/ppermute | solution.py:421
  62.5 5.4 %collective-permute-start.7 = (f32[4,64,128]{2,1,0:T(8,128)S(1)}, f32[4,64,128]{2,1,0:T(8,128)S(1)}, u32[]{:S(2)}, u32[]{:S(2)}) collective-permute-start(f32[4,64,128]{2,1,0:T(8,128)S(1)} %mul.94), channel_id=1, source_target_pairs={{0,4},{1,5},{2,6},{3,7},{4,0},{5,1},{6,2},{7,3},{8,12},{9,13},{10,... | collective-permute-start | bytes 393224 | tf_op jit(solution)/shard_map/ppermute | solution.py:421
  68.7 9.5 %copy-start.1 = (f32[4,64,128]{2,1,0:T(8,128)S(1)}, f32[4,64,128]{2,1,0:T(8,128)}, u32[]{:S(2)}) copy-start(f32[4,64,128]{2,1,0:T(8,128)} %get-tuple-element.35) | copy-start | bytes 393220
  76.5 1.6 %collective-permute-start.10 = (f32[4,64,128]{2,1,0:T(8,128)}, f32[4,64,128]{2,1,0:T(8,128)S(1)}, u32[]{:S(2)}, u32[]{:S(2)}) collective-permute-start(f32[4,64,128]{2,1,0:T(8,128)} %get-tuple-element.39), channel_id=1, source_target_pairs={{0,1},{1,0},{2,3},{3,2},{4,5},{5,4},{6,7},{7,6},{8,9},{9,8},{10,11... | collective-permute-start | bytes 393224 | tf_op jit(solution)/shard_map/ppermute | solution.py:421
  79.1 5.6 %collective-permute-start.11 = (f32[4,64,128]{2,1,0:T(8,128)S(1)}, f32[4,64,128]{2,1,0:T(8,128)S(1)}, u32[]{:S(2)}, u32[]{:S(2)}) collective-permute-start(f32[4,64,128]{2,1,0:T(8,128)S(1)} %multiply_add_fusion.5), channel_id=1, source_target_pairs={{0,2},{1,3},{2,0},{3,1},{4,6},{5,7},{6,4},{7,5},{8,10},{9,11},{10,... | collective-permute-start | bytes 393224 | tf_op jit(solution)/shard_map/ppermute | solution.py:421
  84.7 5.0 %collective-permute-start.12 = (f32[4,64,128]{2,1,0:T(8,128)S(1)}, f32[4,64,128]{2,1,0:T(8,128)S(1)}, u32[]{:S(2)}, u32[]{:S(2)}) collective-permute-start(f32[4,64,128]{2,1,0:T(8,128)S(1)} %multiply_add_fusion.4), channel_id=1, source_target_pairs={{0,4},{1,5},{2,6},{3,7},{4,0},{5,1},{6,2},{7,3},{8,12},{9,13},{10,... | collective-permute-start | bytes 393224 | tf_op jit(solution)/shard_map/ppermute | solution.py:421
  96.9 5.2 %collective-permute-start.13 = (f32[4,64,128]{2,1,0:T(8,128)}, f32[4,64,128]{2,1,0:T(8,128)S(1)}, u32[]{:S(2)}, u32[]{:S(2)}) collective-permute-start(f32[4,64,128]{2,1,0:T(8,128)} %get-tuple-element.42), channel_id=1, source_target_pairs={{0,8},{8,0},{16,24},{24,16},{1,9},{9,1},{17,25},{25,17},{2,10},{10... | collective-permute-start | bytes 393224 | tf_op jit(solution)/shard_map/ppermute | solution.py:421
  103.0 7.3 %collective-permute-start.14 = (f32[4,64,128]{2,1,0:T(8,128)S(1)}, f32[4,64,128]{2,1,0:T(8,128)S(1)}, u32[]{:S(2)}, u32[]{:S(2)}) collective-permute-start(f32[4,64,128]{2,1,0:T(8,128)S(1)} %add.91), channel_id=1, source_target_pairs={{0,16},{8,24},{16,0},{24,8},{1,17},{9,25},{17,1},{25,9},{2,18},{10... | collective-permute-start | bytes 393224 | tf_op jit(solution)/shard_map/ppermute | solution.py:421
  111.0 12.3 %copy-start = (f32[256,128]{1,0:T(8,128)S(1)}, f32[256,128]{1,0:T(8,128)}, u32[]{:S(2)}) copy-start(f32[256,128]{1,0:T(8,128)} %param.13) | copy-start | bytes 393220
  111.0 12.6 %copy-start.2 = (f32[4,64,128]{2,1,0:T(8,128)S(1)}, f32[4,64,128]{2,1,0:T(8,128)}, u32[]{:S(2)}) copy-start(f32[4,64,128]{2,1,0:T(8,128)} %get-tuple-element.36) | copy-start | bytes 393220
  120.6 1.6 %collective-permute-start.15 = (f32[4,64,128]{2,1,0:T(8,128)}, f32[4,64,128]{2,1,0:T(8,128)S(1)}, u32[]{:S(2)}, u32[]{:S(2)}) collective-permute-start(f32[4,64,128]{2,1,0:T(8,128)} %get-tuple-element.48), channel_id=1, source_target_pairs={{0,1},{1,0},{2,3},{3,2},{4,5},{5,4},{6,7},{7,6},{8,9},{9,8},{10,11... | collective-permute-start | bytes 393224 | tf_op jit(solution)/shard_map/ppermute | solution.py:421
  123.2 5.6 %collective-permute-start.16 = (f32[4,64,128]{2,1,0:T(8,128)S(1)}, f32[4,64,128]{2,1,0:T(8,128)S(1)}, u32[]{:S(2)}, u32[]{:S(2)}) collective-permute-start(f32[4,64,128]{2,1,0:T(8,128)S(1)} %multiply_add_fusion.2), channel_id=1, source_target_pairs={{0,2},{1,3},{2,0},{3,1},{4,6},{5,7},{6,4},{7,5},{8,10},{9,11},{10,... | collective-permute-start | bytes 393224 | tf_op jit(solution)/shard_map/ppermute | solution.py:421
  123.6 6.9 %collective-permute-start.8 = (f32[4,64,128]{2,1,0:T(8,128)S(1)}, f32[4,64,128]{2,1,0:T(8,128)S(1)}, u32[]{:S(2)}, u32[]{:S(2)}) collective-permute-start(f32[4,64,128]{2,1,0:T(8,128)S(1)} %copy-done.2), channel_id=1, source_target_pairs={{0,8},{8,0},{16,24},{24,16},{1,9},{9,1},{17,25},{25,17},{2,10},{10... | collective-permute-start | bytes 393224 | tf_op jit(solution)/shard_map/ppermute | solution.py:421
  129.0 5.0 %collective-permute-start.17 = (f32[4,64,128]{2,1,0:T(8,128)S(1)}, f32[4,64,128]{2,1,0:T(8,128)S(1)}, u32[]{:S(2)}, u32[]{:S(2)}) collective-permute-start(f32[4,64,128]{2,1,0:T(8,128)S(1)} %multiply_add_fusion.1), channel_id=1, source_target_pairs={{0,4},{1,5},{2,6},{3,7},{4,0},{5,1},{6,2},{7,3},{8,12},{9,13},{10,... | collective-permute-start | bytes 393224 | tf_op jit(solution)/shard_map/ppermute | solution.py:421
  130.5 11.2 %collective-permute-start.9 = (f32[4,64,128]{2,1,0:T(8,128)S(1)}, f32[4,64,128]{2,1,0:T(8,128)S(1)}, u32[]{:S(2)}, u32[]{:S(2)}) collective-permute-start(f32[4,64,128]{2,1,0:T(8,128)S(1)} %add.83), channel_id=1, source_target_pairs={{0,16},{8,24},{16,0},{24,8},{1,17},{9,25},{17,1},{25,9},{2,18},{10... | collective-permute-start | bytes 393224 | tf_op jit(solution)/shard_map/ppermute | solution.py:421
  141.7 4.1 %collective-permute-start.18 = (f32[2,128]{1,0:T(2,128)S(1)}, f32[2,128]{1,0:T(2,128)S(1)}, u32[]{:S(2)}, u32[]{:S(2)}) collective-permute-start(f32[2,128]{1,0:T(2,128)S(1)} %reshape.64), channel_id=1, source_target_pairs={{0,8},{8,0},{16,24},{24,16},{1,9},{9,1},{17,25},{25,17},{2,10},{10... | collective-permute-start | bytes 3080 | tf_op jit(solution)/shard_map/ppermute | solution.py:421
  145.8 4.5 %collective-permute-start.19 = (f32[2,128]{1,0:T(2,128)S(1)}, f32[2,128]{1,0:T(2,128)S(1)}, u32[]{:S(2)}, u32[]{:S(2)}) collective-permute-start(f32[2,128]{1,0:T(2,128)S(1)} %add.99), channel_id=1, source_target_pairs={{0,16},{8,24},{16,0},{24,8},{1,17},{9,25},{17,1},{25,9},{2,18},{10... | collective-permute-start | bytes 3080 | tf_op jit(solution)/shard_map/ppermute | solution.py:421

commit v17 on v13

--- a/solution.py
+++ b/solution.py
@@ -513,7 +513,7 @@
     dense = (slot_total, TILE, TILE, shots)
     ew = jnp.broadcast_to((edge_t * jnp.swapaxes(weight, 1, 2))[..., None], dense)
     sign_dev = (1.0 - 2.0 * syndrome.astype(jnp.float32)).reshape(check_blocks, TILE, shots)
-    sign_slot = jnp.einsum("kc,crs->krs", row_hot, sign_dev, precision=EXACT)
+    sign_slot = pick(row_hot, sign_dev)
     prior_dev = channel_prior.reshape(column_blocks, TILE)
     spread = jnp.broadcast_to(prior_dev[:, :, None], (column_blocks, TILE, shots))
     u = None

time: 152 us -> 156 us (1.026)
  starting transfers between devices: 33.4 us -> 24.5 us
  waiting for transfers between devices: 42.5 us -> 48.1 us
  between operations: 1.47 us -> 6.46 us
  Pallas kernels: 46.2 us -> 48.3 us
    ppermute x20, starting transfers between devices: 33.4 us -> 24.5 us  [_swap(): return lax.ppermute(value, axis, perm)]
    ppermute x20, waiting for transfers between devices: 42.5 us -> 48.1 us  [_swap(): return lax.ppermute(value, axis, perm)]
    pallas_call x7, Pallas kernels: 46.2 us -> 48.3 us  [_call(): pl.pallas_call(kernel, grid_spec=grid_spec, out_shape=[o for kind, o in o...]
  transfers between devices with their start and end apart: 20 -> 20, of which waited for: 17 -> 17; matrix products, arithmetic and copies ran while one was open for 6% -> 6% of each run, Pallas kernels for 3% -> 4%
where the time goes in v17:
time: 156 us
  Pallas kernels  48.3 us (31%)
  waiting for transfers between devices  48.1 us (31%)
  starting transfers between devices  24.5 us (16%)
  other arithmetic  17.3 us (11%)
  local copies, waits for them, and re-layouts  11.1 us (7%)
  between operations  6.46 us (4%)
    pallas_call x7, Pallas kernels, _call(): pl.pallas_call(kernel, grid_spec=grid_spec, out_shape=[o for kind, o in o...  48.3 us
    ppermute x20, waiting for transfers between devices, _swap(): return lax.ppermute(value, axis, perm)  48.1 us
    ppermute x20, starting transfers between devices, _swap(): return lax.ppermute(value, axis, perm)  24.5 us
    reduce_sum x1, other arithmetic, body(): jnp.sum(acc, axis=3)  3.34 us
  transfers between devices with their start and end apart: 20, of which 17 were waited for; matrix products, arithmetic and copies ran while one was open for 6% of the time, Pallas kernels for 4%

profile of v17, /device:TPU:0, one launch (start us, length us, event | category | flops | bytes accessed | tf_op | source)
XLA Modules:
  0.0 155.7 jit_solution(17000566263061409018)
XLA Ops:
  0.6 0.9 squeeze.7
  2.7 1.0 sort.17
  3.8 0.8 reshape_squeeze.9
  4.6 0.9 reshape_squeeze.10
  7.0 2.6 %broadcast_in_dim.102.refs_1_.ew_ref.refs_2_.refs_5_.refs_6_ = f32[2,64,64,128]{3,2,1,0:T(8,128)} broadcast(f32[2,64,64]{2,1,0:T(8,128)S(1)} %multiply_bitcast_fusion), dimensions={0,1,2} | broadcast | bytes 4227072 | tf_op jit(solution)/shard_map/broadcast_in_dim | solution.py:514
  10.4 6.0 %shard_map.94 = (f32[2,64,64,128]{3,2,1,0:T(8,128)}, f32[2,64,64,128]{3,2,1,0:T(8,128)}, f32[2,64,128]{2,1,0:T(8,128)}, f32[4,64,128]{2,1,0:T(8,128)}, f32[2,64,128]{2,1,0:T(8,128)}) custom-call(s32[134]{0:T(256)} %pad_add_fusion.pos_ref, f32[4,64,128]{2,1,0:T(8,128)} %add.97.refs_0_, f32[2,64,64,128]{3,2,1,0:T(8,128)} %broadcast_in_dim.102.refs_1_.ew_ref.refs_2_.refs_5_.refs_6_), custom_call_target="tpu_custom_call" | custom-call | tf_op jit(solution)/shard_map/pallas_call | solution.py:288
  16.4 1.0 slice_reduce_fusion
  23.9 2.5 %collective-permute-start.1 = (f32[2,128]{1,0:T(2,128)S(1)}, f32[2,128]{1,0:T(2,128)S(1)}, u32[]{:S(2)}, u32[]{:S(2)}) collective-permute-start(f32[2,128]{1,0:T(2,128)S(1)} %mul.88), channel_id=1, source_target_pairs={{0,2},{1,3},{2,0},{3,1},{4,6},{5,7},{6,4},{7,5},{8,10},{9,11},{10,... | collective-permute-start | bytes 3080 | tf_op jit(solution)/shard_map/ppermute | solution.py:419
  26.4 1.5 collective-permute-done.1
  28.0 2.1 %collective-permute-start.2 = (f32[2,128]{1,0:T(2,128)S(1)}, f32[2,128]{1,0:T(2,128)S(1)}, u32[]{:S(2)}, u32[]{:S(2)}) collective-permute-start(f32[2,128]{1,0:T(2,128)S(1)} %mul.90), channel_id=1, source_target_pairs={{0,4},{1,5},{2,6},{3,7},{4,0},{5,1},{6,2},{7,3},{8,12},{9,13},{10,... | collective-permute-start | bytes 3080 | tf_op jit(solution)/shard_map/ppermute | solution.py:419
  30.7 0.9 collective-permute-done.2
  32.4 6.1 %shard_map.95 = (f32[2,64,64,128]{3,2,1,0:T(8,128)}, f32[4,64,128]{2,1,0:T(8,128)}) custom-call(s32[134]{0:T(256)} %pad_add_fusion.pos_ref, f32[2,64,64,128]{3,2,1,0:T(8,128)} %get-tuple-element.28.ba_ref.refs_2_, f32[2,64,128]{2,1,0:T(8,128)} %pad_maximum_fusion.sign_ref.refs_2_.refs_3_, f32[2,64,128]{2,1,0:T(8,128)} %get-tuple-element.29.here_ref.refs_4_.refs_5_, ...), custom_call_target="tpu_custom_call" | custom-call | tf_op jit(solution)/shard_map/pallas_call | solution.py:288
  38.5 1.6 %collective-permute-start.3 = (f32[4,64,128]{2,1,0:T(8,128)}, f32[4,64,128]{2,1,0:T(8,128)S(1)}, u32[]{:S(2)}, u32[]{:S(2)}) collective-permute-start(f32[4,64,128]{2,1,0:T(8,128)} %get-tuple-element.31), channel_id=1, source_target_pairs={{0,8},{8,0},{16,24},{24,16},{1,9},{9,1},{17,25},{25,17},{2,10},{10... | collective-permute-start | bytes 393224 | tf_op jit(solution)/shard_map/ppermute | solution.py:419
  40.1 3.6 %collective-permute-done.3 = f32[4,64,128]{2,1,0:T(8,128)S(1)} collective-permute-done((f32[4,64,128]{2,1,0:T(8,128)}, f32[4,64,128]{2,1,0:T(8,128)S(1)}, u32[]{:S(2)}, u32[]{:S(2)}) %collective-permute-start.3) | collective-permute-done | bytes 131104 | tf_op jit(solution)/shard_map/ppermute | solution.py:419
  43.7 0.9 add.104
  44.6 2.7 %collective-permute-start.4 = (f32[4,64,128]{2,1,0:T(8,128)S(1)}, f32[4,64,128]{2,1,0:T(8,128)S(1)}, u32[]{:S(2)}, u32[]{:S(2)}) collective-permute-start(f32[4,64,128]{2,1,0:T(8,128)S(1)} %add.104), channel_id=1, source_target_pairs={{0,16},{8,24},{16,0},{24,8},{1,17},{9,25},{17,1},{25,9},{2,18},{10... | collective-permute-start | bytes 393224 | tf_op jit(solution)/shard_map/ppermute | solution.py:419
  47.3 4.7 %collective-permute-done.4 = f32[4,64,128]{2,1,0:T(8,128)S(1)} collective-permute-done((f32[4,64,128]{2,1,0:T(8,128)S(1)}, f32[4,64,128]{2,1,0:T(8,128)S(1)}, u32[]{:S(2)}, u32[]{:S(2)}) %collective-permute-start.4) | collective-permute-done | bytes 131104 | tf_op jit(solution)/shard_map/ppermute | solution.py:419
  52.7 6.8 %shard_map.96 = (f32[2,64,64,128]{3,2,1,0:T(8,128)}, f32[2,64,64,128]{3,2,1,0:T(8,128)}, f32[2,64,128]{2,1,0:T(8,128)}, f32[4,64,128]{2,1,0:T(8,128)}, f32[2,64,128]{2,1,0:T(8,128)}) custom-call(s32[134]{0:T(256)} %pad_add_fusion.pos_ref, f32[4,64,128]{2,1,0:T(8,128)} %add_add_fusion.1.refs_0_, f32[2,64,64,128]{3,2,1,0:T(8,128)} %get-tuple-element.32.refs_1_, ...), custom_call_target="tpu_custom_call" | custom-call | tf_op jit(solution)/shard_map/pallas_call | solution.py:288
  59.5 1.5 collective-permute-done.5
  61.1 0.9 mul.92
  62.0 1.5 collective-permute-start.6
  63.5 4.1 %collective-permute-done.6 = f32[4,64,128]{2,1,0:T(8,128)S(1)} collective-permute-done((f32[4,64,128]{2,1,0:T(8,128)S(1)}, f32[4,64,128]{2,1,0:T(8,128)S(1)}, u32[]{:S(2)}, u32[]{:S(2)}) %collective-permute-start.6) | collective-permute-done | bytes 131104 | tf_op jit(solution)/shard_map/ppermute | solution.py:419
  67.6 1.7 %collective-permute-start.7 = (f32[4,64,128]{2,1,0:T(8,128)S(1)}, f32[4,64,128]{2,1,0:T(8,128)S(1)}, u32[]{:S(2)}, u32[]{:S(2)}) collective-permute-start(f32[4,64,128]{2,1,0:T(8,128)S(1)} %mul.94), channel_id=1, source_target_pairs={{0,4},{1,5},{2,6},{3,7},{4,0},{5,1},{6,2},{7,3},{8,12},{9,13},{10,... | collective-permute-start | bytes 393224 | tf_op jit(solution)/shard_map/ppermute | solution.py:419
  69.3 3.3 %collective-permute-done.7 = f32[4,64,128]{2,1,0:T(8,128)S(1)} collective-permute-done((f32[4,64,128]{2,1,0:T(8,128)S(1)}, f32[4,64,128]{2,1,0:T(8,128)S(1)}, u32[]{:S(2)}, u32[]{:S(2)}) %collective-permute-start.7) | collective-permute-done | bytes 131104 | tf_op jit(solution)/shard_map/ppermute | solution.py:419
  73.4 7.6 %shard_map.97 = (f32[2,64,64,128]{3,2,1,0:T(8,128)}, f32[2,64,64,128]{3,2,1,0:T(8,128)}, f32[2,64,128]{2,1,0:T(8,128)}, f32[4,64,128]{2,1,0:T(8,128)}, f32[4,64,128]{2,1,0:T(8,128)}) custom-call(s32[134]{0:T(256)} %pad_add_fusion.pos_ref, f32[4,64,128]{2,1,0:T(8,128)} %bitcast.23, f32[2,64,64,128]{3,2,1,0:T(8,128)} %get-tuple-element.33.refs_1_, ...), custom_call_target="tpu_custom_call" | custom-call | tf_op jit(solution)/shard_map/pallas_call | solution.py:288
  81.1 1.5 collective-permute-done.10
  82.6 0.9 multiply_add_fusion.5
  83.6 1.6 collective-permute-start.11
  85.1 4.1 %collective-permute-done.11 = f32[4,64,128]{2,1,0:T(8,128)S(1)} collective-permute-done((f32[4,64,128]{2,1,0:T(8,128)S(1)}, f32[4,64,128]{2,1,0:T(8,128)S(1)}, u32[]{:S(2)}, u32[]{:S(2)}) %collective-permute-start.11) | collective-permute-done | bytes 131104 | tf_op jit(solution)/shard_map/ppermute | solution.py:419
  89.2 1.8 %collective-permute-start.12 = (f32[4,64,128]{2,1,0:T(8,128)S(1)}, f32[4,64,128]{2,1,0:T(8,128)S(1)}, u32[]{:S(2)}, u32[]{:S(2)}) collective-permute-start(f32[4,64,128]{2,1,0:T(8,128)S(1)} %multiply_add_fusion.4), channel_id=1, source_target_pairs={{0,4},{1,5},{2,6},{3,7},{4,0},{5,1},{6,2},{7,3},{8,12},{9,13},{10,... | collective-permute-start | bytes 393224 | tf_op jit(solution)/shard_map/ppermute | solution.py:419
  91.0 3.2 %collective-permute-done.12 = f32[4,64,128]{2,1,0:T(8,128)S(1)} collective-permute-done((f32[4,64,128]{2,1,0:T(8,128)S(1)}, f32[4,64,128]{2,1,0:T(8,128)S(1)}, u32[]{:S(2)}, u32[]{:S(2)}) %collective-permute-start.12) | collective-permute-done | bytes 131104 | tf_op jit(solution)/shard_map/ppermute | solution.py:419
  95.0 6.5 %shard_map.98 = (f32[2,64,64,128]{3,2,1,0:T(8,128)}, f32[4,64,128]{2,1,0:T(8,128)}) custom-call(s32[134]{0:T(256)} %pad_add_fusion.pos_ref, f32[2,64,64,128]{3,2,1,0:T(8,128)} %get-tuple-element.37.refs_0_, f32[2,64,64,128]{3,2,1,0:T(8,128)} %get-tuple-element.38.refs_1_, f32[4,64,128]{2,1,0:T(8,128)} %multiply_add_fusion.3.refs_2_, ...), custom_call_target="tpu_custom_call" | custom-call | tf_op jit(solution)/shard_map/pallas_call | solution.py:288
  101.5 5.1 %collective-permute-done.13 = f32[4,64,128]{2,1,0:T(8,128)S(1)} collective-permute-done((f32[4,64,128]{2,1,0:T(8,128)}, f32[4,64,128]{2,1,0:T(8,128)S(1)}, u32[]{:S(2)}, u32[]{:S(2)}) %collective-permute-start.13) | collective-permute-done | bytes 131104 | tf_op jit(solution)/shard_map/ppermute | solution.py:419
  106.6 0.9 add.115
  107.6 1.7 %collective-permute-start.14 = (f32[4,64,128]{2,1,0:T(8,128)S(1)}, f32[4,64,128]{2,1,0:T(8,128)S(1)}, u32[]{:S(2)}, u32[]{:S(2)}) collective-permute-start(f32[4,64,128]{2,1,0:T(8,128)S(1)} %add.115), channel_id=1, source_target_pairs={{0,16},{8,24},{16,0},{24,8},{1,17},{9,25},{17,1},{25,9},{2,18},{10... | collective-permute-start | bytes 393224 | tf_op jit(solution)/shard_map/ppermute | solution.py:419
  109.3 5.6 %collective-permute-done.14 = f32[4,64,128]{2,1,0:T(8,128)S(1)} collective-permute-done((f32[4,64,128]{2,1,0:T(8,128)S(1)}, f32[4,64,128]{2,1,0:T(8,128)S(1)}, u32[]{:S(2)}, u32[]{:S(2)}) %collective-permute-start.14) | collective-permute-done | bytes 131104 | tf_op jit(solution)/shard_map/ppermute | solution.py:419
  115.6 9.6 %shard_map.99 = (f32[2,64,64,128]{3,2,1,0:T(8,128)}, f32[2,64,64,128]{3,2,1,0:T(8,128)}, f32[2,64,128]{2,1,0:T(8,128)}, f32[4,64,128]{2,1,0:T(8,128)}) custom-call(s32[134]{0:T(256)} %pad_add_fusion.pos_ref, f32[4,64,128]{2,1,0:T(8,128)} %get-tuple-element.52.refs_0_, f32[2,64,64,128]{3,2,1,0:T(8,128)} %get-tuple-element.43.refs_1_, ...), custom_call_target="tpu_custom_call" | custom-call | tf_op jit(solution)/shard_map/pallas_call | solution.py:288
  125.3 1.5 collective-permute-done.15
  126.8 1.0 multiply_add_fusion.2
  129.1 4.3 %collective-permute-done.16 = f32[4,64,128]{2,1,0:T(8,128)S(1)} collective-permute-done((f32[4,64,128]{2,1,0:T(8,128)S(1)}, f32[4,64,128]{2,1,0:T(8,128)S(1)}, u32[]{:S(2)}, u32[]{:S(2)}) %collective-permute-start.16) | collective-permute-done | bytes 131104 | tf_op jit(solution)/shard_map/ppermute | solution.py:419
  134.0 2.5 %collective-permute-start.9 = (f32[4,64,128]{2,1,0:T(8,128)S(1)}, f32[4,64,128]{2,1,0:T(8,128)S(1)}, u32[]{:S(2)}, u32[]{:S(2)}) collective-permute-start(f32[4,64,128]{2,1,0:T(8,128)S(1)} %add.107), channel_id=1, source_target_pairs={{0,16},{8,24},{16,0},{24,8},{1,17},{9,25},{17,1},{25,9},{2,18},{10... | collective-permute-start | bytes 393224 | tf_op jit(solution)/shard_map/ppermute | solution.py:419
  136.5 2.1 %collective-permute-done.17 = f32[4,64,128]{2,1,0:T(8,128)S(1)} collective-permute-done((f32[4,64,128]{2,1,0:T(8,128)S(1)}, f32[4,64,128]{2,1,0:T(8,128)S(1)}, u32[]{:S(2)}, u32[]{:S(2)}) %collective-permute-start.17) | collective-permute-done | bytes 131104 | tf_op jit(solution)/shard_map/ppermute | solution.py:419
  138.6 0.9 multiply_add_fusion.refs_2_
  139.5 5.7 %shard_map.100 = f32[4,64,128]{2,1,0:T(8,128)} custom-call(s32[134]{0:T(256)} %pad_add_fusion.pos_ref, f32[2,64,64,128]{3,2,1,0:T(8,128)} %get-tuple-element.46.refs_0_, f32[2,64,64,128]{3,2,1,0:T(8,128)} %get-tuple-element.47.refs_1_, f32[4,64,128]{2,1,0:T(8,128)} %multiply_add_fusion.refs_2_, f32[2,64,128]{2,1,0:T(8,128)} %get-tuple-element.49.refs_3_, ...), custom_call_target="tpu_custom_call" | custom-call | tf_op jit(solution)/shard_map/pallas_call | solution.py:288
  145.2 1.0 reduce_sum.52
  147.2 3.3 %reduce_sum.48 = f32[2,64,64]{2,1,0:T(8,128)S(1)} reduce(f32[2,64,64,128]{3,2,1,0:T(8,128)} %get-tuple-element.45, f32[]{:T(128)} %constant.17.clone.1), dimensions={3}, to_apply=%region_3.4 | reduce | flops 1040384 | bytes 4227076 | tf_op jit(solution)/shard_map/reduce_sum | solution.py:561
  150.6 2.8 %collective-permute-start.19 = (f32[2,128]{1,0:T(2,128)S(1)}, f32[2,128]{1,0:T(2,128)S(1)}, u32[]{:S(2)}, u32[]{:S(2)}) collective-permute-start(f32[2,128]{1,0:T(2,128)S(1)} %add.123), channel_id=1, source_target_pairs={{0,16},{8,24},{16,0},{24,8},{1,17},{9,25},{17,1},{25,9},{2,18},{10... | collective-permute-start | bytes 3080 | tf_op jit(solution)/shard_map/ppermute | solution.py:419
  154.3 0.9 collective-permute-done.19
  (71 shorter events, 13.5 us)
Async XLA Ops:
  7.0 11.0 %copy-start.4 = (s32[1,1,2,2]{3,2,1,0:T(2,128)S(1)}, s32[1,1,2,2]{3,2,1,0:T(2,128)}, u32[]{:S(2)}) copy-start(s32[1,1,2,2]{3,2,1,0:T(2,128)} %param.8) | copy-start | bytes 52
  7.0 11.1 %copy-start.3 = (s32[256,128]{1,0:T(8,128)S(1)}, s32[256,128]{1,0:T(8,128)}, u32[]{:S(2)}) copy-start(s32[256,128]{1,0:T(8,128)} %param.11) | copy-start | bytes 393220
  17.5 6.4 %collective-permute-start = (f32[2,128]{1,0:T(2,128)S(1)}, f32[2,128]{1,0:T(2,128)S(1)}, u32[]{:S(2)}, u32[]{:S(2)}) collective-permute-start(f32[2,128]{1,0:T(2,128)S(1)} %reshape_squeeze.11), channel_id=1, source_target_pairs={{0,1},{1,0},{2,3},{3,2},{4,5},{5,4},{6,7},{7,6},{8,9},{9,8},{10,11... | collective-permute-start | bytes 3080 | tf_op jit(solution)/shard_map/ppermute | solution.py:419
  23.9 4.1 %collective-permute-start.1 = (f32[2,128]{1,0:T(2,128)S(1)}, f32[2,128]{1,0:T(2,128)S(1)}, u32[]{:S(2)}, u32[]{:S(2)}) collective-permute-start(f32[2,128]{1,0:T(2,128)S(1)} %mul.88), channel_id=1, source_target_pairs={{0,2},{1,3},{2,0},{3,1},{4,6},{5,7},{6,4},{7,5},{8,10},{9,11},{10,... | collective-permute-start | bytes 3080 | tf_op jit(solution)/shard_map/ppermute | solution.py:419
  28.0 3.6 %collective-permute-start.2 = (f32[2,128]{1,0:T(2,128)S(1)}, f32[2,128]{1,0:T(2,128)S(1)}, u32[]{:S(2)}, u32[]{:S(2)}) collective-permute-start(f32[2,128]{1,0:T(2,128)S(1)} %mul.90), channel_id=1, source_target_pairs={{0,4},{1,5},{2,6},{3,7},{4,0},{5,1},{6,2},{7,3},{8,12},{9,13},{10,... | collective-permute-start | bytes 3080 | tf_op jit(solution)/shard_map/ppermute | solution.py:419
  38.5 5.2 %collective-permute-start.3 = (f32[4,64,128]{2,1,0:T(8,128)}, f32[4,64,128]{2,1,0:T(8,128)S(1)}, u32[]{:S(2)}, u32[]{:S(2)}) collective-permute-start(f32[4,64,128]{2,1,0:T(8,128)} %get-tuple-element.31), channel_id=1, source_target_pairs={{0,8},{8,0},{16,24},{24,16},{1,9},{9,1},{17,25},{25,17},{2,10},{10... | collective-permute-start | bytes 393224 | tf_op jit(solution)/shard_map/ppermute | solution.py:419
  44.6 7.3 %collective-permute-start.4 = (f32[4,64,128]{2,1,0:T(8,128)S(1)}, f32[4,64,128]{2,1,0:T(8,128)S(1)}, u32[]{:S(2)}, u32[]{:S(2)}) collective-permute-start(f32[4,64,128]{2,1,0:T(8,128)S(1)} %add.104), channel_id=1, source_target_pairs={{0,16},{8,24},{16,0},{24,8},{1,17},{9,25},{17,1},{25,9},{2,18},{10... | collective-permute-start | bytes 393224 | tf_op jit(solution)/shard_map/ppermute | solution.py:419
  59.5 1.6 %collective-permute-start.5 = (f32[4,64,128]{2,1,0:T(8,128)}, f32[4,64,128]{2,1,0:T(8,128)S(1)}, u32[]{:S(2)}, u32[]{:S(2)}) collective-permute-start(f32[4,64,128]{2,1,0:T(8,128)} %get-tuple-element.35), channel_id=1, source_target_pairs={{0,1},{1,0},{2,3},{3,2},{4,5},{5,4},{6,7},{7,6},{8,9},{9,8},{10,11... | collective-permute-start | bytes 393224 | tf_op jit(solution)/shard_map/ppermute | solution.py:419
  62.0 5.6 %collective-permute-start.6 = (f32[4,64,128]{2,1,0:T(8,128)S(1)}, f32[4,64,128]{2,1,0:T(8,128)S(1)}, u32[]{:S(2)}, u32[]{:S(2)}) collective-permute-start(f32[4,64,128]{2,1,0:T(8,128)S(1)} %mul.92), channel_id=1, source_target_pairs={{0,2},{1,3},{2,0},{3,1},{4,6},{5,7},{6,4},{7,5},{8,10},{9,11},{10,... | collective-permute-start | bytes 393224 | tf_op jit(solution)/shard_map/ppermute | solution.py:419
  67.6 5.0 %collective-permute-start.7 = (f32[4,64,128]{2,1,0:T(8,128)S(1)}, f32[4,64,128]{2,1,0:T(8,128)S(1)}, u32[]{:S(2)}, u32[]{:S(2)}) collective-permute-start(f32[4,64,128]{2,1,0:T(8,128)S(1)} %mul.94), channel_id=1, source_target_pairs={{0,4},{1,5},{2,6},{3,7},{4,0},{5,1},{6,2},{7,3},{8,12},{9,13},{10,... | collective-permute-start | bytes 393224 | tf_op jit(solution)/shard_map/ppermute | solution.py:419
  73.4 9.3 %copy-start.1 = (f32[4,64,128]{2,1,0:T(8,128)S(1)}, f32[4,64,128]{2,1,0:T(8,128)}, u32[]{:S(2)}) copy-start(f32[4,64,128]{2,1,0:T(8,128)} %get-tuple-element.35) | copy-start | bytes 393220
  81.0 1.6 %collective-permute-start.10 = (f32[4,64,128]{2,1,0:T(8,128)}, f32[4,64,128]{2,1,0:T(8,128)S(1)}, u32[]{:S(2)}, u32[]{:S(2)}) collective-permute-start(f32[4,64,128]{2,1,0:T(8,128)} %get-tuple-element.39), channel_id=1, source_target_pairs={{0,1},{1,0},{2,3},{3,2},{4,5},{5,4},{6,7},{7,6},{8,9},{9,8},{10,11... | collective-permute-start | bytes 393224 | tf_op jit(solution)/shard_map/ppermute | solution.py:419
  83.6 5.6 %collective-permute-start.11 = (f32[4,64,128]{2,1,0:T(8,128)S(1)}, f32[4,64,128]{2,1,0:T(8,128)S(1)}, u32[]{:S(2)}, u32[]{:S(2)}) collective-permute-start(f32[4,64,128]{2,1,0:T(8,128)S(1)} %multiply_add_fusion.5), channel_id=1, source_target_pairs={{0,2},{1,3},{2,0},{3,1},{4,6},{5,7},{6,4},{7,5},{8,10},{9,11},{10,... | collective-permute-start | bytes 393224 | tf_op jit(solution)/shard_map/ppermute | solution.py:419
  89.2 5.0 %collective-permute-start.12 = (f32[4,64,128]{2,1,0:T(8,128)S(1)}, f32[4,64,128]{2,1,0:T(8,128)S(1)}, u32[]{:S(2)}, u32[]{:S(2)}) collective-permute-start(f32[4,64,128]{2,1,0:T(8,128)S(1)} %multiply_add_fusion.4), channel_id=1, source_target_pairs={{0,4},{1,5},{2,6},{3,7},{4,0},{5,1},{6,2},{7,3},{8,12},{9,13},{10,... | collective-permute-start | bytes 393224 | tf_op jit(solution)/shard_map/ppermute | solution.py:419
  101.5 5.2 %collective-permute-start.13 = (f32[4,64,128]{2,1,0:T(8,128)}, f32[4,64,128]{2,1,0:T(8,128)S(1)}, u32[]{:S(2)}, u32[]{:S(2)}) collective-permute-start(f32[4,64,128]{2,1,0:T(8,128)} %get-tuple-element.42), channel_id=1, source_target_pairs={{0,8},{8,0},{16,24},{24,16},{1,9},{9,1},{17,25},{25,17},{2,10},{10... | collective-permute-start | bytes 393224 | tf_op jit(solution)/shard_map/ppermute | solution.py:419
  107.6 7.3 %collective-permute-start.14 = (f32[4,64,128]{2,1,0:T(8,128)S(1)}, f32[4,64,128]{2,1,0:T(8,128)S(1)}, u32[]{:S(2)}, u32[]{:S(2)}) collective-permute-start(f32[4,64,128]{2,1,0:T(8,128)S(1)} %add.115), channel_id=1, source_target_pairs={{0,16},{8,24},{16,0},{24,8},{1,17},{9,25},{17,1},{25,9},{2,18},{10... | collective-permute-start | bytes 393224 | tf_op jit(solution)/shard_map/ppermute | solution.py:419
  115.6 12.9 %copy-start = (f32[256,128]{1,0:T(8,128)S(1)}, f32[256,128]{1,0:T(8,128)}, u32[]{:S(2)}) copy-start(f32[256,128]{1,0:T(8,128)} %param.13) | copy-start | bytes 393220
  115.6 13.2 %copy-start.2 = (f32[4,64,128]{2,1,0:T(8,128)S(1)}, f32[4,64,128]{2,1,0:T(8,128)}, u32[]{:S(2)}) copy-start(f32[4,64,128]{2,1,0:T(8,128)} %get-tuple-element.36) | copy-start | bytes 393220
  125.2 1.6 %collective-permute-start.15 = (f32[4,64,128]{2,1,0:T(8,128)}, f32[4,64,128]{2,1,0:T(8,128)S(1)}, u32[]{:S(2)}, u32[]{:S(2)}) collective-permute-start(f32[4,64,128]{2,1,0:T(8,128)} %get-tuple-element.48), channel_id=1, source_target_pairs={{0,1},{1,0},{2,3},{3,2},{4,5},{5,4},{6,7},{7,6},{8,9},{9,8},{10,11... | collective-permute-start | bytes 393224 | tf_op jit(solution)/shard_map/ppermute | solution.py:419
  127.8 5.6 %collective-permute-start.16 = (f32[4,64,128]{2,1,0:T(8,128)S(1)}, f32[4,64,128]{2,1,0:T(8,128)S(1)}, u32[]{:S(2)}, u32[]{:S(2)}) collective-permute-start(f32[4,64,128]{2,1,0:T(8,128)S(1)} %multiply_add_fusion.2), channel_id=1, source_target_pairs={{0,2},{1,3},{2,0},{3,1},{4,6},{5,7},{6,4},{7,5},{8,10},{9,11},{10,... | collective-permute-start | bytes 393224 | tf_op jit(solution)/shard_map/ppermute | solution.py:419
  128.7 5.3 %collective-permute-start.8 = (f32[4,64,128]{2,1,0:T(8,128)S(1)}, f32[4,64,128]{2,1,0:T(8,128)S(1)}, u32[]{:S(2)}, u32[]{:S(2)}) collective-permute-start(f32[4,64,128]{2,1,0:T(8,128)S(1)} %copy-done.2), channel_id=1, source_target_pairs={{0,8},{8,0},{16,24},{24,16},{1,9},{9,1},{17,25},{25,17},{2,10},{10... | collective-permute-start | bytes 393224 | tf_op jit(solution)/shard_map/ppermute | solution.py:419
  133.6 5.0 %collective-permute-start.17 = (f32[4,64,128]{2,1,0:T(8,128)S(1)}, f32[4,64,128]{2,1,0:T(8,128)S(1)}, u32[]{:S(2)}, u32[]{:S(2)}) collective-permute-start(f32[4,64,128]{2,1,0:T(8,128)S(1)} %multiply_add_fusion.1), channel_id=1, source_target_pairs={{0,4},{1,5},{2,6},{3,7},{4,0},{5,1},{6,2},{7,3},{8,12},{9,13},{10,... | collective-permute-start | bytes 393224 | tf_op jit(solution)/shard_map/ppermute | solution.py:419
  134.0 12.4 %collective-permute-start.9 = (f32[4,64,128]{2,1,0:T(8,128)S(1)}, f32[4,64,128]{2,1,0:T(8,128)S(1)}, u32[]{:S(2)}, u32[]{:S(2)}) collective-permute-start(f32[4,64,128]{2,1,0:T(8,128)S(1)} %add.107), channel_id=1, source_target_pairs={{0,16},{8,24},{16,0},{24,8},{1,17},{9,25},{17,1},{25,9},{2,18},{10... | collective-permute-start | bytes 393224 | tf_op jit(solution)/shard_map/ppermute | solution.py:419
  146.3 4.2 %collective-permute-start.18 = (f32[2,128]{1,0:T(2,128)S(1)}, f32[2,128]{1,0:T(2,128)S(1)}, u32[]{:S(2)}, u32[]{:S(2)}) collective-permute-start(f32[2,128]{1,0:T(2,128)S(1)} %reshape.85), channel_id=1, source_target_pairs={{0,8},{8,0},{16,24},{24,16},{1,9},{9,1},{17,25},{25,17},{2,10},{10... | collective-permute-start | bytes 3080 | tf_op jit(solution)/shard_map/ppermute | solution.py:419
  150.6 4.5 %collective-permute-start.19 = (f32[2,128]{1,0:T(2,128)S(1)}, f32[2,128]{1,0:T(2,128)S(1)}, u32[]{:S(2)}, u32[]{:S(2)}) collective-permute-start(f32[2,128]{1,0:T(2,128)S(1)} %add.123), channel_id=1, source_target_pairs={{0,16},{8,24},{16,0},{24,8},{1,17},{9,25},{17,1},{25,9},{2,18},{10... | collective-permute-start | bytes 3080 | tf_op jit(solution)/shard_map/ppermute | solution.py:419

commit v18 on v13

--- a/solution.py
+++ b/solution.py
@@ -134,7 +134,9 @@
             here_ref[j] = value
 
 
-def _fwd_messages_kernel(slots, pos_ref, ba_ref, sign_ref, here_ref, others_ref, ew_ref, u_ref, col_ref):
+def _fwd_messages_kernel(
+    slots, pos_ref, ba_ref, sign_ref, here_ref, others_ref, ew_ref, u_ref, col_ref, cs_scr
+):
     k = pl.program_id(0)
     n_c = ba_ref.shape[1]
     count, base = _columns(pos_ref, k, slots, n_c)
@@ -151,10 +153,12 @@
         x = ba_ref[0, c] * f
         u = ew_ref[0, c] * jnp.log((1.0 + DAMP * x) / (1.0 - DAMP * x))
         u_ref[0, c] = u
-        col_ref[q, pl.ds(c, 1), :] = col_ref[q, pl.ds(c, 1), :] + jnp.sum(u, axis=0, keepdims=True)
+        cs_scr[pl.ds(c, 1), :] = jnp.sum(u, axis=0, keepdims=True)
         return carry
 
+    cs_scr[...] = jnp.zeros(cs_scr.shape, F32)
     _loop(count, body, 0)
+    col_ref[q] = col_ref[q] + cs_scr[...]
 
 
 def _bwd_messages_kernel(has_next, has_acc, emit_column, slots, pos_ref, *refs):
@@ -166,6 +170,7 @@
     acc_ref = refs.pop(0) if has_acc else None
     gw_ref, gba_ref, ghere_ref, gothers_ref = refs[:4]
     col_ref = refs[4] if emit_column else None
+    cs_scr = refs[5] if emit_column else None
     k = pl.program_id(0)
     n_c = ba_ref.shape[1]
     shape = ba_ref.shape[2:]
@@ -196,7 +201,7 @@
         ratio = jnp.log(high / low)
         if emit_column:
             u = ew_ref[0, c] * ratio
-            col_ref[q, pl.ds(c, 1), :] = col_ref[q, pl.ds(c, 1), :] + jnp.sum(u, axis=0, keepdims=True)
+            cs_scr[pl.ds(c, 1), :] = jnp.sum(u, axis=0, keepdims=True)
         gw = gu * ratio
         if has_acc:
             gw = gw + acc_ref[0, c]
@@ -205,7 +210,11 @@
         gba_ref[0, c] = gx * f
         return total + gx * ba
 
+    if emit_column:
+        cs_scr[...] = jnp.zeros(cs_scr.shape, F32)
     grad_factor = _loop(count, body, jnp.zeros(shape, F32))
+    if emit_column:
+        col_ref[q] = col_ref[q] + cs_scr[...]
     ghere_ref[k] = grad_factor * sign * others
     gothers_ref[p] = gothers_ref[p] + grad_factor * sign * here
 
@@ -215,7 +224,7 @@
     h_ref, gba_ref, grows_ref, ghere_ref, whole_ref, here_ref = refs[:6]
     refs = refs[6:]
     gm_ref = refs.pop(0) if emit_gm else None
-    col_ref, p_scr, q_scr = refs
+    col_ref, p_scr, q_scr, cs_scr = refs
     k = pl.program_id(0)
     n_c = h_ref.shape[1]
     shape = h_ref.shape[2:]
@@ -260,10 +269,12 @@
         gm = gh * (0.5 * (1.0 - h * h))
         if emit_gm:
             gm_ref[0, c] = gm
-        col_ref[q, pl.ds(c, 1), :] = col_ref[q, pl.ds(c, 1), :] + jnp.sum(gm, axis=0, keepdims=True)
+        cs_scr[pl.ds(c, 1), :] = jnp.sum(gm, axis=0, keepdims=True)
         return (prod * h, grad * h + gba_ref[0, c] * prod)
 
+    cs_scr[...] = jnp.zeros(cs_scr.shape, F32)
     _loop(count, backward, (ones, zeros))
+    col_ref[q] = col_ref[q] + cs_scr[...]
 
 
 def _spec(kind, shape):
@@ -319,7 +330,7 @@
         ("dense", jax.ShapeDtypeStruct(ba.shape, F32)),
         ("full", jax.ShapeDtypeStruct((col_blocks, c, s), F32)),
     ]
-    return _call(functools.partial(_fwd_messages_kernel, k), pos, inputs, outs)
+    return _call(functools.partial(_fwd_messages_kernel, k), pos, inputs, outs, [_vmem((c, s))])
 
 
 def bwd_messages(pos, gsp, gm, ba, sign, here, others, ew, acc, col_blocks=0):
@@ -341,7 +352,11 @@
     if col_blocks:
         outs.append(("full", jax.ShapeDtypeStruct((col_blocks, c, s), F32)))
     return _call(
-        functools.partial(_bwd_messages_kernel, has_next, has_acc, col_blocks > 0, k), pos, inputs, outs
+        functools.partial(_bwd_messages_kernel, has_next, has_acc, col_blocks > 0, k),
+        pos,
+        inputs,
+        outs,
+        [_vmem((c, s))] if col_blocks else [],
     )
 
 
@@ -363,7 +378,7 @@
         pos,
         inputs,
         outs,
-        [_vmem((c, r, s)) for _ in range(2)],
+        [_vmem((c, r, s)) for _ in range(2)] + [_vmem((c, s))],
     )
     if emit_gm:
         return results[0], results[1]

time: 152 us -> 152 us (level)
  starting transfers between devices: 33.4 us -> 31.6 us
    ppermute x20, starting transfers between devices: 33.4 us -> 31.6 us  [_swap(): return lax.ppermute(value, axis, perm)]
where the time goes in v18:
time: 152 us; the launch traced here: 151 us
  Pallas kernels  47.1 us (31%)
  waiting for transfers between devices  43.1 us (28%)
  starting transfers between devices  31.6 us (21%)
  other arithmetic  16.5 us (11%)
  local copies, waits for them, and re-layouts  11.1 us (7%)
    pallas_call x7, Pallas kernels, _call(): pl.pallas_call(kernel, grid_spec=grid_spec, out_shape=[o for kind, o in o...  47.1 us
    ppermute x20, waiting for transfers between devices, _swap(): return lax.ppermute(value, axis, perm)  43.1 us
    ppermute x20, starting transfers between devices, _swap(): return lax.ppermute(value, axis, perm)  31.6 us
    reduce_sum x1, other arithmetic, body(): jnp.sum(acc, axis=3)  3.34 us
  transfers between devices with their start and end apart: 20, of which 17 were waited for; matrix products, arithmetic and copies ran while one was open for 6% of the time, Pallas kernels for 3%

profile of v18, /device:TPU:0, one launch (start us, length us, event | category | flops | bytes accessed | tf_op | source)
XLA Modules:
  0.0 151.1 jit_solution(11912434653333606093)
XLA Ops:
  0.6 0.9 squeeze.10
  2.7 1.0 sort.17
  7.0 2.6 %broadcast_in_dim.91.refs_1_.ew_ref.refs_2_.refs_5_.refs_6_ = f32[2,64,64,128]{3,2,1,0:T(8,128)} broadcast(f32[2,64,64]{2,1,0:T(8,128)S(1)} %multiply_bitcast_fusion), dimensions={0,1,2} | broadcast | bytes 4227072 | tf_op jit(solution)/shard_map/broadcast_in_dim | solution.py:529
  10.4 6.2 %shard_map.94 = (f32[2,64,64,128]{3,2,1,0:T(8,128)}, f32[2,64,64,128]{3,2,1,0:T(8,128)}, f32[2,64,128]{2,1,0:T(8,128)}, f32[4,64,128]{2,1,0:T(8,128)}, f32[2,64,128]{2,1,0:T(8,128)}) custom-call(s32[134]{0:T(256)} %pad_add_fusion.pos_ref, f32[4,64,128]{2,1,0:T(8,128)} %add.79.refs_0_, f32[2,64,64,128]{3,2,1,0:T(8,128)} %broadcast_in_dim.91.refs_1_.ew_ref.refs_2_.refs_5_.refs_6_), custom_call_target="tpu_custom_call" | custom-call | tf_op jit(solution)/shard_map/pallas_call | solution.py:299
  16.5 1.0 slice_reduce_fusion
  17.9 0.9 collective-permute-done
  18.8 2.8 %collective-permute-start.1 = (f32[2,128]{1,0:T(2,128)S(1)}, f32[2,128]{1,0:T(2,128)S(1)}, u32[]{:S(2)}, u32[]{:S(2)}) collective-permute-start(f32[2,128]{1,0:T(2,128)S(1)} %mul.88), channel_id=1, source_target_pairs={{0,2},{1,3},{2,0},{3,1},{4,6},{5,7},{6,4},{7,5},{8,10},{9,11},{10,... | collective-permute-start | bytes 3080 | tf_op jit(solution)/shard_map/ppermute | solution.py:434
  21.7 1.4 collective-permute-done.1
  23.1 2.1 %collective-permute-start.2 = (f32[2,128]{1,0:T(2,128)S(1)}, f32[2,128]{1,0:T(2,128)S(1)}, u32[]{:S(2)}, u32[]{:S(2)}) collective-permute-start(f32[2,128]{1,0:T(2,128)S(1)} %mul.90), channel_id=1, source_target_pairs={{0,4},{1,5},{2,6},{3,7},{4,0},{5,1},{6,2},{7,3},{8,12},{9,13},{10,... | collective-permute-start | bytes 3080 | tf_op jit(solution)/shard_map/ppermute | solution.py:434
  27.6 5.6 %shard_map.95 = (f32[2,64,64,128]{3,2,1,0:T(8,128)}, f32[4,64,128]{2,1,0:T(8,128)}) custom-call(s32[134]{0:T(256)} %pad_add_fusion.pos_ref, f32[2,64,64,128]{3,2,1,0:T(8,128)} %get-tuple-element.28.ba_ref.refs_2_, f32[2,64,128]{2,1,0:T(8,128)} %copy.30.sign_ref.refs_2_.refs_3_, f32[2,64,128]{2,1,0:T(8,128)} %get-tuple-element.29.here_ref.refs_4_.refs_5_, ...), custom_call_target="tpu_custom_call" | custom-call | tf_op jit(solution)/shard_map/pallas_call | solution.py:299
  33.2 2.0 %collective-permute-start.3 = (f32[4,64,128]{2,1,0:T(8,128)}, f32[4,64,128]{2,1,0:T(8,128)S(1)}, u32[]{:S(2)}, u32[]{:S(2)}) collective-permute-start(f32[4,64,128]{2,1,0:T(8,128)} %get-tuple-element.31), channel_id=1, source_target_pairs={{0,8},{8,0},{16,24},{24,16},{1,9},{9,1},{17,25},{25,17},{2,10},{10... | collective-permute-start | bytes 393224 | tf_op jit(solution)/shard_map/ppermute | solution.py:434
  35.2 3.2 %collective-permute-done.3 = f32[4,64,128]{2,1,0:T(8,128)S(1)} collective-permute-done((f32[4,64,128]{2,1,0:T(8,128)}, f32[4,64,128]{2,1,0:T(8,128)S(1)}, u32[]{:S(2)}, u32[]{:S(2)}) %collective-permute-start.3) | collective-permute-done | bytes 131104 | tf_op jit(solution)/shard_map/ppermute | solution.py:434
  38.4 0.9 add.80
  39.3 3.1 %collective-permute-start.4 = (f32[4,64,128]{2,1,0:T(8,128)S(1)}, f32[4,64,128]{2,1,0:T(8,128)S(1)}, u32[]{:S(2)}, u32[]{:S(2)}) collective-permute-start(f32[4,64,128]{2,1,0:T(8,128)S(1)} %add.80), channel_id=1, source_target_pairs={{0,16},{8,24},{16,0},{24,8},{1,17},{9,25},{17,1},{25,9},{2,18},{10... | collective-permute-start | bytes 393224 | tf_op jit(solution)/shard_map/ppermute | solution.py:434
  42.4 3.0 %collective-permute-done.4 = f32[4,64,128]{2,1,0:T(8,128)S(1)} collective-permute-done((f32[4,64,128]{2,1,0:T(8,128)S(1)}, f32[4,64,128]{2,1,0:T(8,128)S(1)}, u32[]{:S(2)}, u32[]{:S(2)}) %collective-permute-start.4) | collective-permute-done | bytes 131104 | tf_op jit(solution)/shard_map/ppermute | solution.py:434
  46.1 6.8 %shard_map.96 = (f32[2,64,64,128]{3,2,1,0:T(8,128)}, f32[2,64,64,128]{3,2,1,0:T(8,128)}, f32[2,64,128]{2,1,0:T(8,128)}, f32[4,64,128]{2,1,0:T(8,128)}, f32[2,64,128]{2,1,0:T(8,128)}) custom-call(s32[134]{0:T(256)} %pad_add_fusion.pos_ref, f32[4,64,128]{2,1,0:T(8,128)} %add_add_fusion.1.refs_0_, f32[2,64,64,128]{3,2,1,0:T(8,128)} %get-tuple-element.32.refs_1_, ...), custom_call_target="tpu_custom_call" | custom-call | tf_op jit(solution)/shard_map/pallas_call | solution.py:299
  53.0 1.5 %collective-permute-done.5 = f32[4,64,128]{2,1,0:T(8,128)S(1)} collective-permute-done((f32[4,64,128]{2,1,0:T(8,128)}, f32[4,64,128]{2,1,0:T(8,128)S(1)}, u32[]{:S(2)}, u32[]{:S(2)}) %collective-permute-start.5) | collective-permute-done | bytes 131104 | tf_op jit(solution)/shard_map/ppermute | solution.py:434
  54.6 0.9 mul.92
  55.5 3.1 %collective-permute-start.6 = (f32[4,64,128]{2,1,0:T(8,128)S(1)}, f32[4,64,128]{2,1,0:T(8,128)S(1)}, u32[]{:S(2)}, u32[]{:S(2)}) collective-permute-start(f32[4,64,128]{2,1,0:T(8,128)S(1)} %mul.92), channel_id=1, source_target_pairs={{0,2},{1,3},{2,0},{3,1},{4,6},{5,7},{6,4},{7,5},{8,10},{9,11},{10,... | collective-permute-start | bytes 393224 | tf_op jit(solution)/shard_map/ppermute | solution.py:434
  58.6 3.8 %collective-permute-done.6 = f32[4,64,128]{2,1,0:T(8,128)S(1)} collective-permute-done((f32[4,64,128]{2,1,0:T(8,128)S(1)}, f32[4,64,128]{2,1,0:T(8,128)S(1)}, u32[]{:S(2)}, u32[]{:S(2)}) %collective-permute-start.6) | collective-permute-done | bytes 131104 | tf_op jit(solution)/shard_map/ppermute | solution.py:434
  62.4 2.1 %collective-permute-start.7 = (f32[4,64,128]{2,1,0:T(8,128)S(1)}, f32[4,64,128]{2,1,0:T(8,128)S(1)}, u32[]{:S(2)}, u32[]{:S(2)}) collective-permute-start(f32[4,64,128]{2,1,0:T(8,128)S(1)} %mul.94), channel_id=1, source_target_pairs={{0,4},{1,5},{2,6},{3,7},{4,0},{5,1},{6,2},{7,3},{8,12},{9,13},{10,... | collective-permute-start | bytes 393224 | tf_op jit(solution)/shard_map/ppermute | solution.py:434
  64.6 3.1 %collective-permute-done.7 = f32[4,64,128]{2,1,0:T(8,128)S(1)} collective-permute-done((f32[4,64,128]{2,1,0:T(8,128)S(1)}, f32[4,64,128]{2,1,0:T(8,128)S(1)}, u32[]{:S(2)}, u32[]{:S(2)}) %collective-permute-start.7) | collective-permute-done | bytes 131104 | tf_op jit(solution)/shard_map/ppermute | solution.py:434
  68.4 7.9 %shard_map.97 = (f32[2,64,64,128]{3,2,1,0:T(8,128)}, f32[2,64,64,128]{3,2,1,0:T(8,128)}, f32[2,64,128]{2,1,0:T(8,128)}, f32[4,64,128]{2,1,0:T(8,128)}, f32[4,64,128]{2,1,0:T(8,128)}) custom-call(s32[134]{0:T(256)} %pad_add_fusion.pos_ref, f32[4,64,128]{2,1,0:T(8,128)} %bitcast.15, f32[2,64,64,128]{3,2,1,0:T(8,128)} %get-tuple-element.33.refs_1_, ...), custom_call_target="tpu_custom_call" | custom-call | tf_op jit(solution)/shard_map/pallas_call | solution.py:299
  76.4 1.5 %collective-permute-done.10 = f32[4,64,128]{2,1,0:T(8,128)S(1)} collective-permute-done((f32[4,64,128]{2,1,0:T(8,128)}, f32[4,64,128]{2,1,0:T(8,128)S(1)}, u32[]{:S(2)}, u32[]{:S(2)}) %collective-permute-start.10) | collective-permute-done | bytes 131104 | tf_op jit(solution)/shard_map/ppermute | solution.py:434
  77.9 0.9 multiply_add_fusion.5
  78.9 1.4 collective-permute-start.11
  80.2 4.3 %collective-permute-done.11 = f32[4,64,128]{2,1,0:T(8,128)S(1)} collective-permute-done((f32[4,64,128]{2,1,0:T(8,128)S(1)}, f32[4,64,128]{2,1,0:T(8,128)S(1)}, u32[]{:S(2)}, u32[]{:S(2)}) %collective-permute-start.11) | collective-permute-done | bytes 131104 | tf_op jit(solution)/shard_map/ppermute | solution.py:434
  84.5 1.9 %collective-permute-start.12 = (f32[4,64,128]{2,1,0:T(8,128)S(1)}, f32[4,64,128]{2,1,0:T(8,128)S(1)}, u32[]{:S(2)}, u32[]{:S(2)}) collective-permute-start(f32[4,64,128]{2,1,0:T(8,128)S(1)} %multiply_add_fusion.4), channel_id=1, source_target_pairs={{0,4},{1,5},{2,6},{3,7},{4,0},{5,1},{6,2},{7,3},{8,12},{9,13},{10,... | collective-permute-start | bytes 393224 | tf_op jit(solution)/shard_map/ppermute | solution.py:434
  86.4 3.2 %collective-permute-done.12 = f32[4,64,128]{2,1,0:T(8,128)S(1)} collective-permute-done((f32[4,64,128]{2,1,0:T(8,128)S(1)}, f32[4,64,128]{2,1,0:T(8,128)S(1)}, u32[]{:S(2)}, u32[]{:S(2)}) %collective-permute-start.12) | collective-permute-done | bytes 131104 | tf_op jit(solution)/shard_map/ppermute | solution.py:434
  90.2 6.0 %shard_map.98 = (f32[2,64,64,128]{3,2,1,0:T(8,128)}, f32[4,64,128]{2,1,0:T(8,128)}) custom-call(s32[134]{0:T(256)} %pad_add_fusion.pos_ref, f32[2,64,64,128]{3,2,1,0:T(8,128)} %get-tuple-element.37.refs_0_, f32[2,64,64,128]{3,2,1,0:T(8,128)} %get-tuple-element.38.refs_1_, f32[4,64,128]{2,1,0:T(8,128)} %multiply_add_fusion.3.refs_2_, ...), custom_call_target="tpu_custom_call" | custom-call | tf_op jit(solution)/shard_map/pallas_call | solution.py:299
  96.7 4.7 %collective-permute-done.13 = f32[4,64,128]{2,1,0:T(8,128)S(1)} collective-permute-done((f32[4,64,128]{2,1,0:T(8,128)}, f32[4,64,128]{2,1,0:T(8,128)S(1)}, u32[]{:S(2)}, u32[]{:S(2)}) %collective-permute-start.13) | collective-permute-done | bytes 131104 | tf_op jit(solution)/shard_map/ppermute | solution.py:434
  101.4 0.9 add.91
  102.3 2.5 %collective-permute-start.14 = (f32[4,64,128]{2,1,0:T(8,128)S(1)}, f32[4,64,128]{2,1,0:T(8,128)S(1)}, u32[]{:S(2)}, u32[]{:S(2)}) collective-permute-start(f32[4,64,128]{2,1,0:T(8,128)S(1)} %add.91), channel_id=1, source_target_pairs={{0,16},{8,24},{16,0},{24,8},{1,17},{9,25},{17,1},{25,9},{2,18},{10... | collective-permute-start | bytes 393224 | tf_op jit(solution)/shard_map/ppermute | solution.py:434
  104.8 4.9 %collective-permute-done.14 = f32[4,64,128]{2,1,0:T(8,128)S(1)} collective-permute-done((f32[4,64,128]{2,1,0:T(8,128)S(1)}, f32[4,64,128]{2,1,0:T(8,128)S(1)}, u32[]{:S(2)}, u32[]{:S(2)}) %collective-permute-start.14) | collective-permute-done | bytes 131104 | tf_op jit(solution)/shard_map/ppermute | solution.py:434
  110.3 9.7 %shard_map.99 = (f32[2,64,64,128]{3,2,1,0:T(8,128)}, f32[2,64,64,128]{3,2,1,0:T(8,128)}, f32[2,64,128]{2,1,0:T(8,128)}, f32[4,64,128]{2,1,0:T(8,128)}) custom-call(s32[134]{0:T(256)} %pad_add_fusion.pos_ref, f32[4,64,128]{2,1,0:T(8,128)} %get-tuple-element.52.refs_0_, f32[2,64,64,128]{3,2,1,0:T(8,128)} %get-tuple-element.43.refs_1_, ...), custom_call_target="tpu_custom_call" | custom-call | tf_op jit(solution)/shard_map/pallas_call | solution.py:299
  120.1 1.5 collective-permute-done.15
  121.6 1.0 multiply_add_fusion.2
  122.6 1.1 collective-permute-start.16
  124.6 3.6 %collective-permute-done.16 = f32[4,64,128]{2,1,0:T(8,128)S(1)} collective-permute-done((f32[4,64,128]{2,1,0:T(8,128)S(1)}, f32[4,64,128]{2,1,0:T(8,128)S(1)}, u32[]{:S(2)}, u32[]{:S(2)}) %collective-permute-start.16) | collective-permute-done | bytes 131104 | tf_op jit(solution)/shard_map/ppermute | solution.py:434
  128.4 1.5 %collective-permute-start.17 = (f32[4,64,128]{2,1,0:T(8,128)S(1)}, f32[4,64,128]{2,1,0:T(8,128)S(1)}, u32[]{:S(2)}, u32[]{:S(2)}) collective-permute-start(f32[4,64,128]{2,1,0:T(8,128)S(1)} %multiply_add_fusion.1), channel_id=1, source_target_pairs={{0,4},{1,5},{2,6},{3,7},{4,0},{5,1},{6,2},{7,3},{8,12},{9,13},{10,... | collective-permute-start | bytes 393224 | tf_op jit(solution)/shard_map/ppermute | solution.py:434
  130.1 1.9 %collective-permute-start.9 = (f32[4,64,128]{2,1,0:T(8,128)S(1)}, f32[4,64,128]{2,1,0:T(8,128)S(1)}, u32[]{:S(2)}, u32[]{:S(2)}) collective-permute-start(f32[4,64,128]{2,1,0:T(8,128)S(1)} %add.83), channel_id=1, source_target_pairs={{0,16},{8,24},{16,0},{24,8},{1,17},{9,25},{17,1},{25,9},{2,18},{10... | collective-permute-start | bytes 393224 | tf_op jit(solution)/shard_map/ppermute | solution.py:434
  132.0 1.4 collective-permute-done.17
  133.4 0.9 multiply_add_fusion.refs_2_
  134.3 4.9 %shard_map.100 = f32[4,64,128]{2,1,0:T(8,128)} custom-call(s32[134]{0:T(256)} %pad_add_fusion.pos_ref, f32[2,64,64,128]{3,2,1,0:T(8,128)} %get-tuple-element.46.refs_0_, f32[2,64,64,128]{3,2,1,0:T(8,128)} %get-tuple-element.47.refs_1_, f32[4,64,128]{2,1,0:T(8,128)} %multiply_add_fusion.refs_2_, f32[2,64,128]{2,1,0:T(8,128)} %get-tuple-element.49.refs_3_, ...), custom_call_target="tpu_custom_call" | custom-call | tf_op jit(solution)/shard_map/pallas_call | solution.py:299
  139.3 1.0 reduce_sum.52
  140.4 1.4 collective-permute-start.18
  142.6 3.3 %reduce_sum.48 = f32[2,64,64]{2,1,0:T(8,128)S(1)} reduce(f32[2,64,64,128]{3,2,1,0:T(8,128)} %get-tuple-element.45, f32[]{:T(128)} %constant.7.clone.1), dimensions={3}, to_apply=%region_3.4 | reduce | flops 1040384 | bytes 4227076 | tf_op jit(solution)/shard_map/reduce_sum | solution.py:576
  145.9 3.1 %collective-permute-start.19 = (f32[2,128]{1,0:T(2,128)S(1)}, f32[2,128]{1,0:T(2,128)S(1)}, u32[]{:S(2)}, u32[]{:S(2)}) collective-permute-start(f32[2,128]{1,0:T(2,128)S(1)} %add.99), channel_id=1, source_target_pairs={{0,16},{8,24},{16,0},{24,8},{1,17},{9,25},{17,1},{25,9},{2,18},{10... | collective-permute-start | bytes 3080 | tf_op jit(solution)/shard_map/ppermute | solution.py:434
  (69 shorter events, 15.3 us)
Async XLA Ops:
  7.0 10.8 %copy-start.3 = (s32[256,128]{1,0:T(8,128)S(1)}, s32[256,128]{1,0:T(8,128)}, u32[]{:S(2)}) copy-start(s32[256,128]{1,0:T(8,128)} %param.11) | copy-start | bytes 393220
  7.0 14.5 %copy-start.4 = (s32[1,1,2,2]{3,2,1,0:T(2,128)S(1)}, s32[1,1,2,2]{3,2,1,0:T(2,128)}, u32[]{:S(2)}) copy-start(s32[1,1,2,2]{3,2,1,0:T(2,128)} %param.8) | copy-start | bytes 52
  17.6 1.1 collective-permute-start
  18.8 4.3 %collective-permute-start.1 = (f32[2,128]{1,0:T(2,128)S(1)}, f32[2,128]{1,0:T(2,128)S(1)}, u32[]{:S(2)}, u32[]{:S(2)}) collective-permute-start(f32[2,128]{1,0:T(2,128)S(1)} %mul.88), channel_id=1, source_target_pairs={{0,2},{1,3},{2,0},{3,1},{4,6},{5,7},{6,4},{7,5},{8,10},{9,11},{10,... | collective-permute-start | bytes 3080 | tf_op jit(solution)/shard_map/ppermute | solution.py:434
  23.1 3.7 %collective-permute-start.2 = (f32[2,128]{1,0:T(2,128)S(1)}, f32[2,128]{1,0:T(2,128)S(1)}, u32[]{:S(2)}, u32[]{:S(2)}) collective-permute-start(f32[2,128]{1,0:T(2,128)S(1)} %mul.90), channel_id=1, source_target_pairs={{0,4},{1,5},{2,6},{3,7},{4,0},{5,1},{6,2},{7,3},{8,12},{9,13},{10,... | collective-permute-start | bytes 3080 | tf_op jit(solution)/shard_map/ppermute | solution.py:434
  33.2 5.2 %collective-permute-start.3 = (f32[4,64,128]{2,1,0:T(8,128)}, f32[4,64,128]{2,1,0:T(8,128)S(1)}, u32[]{:S(2)}, u32[]{:S(2)}) collective-permute-start(f32[4,64,128]{2,1,0:T(8,128)} %get-tuple-element.31), channel_id=1, source_target_pairs={{0,8},{8,0},{16,24},{24,16},{1,9},{9,1},{17,25},{25,17},{2,10},{10... | collective-permute-start | bytes 393224 | tf_op jit(solution)/shard_map/ppermute | solution.py:434
  39.3 6.0 %collective-permute-start.4 = (f32[4,64,128]{2,1,0:T(8,128)S(1)}, f32[4,64,128]{2,1,0:T(8,128)S(1)}, u32[]{:S(2)}, u32[]{:S(2)}) collective-permute-start(f32[4,64,128]{2,1,0:T(8,128)S(1)} %add.80), channel_id=1, source_target_pairs={{0,16},{8,24},{16,0},{24,8},{1,17},{9,25},{17,1},{25,9},{2,18},{10... | collective-permute-start | bytes 393224 | tf_op jit(solution)/shard_map/ppermute | solution.py:434
  53.0 1.6 %collective-permute-start.5 = (f32[4,64,128]{2,1,0:T(8,128)}, f32[4,64,128]{2,1,0:T(8,128)S(1)}, u32[]{:S(2)}, u32[]{:S(2)}) collective-permute-start(f32[4,64,128]{2,1,0:T(8,128)} %get-tuple-element.35), channel_id=1, source_target_pairs={{0,1},{1,0},{2,3},{3,2},{4,5},{5,4},{6,7},{7,6},{8,9},{9,8},{10,11... | collective-permute-start | bytes 393224 | tf_op jit(solution)/shard_map/ppermute | solution.py:434
  55.5 6.9 %collective-permute-start.6 = (f32[4,64,128]{2,1,0:T(8,128)S(1)}, f32[4,64,128]{2,1,0:T(8,128)S(1)}, u32[]{:S(2)}, u32[]{:S(2)}) collective-permute-start(f32[4,64,128]{2,1,0:T(8,128)S(1)} %mul.92), channel_id=1, source_target_pairs={{0,2},{1,3},{2,0},{3,1},{4,6},{5,7},{6,4},{7,5},{8,10},{9,11},{10,... | collective-permute-start | bytes 393224 | tf_op jit(solution)/shard_map/ppermute | solution.py:434
  62.4 5.3 %collective-permute-start.7 = (f32[4,64,128]{2,1,0:T(8,128)S(1)}, f32[4,64,128]{2,1,0:T(8,128)S(1)}, u32[]{:S(2)}, u32[]{:S(2)}) collective-permute-start(f32[4,64,128]{2,1,0:T(8,128)S(1)} %mul.94), channel_id=1, source_target_pairs={{0,4},{1,5},{2,6},{3,7},{4,0},{5,1},{6,2},{7,3},{8,12},{9,13},{10,... | collective-permute-start | bytes 393224 | tf_op jit(solution)/shard_map/ppermute | solution.py:434
  68.4 9.5 %copy-start.1 = (f32[4,64,128]{2,1,0:T(8,128)S(1)}, f32[4,64,128]{2,1,0:T(8,128)}, u32[]{:S(2)}) copy-start(f32[4,64,128]{2,1,0:T(8,128)} %get-tuple-element.35) | copy-start | bytes 393220
  76.3 1.6 %collective-permute-start.10 = (f32[4,64,128]{2,1,0:T(8,128)}, f32[4,64,128]{2,1,0:T(8,128)S(1)}, u32[]{:S(2)}, u32[]{:S(2)}) collective-permute-start(f32[4,64,128]{2,1,0:T(8,128)} %get-tuple-element.39), channel_id=1, source_target_pairs={{0,1},{1,0},{2,3},{3,2},{4,5},{5,4},{6,7},{7,6},{8,9},{9,8},{10,11... | collective-permute-start | bytes 393224 | tf_op jit(solution)/shard_map/ppermute | solution.py:434
  78.9 5.6 %collective-permute-start.11 = (f32[4,64,128]{2,1,0:T(8,128)S(1)}, f32[4,64,128]{2,1,0:T(8,128)S(1)}, u32[]{:S(2)}, u32[]{:S(2)}) collective-permute-start(f32[4,64,128]{2,1,0:T(8,128)S(1)} %multiply_add_fusion.5), channel_id=1, source_target_pairs={{0,2},{1,3},{2,0},{3,1},{4,6},{5,7},{6,4},{7,5},{8,10},{9,11},{10,... | collective-permute-start | bytes 393224 | tf_op jit(solution)/shard_map/ppermute | solution.py:434
  84.5 5.0 %collective-permute-start.12 = (f32[4,64,128]{2,1,0:T(8,128)S(1)}, f32[4,64,128]{2,1,0:T(8,128)S(1)}, u32[]{:S(2)}, u32[]{:S(2)}) collective-permute-start(f32[4,64,128]{2,1,0:T(8,128)S(1)} %multiply_add_fusion.4), channel_id=1, source_target_pairs={{0,4},{1,5},{2,6},{3,7},{4,0},{5,1},{6,2},{7,3},{8,12},{9,13},{10,... | collective-permute-start | bytes 393224 | tf_op jit(solution)/shard_map/ppermute | solution.py:434
  96.2 5.2 %collective-permute-start.13 = (f32[4,64,128]{2,1,0:T(8,128)}, f32[4,64,128]{2,1,0:T(8,128)S(1)}, u32[]{:S(2)}, u32[]{:S(2)}) collective-permute-start(f32[4,64,128]{2,1,0:T(8,128)} %get-tuple-element.42), channel_id=1, source_target_pairs={{0,8},{8,0},{16,24},{24,16},{1,9},{9,1},{17,25},{25,17},{2,10},{10... | collective-permute-start | bytes 393224 | tf_op jit(solution)/shard_map/ppermute | solution.py:434
  102.3 7.3 %collective-permute-start.14 = (f32[4,64,128]{2,1,0:T(8,128)S(1)}, f32[4,64,128]{2,1,0:T(8,128)S(1)}, u32[]{:S(2)}, u32[]{:S(2)}) collective-permute-start(f32[4,64,128]{2,1,0:T(8,128)S(1)} %add.91), channel_id=1, source_target_pairs={{0,16},{8,24},{16,0},{24,8},{1,17},{9,25},{17,1},{25,9},{2,18},{10... | collective-permute-start | bytes 393224 | tf_op jit(solution)/shard_map/ppermute | solution.py:434
  110.3 13.4 %copy-start = (f32[256,128]{1,0:T(8,128)S(1)}, f32[256,128]{1,0:T(8,128)}, u32[]{:S(2)}) copy-start(f32[256,128]{1,0:T(8,128)} %param.13) | copy-start | bytes 393220
  110.3 13.7 %copy-start.2 = (f32[4,64,128]{2,1,0:T(8,128)S(1)}, f32[4,64,128]{2,1,0:T(8,128)}, u32[]{:S(2)}) copy-start(f32[4,64,128]{2,1,0:T(8,128)} %get-tuple-element.36) | copy-start | bytes 393220
  120.0 1.6 %collective-permute-start.15 = (f32[4,64,128]{2,1,0:T(8,128)}, f32[4,64,128]{2,1,0:T(8,128)S(1)}, u32[]{:S(2)}, u32[]{:S(2)}) collective-permute-start(f32[4,64,128]{2,1,0:T(8,128)} %get-tuple-element.48), channel_id=1, source_target_pairs={{0,1},{1,0},{2,3},{3,2},{4,5},{5,4},{6,7},{7,6},{8,9},{9,8},{10,11... | collective-permute-start | bytes 393224 | tf_op jit(solution)/shard_map/ppermute | solution.py:434
  122.6 5.6 %collective-permute-start.16 = (f32[4,64,128]{2,1,0:T(8,128)S(1)}, f32[4,64,128]{2,1,0:T(8,128)S(1)}, u32[]{:S(2)}, u32[]{:S(2)}) collective-permute-start(f32[4,64,128]{2,1,0:T(8,128)S(1)} %multiply_add_fusion.2), channel_id=1, source_target_pairs={{0,2},{1,3},{2,0},{3,1},{4,6},{5,7},{6,4},{7,5},{8,10},{9,11},{10,... | collective-permute-start | bytes 393224 | tf_op jit(solution)/shard_map/ppermute | solution.py:434
  124.0 6.1 %collective-permute-start.8 = (f32[4,64,128]{2,1,0:T(8,128)S(1)}, f32[4,64,128]{2,1,0:T(8,128)S(1)}, u32[]{:S(2)}, u32[]{:S(2)}) collective-permute-start(f32[4,64,128]{2,1,0:T(8,128)S(1)} %copy-done.2), channel_id=1, source_target_pairs={{0,8},{8,0},{16,24},{24,16},{1,9},{9,1},{17,25},{25,17},{2,10},{10... | collective-permute-start | bytes 393224 | tf_op jit(solution)/shard_map/ppermute | solution.py:434
  128.4 5.0 %collective-permute-start.17 = (f32[4,64,128]{2,1,0:T(8,128)S(1)}, f32[4,64,128]{2,1,0:T(8,128)S(1)}, u32[]{:S(2)}, u32[]{:S(2)}) collective-permute-start(f32[4,64,128]{2,1,0:T(8,128)S(1)} %multiply_add_fusion.1), channel_id=1, source_target_pairs={{0,4},{1,5},{2,6},{3,7},{4,0},{5,1},{6,2},{7,3},{8,12},{9,13},{10,... | collective-permute-start | bytes 393224 | tf_op jit(solution)/shard_map/ppermute | solution.py:434
  130.1 11.7 %collective-permute-start.9 = (f32[4,64,128]{2,1,0:T(8,128)S(1)}, f32[4,64,128]{2,1,0:T(8,128)S(1)}, u32[]{:S(2)}, u32[]{:S(2)}) collective-permute-start(f32[4,64,128]{2,1,0:T(8,128)S(1)} %add.83), channel_id=1, source_target_pairs={{0,16},{8,24},{16,0},{24,8},{1,17},{9,25},{17,1},{25,9},{2,18},{10... | collective-permute-start | bytes 393224 | tf_op jit(solution)/shard_map/ppermute | solution.py:434
  140.4 5.5 %collective-permute-start.18 = (f32[2,128]{1,0:T(2,128)S(1)}, f32[2,128]{1,0:T(2,128)S(1)}, u32[]{:S(2)}, u32[]{:S(2)}) collective-permute-start(f32[2,128]{1,0:T(2,128)S(1)} %reshape.64), channel_id=1, source_target_pairs={{0,8},{8,0},{16,24},{24,16},{1,9},{9,1},{17,25},{25,17},{2,10},{10... | collective-permute-start | bytes 3080 | tf_op jit(solution)/shard_map/ppermute | solution.py:434
  145.9 4.7 %collective-permute-start.19 = (f32[2,128]{1,0:T(2,128)S(1)}, f32[2,128]{1,0:T(2,128)S(1)}, u32[]{:S(2)}, u32[]{:S(2)}) collective-permute-start(f32[2,128]{1,0:T(2,128)S(1)} %add.99), channel_id=1, source_target_pairs={{0,16},{8,24},{16,0},{24,8},{1,17},{9,25},{17,1},{25,9},{2,18},{10... | collective-permute-start | bytes 3080 | tf_op jit(solution)/shard_map/ppermute | solution.py:434

commit v19 on v13

--- a/solution.py
+++ b/solution.py
@@ -193,7 +193,8 @@
         x = ba * f
         low = 1.0 - DAMP * x
         high = 1.0 + DAMP * x
-        ratio = jnp.log(high / low)
+        inverse = 1.0 / (low * high)
+        ratio = jnp.log(high * high * inverse)
         if emit_column:
             u = ew_ref[0, c] * ratio
             col_ref[q, pl.ds(c, 1), :] = col_ref[q, pl.ds(c, 1), :] + jnp.sum(u, axis=0, keepdims=True)
@@ -201,7 +202,7 @@
         if has_acc:
             gw = gw + acc_ref[0, c]
         gw_ref[0, c] = gw
-        gx = gu * ew_ref[0, c] * ((2.0 * DAMP) / (low * high))
+        gx = gu * ew_ref[0, c] * ((2.0 * DAMP) * inverse)
         gba_ref[0, c] = gx * f
         return total + gx * ba
 

time: 152 us -> 152 us (level)
  starting transfers between devices: 33.4 us -> 27.7 us
  waiting for transfers between devices: 42.5 us -> 47.4 us
    ppermute x20, starting transfers between devices: 33.4 us -> 27.7 us  [_swap(): return lax.ppermute(value, axis, perm)]
    ppermute x20, waiting for transfers between devices: 42.5 us -> 47.4 us  [_swap(): return lax.ppermute(value, axis, perm)]
where the time goes in v19:
time: 152 us; the launch traced here: 151 us
  waiting for transfers between devices  47.4 us (31%)
  Pallas kernels  46.7 us (31%)
  starting transfers between devices  27.7 us (18%)
  other arithmetic  16.5 us (11%)
  local copies, waits for them, and re-layouts  11.1 us (7%)
    ppermute x20, waiting for transfers between devices, _swap(): return lax.ppermute(value, axis, perm)  47.4 us
    pallas_call x7, Pallas kernels, _call(): pl.pallas_call(kernel, grid_spec=grid_spec, out_shape=[o for kind, o in o...  46.7 us
    ppermute x20, starting transfers between devices, _swap(): return lax.ppermute(value, axis, perm)  27.7 us
    reduce_sum x1, other arithmetic, body(): jnp.sum(acc, axis=3)  3.34 us
  transfers between devices with their start and end apart: 20, of which 17 were waited for; matrix products, arithmetic and copies ran while one was open for 6% of the time, Pallas kernels for 3%

profile of v19, /device:TPU:0, one launch (start us, length us, event | category | flops | bytes accessed | tf_op | source)
XLA Modules:
  0.0 151.2 jit_solution(10823332801033947917)
XLA Ops:
  0.6 0.9 squeeze.10
  2.7 1.0 sort.17
  3.8 0.8 reshape_squeeze.9
  4.6 0.9 reshape_squeeze.10
  7.0 2.6 %broadcast_in_dim.91.refs_1_.ew_ref.refs_2_.refs_5_.refs_6_ = f32[2,64,64,128]{3,2,1,0:T(8,128)} broadcast(f32[2,64,64]{2,1,0:T(8,128)S(1)} %multiply_bitcast_fusion), dimensions={0,1,2} | broadcast | bytes 4227072 | tf_op jit(solution)/shard_map/broadcast_in_dim | solution.py:515
  10.4 6.1 %shard_map.94 = (f32[2,64,64,128]{3,2,1,0:T(8,128)}, f32[2,64,64,128]{3,2,1,0:T(8,128)}, f32[2,64,128]{2,1,0:T(8,128)}, f32[4,64,128]{2,1,0:T(8,128)}, f32[2,64,128]{2,1,0:T(8,128)}) custom-call(s32[134]{0:T(256)} %pad_add_fusion.pos_ref, f32[4,64,128]{2,1,0:T(8,128)} %add.79.refs_0_, f32[2,64,64,128]{3,2,1,0:T(8,128)} %broadcast_in_dim.91.refs_1_.ew_ref.refs_2_.refs_5_.refs_6_), custom_call_target="tpu_custom_call" | custom-call | tf_op jit(solution)/shard_map/pallas_call | solution.py:289
  16.5 1.0 slice_reduce_fusion
  18.0 0.8 collective-permute-done
  18.8 2.8 %collective-permute-start.1 = (f32[2,128]{1,0:T(2,128)S(1)}, f32[2,128]{1,0:T(2,128)S(1)}, u32[]{:S(2)}, u32[]{:S(2)}) collective-permute-start(f32[2,128]{1,0:T(2,128)S(1)} %mul.88), channel_id=1, source_target_pairs={{0,2},{1,3},{2,0},{3,1},{4,6},{5,7},{6,4},{7,5},{8,10},{9,11},{10,... | collective-permute-start | bytes 3080 | tf_op jit(solution)/shard_map/ppermute | solution.py:420
  21.8 1.4 collective-permute-done.1
  23.2 2.0 %collective-permute-start.2 = (f32[2,128]{1,0:T(2,128)S(1)}, f32[2,128]{1,0:T(2,128)S(1)}, u32[]{:S(2)}, u32[]{:S(2)}) collective-permute-start(f32[2,128]{1,0:T(2,128)S(1)} %mul.90), channel_id=1, source_target_pairs={{0,4},{1,5},{2,6},{3,7},{4,0},{5,1},{6,2},{7,3},{8,12},{9,13},{10,... | collective-permute-start | bytes 3080 | tf_op jit(solution)/shard_map/ppermute | solution.py:420
  27.7 5.6 %shard_map.95 = (f32[2,64,64,128]{3,2,1,0:T(8,128)}, f32[4,64,128]{2,1,0:T(8,128)}) custom-call(s32[134]{0:T(256)} %pad_add_fusion.pos_ref, f32[2,64,64,128]{3,2,1,0:T(8,128)} %get-tuple-element.28.ba_ref.refs_2_, f32[2,64,128]{2,1,0:T(8,128)} %copy.30.sign_ref.refs_2_.refs_3_, f32[2,64,128]{2,1,0:T(8,128)} %get-tuple-element.29.here_ref.refs_4_.refs_5_, ...), custom_call_target="tpu_custom_call" | custom-call | tf_op jit(solution)/shard_map/pallas_call | solution.py:289
  33.2 2.0 %collective-permute-start.3 = (f32[4,64,128]{2,1,0:T(8,128)}, f32[4,64,128]{2,1,0:T(8,128)S(1)}, u32[]{:S(2)}, u32[]{:S(2)}) collective-permute-start(f32[4,64,128]{2,1,0:T(8,128)} %get-tuple-element.31), channel_id=1, source_target_pairs={{0,8},{8,0},{16,24},{24,16},{1,9},{9,1},{17,25},{25,17},{2,10},{10... | collective-permute-start | bytes 393224 | tf_op jit(solution)/shard_map/ppermute | solution.py:420
  35.2 3.2 %collective-permute-done.3 = f32[4,64,128]{2,1,0:T(8,128)S(1)} collective-permute-done((f32[4,64,128]{2,1,0:T(8,128)}, f32[4,64,128]{2,1,0:T(8,128)S(1)}, u32[]{:S(2)}, u32[]{:S(2)}) %collective-permute-start.3) | collective-permute-done | bytes 131104 | tf_op jit(solution)/shard_map/ppermute | solution.py:420
  38.4 0.9 add.80
  39.4 3.2 %collective-permute-start.4 = (f32[4,64,128]{2,1,0:T(8,128)S(1)}, f32[4,64,128]{2,1,0:T(8,128)S(1)}, u32[]{:S(2)}, u32[]{:S(2)}) collective-permute-start(f32[4,64,128]{2,1,0:T(8,128)S(1)} %add.80), channel_id=1, source_target_pairs={{0,16},{8,24},{16,0},{24,8},{1,17},{9,25},{17,1},{25,9},{2,18},{10... | collective-permute-start | bytes 393224 | tf_op jit(solution)/shard_map/ppermute | solution.py:420
  42.5 4.4 %collective-permute-done.4 = f32[4,64,128]{2,1,0:T(8,128)S(1)} collective-permute-done((f32[4,64,128]{2,1,0:T(8,128)S(1)}, f32[4,64,128]{2,1,0:T(8,128)S(1)}, u32[]{:S(2)}, u32[]{:S(2)}) %collective-permute-start.4) | collective-permute-done | bytes 131104 | tf_op jit(solution)/shard_map/ppermute | solution.py:420
  47.6 6.8 %shard_map.96 = (f32[2,64,64,128]{3,2,1,0:T(8,128)}, f32[2,64,64,128]{3,2,1,0:T(8,128)}, f32[2,64,128]{2,1,0:T(8,128)}, f32[4,64,128]{2,1,0:T(8,128)}, f32[2,64,128]{2,1,0:T(8,128)}) custom-call(s32[134]{0:T(256)} %pad_add_fusion.pos_ref, f32[4,64,128]{2,1,0:T(8,128)} %add_add_fusion.1.refs_0_, f32[2,64,64,128]{3,2,1,0:T(8,128)} %get-tuple-element.32.refs_1_, ...), custom_call_target="tpu_custom_call" | custom-call | tf_op jit(solution)/shard_map/pallas_call | solution.py:289
  54.5 1.5 %collective-permute-done.5 = f32[4,64,128]{2,1,0:T(8,128)S(1)} collective-permute-done((f32[4,64,128]{2,1,0:T(8,128)}, f32[4,64,128]{2,1,0:T(8,128)S(1)}, u32[]{:S(2)}, u32[]{:S(2)}) %collective-permute-start.5) | collective-permute-done | bytes 131104 | tf_op jit(solution)/shard_map/ppermute | solution.py:420
  56.0 0.9 mul.92
  57.0 2.6 %collective-permute-start.6 = (f32[4,64,128]{2,1,0:T(8,128)S(1)}, f32[4,64,128]{2,1,0:T(8,128)S(1)}, u32[]{:S(2)}, u32[]{:S(2)}) collective-permute-start(f32[4,64,128]{2,1,0:T(8,128)S(1)} %mul.92), channel_id=1, source_target_pairs={{0,2},{1,3},{2,0},{3,1},{4,6},{5,7},{6,4},{7,5},{8,10},{9,11},{10,... | collective-permute-start | bytes 393224 | tf_op jit(solution)/shard_map/ppermute | solution.py:420
  59.5 3.8 %collective-permute-done.6 = f32[4,64,128]{2,1,0:T(8,128)S(1)} collective-permute-done((f32[4,64,128]{2,1,0:T(8,128)S(1)}, f32[4,64,128]{2,1,0:T(8,128)S(1)}, u32[]{:S(2)}, u32[]{:S(2)}) %collective-permute-start.6) | collective-permute-done | bytes 131104 | tf_op jit(solution)/shard_map/ppermute | solution.py:420
  63.4 1.5 collective-permute-start.7
  64.9 3.6 %collective-permute-done.7 = f32[4,64,128]{2,1,0:T(8,128)S(1)} collective-permute-done((f32[4,64,128]{2,1,0:T(8,128)S(1)}, f32[4,64,128]{2,1,0:T(8,128)S(1)}, u32[]{:S(2)}, u32[]{:S(2)}) %collective-permute-start.7) | collective-permute-done | bytes 131104 | tf_op jit(solution)/shard_map/ppermute | solution.py:420
  69.2 7.9 %shard_map.97 = (f32[2,64,64,128]{3,2,1,0:T(8,128)}, f32[2,64,64,128]{3,2,1,0:T(8,128)}, f32[2,64,128]{2,1,0:T(8,128)}, f32[4,64,128]{2,1,0:T(8,128)}, f32[4,64,128]{2,1,0:T(8,128)}) custom-call(s32[134]{0:T(256)} %pad_add_fusion.pos_ref, f32[4,64,128]{2,1,0:T(8,128)} %bitcast.15, f32[2,64,64,128]{3,2,1,0:T(8,128)} %get-tuple-element.33.refs_1_, ...), custom_call_target="tpu_custom_call" | custom-call | tf_op jit(solution)/shard_map/pallas_call | solution.py:289
  77.1 1.5 %collective-permute-done.10 = f32[4,64,128]{2,1,0:T(8,128)S(1)} collective-permute-done((f32[4,64,128]{2,1,0:T(8,128)}, f32[4,64,128]{2,1,0:T(8,128)S(1)}, u32[]{:S(2)}, u32[]{:S(2)}) %collective-permute-start.10) | collective-permute-done | bytes 131104 | tf_op jit(solution)/shard_map/ppermute | solution.py:420
  78.6 0.9 multiply_add_fusion.5
  79.6 1.8 %collective-permute-start.11 = (f32[4,64,128]{2,1,0:T(8,128)S(1)}, f32[4,64,128]{2,1,0:T(8,128)S(1)}, u32[]{:S(2)}, u32[]{:S(2)}) collective-permute-start(f32[4,64,128]{2,1,0:T(8,128)S(1)} %multiply_add_fusion.5), channel_id=1, source_target_pairs={{0,2},{1,3},{2,0},{3,1},{4,6},{5,7},{6,4},{7,5},{8,10},{9,11},{10,... | collective-permute-start | bytes 393224 | tf_op jit(solution)/shard_map/ppermute | solution.py:420
  81.4 3.8 %collective-permute-done.11 = f32[4,64,128]{2,1,0:T(8,128)S(1)} collective-permute-done((f32[4,64,128]{2,1,0:T(8,128)S(1)}, f32[4,64,128]{2,1,0:T(8,128)S(1)}, u32[]{:S(2)}, u32[]{:S(2)}) %collective-permute-start.11) | collective-permute-done | bytes 131104 | tf_op jit(solution)/shard_map/ppermute | solution.py:420
  85.2 1.3 collective-permute-start.12
  86.6 3.7 %collective-permute-done.12 = f32[4,64,128]{2,1,0:T(8,128)S(1)} collective-permute-done((f32[4,64,128]{2,1,0:T(8,128)S(1)}, f32[4,64,128]{2,1,0:T(8,128)S(1)}, u32[]{:S(2)}, u32[]{:S(2)}) %collective-permute-start.12) | collective-permute-done | bytes 131104 | tf_op jit(solution)/shard_map/ppermute | solution.py:420
  91.0 5.9 %shard_map.98 = (f32[2,64,64,128]{3,2,1,0:T(8,128)}, f32[4,64,128]{2,1,0:T(8,128)}) custom-call(s32[134]{0:T(256)} %pad_add_fusion.pos_ref, f32[2,64,64,128]{3,2,1,0:T(8,128)} %get-tuple-element.37.refs_0_, f32[2,64,64,128]{3,2,1,0:T(8,128)} %get-tuple-element.38.refs_1_, f32[4,64,128]{2,1,0:T(8,128)} %multiply_add_fusion.3.refs_2_, ...), custom_call_target="tpu_custom_call" | custom-call | tf_op jit(solution)/shard_map/pallas_call | solution.py:289
  96.8 5.2 %collective-permute-done.13 = f32[4,64,128]{2,1,0:T(8,128)S(1)} collective-permute-done((f32[4,64,128]{2,1,0:T(8,128)}, f32[4,64,128]{2,1,0:T(8,128)S(1)}, u32[]{:S(2)}, u32[]{:S(2)}) %collective-permute-start.13) | collective-permute-done | bytes 131104 | tf_op jit(solution)/shard_map/ppermute | solution.py:420
  102.0 0.9 add.91
  102.9 1.6 %collective-permute-start.14 = (f32[4,64,128]{2,1,0:T(8,128)S(1)}, f32[4,64,128]{2,1,0:T(8,128)S(1)}, u32[]{:S(2)}, u32[]{:S(2)}) collective-permute-start(f32[4,64,128]{2,1,0:T(8,128)S(1)} %add.91), channel_id=1, source_target_pairs={{0,16},{8,24},{16,0},{24,8},{1,17},{9,25},{17,1},{25,9},{2,18},{10... | collective-permute-start | bytes 393224 | tf_op jit(solution)/shard_map/ppermute | solution.py:420
  104.6 5.7 %collective-permute-done.14 = f32[4,64,128]{2,1,0:T(8,128)S(1)} collective-permute-done((f32[4,64,128]{2,1,0:T(8,128)S(1)}, f32[4,64,128]{2,1,0:T(8,128)S(1)}, u32[]{:S(2)}, u32[]{:S(2)}) %collective-permute-start.14) | collective-permute-done | bytes 131104 | tf_op jit(solution)/shard_map/ppermute | solution.py:420
  111.0 9.6 %shard_map.99 = (f32[2,64,64,128]{3,2,1,0:T(8,128)}, f32[2,64,64,128]{3,2,1,0:T(8,128)}, f32[2,64,128]{2,1,0:T(8,128)}, f32[4,64,128]{2,1,0:T(8,128)}) custom-call(s32[134]{0:T(256)} %pad_add_fusion.pos_ref, f32[4,64,128]{2,1,0:T(8,128)} %get-tuple-element.52.refs_0_, f32[2,64,64,128]{3,2,1,0:T(8,128)} %get-tuple-element.43.refs_1_, ...), custom_call_target="tpu_custom_call" | custom-call | tf_op jit(solution)/shard_map/pallas_call | solution.py:289
  120.7 1.5 collective-permute-done.15
  122.1 1.0 multiply_add_fusion.2
  123.2 2.2 %collective-permute-start.16 = (f32[4,64,128]{2,1,0:T(8,128)S(1)}, f32[4,64,128]{2,1,0:T(8,128)S(1)}, u32[]{:S(2)}, u32[]{:S(2)}) collective-permute-start(f32[4,64,128]{2,1,0:T(8,128)S(1)} %multiply_add_fusion.2), channel_id=1, source_target_pairs={{0,2},{1,3},{2,0},{3,1},{4,6},{5,7},{6,4},{7,5},{8,10},{9,11},{10,... | collective-permute-start | bytes 393224 | tf_op jit(solution)/shard_map/ppermute | solution.py:420
  125.7 3.5 %collective-permute-done.16 = f32[4,64,128]{2,1,0:T(8,128)S(1)} collective-permute-done((f32[4,64,128]{2,1,0:T(8,128)S(1)}, f32[4,64,128]{2,1,0:T(8,128)S(1)}, u32[]{:S(2)}, u32[]{:S(2)}) %collective-permute-start.16) | collective-permute-done | bytes 131104 | tf_op jit(solution)/shard_map/ppermute | solution.py:420
  129.3 1.7 %collective-permute-start.17 = (f32[4,64,128]{2,1,0:T(8,128)S(1)}, f32[4,64,128]{2,1,0:T(8,128)S(1)}, u32[]{:S(2)}, u32[]{:S(2)}) collective-permute-start(f32[4,64,128]{2,1,0:T(8,128)S(1)} %multiply_add_fusion.1), channel_id=1, source_target_pairs={{0,4},{1,5},{2,6},{3,7},{4,0},{5,1},{6,2},{7,3},{8,12},{9,13},{10,... | collective-permute-start | bytes 393224 | tf_op jit(solution)/shard_map/ppermute | solution.py:420
  132.0 2.5 %collective-permute-done.17 = f32[4,64,128]{2,1,0:T(8,128)S(1)} collective-permute-done((f32[4,64,128]{2,1,0:T(8,128)S(1)}, f32[4,64,128]{2,1,0:T(8,128)S(1)}, u32[]{:S(2)}, u32[]{:S(2)}) %collective-permute-start.17) | collective-permute-done | bytes 131104 | tf_op jit(solution)/shard_map/ppermute | solution.py:420
  134.4 0.9 multiply_add_fusion.refs_2_
  135.3 4.9 %shard_map.100 = f32[4,64,128]{2,1,0:T(8,128)} custom-call(s32[134]{0:T(256)} %pad_add_fusion.pos_ref, f32[2,64,64,128]{3,2,1,0:T(8,128)} %get-tuple-element.46.refs_0_, f32[2,64,64,128]{3,2,1,0:T(8,128)} %get-tuple-element.47.refs_1_, f32[4,64,128]{2,1,0:T(8,128)} %multiply_add_fusion.refs_2_, f32[2,64,128]{2,1,0:T(8,128)} %get-tuple-element.49.refs_3_, ...), custom_call_target="tpu_custom_call" | custom-call | tf_op jit(solution)/shard_map/pallas_call | solution.py:289
  140.3 1.0 reduce_sum.52
  142.6 3.3 %reduce_sum.48 = f32[2,64,64]{2,1,0:T(8,128)S(1)} reduce(f32[2,64,64,128]{3,2,1,0:T(8,128)} %get-tuple-element.45, f32[]{:T(128)} %constant.7.clone.1), dimensions={3}, to_apply=%region_3.4 | reduce | flops 1040384 | bytes 4227076 | tf_op jit(solution)/shard_map/reduce_sum | solution.py:562
  145.9 3.1 %collective-permute-start.19 = (f32[2,128]{1,0:T(2,128)S(1)}, f32[2,128]{1,0:T(2,128)S(1)}, u32[]{:S(2)}, u32[]{:S(2)}) collective-permute-start(f32[2,128]{1,0:T(2,128)S(1)} %add.99), channel_id=1, source_target_pairs={{0,16},{8,24},{16,0},{24,8},{1,17},{9,25},{17,1},{25,9},{2,18},{10... | collective-permute-start | bytes 3080 | tf_op jit(solution)/shard_map/ppermute | solution.py:420
  (69 shorter events, 14.0 us)
Async XLA Ops:
  7.0 11.0 %copy-start.3 = (s32[256,128]{1,0:T(8,128)S(1)}, s32[256,128]{1,0:T(8,128)}, u32[]{:S(2)}) copy-start(s32[256,128]{1,0:T(8,128)} %param.11) | copy-start | bytes 393220
  7.0 14.7 %copy-start.4 = (s32[1,1,2,2]{3,2,1,0:T(2,128)S(1)}, s32[1,1,2,2]{3,2,1,0:T(2,128)}, u32[]{:S(2)}) copy-start(s32[1,1,2,2]{3,2,1,0:T(2,128)} %param.8) | copy-start | bytes 52
  17.6 1.3 collective-permute-start
  18.8 4.4 %collective-permute-start.1 = (f32[2,128]{1,0:T(2,128)S(1)}, f32[2,128]{1,0:T(2,128)S(1)}, u32[]{:S(2)}, u32[]{:S(2)}) collective-permute-start(f32[2,128]{1,0:T(2,128)S(1)} %mul.88), channel_id=1, source_target_pairs={{0,2},{1,3},{2,0},{3,1},{4,6},{5,7},{6,4},{7,5},{8,10},{9,11},{10,... | collective-permute-start | bytes 3080 | tf_op jit(solution)/shard_map/ppermute | solution.py:420
  23.2 3.6 %collective-permute-start.2 = (f32[2,128]{1,0:T(2,128)S(1)}, f32[2,128]{1,0:T(2,128)S(1)}, u32[]{:S(2)}, u32[]{:S(2)}) collective-permute-start(f32[2,128]{1,0:T(2,128)S(1)} %mul.90), channel_id=1, source_target_pairs={{0,4},{1,5},{2,6},{3,7},{4,0},{5,1},{6,2},{7,3},{8,12},{9,13},{10,... | collective-permute-start | bytes 3080 | tf_op jit(solution)/shard_map/ppermute | solution.py:420
  33.2 5.2 %collective-permute-start.3 = (f32[4,64,128]{2,1,0:T(8,128)}, f32[4,64,128]{2,1,0:T(8,128)S(1)}, u32[]{:S(2)}, u32[]{:S(2)}) collective-permute-start(f32[4,64,128]{2,1,0:T(8,128)} %get-tuple-element.31), channel_id=1, source_target_pairs={{0,8},{8,0},{16,24},{24,16},{1,9},{9,1},{17,25},{25,17},{2,10},{10... | collective-permute-start | bytes 393224 | tf_op jit(solution)/shard_map/ppermute | solution.py:420
  39.4 7.5 %collective-permute-start.4 = (f32[4,64,128]{2,1,0:T(8,128)S(1)}, f32[4,64,128]{2,1,0:T(8,128)S(1)}, u32[]{:S(2)}, u32[]{:S(2)}) collective-permute-start(f32[4,64,128]{2,1,0:T(8,128)S(1)} %add.80), channel_id=1, source_target_pairs={{0,16},{8,24},{16,0},{24,8},{1,17},{9,25},{17,1},{25,9},{2,18},{10... | collective-permute-start | bytes 393224 | tf_op jit(solution)/shard_map/ppermute | solution.py:420
  54.4 1.6 %collective-permute-start.5 = (f32[4,64,128]{2,1,0:T(8,128)}, f32[4,64,128]{2,1,0:T(8,128)S(1)}, u32[]{:S(2)}, u32[]{:S(2)}) collective-permute-start(f32[4,64,128]{2,1,0:T(8,128)} %get-tuple-element.35), channel_id=1, source_target_pairs={{0,1},{1,0},{2,3},{3,2},{4,5},{5,4},{6,7},{7,6},{8,9},{9,8},{10,11... | collective-permute-start | bytes 393224 | tf_op jit(solution)/shard_map/ppermute | solution.py:420
  57.0 6.4 %collective-permute-start.6 = (f32[4,64,128]{2,1,0:T(8,128)S(1)}, f32[4,64,128]{2,1,0:T(8,128)S(1)}, u32[]{:S(2)}, u32[]{:S(2)}) collective-permute-start(f32[4,64,128]{2,1,0:T(8,128)S(1)} %mul.92), channel_id=1, source_target_pairs={{0,2},{1,3},{2,0},{3,1},{4,6},{5,7},{6,4},{7,5},{8,10},{9,11},{10,... | collective-permute-start | bytes 393224 | tf_op jit(solution)/shard_map/ppermute | solution.py:420
  63.4 5.1 %collective-permute-start.7 = (f32[4,64,128]{2,1,0:T(8,128)S(1)}, f32[4,64,128]{2,1,0:T(8,128)S(1)}, u32[]{:S(2)}, u32[]{:S(2)}) collective-permute-start(f32[4,64,128]{2,1,0:T(8,128)S(1)} %mul.94), channel_id=1, source_target_pairs={{0,4},{1,5},{2,6},{3,7},{4,0},{5,1},{6,2},{7,3},{8,12},{9,13},{10,... | collective-permute-start | bytes 393224 | tf_op jit(solution)/shard_map/ppermute | solution.py:420
  69.2 9.5 %copy-start.1 = (f32[4,64,128]{2,1,0:T(8,128)S(1)}, f32[4,64,128]{2,1,0:T(8,128)}, u32[]{:S(2)}) copy-start(f32[4,64,128]{2,1,0:T(8,128)} %get-tuple-element.35) | copy-start | bytes 393220
  77.0 1.6 %collective-permute-start.10 = (f32[4,64,128]{2,1,0:T(8,128)}, f32[4,64,128]{2,1,0:T(8,128)S(1)}, u32[]{:S(2)}, u32[]{:S(2)}) collective-permute-start(f32[4,64,128]{2,1,0:T(8,128)} %get-tuple-element.39), channel_id=1, source_target_pairs={{0,1},{1,0},{2,3},{3,2},{4,5},{5,4},{6,7},{7,6},{8,9},{9,8},{10,11... | collective-permute-start | bytes 393224 | tf_op jit(solution)/shard_map/ppermute | solution.py:420
  79.6 5.6 %collective-permute-start.11 = (f32[4,64,128]{2,1,0:T(8,128)S(1)}, f32[4,64,128]{2,1,0:T(8,128)S(1)}, u32[]{:S(2)}, u32[]{:S(2)}) collective-permute-start(f32[4,64,128]{2,1,0:T(8,128)S(1)} %multiply_add_fusion.5), channel_id=1, source_target_pairs={{0,2},{1,3},{2,0},{3,1},{4,6},{5,7},{6,4},{7,5},{8,10},{9,11},{10,... | collective-permute-start | bytes 393224 | tf_op jit(solution)/shard_map/ppermute | solution.py:420
  85.2 5.0 %collective-permute-start.12 = (f32[4,64,128]{2,1,0:T(8,128)S(1)}, f32[4,64,128]{2,1,0:T(8,128)S(1)}, u32[]{:S(2)}, u32[]{:S(2)}) collective-permute-start(f32[4,64,128]{2,1,0:T(8,128)S(1)} %multiply_add_fusion.4), channel_id=1, source_target_pairs={{0,4},{1,5},{2,6},{3,7},{4,0},{5,1},{6,2},{7,3},{8,12},{9,13},{10,... | collective-permute-start | bytes 393224 | tf_op jit(solution)/shard_map/ppermute | solution.py:420
  96.8 5.2 %collective-permute-start.13 = (f32[4,64,128]{2,1,0:T(8,128)}, f32[4,64,128]{2,1,0:T(8,128)S(1)}, u32[]{:S(2)}, u32[]{:S(2)}) collective-permute-start(f32[4,64,128]{2,1,0:T(8,128)} %get-tuple-element.42), channel_id=1, source_target_pairs={{0,8},{8,0},{16,24},{24,16},{1,9},{9,1},{17,25},{25,17},{2,10},{10... | collective-permute-start | bytes 393224 | tf_op jit(solution)/shard_map/ppermute | solution.py:420
  102.9 7.3 %collective-permute-start.14 = (f32[4,64,128]{2,1,0:T(8,128)S(1)}, f32[4,64,128]{2,1,0:T(8,128)S(1)}, u32[]{:S(2)}, u32[]{:S(2)}) collective-permute-start(f32[4,64,128]{2,1,0:T(8,128)S(1)} %add.91), channel_id=1, source_target_pairs={{0,16},{8,24},{16,0},{24,8},{1,17},{9,25},{17,1},{25,9},{2,18},{10... | collective-permute-start | bytes 393224 | tf_op jit(solution)/shard_map/ppermute | solution.py:420
  110.9 14.4 %copy-start = (f32[256,128]{1,0:T(8,128)S(1)}, f32[256,128]{1,0:T(8,128)}, u32[]{:S(2)}) copy-start(f32[256,128]{1,0:T(8,128)} %param.13) | copy-start | bytes 393220
  111.0 14.7 %copy-start.2 = (f32[4,64,128]{2,1,0:T(8,128)S(1)}, f32[4,64,128]{2,1,0:T(8,128)}, u32[]{:S(2)}) copy-start(f32[4,64,128]{2,1,0:T(8,128)} %get-tuple-element.36) | copy-start | bytes 393220
  120.5 1.6 %collective-permute-start.15 = (f32[4,64,128]{2,1,0:T(8,128)}, f32[4,64,128]{2,1,0:T(8,128)S(1)}, u32[]{:S(2)}, u32[]{:S(2)}) collective-permute-start(f32[4,64,128]{2,1,0:T(8,128)} %get-tuple-element.48), channel_id=1, source_target_pairs={{0,1},{1,0},{2,3},{3,2},{4,5},{5,4},{6,7},{7,6},{8,9},{9,8},{10,11... | collective-permute-start | bytes 393224 | tf_op jit(solution)/shard_map/ppermute | solution.py:420
  123.2 6.0 %collective-permute-start.16 = (f32[4,64,128]{2,1,0:T(8,128)S(1)}, f32[4,64,128]{2,1,0:T(8,128)S(1)}, u32[]{:S(2)}, u32[]{:S(2)}) collective-permute-start(f32[4,64,128]{2,1,0:T(8,128)S(1)} %multiply_add_fusion.2), channel_id=1, source_target_pairs={{0,2},{1,3},{2,0},{3,1},{4,6},{5,7},{6,4},{7,5},{8,10},{9,11},{10,... | collective-permute-start | bytes 393224 | tf_op jit(solution)/shard_map/ppermute | solution.py:420
  125.7 5.5 %collective-permute-start.8 = (f32[4,64,128]{2,1,0:T(8,128)S(1)}, f32[4,64,128]{2,1,0:T(8,128)S(1)}, u32[]{:S(2)}, u32[]{:S(2)}) collective-permute-start(f32[4,64,128]{2,1,0:T(8,128)S(1)} %copy-done.2), channel_id=1, source_target_pairs={{0,8},{8,0},{16,24},{24,16},{1,9},{9,1},{17,25},{25,17},{2,10},{10... | collective-permute-start | bytes 393224 | tf_op jit(solution)/shard_map/ppermute | solution.py:420
  129.3 5.1 %collective-permute-start.17 = (f32[4,64,128]{2,1,0:T(8,128)S(1)}, f32[4,64,128]{2,1,0:T(8,128)S(1)}, u32[]{:S(2)}, u32[]{:S(2)}) collective-permute-start(f32[4,64,128]{2,1,0:T(8,128)S(1)} %multiply_add_fusion.1), channel_id=1, source_target_pairs={{0,4},{1,5},{2,6},{3,7},{4,0},{5,1},{6,2},{7,3},{8,12},{9,13},{10,... | collective-permute-start | bytes 393224 | tf_op jit(solution)/shard_map/ppermute | solution.py:420
  131.2 10.6 %collective-permute-start.9 = (f32[4,64,128]{2,1,0:T(8,128)S(1)}, f32[4,64,128]{2,1,0:T(8,128)S(1)}, u32[]{:S(2)}, u32[]{:S(2)}) collective-permute-start(f32[4,64,128]{2,1,0:T(8,128)S(1)} %add.83), channel_id=1, source_target_pairs={{0,16},{8,24},{16,0},{24,8},{1,17},{9,25},{17,1},{25,9},{2,18},{10... | collective-permute-start | bytes 393224 | tf_op jit(solution)/shard_map/ppermute | solution.py:420
  141.4 4.6 %collective-permute-start.18 = (f32[2,128]{1,0:T(2,128)S(1)}, f32[2,128]{1,0:T(2,128)S(1)}, u32[]{:S(2)}, u32[]{:S(2)}) collective-permute-start(f32[2,128]{1,0:T(2,128)S(1)} %reshape.64), channel_id=1, source_target_pairs={{0,8},{8,0},{16,24},{24,16},{1,9},{9,1},{17,25},{25,17},{2,10},{10... | collective-permute-start | bytes 3080 | tf_op jit(solution)/shard_map/ppermute | solution.py:420
  145.9 4.7 %collective-permute-start.19 = (f32[2,128]{1,0:T(2,128)S(1)}, f32[2,128]{1,0:T(2,128)S(1)}, u32[]{:S(2)}, u32[]{:S(2)}) collective-permute-start(f32[2,128]{1,0:T(2,128)S(1)} %add.99), channel_id=1, source_target_pairs={{0,16},{8,24},{16,0},{24,8},{1,17},{9,25},{17,1},{25,9},{2,18},{10... | collective-permute-start | bytes 3080 | tf_op jit(solution)/shard_map/ppermute | solution.py:420
